TPU v7x, 32 devices: a whole 2x2x4 slice. The times are simulated.
32 devices in a mesh: gx: 2 (over core), gy: 4 (over y, x), gz: 4 (over z).
Axes of the slice: x: 2, y: 2, z: 4, core: 2. Of those that a mesh axis runs over, the one named last changes fastest.
Arguments:
- labels: int32 [16, 32, 512], P('gx', 'gy', 'gz'), may hold values from 0 to 3, as said below
- mu_start: float32 [2, 16, 32, 512], P(None, 'gx', 'gy', 'gz'), may hold values from -4 to 4
- front_blocks: int32 [32, 3], replicated, may hold values from 0 to 26, as said below
Outputs:
- phases: float32 [4, 16, 32, 512], P(None, 'gx', 'gy', 'gz')
- potentials: float32 [2, 16, 32, 512], P(None, 'gx', 'gy', 'gz')
Inputs may be any that keep to these rules, and one draw needn't show every extreme that they name: `front_blocks`: each row is (x brick, y brick, z block) of one block; no block is listed twice; each lateral brick column has 4 rows with consecutive z blocks; the z blocks lie from 4 // 2 * (8) to (4 // 2 + 1) * 8 + 2, and the first blocks of all columns lie within 8 blocks of one another; one brick of 8 x 8 x 128 cells holds at most 4 listed blocks, and some brick holds exactly 4. `labels`: 0 is liquid, 1 to 3 the solids; in each lateral column the cells below a front height are solid and those above it liquid, and the front height lies inside that column's listed blocks.
All inputs are finite; a program needn't handle non-finite values.
Results may differ from a plain program's by a relative error of at most 0.00002.
Values sent between devices are 32-bit elements; how exact they have to be, the bound alone decides.
No kernel may reach another device: no remote copies, remote signals or barrier semaphores. Data moves between devices by JAX's collectives and lax.ppermute only.
A program may use at most 64 MiB of HBM per device.

v0:
```python
import jax
import jax.numpy as jnp
from jax import lax
from jax.sharding import PartitionSpec as P

BZ = 16
STEPS = 4


COMP = ((0.0, 0.0), (1.0, -0.5), (-0.5, 1.0), (-0.5, -0.5))
LATENT = (0.0, 1.0, 1.0, 1.0)
DT = 0.05
KAPPA = 1.5
WELL = 12.0
DLIQ = 3.0
DSOL = 0.3


def with_halo(block, sides, width):
    for axis, dim in sides:
        count = lax.axis_size(axis)
        forward = [(i, i + 1) for i in range(count - 1)]
        forward.append((count - 1, 0))
        backward = [(target, source) for source, target in forward]
        low = lax.ppermute(
            lax.slice_in_dim(block, block.shape[dim] - width, None, axis=dim), axis, forward
        )
        high = lax.ppermute(lax.slice_in_dim(block, 0, width, axis=dim), axis, backward)
        block = jnp.concatenate([low, block, high], axis=dim)
    return block


def shifted(shard, axis, by):
    length = lax.axis_size(axis)
    pairs = [(i, i + by) for i in range(length) if 0 <= i + by < length]
    return lax.ppermute(shard, axis, pairs)


def neighbours(padded):
    return [
        padded[..., 2:, 1:-1, 1:-1],
        padded[..., :-2, 1:-1, 1:-1],
        padded[..., 1:-1, 2:, 1:-1],
        padded[..., 1:-1, :-2, 1:-1],
        padded[..., 1:-1, 1:-1, 2:],
        padded[..., 1:-1, 1:-1, :-2],
    ]


def phase_update(padded, zglob, offset, depth):
    centre = padded[:, 1:-1, 1:-1, 1:-1]
    phi = centre[:4]
    chem = centre[4:]
    beside_all = neighbours(padded[:4])
    total = (
        beside_all[0]
        + beside_all[1]
        + beside_all[2]
        + beside_all[3]
        + beside_all[4]
        + beside_all[5]
    )
    lap = total - 6.0 * phi
    square = phi * phi
    summed = square[0] + square[1] + square[2] + square[3]
    under = 2.0 * ((zglob + offset).astype(jnp.float32) / depth - 0.5)
    rates = []
    for phase in range(4):
        psi = -(COMP[phase][0] * chem[0] + COMP[phase][1] * chem[1]) + LATENT[phase] * under
        rate = (
            KAPPA * lap[phase]
            - WELL * phi[phase] * (summed - square[phase])
            - 6.0 * phi[phase] * (1.0 - phi[phase]) * psi
        )
        rates.append(rate)
    mean_rate = (rates[0] + rates[1] + rates[2] + rates[3]) * 0.25
    return jnp.stack([phi[phase] + DT * (rates[phase] - mean_rate) for phase in range(4)])


def shape_fn(values):
    return values * values * (3.0 - 2.0 * values)


def chem_update(padded, phi_old, phi_new):
    chem = padded[4:, 1:-1, 1:-1, 1:-1]
    diffuse = DSOL + (DLIQ - DSOL) * padded[0]
    centre_d = diffuse[1:-1, 1:-1, 1:-1]
    side_d = neighbours(diffuse)
    side_m = neighbours(padded[4:])
    flux = jnp.zeros_like(chem)
    for way in range(6):
        flux = flux + 0.5 * (centre_d + side_d[way]) * (side_m[way] - chem)
    delta = shape_fn(phi_new) - shape_fn(phi_old)
    result = []
    for comp in range(2):
        change = (
            COMP[0][comp] * delta[0]
            + COMP[1][comp] * delta[1]
            + COMP[2][comp] * delta[2]
            + COMP[3][comp] * delta[3]
        )
        result.append(chem[comp] + DT * flux[comp] - change)
    return jnp.stack(result)


def shards(labels, mu_start, front_blocks):
    cells_x, cells_y, cells_z = labels.shape
    lift = cells_z // 4
    bricks_z = lax.axis_size("gz")
    depth = cells_z * bricks_z
    index_x = lax.axis_index("gx")
    index_y = lax.axis_index("gy")
    index_z = lax.axis_index("gz")
    zglob = index_z * cells_z + jnp.arange(cells_z, dtype=jnp.int32)
    per_brick = cells_z // BZ

    def close_ends(padded):
        bottom = jnp.where(index_z == 0, padded[..., 1:2], padded[..., 0:1])
        top = jnp.where(index_z == bricks_z - 1, padded[..., -2:-1], padded[..., -1:])
        return jnp.concatenate([bottom, padded[..., 1:-1], top], 3)

    matched = (
        (front_blocks[:, 0] == index_x)
        & (front_blocks[:, 1] == index_y)
        & (front_blocks[:, 2] // per_brick == index_z)
    )
    local_block = front_blocks[:, 2] - index_z * per_brick
    top_brick = index_z == bricks_z - 1
    phi_start = jnp.stack([(labels == phase).astype(jnp.float32) for phase in range(4)])
    fields = jnp.concatenate([phi_start, mu_start], 0)
    offset = 0
    for step in range(STEPS):
        if step == STEPS // 2:
            offset = lift
            incoming = shifted(fields[..., : lift + 1], "gz", -1)
            count = lift + 1
            ones = jnp.ones((1, cells_x, cells_y, count), jnp.float32)
            incoming = jnp.where(
                top_brick,
                jnp.concatenate([ones, jnp.zeros((5, cells_x, cells_y, count), jnp.float32)], 0),
                incoming,
            )
            extended = jnp.concatenate([fields[..., lift - 1 :], incoming], 3)
            fields = extended[..., 1:-1]
            padded = close_ends(with_halo(extended, (("gx", 1), ("gy", 2)), 1))
        else:
            padded = close_ends(with_halo(fields, (("gx", 1), ("gy", 2), ("gz", 3)), 1))
        hits = matched[:, None] & (
            local_block[:, None] == jnp.arange(per_brick, dtype=jnp.int32)[None, :]
        )
        block_on = jnp.any(hits, 0)
        cell_on = jnp.repeat(block_on, BZ)
        phi_new = jnp.where(
            cell_on[None, None, None, :], phase_update(padded, zglob, offset, depth), fields[:4]
        )
        mu_new = chem_update(padded, fields[:4], phi_new)
        fields = jnp.concatenate([phi_new, mu_new], 0)
    return (fields[:4], fields[4:])


def solution(mesh):
    placed = (P("gx", "gy", "gz"), P(None, "gx", "gy", "gz"), P())
    return jax.shard_map(
        shards,
        mesh=mesh,
        in_specs=placed,
        out_specs=(P(None, "gx", "gy", "gz"), P(None, "gx", "gy", "gz")),
        check_vma=False,
    )
```

profile of v0, /device:TPU:0, one launch (start us, length us, event | category | flops | bytes accessed | tf_op | source)
XLA Modules:
  0.0 123.8 jit_solution(4116414588169688014)
XLA Ops:
  0.6 0.8 convert_bitcast_fusion
  1.5 0.8 copy-done
  2.3 0.5 collective-permute-start.1
  2.9 0.7 copy-done.2
  3.7 0.3 collective-permute-done
  4.0 2.7 %collective-permute-start.3 = (f32[6,10,1,128]{3,2,1,0:T(1,128)S(1)}, f32[6,10,1,128]{3,2,1,0:T(1,128)S(1)}, u32[]{:S(2)}, u32[]{:S(2)}) collective-permute-start(f32[6,10,1,128]{3,2,1,0:T(1,128)S(1)} %get-tuple-element.82), channel_id=1, source_target_pairs={{0,4},{4,8},{8,12},{12,0},{1,5},{5,9},{9,13},{13,1},{2,6},{6,10},{... | collective-permute-start | bytes 92168 | tf_op jit(solution)/shard_map/ppermute | solution.py:25
  6.7 1.0 collective-permute-start.2
  7.9 1.7 %collective-permute-done.3 = f32[6,10,1,128]{3,2,1,0:T(1,128)S(1)} collective-permute-done((f32[6,10,1,128]{3,2,1,0:T(1,128)S(1)}, f32[6,10,1,128]{3,2,1,0:T(1,128)S(1)}, u32[]{:S(2)}, u32[]{:S(2)}) %collective-permute-start.3) | collective-permute-done | bytes 30752 | tf_op jit(solution)/shard_map/ppermute | solution.py:25
  9.6 1.1 collective-permute-done.2
  10.7 0.2 fusion.213
  10.9 3.7 %collective-permute-start.4 = (f32[6,10,10,1]{3,2,1,0:T(8,128)S(1)}, f32[6,10,10,1]{3,2,1,0:T(8,128)S(1)}, u32[]{:S(2)}, u32[]{:S(2)}) collective-permute-start(f32[6,10,10,1]{3,2,1,0:T(8,128)S(1)} %get-tuple-element.65), channel_id=1, source_target_pairs={{1,0},{2,1},{3,2},{0,3},{5,4},{6,5},{7,6},{4,7},{9,8},{10,9},{11,1... | collective-permute-start | bytes 7208 | tf_op jit(solution)/shard_map/ppermute | solution.py:28
  14.8 11.5 %collective-permute-done.4 = f32[6,10,10,1]{3,2,1,0:T(8,128)S(1)} collective-permute-done((f32[6,10,10,1]{3,2,1,0:T(8,128)S(1)}, f32[6,10,10,1]{3,2,1,0:T(8,128)S(1)}, u32[]{:S(2)}, u32[]{:S(2)}) %collective-permute-start.4) | collective-permute-done | bytes 2432 | tf_op jit(solution)/shard_map/ppermute | solution.py:28
  26.3 9.8 %collective-permute-done.5 = f32[6,10,10,1]{3,2,1,0:T(8,128)S(1)} collective-permute-done((f32[6,10,10,1]{3,2,1,0:T(8,128)S(1)}, f32[6,10,10,1]{3,2,1,0:T(8,128)S(1)}, u32[]{:S(2)}, u32[]{:S(2)}) %collective-permute-start.5) | collective-permute-done | bytes 2432 | tf_op jit(solution)/shard_map/ppermute | solution.py:25
  36.0 0.2 broadcast_select_fusion.5
  36.2 0.2 fusion.18
  36.7 0.2 fusion.11
  37.0 0.2 fusion.67
  37.3 0.5 collective-permute-start.6
  37.8 0.7 collective-permute-done.7
  38.5 0.2 collective-permute-done.6
  38.7 2.0 %collective-permute-start.9 = (f32[6,10,1,128]{3,2,1,0:T(1,128)S(1)}, f32[6,10,1,128]{3,2,1,0:T(1,128)S(1)}, u32[]{:S(2)}, u32[]{:S(2)}) collective-permute-start(f32[6,10,1,128]{3,2,1,0:T(1,128)S(1)} %get-tuple-element.80), channel_id=1, source_target_pairs={{0,4},{4,8},{8,12},{12,0},{1,5},{5,9},{9,13},{13,1},{2,6},{6,10},{... | collective-permute-start | bytes 92168 | tf_op jit(solution)/shard_map/ppermute | solution.py:25
  40.7 1.0 collective-permute-start.8
  41.7 0.3 pad_maximum_fusion.1
  42.0 1.8 %collective-permute-done.9 = f32[6,10,1,128]{3,2,1,0:T(1,128)S(1)} collective-permute-done((f32[6,10,1,128]{3,2,1,0:T(1,128)S(1)}, f32[6,10,1,128]{3,2,1,0:T(1,128)S(1)}, u32[]{:S(2)}, u32[]{:S(2)}) %collective-permute-start.9) | collective-permute-done | bytes 30752 | tf_op jit(solution)/shard_map/ppermute | solution.py:25
  43.8 0.8 collective-permute-done.8
  44.7 0.2 fusion.212
  44.9 1.8 %collective-permute-start.10 = (f32[6,10,10,1]{3,2,1,0:T(8,128)S(1)}, f32[6,10,10,1]{3,2,1,0:T(8,128)S(1)}, u32[]{:S(2)}, u32[]{:S(2)}) collective-permute-start(f32[6,10,10,1]{3,2,1,0:T(8,128)S(1)} %get-tuple-element.61), channel_id=1, source_target_pairs={{1,0},{2,1},{3,2},{0,3},{5,4},{6,5},{7,6},{4,7},{9,8},{10,9},{11,1... | collective-permute-start | bytes 7208 | tf_op jit(solution)/shard_map/ppermute | solution.py:28
  46.7 0.3 collective-permute-start.11
  47.0 11.9 %collective-permute-done.10 = f32[6,10,10,1]{3,2,1,0:T(8,128)S(1)} collective-permute-done((f32[6,10,10,1]{3,2,1,0:T(8,128)S(1)}, f32[6,10,10,1]{3,2,1,0:T(8,128)S(1)}, u32[]{:S(2)}, u32[]{:S(2)}) %collective-permute-start.10) | collective-permute-done | bytes 2432 | tf_op jit(solution)/shard_map/ppermute | solution.py:28
  58.9 9.3 %collective-permute-done.11 = f32[6,10,10,1]{3,2,1,0:T(8,128)S(1)} collective-permute-done((f32[6,10,10,1]{3,2,1,0:T(8,128)S(1)}, f32[6,10,10,1]{3,2,1,0:T(8,128)S(1)}, u32[]{:S(2)}, u32[]{:S(2)}) %collective-permute-start.11) | collective-permute-done | bytes 2432 | tf_op jit(solution)/shard_map/ppermute | solution.py:25
  68.2 0.2 broadcast_select_fusion.4
  68.4 0.1 fusion.8
  68.7 0.6 pad_maximum_fusion
  69.8 1.4 %collective-permute-start.12 = (f32[6,8,8,33]{3,2,1,0:T(8,128)S(1)}, f32[6,8,8,33]{3,2,1,0:T(8,128)S(1)}, u32[]{:S(2)}, u32[]{:S(2)}) collective-permute-start(f32[6,8,8,33]{3,2,1,0:T(8,128)S(1)} %bitcast.137), channel_id=1, source_target_pairs={{1,0},{2,1},{3,2},{5,4},{6,5},{7,6},{9,8},{10,9},{11,10},{13,12},{... | collective-permute-start | bytes 152072 | tf_op jit(solution)/shard_map/ppermute | solution.py:36
  71.3 6.1 %collective-permute-done.12 = f32[6,8,8,33]{3,2,1,0:T(8,128)S(1)} collective-permute-done((f32[6,8,8,33]{3,2,1,0:T(8,128)S(1)}, f32[6,8,8,33]{3,2,1,0:T(8,128)S(1)}, u32[]{:S(2)}, u32[]{:S(2)}) %collective-permute-start.12) | collective-permute-done | bytes 50720 | tf_op jit(solution)/shard_map/ppermute | solution.py:36
  77.7 0.5 collective-permute-start.13
  78.2 0.7 collective-permute-done.14
  78.9 0.2 collective-permute-done.13
  79.1 0.3 pad_maximum_fusion.83
  79.3 1.4 %collective-permute-start.16 = (f32[6,10,1,130]{3,2,1,0:T(1,128)S(1)}, f32[6,10,1,130]{3,2,1,0:T(1,128)S(1)}, u32[]{:S(2)}, u32[]{:S(2)}) collective-permute-start(f32[6,10,1,130]{3,2,1,0:T(1,128)S(1)} %get-tuple-element.57), channel_id=1, source_target_pairs={{0,4},{4,8},{8,12},{12,0},{1,5},{5,9},{9,13},{13,1},{2,6},{6,10},{... | collective-permute-start | bytes 93608 | tf_op jit(solution)/shard_map/ppermute | solution.py:25
  80.8 1.5 %collective-permute-start.15 = (f32[6,10,1,130]{3,2,1,0:T(1,128)S(1)}, f32[6,10,1,130]{3,2,1,0:T(1,128)S(1)}, u32[]{:S(2)}, u32[]{:S(2)}) collective-permute-start(f32[6,10,1,130]{3,2,1,0:T(1,128)S(1)} %get-tuple-element.58), channel_id=1, source_target_pairs={{4,0},{8,4},{12,8},{0,12},{5,1},{9,5},{13,9},{1,13},{6,2},{10,6},{... | collective-permute-start | bytes 93608 | tf_op jit(solution)/shard_map/ppermute | solution.py:28
  82.5 2.7 %collective-permute-done.16 = f32[6,10,1,130]{3,2,1,0:T(1,128)S(1)} collective-permute-done((f32[6,10,1,130]{3,2,1,0:T(1,128)S(1)}, f32[6,10,1,130]{3,2,1,0:T(1,128)S(1)}, u32[]{:S(2)}, u32[]{:S(2)}) %collective-permute-start.16) | collective-permute-done | bytes 31232 | tf_op jit(solution)/shard_map/ppermute | solution.py:25
  85.1 0.3 pad_maximum_fusion.2
  85.4 0.2 slice.1093
  85.6 0.3 slice_select_fusion.1
  86.2 0.5 fusion.22
  87.2 0.3 fusion.39
  87.7 0.5 collective-permute-start.17
  88.2 0.7 collective-permute-done.18
  88.9 0.2 collective-permute-done.17
  89.1 1.6 %collective-permute-start.20 = (f32[6,10,1,128]{3,2,1,0:T(1,128)S(1)}, f32[6,10,1,128]{3,2,1,0:T(1,128)S(1)}, u32[]{:S(2)}, u32[]{:S(2)}) collective-permute-start(f32[6,10,1,128]{3,2,1,0:T(1,128)S(1)} %get-tuple-element.78), channel_id=1, source_target_pairs={{0,4},{4,8},{8,12},{12,0},{1,5},{5,9},{9,13},{13,1},{2,6},{6,10},{... | collective-permute-start | bytes 92168 | tf_op jit(solution)/shard_map/ppermute | solution.py:25
  90.7 1.3 %collective-permute-start.19 = (f32[6,10,1,128]{3,2,1,0:T(1,128)S(1)}, f32[6,10,1,128]{3,2,1,0:T(1,128)S(1)}, u32[]{:S(2)}, u32[]{:S(2)}) collective-permute-start(f32[6,10,1,128]{3,2,1,0:T(1,128)S(1)} %get-tuple-element.79), channel_id=1, source_target_pairs={{4,0},{8,4},{12,8},{0,12},{5,1},{9,5},{13,9},{1,13},{6,2},{10,6},{... | collective-permute-start | bytes 92168 | tf_op jit(solution)/shard_map/ppermute | solution.py:28
  92.0 0.3 pad_maximum_fusion.4
  92.3 1.6 %collective-permute-done.20 = f32[6,10,1,128]{3,2,1,0:T(1,128)S(1)} collective-permute-done((f32[6,10,1,128]{3,2,1,0:T(1,128)S(1)}, f32[6,10,1,128]{3,2,1,0:T(1,128)S(1)}, u32[]{:S(2)}, u32[]{:S(2)}) %collective-permute-start.20) | collective-permute-done | bytes 30752 | tf_op jit(solution)/shard_map/ppermute | solution.py:25
  93.9 0.7 collective-permute-done.19
  94.7 0.2 fusion.211
  94.9 2.6 %collective-permute-start.21 = (f32[6,10,10,1]{3,2,1,0:T(8,128)S(1)}, f32[6,10,10,1]{3,2,1,0:T(8,128)S(1)}, u32[]{:S(2)}, u32[]{:S(2)}) collective-permute-start(f32[6,10,10,1]{3,2,1,0:T(8,128)S(1)} %get-tuple-element.55), channel_id=1, source_target_pairs={{1,0},{2,1},{3,2},{0,3},{5,4},{6,5},{7,6},{4,7},{9,8},{10,9},{11,1... | collective-permute-start | bytes 7208 | tf_op jit(solution)/shard_map/ppermute | solution.py:28
  97.5 11.7 %collective-permute-done.21 = f32[6,10,10,1]{3,2,1,0:T(8,128)S(1)} collective-permute-done((f32[6,10,10,1]{3,2,1,0:T(8,128)S(1)}, f32[6,10,10,1]{3,2,1,0:T(8,128)S(1)}, u32[]{:S(2)}, u32[]{:S(2)}) %collective-permute-start.21) | collective-permute-done | bytes 2432 | tf_op jit(solution)/shard_map/ppermute | solution.py:28
  109.2 11.8 %collective-permute-done.22 = f32[6,10,10,1]{3,2,1,0:T(8,128)S(1)} collective-permute-done((f32[6,10,10,1]{3,2,1,0:T(8,128)S(1)}, f32[6,10,10,1]{3,2,1,0:T(8,128)S(1)}, u32[]{:S(2)}, u32[]{:S(2)}) %collective-permute-start.22) | collective-permute-done | bytes 2432 | tf_op jit(solution)/shard_map/ppermute | solution.py:25
  121.0 0.2 broadcast_select_fusion.3
  121.2 0.1 fusion.2
  121.5 0.6 pad_maximum_fusion.3
  122.4 0.7 multiply_subtract_fusion
  123.2 0.6 pad_maximum_fusion.82
  (71 shorter events, 3.6 us)
Async XLA Ops:
  1.4 0.8 copy-start
  2.3 1.4 %collective-permute-start.1 = (f32[6,1,8,128]{3,2,1,0:T(8,128)S(1)}, f32[6,1,8,128]{3,2,1,0:T(8,128)S(1)}, u32[]{:S(2)}, u32[]{:S(2)}) collective-permute-start(f32[6,1,8,128]{3,2,1,0:T(8,128)S(1)} %get-tuple-element.98), channel_id=1, source_target_pairs={{0,16},{16,0},{1,17},{17,1},{2,18},{18,2},{3,19},{19,3},{4,20},{20... | collective-permute-start | bytes 73736 | tf_op jit(solution)/shard_map/ppermute | solution.py:25
  2.8 1.2 collective-permute-start
  2.9 0.7 copy-start.2
  4.0 5.5 %collective-permute-start.3 = (f32[6,10,1,128]{3,2,1,0:T(1,128)S(1)}, f32[6,10,1,128]{3,2,1,0:T(1,128)S(1)}, u32[]{:S(2)}, u32[]{:S(2)}) collective-permute-start(f32[6,10,1,128]{3,2,1,0:T(1,128)S(1)} %get-tuple-element.82), channel_id=1, source_target_pairs={{0,4},{4,8},{8,12},{12,0},{1,5},{5,9},{9,13},{13,1},{2,6},{6,10},{... | collective-permute-start | bytes 92168 | tf_op jit(solution)/shard_map/ppermute | solution.py:25
  6.7 3.9 %collective-permute-start.2 = (f32[6,10,1,128]{3,2,1,0:T(1,128)S(1)}, f32[6,10,1,128]{3,2,1,0:T(1,128)S(1)}, u32[]{:S(2)}, u32[]{:S(2)}) collective-permute-start(f32[6,10,1,128]{3,2,1,0:T(1,128)S(1)} %get-tuple-element.83), channel_id=1, source_target_pairs={{4,0},{8,4},{12,8},{0,12},{5,1},{9,5},{13,9},{1,13},{6,2},{10,6},{... | collective-permute-start | bytes 92168 | tf_op jit(solution)/shard_map/ppermute | solution.py:28
  10.9 15.3 %collective-permute-start.4 = (f32[6,10,10,1]{3,2,1,0:T(8,128)S(1)}, f32[6,10,10,1]{3,2,1,0:T(8,128)S(1)}, u32[]{:S(2)}, u32[]{:S(2)}) collective-permute-start(f32[6,10,10,1]{3,2,1,0:T(8,128)S(1)} %get-tuple-element.65), channel_id=1, source_target_pairs={{1,0},{2,1},{3,2},{0,3},{5,4},{6,5},{7,6},{4,7},{9,8},{10,9},{11,1... | collective-permute-start | bytes 7208 | tf_op jit(solution)/shard_map/ppermute | solution.py:28
  14.6 21.5 %collective-permute-start.5 = (f32[6,10,10,1]{3,2,1,0:T(8,128)S(1)}, f32[6,10,10,1]{3,2,1,0:T(8,128)S(1)}, u32[]{:S(2)}, u32[]{:S(2)}) collective-permute-start(f32[6,10,10,1]{3,2,1,0:T(8,128)S(1)} %get-tuple-element.66), channel_id=1, source_target_pairs={{0,1},{1,2},{2,3},{3,0},{4,5},{5,6},{6,7},{7,4},{8,9},{9,10},{10,1... | collective-permute-start | bytes 7208 | tf_op jit(solution)/shard_map/ppermute | solution.py:25
  37.2 1.3 %collective-permute-start.7 = (f32[6,1,8,128]{3,2,1,0:T(8,128)S(1)}, f32[6,1,8,128]{3,2,1,0:T(8,128)S(1)}, u32[]{:S(2)}, u32[]{:S(2)}) collective-permute-start(f32[6,1,8,128]{3,2,1,0:T(8,128)S(1)} %get-tuple-element.96), channel_id=1, source_target_pairs={{0,16},{16,0},{1,17},{17,1},{2,18},{18,2},{3,19},{19,3},{4,20},{20... | collective-permute-start | bytes 73736 | tf_op jit(solution)/shard_map/ppermute | solution.py:25
  37.3 1.3 %collective-permute-start.6 = (f32[6,1,8,128]{3,2,1,0:T(8,128)S(1)}, f32[6,1,8,128]{3,2,1,0:T(8,128)S(1)}, u32[]{:S(2)}, u32[]{:S(2)}) collective-permute-start(f32[6,1,8,128]{3,2,1,0:T(8,128)S(1)} %get-tuple-element.97), channel_id=1, source_target_pairs={{16,0},{0,16},{17,1},{1,17},{18,2},{2,18},{19,3},{3,19},{20,4},{4,... | collective-permute-start | bytes 73736 | tf_op jit(solution)/shard_map/ppermute | solution.py:28
  38.7 5.1 %collective-permute-start.9 = (f32[6,10,1,128]{3,2,1,0:T(1,128)S(1)}, f32[6,10,1,128]{3,2,1,0:T(1,128)S(1)}, u32[]{:S(2)}, u32[]{:S(2)}) collective-permute-start(f32[6,10,1,128]{3,2,1,0:T(1,128)S(1)} %get-tuple-element.80), channel_id=1, source_target_pairs={{0,4},{4,8},{8,12},{12,0},{1,5},{5,9},{9,13},{13,1},{2,6},{6,10},{... | collective-permute-start | bytes 92168 | tf_op jit(solution)/shard_map/ppermute | solution.py:25
  40.7 3.9 %collective-permute-start.8 = (f32[6,10,1,128]{3,2,1,0:T(1,128)S(1)}, f32[6,10,1,128]{3,2,1,0:T(1,128)S(1)}, u32[]{:S(2)}, u32[]{:S(2)}) collective-permute-start(f32[6,10,1,128]{3,2,1,0:T(1,128)S(1)} %get-tuple-element.81), channel_id=1, source_target_pairs={{4,0},{8,4},{12,8},{0,12},{5,1},{9,5},{13,9},{1,13},{6,2},{10,6},{... | collective-permute-start | bytes 92168 | tf_op jit(solution)/shard_map/ppermute | solution.py:28
  44.9 14.0 %collective-permute-start.10 = (f32[6,10,10,1]{3,2,1,0:T(8,128)S(1)}, f32[6,10,10,1]{3,2,1,0:T(8,128)S(1)}, u32[]{:S(2)}, u32[]{:S(2)}) collective-permute-start(f32[6,10,10,1]{3,2,1,0:T(8,128)S(1)} %get-tuple-element.61), channel_id=1, source_target_pairs={{1,0},{2,1},{3,2},{0,3},{5,4},{6,5},{7,6},{4,7},{9,8},{10,9},{11,1... | collective-permute-start | bytes 7208 | tf_op jit(solution)/shard_map/ppermute | solution.py:28
  46.7 21.5 %collective-permute-start.11 = (f32[6,10,10,1]{3,2,1,0:T(8,128)S(1)}, f32[6,10,10,1]{3,2,1,0:T(8,128)S(1)}, u32[]{:S(2)}, u32[]{:S(2)}) collective-permute-start(f32[6,10,10,1]{3,2,1,0:T(8,128)S(1)} %get-tuple-element.62), channel_id=1, source_target_pairs={{0,1},{1,2},{2,3},{3,0},{4,5},{5,6},{6,7},{7,4},{8,9},{9,10},{10,1... | collective-permute-start | bytes 7208 | tf_op jit(solution)/shard_map/ppermute | solution.py:25
  69.8 7.7 %copy-start.1 = (f32[6,8,8,33]{3,2,1,0:T(8,128)S(1)}, f32[6,8,8,33]{3,2,1,0:T(8,128)}, u32[]{:S(2)}) copy-start(f32[6,8,8,33]{3,2,1,0:T(8,128)} %constant.89.clone.1) | copy-start | bytes 152068
  69.8 7.7 %collective-permute-start.12 = (f32[6,8,8,33]{3,2,1,0:T(8,128)S(1)}, f32[6,8,8,33]{3,2,1,0:T(8,128)S(1)}, u32[]{:S(2)}, u32[]{:S(2)}) collective-permute-start(f32[6,8,8,33]{3,2,1,0:T(8,128)S(1)} %bitcast.137), channel_id=1, source_target_pairs={{1,0},{2,1},{3,2},{5,4},{6,5},{7,6},{9,8},{10,9},{11,10},{13,12},{... | collective-permute-start | bytes 152072 | tf_op jit(solution)/shard_map/ppermute | solution.py:36
  77.6 1.3 %collective-permute-start.14 = (f32[6,1,8,130]{3,2,1,0:T(8,128)S(1)}, f32[6,1,8,130]{3,2,1,0:T(8,128)S(1)}, u32[]{:S(2)}, u32[]{:S(2)}) collective-permute-start(f32[6,1,8,130]{3,2,1,0:T(8,128)S(1)} %get-tuple-element.70), channel_id=1, source_target_pairs={{0,16},{16,0},{1,17},{17,1},{2,18},{18,2},{3,19},{19,3},{4,20},{20... | collective-permute-start | bytes 74888 | tf_op jit(solution)/shard_map/ppermute | solution.py:25
  77.7 1.4 %collective-permute-start.13 = (f32[6,1,8,130]{3,2,1,0:T(8,128)S(1)}, f32[6,1,8,130]{3,2,1,0:T(8,128)S(1)}, u32[]{:S(2)}, u32[]{:S(2)}) collective-permute-start(f32[6,1,8,130]{3,2,1,0:T(8,128)S(1)} %get-tuple-element.71), channel_id=1, source_target_pairs={{16,0},{0,16},{17,1},{1,17},{18,2},{2,18},{19,3},{3,19},{20,4},{4,... | collective-permute-start | bytes 74888 | tf_op jit(solution)/shard_map/ppermute | solution.py:28
  79.3 5.8 %collective-permute-start.16 = (f32[6,10,1,130]{3,2,1,0:T(1,128)S(1)}, f32[6,10,1,130]{3,2,1,0:T(1,128)S(1)}, u32[]{:S(2)}, u32[]{:S(2)}) collective-permute-start(f32[6,10,1,130]{3,2,1,0:T(1,128)S(1)} %get-tuple-element.57), channel_id=1, source_target_pairs={{0,4},{4,8},{8,12},{12,0},{1,5},{5,9},{9,13},{13,1},{2,6},{6,10},{... | collective-permute-start | bytes 93608 | tf_op jit(solution)/shard_map/ppermute | solution.py:25
  80.8 4.3 %collective-permute-start.15 = (f32[6,10,1,130]{3,2,1,0:T(1,128)S(1)}, f32[6,10,1,130]{3,2,1,0:T(1,128)S(1)}, u32[]{:S(2)}, u32[]{:S(2)}) collective-permute-start(f32[6,10,1,130]{3,2,1,0:T(1,128)S(1)} %get-tuple-element.58), channel_id=1, source_target_pairs={{4,0},{8,4},{12,8},{0,12},{5,1},{9,5},{13,9},{1,13},{6,2},{10,6},{... | collective-permute-start | bytes 93608 | tf_op jit(solution)/shard_map/ppermute | solution.py:28
  87.6 1.3 %collective-permute-start.18 = (f32[6,1,8,128]{3,2,1,0:T(8,128)S(1)}, f32[6,1,8,128]{3,2,1,0:T(8,128)S(1)}, u32[]{:S(2)}, u32[]{:S(2)}) collective-permute-start(f32[6,1,8,128]{3,2,1,0:T(8,128)S(1)} %get-tuple-element.88), channel_id=1, source_target_pairs={{0,16},{16,0},{1,17},{17,1},{2,18},{18,2},{3,19},{19,3},{4,20},{20... | collective-permute-start | bytes 73736 | tf_op jit(solution)/shard_map/ppermute | solution.py:25
  87.7 1.3 %collective-permute-start.17 = (f32[6,1,8,128]{3,2,1,0:T(8,128)S(1)}, f32[6,1,8,128]{3,2,1,0:T(8,128)S(1)}, u32[]{:S(2)}, u32[]{:S(2)}) collective-permute-start(f32[6,1,8,128]{3,2,1,0:T(8,128)S(1)} %get-tuple-element.89), channel_id=1, source_target_pairs={{16,0},{0,16},{17,1},{1,17},{18,2},{2,18},{19,3},{3,19},{20,4},{4,... | collective-permute-start | bytes 73736 | tf_op jit(solution)/shard_map/ppermute | solution.py:28
  89.1 4.8 %collective-permute-start.20 = (f32[6,10,1,128]{3,2,1,0:T(1,128)S(1)}, f32[6,10,1,128]{3,2,1,0:T(1,128)S(1)}, u32[]{:S(2)}, u32[]{:S(2)}) collective-permute-start(f32[6,10,1,128]{3,2,1,0:T(1,128)S(1)} %get-tuple-element.78), channel_id=1, source_target_pairs={{0,4},{4,8},{8,12},{12,0},{1,5},{5,9},{9,13},{13,1},{2,6},{6,10},{... | collective-permute-start | bytes 92168 | tf_op jit(solution)/shard_map/ppermute | solution.py:25
  90.7 3.9 %collective-permute-start.19 = (f32[6,10,1,128]{3,2,1,0:T(1,128)S(1)}, f32[6,10,1,128]{3,2,1,0:T(1,128)S(1)}, u32[]{:S(2)}, u32[]{:S(2)}) collective-permute-start(f32[6,10,1,128]{3,2,1,0:T(1,128)S(1)} %get-tuple-element.79), channel_id=1, source_target_pairs={{4,0},{8,4},{12,8},{0,12},{5,1},{9,5},{13,9},{1,13},{6,2},{10,6},{... | collective-permute-start | bytes 92168 | tf_op jit(solution)/shard_map/ppermute | solution.py:28
  94.9 14.3 %collective-permute-start.21 = (f32[6,10,10,1]{3,2,1,0:T(8,128)S(1)}, f32[6,10,10,1]{3,2,1,0:T(8,128)S(1)}, u32[]{:S(2)}, u32[]{:S(2)}) collective-permute-start(f32[6,10,10,1]{3,2,1,0:T(8,128)S(1)} %get-tuple-element.55), channel_id=1, source_target_pairs={{1,0},{2,1},{3,2},{0,3},{5,4},{6,5},{7,6},{4,7},{9,8},{10,9},{11,1... | collective-permute-start | bytes 7208 | tf_op jit(solution)/shard_map/ppermute | solution.py:28
  97.4 23.5 %collective-permute-start.22 = (f32[6,10,10,1]{3,2,1,0:T(8,128)S(1)}, f32[6,10,10,1]{3,2,1,0:T(8,128)S(1)}, u32[]{:S(2)}, u32[]{:S(2)}) collective-permute-start(f32[6,10,10,1]{3,2,1,0:T(8,128)S(1)} %get-tuple-element.56), channel_id=1, source_target_pairs={{0,1},{1,2},{2,3},{3,0},{4,5},{5,6},{6,7},{7,4},{8,9},{9,10},{10,1... | collective-permute-start | bytes 7208 | tf_op jit(solution)/shard_map/ppermute | solution.py:25
where the time goes:
time: 124 us
  waiting for transfers between devices  85.4 us (69%)
  starting transfers between devices  24.7 us (20%)
  other arithmetic  10.1 us (8%)
  local copies, waits for them, and re-layouts  2.53 us (2%)
    ppermute x11, waiting for transfers between devices, with_halo(): lax.ppermute(lax.slice_in_dim(block, block.shape[dim] - width, None, axis...  40.7 us
    ppermute x11, waiting for transfers between devices, with_halo(): lax.ppermute(lax.slice_in_dim(block, 0, width, axis=dim), axis, backward)  38.5 us
    ppermute x11, starting transfers between devices, with_halo(): lax.ppermute(lax.slice_in_dim(block, 0, width, axis=dim), axis, backward)  14.4 us
    ppermute x11, starting transfers between devices, with_halo(): lax.ppermute(lax.slice_in_dim(block, block.shape[dim] - width, None, axis...  8.79 us
    ppermute x1, waiting for transfers between devices, shifted(): return lax.ppermute(shard, axis, pairs)  6.15 us
  transfers between devices with their start and end apart: 23, of which 21 were waited for; matrix products, arithmetic and copies ran while one was open for 1% of the time, Pallas kernels for 0%

commit v1 on v0

v1 whole, which is shorter than its diff:
```python
import jax
import jax.numpy as jnp
from jax import lax
from jax.sharding import PartitionSpec as P

BZ = 16
STEPS = 4


COMP = ((0.0, 0.0), (1.0, -0.5), (-0.5, 1.0), (-0.5, -0.5))
LATENT = (0.0, 1.0, 1.0, 1.0)
DT = 0.05
KAPPA = 1.5
WELL = 12.0
DLIQ = 3.0
DSOL = 0.3


def ring(axis, by):
    count = lax.axis_size(axis)
    return [(i, (i + by) % count) for i in range(count)]


def line(axis, by):
    count = lax.axis_size(axis)
    return [(i, i + by) for i in range(count) if 0 <= i + by < count]


def flat_z(face):
    return face.reshape(face.shape[0], -1)


def lateral_halos(block):
    xlo = lax.ppermute(block[:, -1], "gx", ring("gx", 1))
    xhi = lax.ppermute(block[:, 0], "gx", ring("gx", -1))
    ylo = lax.ppermute(block[:, :, -1], "gy", ring("gy", 1))
    yhi = lax.ppermute(block[:, :, 0], "gy", ring("gy", -1))
    return xlo, xhi, ylo, yhi


def neighbours(fields, halos):
    xlo, xhi, ylo, yhi, zlo, zhi = halos
    return [
        jnp.concatenate([fields[:, 1:], xhi[:, None]], 1),
        jnp.concatenate([xlo[:, None], fields[:, :-1]], 1),
        jnp.concatenate([fields[:, :, 1:], yhi[:, :, None]], 2),
        jnp.concatenate([ylo[:, :, None], fields[:, :, :-1]], 2),
        jnp.concatenate([fields[..., 1:], zhi[..., None]], 3),
        jnp.concatenate([zlo[..., None], fields[..., :-1]], 3),
    ]


def phase_update(fields, side, zglob, offset, depth):
    phi = fields[:4]
    chem = fields[4:]
    beside_all = [s[:4] for s in side]
    total = (
        beside_all[0]
        + beside_all[1]
        + beside_all[2]
        + beside_all[3]
        + beside_all[4]
        + beside_all[5]
    )
    lap = total - 6.0 * phi
    square = phi * phi
    summed = square[0] + square[1] + square[2] + square[3]
    under = 2.0 * ((zglob + offset).astype(jnp.float32) / depth - 0.5)
    rates = []
    for phase in range(4):
        psi = -(COMP[phase][0] * chem[0] + COMP[phase][1] * chem[1]) + LATENT[phase] * under
        rate = (
            KAPPA * lap[phase]
            - WELL * phi[phase] * (summed - square[phase])
            - 6.0 * phi[phase] * (1.0 - phi[phase]) * psi
        )
        rates.append(rate)
    mean_rate = (rates[0] + rates[1] + rates[2] + rates[3]) * 0.25
    return jnp.stack([phi[phase] + DT * (rates[phase] - mean_rate) for phase in range(4)])


def shape_fn(values):
    return values * values * (3.0 - 2.0 * values)


def chem_update(fields, side, phi_old, phi_new):
    chem = fields[4:]
    centre_d = DSOL + (DLIQ - DSOL) * fields[0]
    side_d = [DSOL + (DLIQ - DSOL) * s[0] for s in side]
    side_m = [s[4:] for s in side]
    flux = jnp.zeros_like(chem)
    for way in range(6):
        flux = flux + 0.5 * (centre_d + side_d[way]) * (side_m[way] - chem)
    delta = shape_fn(phi_new) - shape_fn(phi_old)
    result = []
    for comp in range(2):
        change = (
            COMP[0][comp] * delta[0]
            + COMP[1][comp] * delta[1]
            + COMP[2][comp] * delta[2]
            + COMP[3][comp] * delta[3]
        )
        result.append(chem[comp] + DT * flux[comp] - change)
    return jnp.stack(result)


def shards(labels, mu_start, front_blocks):
    cells_x, cells_y, cells_z = labels.shape
    lift = cells_z // 4
    bricks_z = lax.axis_size("gz")
    depth = cells_z * bricks_z
    index_x = lax.axis_index("gx")
    index_y = lax.axis_index("gy")
    index_z = lax.axis_index("gz")
    zglob = index_z * cells_z + jnp.arange(cells_z, dtype=jnp.int32)
    per_brick = cells_z // BZ
    bottom_brick = index_z == 0
    top_brick = index_z == bricks_z - 1

    matched = (
        (front_blocks[:, 0] == index_x)
        & (front_blocks[:, 1] == index_y)
        & (front_blocks[:, 2] // per_brick == index_z)
    )
    local_block = front_blocks[:, 2] - index_z * per_brick
    hits = matched[:, None] & (
        local_block[:, None] == jnp.arange(per_brick, dtype=jnp.int32)[None, :]
    )
    block_on = jnp.any(hits, 0)
    cell_on = jnp.repeat(block_on, BZ)

    phi_start = jnp.stack([(labels == phase).astype(jnp.float32) for phase in range(4)])
    fields = jnp.concatenate([phi_start, mu_start], 0)
    nf = fields.shape[0]
    offset = 0
    for step in range(STEPS):
        if step == STEPS // 2:
            offset = lift
            incoming = lax.ppermute(fields[..., : lift + 1], "gz", line("gz", -1))
            count = lift + 1
            ones = jnp.ones((1, cells_x, cells_y, count), jnp.float32)
            incoming = jnp.where(
                top_brick,
                jnp.concatenate([ones, jnp.zeros((nf - 1, cells_x, cells_y, count), jnp.float32)], 0),
                incoming,
            )
            zlo = jnp.where(bottom_brick, fields[..., lift], fields[..., lift - 1])
            fields = jnp.concatenate([fields[..., lift:], incoming[..., :lift]], 3)
            zhi = incoming[..., lift]
            xlo, xhi, ylo, yhi = lateral_halos(fields)
        else:
            xlo, xhi, ylo, yhi = lateral_halos(fields)
            from_below = lax.ppermute(flat_z(fields[..., -1]), "gz", line("gz", 1))
            from_above = lax.ppermute(flat_z(fields[..., 0]), "gz", line("gz", -1))
            zlo = jnp.where(bottom_brick, fields[..., 0], from_below.reshape(fields.shape[:3]))
            zhi = jnp.where(top_brick, fields[..., -1], from_above.reshape(fields.shape[:3]))
        side = neighbours(fields, (xlo, xhi, ylo, yhi, zlo, zhi))
        phi_new = jnp.where(
            cell_on[None, None, None, :],
            phase_update(fields, side, zglob, offset, depth),
            fields[:4],
        )
        mu_new = chem_update(fields, side, fields[:4], phi_new)
        fields = jnp.concatenate([phi_new, mu_new], 0)
    return (fields[:4], fields[4:])


def solution(mesh):
    placed = (P("gx", "gy", "gz"), P(None, "gx", "gy", "gz"), P())
    return jax.shard_map(
        shards,
        mesh=mesh,
        in_specs=placed,
        out_specs=(P(None, "gx", "gy", "gz"), P(None, "gx", "gy", "gz")),
        check_vma=False,
    )
```

time: 124 us -> 67.9 us (0.55)
  waiting for transfers between devices: 85.4 us -> 20.7 us
  local copies, waits for them, and re-layouts: 2.53 us -> 9.58 us
  starting transfers between devices: 24.7 us -> 30 us
  other arithmetic: 10.1 us -> 5.43 us
    ppermute x23, waiting for transfers between devices: 85.4 us -> 20.7 us  [the longest x3 6.14 us: shards(): from_above = lax.ppermute(flat_z(fields[..., 0]), 'gz', line('gz', -1))]
    ppermute x23, starting transfers between devices: 24.7 us -> 30 us  [the longest x3 11.6 us: shards(): from_below = lax.ppermute(flat_z(fields[..., -1]), 'gz', line('gz', 1))]
    reshape x0 -> x12, local copies, waits for them, and re-layouts: none -> 2.62 us  [the longest x6 1.31 us: shards(): from_above.reshape(fields.shape[:3])]
    slice x6 -> x27, local copies, waits for them, and re-layouts: 0.88 us -> 3.33 us  [the longest x5 1.31 us: shards(): fields[..., -1]]
    concatenate x13 -> x6, other arithmetic: 2.39 us -> 0.88 us  [the longest x4 0.72 us: shards(): fields = jnp.concatenate([fields[..., lift:], incoming[..., :lift]], 3)]
    unnamed x6 -> x10, local copies, waits for them, and re-layouts: 1.48 us -> 2.87 us
  transfers between devices with their start and end apart: 23 -> 23, of which waited for: 21 -> 10; matrix products, arithmetic and copies ran while one was open for 1% -> 8% of each run, Pallas kernels for 0% -> 0%
where the time goes in v1:
time: 67.9 us; the launch traced here: 67.2 us
  starting transfers between devices  30 us (44%)
  waiting for transfers between devices  20.7 us (30%)
  local copies, waits for them, and re-layouts  9.58 us (14%)
  other arithmetic  5.43 us (8%)
  between operations  1.39 us (2%)
    ppermute x3, starting transfers between devices, shards(): from_below = lax.ppermute(flat_z(fields[..., -1]), 'gz', line('gz', 1))  11.6 us
    ppermute x4, starting transfers between devices, lateral_halos(): yhi = lax.ppermute(block[:, :, 0], 'gy', ring('gy', -1))  8.2 us
    ppermute x3, waiting for transfers between devices, shards(): from_above = lax.ppermute(flat_z(fields[..., 0]), 'gz', line('gz', -1))  6.14 us
    ppermute x1, waiting for transfers between devices, shards(): incoming = lax.ppermute(fields[..., :lift + 1], 'gz', line('gz', -1))  6.03 us
    ppermute x4, waiting for transfers between devices, lateral_halos(): ylo = lax.ppermute(block[:, :, -1], 'gy', ring('gy', 1))  5.06 us
    ppermute x3, starting transfers between devices, shards(): from_above = lax.ppermute(flat_z(fields[..., 0]), 'gz', line('gz', -1))  3.85 us
    unnamed x10, local copies, waits for them, and re-layouts  2.87 us
    ppermute x4, starting transfers between devices, lateral_halos(): ylo = lax.ppermute(block[:, :, -1], 'gy', ring('gy', 1))  2.77 us
  transfers between devices with their start and end apart: 23, of which 10 were waited for; matrix products, arithmetic and copies ran while one was open for 8% of the time, Pallas kernels for 0%

profile of v1, /device:TPU:0, one launch (start us, length us, event | category | flops | bytes accessed | tf_op | source)
XLA Modules:
  0.0 67.2 jit_solution(11485418656452658747)
XLA Ops:
  0.6 0.8 %convert_bitcast_fusion.1 = (f32[1,8,8,128]{3,1,2,0:T(8,128)S(1)}, pred[8,8,128]{2,0,1:T(8,128)(4,1)S(1)}, f32[1,8,8,128]{3,1,2,0:T(8,128)S(1)}, pred[8,8,128]{2...) fusion(s32[8,8,128]{2,1,0:T(8,128)} %param.3), kind=kLoop, calls=%fused_computation.206 | loop fusion | flops 65536 | bytes 196608 | tf_op jit(solution)/shard_map/stack | solution.py:132
  1.5 0.8 %copy-done = f32[2,8,8,128]{3,2,1,0:T(8,128)S(1)} copy-done((f32[2,8,8,128]{3,2,1,0:T(8,128)S(1)}, f32[2,8,8,128]{3,2,1,0:T(8,128)}, u32[]{:S(2)}) %copy-start) | copy-done | bytes 65560
  2.3 3.9 %collective-permute-start.2 = (f32[6,8,128]{2,1,0:T(8,128)S(1)}, f32[6,8,128]{2,1,0:T(8,128)S(1)}, u32[]{:S(2)}, u32[]{:S(2)}) collective-permute-start(f32[6,8,128]{2,1,0:T(8,128)S(1)} %get-tuple-element.113), channel_id=1, source_target_pairs={{0,12},{4,0},{8,4},{12,8},{1,13},{5,1},{9,5},{13,9},{2,14},{6,2},{... | collective-permute-start | bytes 73736 | tf_op jit(solution)/shard_map/ppermute | solution.py:37
  6.4 0.5 collective-permute-start
  7.0 0.4 copy.402
  7.4 3.5 %collective-permute-start.5 = (f32[6,64]{1,0:T(8,128)S(1)}, f32[6,64]{1,0:T(8,128)S(1)}, u32[]{:S(2)}, u32[]{:S(2)}) collective-permute-start(f32[6,64]{1,0:T(8,128)S(1)} %reshape_squeeze.19), channel_id=1, source_target_pairs={{0,1},{1,2},{2,3},{4,5},{5,6},{6,7},{8,9},{9,10},{10,11},{12,13},{... | collective-permute-start | bytes 4616 | tf_op jit(solution)/shard_map/ppermute | solution.py:153
  11.1 0.7 %copy-done.2 = s32[32,3]{0,1:T(4,128)S(1)} copy-done((s32[32,3]{0,1:T(4,128)S(1)}, s32[32,3]{0,1:T(4,128)}, u32[]{:S(2)}) %copy-start.2) | copy-done | bytes 408
  11.8 0.1 fusion.320
  12.0 0.3 collective-permute-done.5
  12.3 0.4 copy.403
  12.7 0.4 copy.400
  13.1 1.3 %collective-permute-start.4 = (f32[6,64]{1,0:T(8,128)S(1)}, f32[6,64]{1,0:T(8,128)S(1)}, u32[]{:S(2)}, u32[]{:S(2)}) collective-permute-start(f32[6,64]{1,0:T(8,128)S(1)} %reshape_squeeze.18), channel_id=1, source_target_pairs={{1,0},{2,1},{3,2},{5,4},{6,5},{7,6},{9,8},{10,9},{11,10},{13,12},{... | collective-permute-start | bytes 4616 | tf_op jit(solution)/shard_map/ppermute | solution.py:154
  14.6 4.3 %collective-permute-done.4 = f32[6,64]{1,0:T(8,128)S(1)} collective-permute-done((f32[6,64]{1,0:T(8,128)S(1)}, f32[6,64]{1,0:T(8,128)S(1)}, u32[]{:S(2)}, u32[]{:S(2)}) %collective-permute-start.4) | collective-permute-done | bytes 1568 | tf_op jit(solution)/shard_map/ppermute | solution.py:154
  19.0 0.4 copy.401
  19.3 0.1 copy_select_fusion.1
  19.6 0.2 fusion.32
  20.4 0.1 fusion.345
  20.5 0.1 fusion.344
  20.6 0.4 copy.451
  21.1 1.3 %collective-permute-start.10 = (f32[6,64]{1,0:T(8,128)S(1)}, f32[6,64]{1,0:T(8,128)S(1)}, u32[]{:S(2)}, u32[]{:S(2)}) collective-permute-start(f32[6,64]{1,0:T(8,128)S(1)} %reshape_squeeze.20), channel_id=1, source_target_pairs={{1,0},{2,1},{3,2},{5,4},{6,5},{7,6},{9,8},{10,9},{11,10},{13,12},{... | collective-permute-start | bytes 4616 | tf_op jit(solution)/shard_map/ppermute | solution.py:154
  22.4 0.4 copy.456
  22.8 4.5 %collective-permute-start.11 = (f32[6,64]{1,0:T(8,128)S(1)}, f32[6,64]{1,0:T(8,128)S(1)}, u32[]{:S(2)}, u32[]{:S(2)}) collective-permute-start(f32[6,64]{1,0:T(8,128)S(1)} %reshape_squeeze.21), channel_id=1, source_target_pairs={{0,1},{1,2},{2,3},{4,5},{5,6},{6,7},{8,9},{9,10},{10,11},{12,13},{... | collective-permute-start | bytes 4616 | tf_op jit(solution)/shard_map/ppermute | solution.py:153
  27.4 0.5 collective-permute-start.6
  27.9 2.9 %collective-permute-start.8 = (f32[6,8,128]{2,1,0:T(8,128)S(1)}, f32[6,8,128]{2,1,0:T(8,128)S(1)}, u32[]{:S(2)}, u32[]{:S(2)}) collective-permute-start(f32[6,8,128]{2,1,0:T(8,128)S(1)} %get-tuple-element.99), channel_id=1, source_target_pairs={{0,12},{4,0},{8,4},{12,8},{1,13},{5,1},{9,5},{13,9},{2,14},{6,2},{... | collective-permute-start | bytes 73736 | tf_op jit(solution)/shard_map/ppermute | solution.py:37
  30.9 0.4 copy.458
  31.4 0.4 copy.452
  31.8 0.1 broadcast_select_fusion.4
  32.1 0.3 collective-permute-done.8
  32.4 3.2 %collective-permute-done.9 = f32[6,8,128]{2,1,0:T(8,128)S(1)} collective-permute-done((f32[6,8,128]{2,1,0:T(8,128)S(1)}, f32[6,8,128]{2,1,0:T(8,128)S(1)}, u32[]{:S(2)}, u32[]{:S(2)}) %collective-permute-start.9) | collective-permute-done | bytes 24608 | tf_op jit(solution)/shard_map/ppermute | solution.py:36
  35.6 0.2 fusion.46
  36.2 1.3 %collective-permute-start.12 = (f32[6,8,8,33]{3,1,0,2:T(8,128)S(1)}, f32[6,8,8,33]{3,1,0,2:T(8,128)S(1)}, u32[]{:S(2)}, u32[]{:S(2)}) collective-permute-start(f32[6,8,8,33]{3,1,0,2:T(8,128)S(1)} %bitcast.561), channel_id=1, source_target_pairs={{1,0},{2,1},{3,2},{5,4},{6,5},{7,6},{9,8},{10,9},{11,10},{13,12},{... | collective-permute-start | bytes 152072 | tf_op jit(solution)/shard_map/ppermute | solution.py:139
  37.5 0.2 slice_select_fusion
  37.8 6.0 %collective-permute-done.12 = f32[6,8,8,33]{3,1,0,2:T(8,128)S(1)} collective-permute-done((f32[6,8,8,33]{3,1,0,2:T(8,128)S(1)}, f32[6,8,8,33]{3,1,0,2:T(8,128)S(1)}, u32[]{:S(2)}, u32[]{:S(2)}) %collective-permute-start.12) | collective-permute-done | bytes 50720 | tf_op jit(solution)/shard_map/ppermute | solution.py:139
  43.9 0.2 slice_maximum_fusion.13
  44.2 0.2 slice_maximum_fusion.5
  44.3 0.2 slice_maximum_fusion.1
  44.5 0.2 slice_maximum_fusion.2
  44.9 0.1 slice.1044
  45.0 0.6 collective-permute-start.14
  45.6 0.3 collective-permute-start.15
  45.9 1.7 %collective-permute-start.16 = (f32[6,8,128]{2,1,0:T(8,128)S(1)}, f32[6,8,128]{2,1,0:T(8,128)S(1)}, u32[]{:S(2)}, u32[]{:S(2)}) collective-permute-start(f32[6,8,128]{2,1,0:T(8,128)S(1)} %get-tuple-element.66), channel_id=1, source_target_pairs={{0,4},{4,8},{8,12},{12,0},{1,5},{5,9},{9,13},{13,1},{2,6},{6,10},{... | collective-permute-start | bytes 73736 | tf_op jit(solution)/shard_map/ppermute | solution.py:36
  47.8 1.6 %collective-permute-done.15 = f32[6,8,128]{2,1,0:T(8,128)S(1)} collective-permute-done((f32[6,8,128]{2,1,0:T(8,128)S(1)}, f32[6,8,128]{2,1,0:T(8,128)S(1)}, u32[]{:S(2)}, u32[]{:S(2)}) %collective-permute-start.15) | collective-permute-done | bytes 24608 | tf_op jit(solution)/shard_map/ppermute | solution.py:37
  49.4 1.2 %collective-permute-done.16 = f32[6,8,128]{2,1,0:T(8,128)S(1)} collective-permute-done((f32[6,8,128]{2,1,0:T(8,128)S(1)}, f32[6,8,128]{2,1,0:T(8,128)S(1)}, u32[]{:S(2)}, u32[]{:S(2)}) %collective-permute-start.16) | collective-permute-done | bytes 24608 | tf_op jit(solution)/shard_map/ppermute | solution.py:36
  50.6 0.2 fusion.12
  51.0 0.1 multiply_add_fusion.9
  51.3 0.1 fusion.66
  51.6 0.1 fusion.340
  51.8 0.4 copy.495
  52.2 3.6 %collective-permute-start.22 = (f32[6,64]{1,0:T(8,128)S(1)}, f32[6,64]{1,0:T(8,128)S(1)}, u32[]{:S(2)}, u32[]{:S(2)}) collective-permute-start(f32[6,64]{1,0:T(8,128)S(1)} %reshape_squeeze.23), channel_id=1, source_target_pairs={{0,1},{1,2},{2,3},{4,5},{5,6},{6,7},{8,9},{9,10},{10,11},{12,13},{... | collective-permute-start | bytes 4616 | tf_op jit(solution)/shard_map/ppermute | solution.py:153
  55.9 1.3 %collective-permute-done.22 = f32[6,64]{1,0:T(8,128)S(1)} collective-permute-done((f32[6,64]{1,0:T(8,128)S(1)}, f32[6,64]{1,0:T(8,128)S(1)}, u32[]{:S(2)}, u32[]{:S(2)}) %collective-permute-start.22) | collective-permute-done | bytes 1568 | tf_op jit(solution)/shard_map/ppermute | solution.py:153
  57.2 0.4 copy.496
  57.6 0.4 copy.492
  58.1 1.3 %collective-permute-start.21 = (f32[6,64]{1,0:T(8,128)S(1)}, f32[6,64]{1,0:T(8,128)S(1)}, u32[]{:S(2)}, u32[]{:S(2)}) collective-permute-start(f32[6,64]{1,0:T(8,128)S(1)} %reshape_squeeze.22), channel_id=1, source_target_pairs={{1,0},{2,1},{3,2},{5,4},{6,5},{7,6},{9,8},{10,9},{11,10},{13,12},{... | collective-permute-start | bytes 4616 | tf_op jit(solution)/shard_map/ppermute | solution.py:154
  59.4 1.0 %collective-permute-start.19 = (f32[6,8,128]{2,1,0:T(8,128)S(1)}, f32[6,8,128]{2,1,0:T(8,128)S(1)}, u32[]{:S(2)}, u32[]{:S(2)}) collective-permute-start(f32[6,8,128]{2,1,0:T(8,128)S(1)} %get-tuple-element.79), channel_id=1, source_target_pairs={{0,12},{4,0},{8,4},{12,8},{1,13},{5,1},{9,5},{13,9},{2,14},{6,2},{... | collective-permute-start | bytes 73736 | tf_op jit(solution)/shard_map/ppermute | solution.py:37
  60.4 1.0 %collective-permute-start.20 = (f32[6,8,128]{2,1,0:T(8,128)S(1)}, f32[6,8,128]{2,1,0:T(8,128)S(1)}, u32[]{:S(2)}, u32[]{:S(2)}) collective-permute-start(f32[6,8,128]{2,1,0:T(8,128)S(1)} %get-tuple-element.80), channel_id=1, source_target_pairs={{0,4},{4,8},{8,12},{12,0},{1,5},{5,9},{9,13},{13,1},{2,6},{6,10},{... | collective-permute-start | bytes 73736 | tf_op jit(solution)/shard_map/ppermute | solution.py:36
  61.5 0.5 collective-permute-start.17
  62.0 1.9 %collective-permute-done.21 = f32[6,64]{1,0:T(8,128)S(1)} collective-permute-done((f32[6,64]{1,0:T(8,128)S(1)}, f32[6,64]{1,0:T(8,128)S(1)}, u32[]{:S(2)}, u32[]{:S(2)}) %collective-permute-start.21) | collective-permute-done | bytes 1568 | tf_op jit(solution)/shard_map/ppermute | solution.py:154
  63.9 0.4 copy.493
  64.3 0.1 copy_select_fusion
  64.5 0.6 collective-permute-done.20
  65.1 0.2 fusion.2
  65.6 0.1 fusion.49
  65.8 0.7 copy.498
  66.4 0.7 %copy.497 = f32[4,8,8,128]{3,2,1,0:T(8,128)} copy(f32[4,8,8,128]{3,1,0,2:T(8,128)S(1)} %get-tuple-element.11) | data formatting | bytes 262144
  (112 shorter events, 4.4 us)
Async XLA Ops:
  1.4 0.8 %copy-start = (f32[2,8,8,128]{3,2,1,0:T(8,128)S(1)}, f32[2,8,8,128]{3,2,1,0:T(8,128)}, u32[]{:S(2)}) copy-start(f32[2,8,8,128]{3,2,1,0:T(8,128)} %param.4) | copy-start | bytes 196612
  2.3 17.2 %collective-permute-start.2 = (f32[6,8,128]{2,1,0:T(8,128)S(1)}, f32[6,8,128]{2,1,0:T(8,128)S(1)}, u32[]{:S(2)}, u32[]{:S(2)}) collective-permute-start(f32[6,8,128]{2,1,0:T(8,128)S(1)} %get-tuple-element.113), channel_id=1, source_target_pairs={{0,12},{4,0},{8,4},{12,8},{1,13},{5,1},{9,5},{13,9},{2,14},{6,2},{... | collective-permute-start | bytes 73736 | tf_op jit(solution)/shard_map/ppermute | solution.py:37
  6.3 13.2 %collective-permute-start.3 = (f32[6,8,128]{2,1,0:T(8,128)S(1)}, f32[6,8,128]{2,1,0:T(8,128)S(1)}, u32[]{:S(2)}, u32[]{:S(2)}) collective-permute-start(f32[6,8,128]{2,1,0:T(8,128)S(1)} %get-tuple-element.114), channel_id=1, source_target_pairs={{0,4},{4,8},{8,12},{12,0},{1,5},{5,9},{9,13},{13,1},{2,6},{6,10},{... | collective-permute-start | bytes 73736 | tf_op jit(solution)/shard_map/ppermute | solution.py:36
  6.3 13.2 %collective-permute-start.1 = (f32[6,8,128]{2,1,0:T(8,128)S(1)}, f32[6,8,128]{2,1,0:T(8,128)S(1)}, u32[]{:S(2)}, u32[]{:S(2)}) collective-permute-start(f32[6,8,128]{2,1,0:T(8,128)S(1)} %bitcast.600), channel_id=1, source_target_pairs={{0,16},{16,0},{1,17},{17,1},{2,18},{18,2},{3,19},{19,3},{4,20},{20... | collective-permute-start | bytes 73736 | tf_op jit(solution)/shard_map/ppermute | solution.py:34
  6.4 13.1 %collective-permute-start = (f32[6,8,128]{2,1,0:T(8,128)S(1)}, f32[6,8,128]{2,1,0:T(8,128)S(1)}, u32[]{:S(2)}, u32[]{:S(2)}) collective-permute-start(f32[6,8,128]{2,1,0:T(8,128)S(1)} %bitcast.601), channel_id=1, source_target_pairs={{0,16},{16,0},{1,17},{17,1},{2,18},{18,2},{3,19},{19,3},{4,20},{20... | collective-permute-start | bytes 73736 | tf_op jit(solution)/shard_map/ppermute | solution.py:35
  7.4 4.8 %collective-permute-start.5 = (f32[6,64]{1,0:T(8,128)S(1)}, f32[6,64]{1,0:T(8,128)S(1)}, u32[]{:S(2)}, u32[]{:S(2)}) collective-permute-start(f32[6,64]{1,0:T(8,128)S(1)} %reshape_squeeze.19), channel_id=1, source_target_pairs={{0,1},{1,2},{2,3},{4,5},{5,6},{6,7},{8,9},{9,10},{10,11},{12,13},{... | collective-permute-start | bytes 4616 | tf_op jit(solution)/shard_map/ppermute | solution.py:153
  11.1 0.7 %copy-start.2 = (s32[32,3]{0,1:T(4,128)S(1)}, s32[32,3]{0,1:T(4,128)}, u32[]{:S(2)}) copy-start(s32[32,3]{0,1:T(4,128)} %param.5) | copy-start | bytes 1156
  13.1 5.8 %collective-permute-start.4 = (f32[6,64]{1,0:T(8,128)S(1)}, f32[6,64]{1,0:T(8,128)S(1)}, u32[]{:S(2)}, u32[]{:S(2)}) collective-permute-start(f32[6,64]{1,0:T(8,128)S(1)} %reshape_squeeze.18), channel_id=1, source_target_pairs={{1,0},{2,1},{3,2},{5,4},{6,5},{7,6},{9,8},{10,9},{11,10},{13,12},{... | collective-permute-start | bytes 4616 | tf_op jit(solution)/shard_map/ppermute | solution.py:154
  21.1 10.2 %collective-permute-start.10 = (f32[6,64]{1,0:T(8,128)S(1)}, f32[6,64]{1,0:T(8,128)S(1)}, u32[]{:S(2)}, u32[]{:S(2)}) collective-permute-start(f32[6,64]{1,0:T(8,128)S(1)} %reshape_squeeze.20), channel_id=1, source_target_pairs={{1,0},{2,1},{3,2},{5,4},{6,5},{7,6},{9,8},{10,9},{11,10},{13,12},{... | collective-permute-start | bytes 4616 | tf_op jit(solution)/shard_map/ppermute | solution.py:154
  22.8 8.1 %collective-permute-start.11 = (f32[6,64]{1,0:T(8,128)S(1)}, f32[6,64]{1,0:T(8,128)S(1)}, u32[]{:S(2)}, u32[]{:S(2)}) collective-permute-start(f32[6,64]{1,0:T(8,128)S(1)} %reshape_squeeze.21), channel_id=1, source_target_pairs={{0,1},{1,2},{2,3},{4,5},{5,6},{6,7},{8,9},{9,10},{10,11},{12,13},{... | collective-permute-start | bytes 4616 | tf_op jit(solution)/shard_map/ppermute | solution.py:153
  27.4 4.7 %collective-permute-start.7 = (f32[6,8,128]{2,1,0:T(8,128)S(1)}, f32[6,8,128]{2,1,0:T(8,128)S(1)}, u32[]{:S(2)}, u32[]{:S(2)}) collective-permute-start(f32[6,8,128]{2,1,0:T(8,128)S(1)} %bitcast.611), channel_id=1, source_target_pairs={{0,16},{16,0},{1,17},{17,1},{2,18},{18,2},{3,19},{19,3},{4,20},{20... | collective-permute-start | bytes 73736 | tf_op jit(solution)/shard_map/ppermute | solution.py:34
  27.4 4.6 %collective-permute-start.6 = (f32[6,8,128]{2,1,0:T(8,128)S(1)}, f32[6,8,128]{2,1,0:T(8,128)S(1)}, u32[]{:S(2)}, u32[]{:S(2)}) collective-permute-start(f32[6,8,128]{2,1,0:T(8,128)S(1)} %bitcast.610), channel_id=1, source_target_pairs={{0,16},{16,0},{1,17},{17,1},{2,18},{18,2},{3,19},{19,3},{4,20},{20... | collective-permute-start | bytes 73736 | tf_op jit(solution)/shard_map/ppermute | solution.py:35
  27.9 4.4 %collective-permute-start.8 = (f32[6,8,128]{2,1,0:T(8,128)S(1)}, f32[6,8,128]{2,1,0:T(8,128)S(1)}, u32[]{:S(2)}, u32[]{:S(2)}) collective-permute-start(f32[6,8,128]{2,1,0:T(8,128)S(1)} %get-tuple-element.99), channel_id=1, source_target_pairs={{0,12},{4,0},{8,4},{12,8},{1,13},{5,1},{9,5},{13,9},{2,14},{6,2},{... | collective-permute-start | bytes 73736 | tf_op jit(solution)/shard_map/ppermute | solution.py:37
  30.9 4.7 %collective-permute-start.9 = (f32[6,8,128]{2,1,0:T(8,128)S(1)}, f32[6,8,128]{2,1,0:T(8,128)S(1)}, u32[]{:S(2)}, u32[]{:S(2)}) collective-permute-start(f32[6,8,128]{2,1,0:T(8,128)S(1)} %get-tuple-element.100), channel_id=1, source_target_pairs={{0,4},{4,8},{8,12},{12,0},{1,5},{5,9},{9,13},{13,1},{2,6},{6,10},{... | collective-permute-start | bytes 73736 | tf_op jit(solution)/shard_map/ppermute | solution.py:36
  36.2 7.6 %collective-permute-start.12 = (f32[6,8,8,33]{3,1,0,2:T(8,128)S(1)}, f32[6,8,8,33]{3,1,0,2:T(8,128)S(1)}, u32[]{:S(2)}, u32[]{:S(2)}) collective-permute-start(f32[6,8,8,33]{3,1,0,2:T(8,128)S(1)} %bitcast.561), channel_id=1, source_target_pairs={{1,0},{2,1},{3,2},{5,4},{6,5},{7,6},{9,8},{10,9},{11,10},{13,12},{... | collective-permute-start | bytes 152072 | tf_op jit(solution)/shard_map/ppermute | solution.py:139
  37.7 6.2 %copy-start.1 = (f32[6,8,8,33]{3,1,0,2:T(8,128)S(1)}, f32[6,8,8,33]{3,1,0,2:T(8,128)}, u32[]{:S(2)}) copy-start(f32[6,8,8,33]{3,1,0,2:T(8,128)} %constant.90.clone.1) | copy-start | bytes 152068
  44.7 2.9 %collective-permute-start.13 = (f32[6,8,128]{2,1,0:T(8,128)S(1)}, f32[6,8,128]{2,1,0:T(8,128)S(1)}, u32[]{:S(2)}, u32[]{:S(2)}) collective-permute-start(f32[6,8,128]{2,1,0:T(8,128)S(1)} %bitcast.603), channel_id=1, source_target_pairs={{0,16},{16,0},{1,17},{17,1},{2,18},{18,2},{3,19},{19,3},{4,20},{20... | collective-permute-start | bytes 73736 | tf_op jit(solution)/shard_map/ppermute | solution.py:35
  45.0 2.7 %collective-permute-start.14 = (f32[6,8,128]{2,1,0:T(8,128)S(1)}, f32[6,8,128]{2,1,0:T(8,128)S(1)}, u32[]{:S(2)}, u32[]{:S(2)}) collective-permute-start(f32[6,8,128]{2,1,0:T(8,128)S(1)} %bitcast.605), channel_id=1, source_target_pairs={{0,16},{16,0},{1,17},{17,1},{2,18},{18,2},{3,19},{19,3},{4,20},{20... | collective-permute-start | bytes 73736 | tf_op jit(solution)/shard_map/ppermute | solution.py:34
  45.6 3.8 %collective-permute-start.15 = (f32[6,8,128]{2,1,0:T(8,128)S(1)}, f32[6,8,128]{2,1,0:T(8,128)S(1)}, u32[]{:S(2)}, u32[]{:S(2)}) collective-permute-start(f32[6,8,128]{2,1,0:T(8,128)S(1)} %get-tuple-element.65), channel_id=1, source_target_pairs={{0,12},{4,0},{8,4},{12,8},{1,13},{5,1},{9,5},{13,9},{2,14},{6,2},{... | collective-permute-start | bytes 73736 | tf_op jit(solution)/shard_map/ppermute | solution.py:37
  45.9 4.7 %collective-permute-start.16 = (f32[6,8,128]{2,1,0:T(8,128)S(1)}, f32[6,8,128]{2,1,0:T(8,128)S(1)}, u32[]{:S(2)}, u32[]{:S(2)}) collective-permute-start(f32[6,8,128]{2,1,0:T(8,128)S(1)} %get-tuple-element.66), channel_id=1, source_target_pairs={{0,4},{4,8},{8,12},{12,0},{1,5},{5,9},{9,13},{13,1},{2,6},{6,10},{... | collective-permute-start | bytes 73736 | tf_op jit(solution)/shard_map/ppermute | solution.py:36
  52.2 4.9 %collective-permute-start.22 = (f32[6,64]{1,0:T(8,128)S(1)}, f32[6,64]{1,0:T(8,128)S(1)}, u32[]{:S(2)}, u32[]{:S(2)}) collective-permute-start(f32[6,64]{1,0:T(8,128)S(1)} %reshape_squeeze.23), channel_id=1, source_target_pairs={{0,1},{1,2},{2,3},{4,5},{5,6},{6,7},{8,9},{9,10},{10,11},{12,13},{... | collective-permute-start | bytes 4616 | tf_op jit(solution)/shard_map/ppermute | solution.py:153
  58.1 5.8 %collective-permute-start.21 = (f32[6,64]{1,0:T(8,128)S(1)}, f32[6,64]{1,0:T(8,128)S(1)}, u32[]{:S(2)}, u32[]{:S(2)}) collective-permute-start(f32[6,64]{1,0:T(8,128)S(1)} %reshape_squeeze.22), channel_id=1, source_target_pairs={{1,0},{2,1},{3,2},{5,4},{6,5},{7,6},{9,8},{10,9},{11,10},{13,12},{... | collective-permute-start | bytes 4616 | tf_op jit(solution)/shard_map/ppermute | solution.py:154
  59.4 5.1 %collective-permute-start.19 = (f32[6,8,128]{2,1,0:T(8,128)S(1)}, f32[6,8,128]{2,1,0:T(8,128)S(1)}, u32[]{:S(2)}, u32[]{:S(2)}) collective-permute-start(f32[6,8,128]{2,1,0:T(8,128)S(1)} %get-tuple-element.79), channel_id=1, source_target_pairs={{0,12},{4,0},{8,4},{12,8},{1,13},{5,1},{9,5},{13,9},{2,14},{6,2},{... | collective-permute-start | bytes 73736 | tf_op jit(solution)/shard_map/ppermute | solution.py:37
  60.4 4.7 %collective-permute-start.20 = (f32[6,8,128]{2,1,0:T(8,128)S(1)}, f32[6,8,128]{2,1,0:T(8,128)S(1)}, u32[]{:S(2)}, u32[]{:S(2)}) collective-permute-start(f32[6,8,128]{2,1,0:T(8,128)S(1)} %get-tuple-element.80), channel_id=1, source_target_pairs={{0,4},{4,8},{8,12},{12,0},{1,5},{5,9},{9,13},{13,1},{2,6},{6,10},{... | collective-permute-start | bytes 73736 | tf_op jit(solution)/shard_map/ppermute | solution.py:36
  61.5 2.9 %collective-permute-start.18 = (f32[6,8,128]{2,1,0:T(8,128)S(1)}, f32[6,8,128]{2,1,0:T(8,128)S(1)}, u32[]{:S(2)}, u32[]{:S(2)}) collective-permute-start(f32[6,8,128]{2,1,0:T(8,128)S(1)} %bitcast.608), channel_id=1, source_target_pairs={{0,16},{16,0},{1,17},{17,1},{2,18},{18,2},{3,19},{19,3},{4,20},{20... | collective-permute-start | bytes 73736 | tf_op jit(solution)/shard_map/ppermute | solution.py:34
  61.5 3.0 %collective-permute-start.17 = (f32[6,8,128]{2,1,0:T(8,128)S(1)}, f32[6,8,128]{2,1,0:T(8,128)S(1)}, u32[]{:S(2)}, u32[]{:S(2)}) collective-permute-start(f32[6,8,128]{2,1,0:T(8,128)S(1)} %bitcast.602), channel_id=1, source_target_pairs={{0,16},{16,0},{1,17},{17,1},{2,18},{18,2},{3,19},{19,3},{4,20},{20... | collective-permute-start | bytes 73736 | tf_op jit(solution)/shard_map/ppermute | solution.py:35

commit v2 on v1

--- a/solution.py
+++ b/solution.py
@@ -4,7 +4,6 @@
 from jax.sharding import PartitionSpec as P
 
 BZ = 16
-STEPS = 4
 
 
 COMP = ((0.0, 0.0), (1.0, -0.5), (-0.5, 1.0), (-0.5, -0.5))
@@ -26,13 +25,14 @@
     return [(i, i + by) for i in range(count) if 0 <= i + by < count]
 
 
-def flat_z(face):
-    return face.reshape(face.shape[0], -1)
-
-
 def lateral_halos(block):
-    xlo = lax.ppermute(block[:, -1], "gx", ring("gx", 1))
-    xhi = lax.ppermute(block[:, 0], "gx", ring("gx", -1))
+    if lax.axis_size("gx") == 2:
+        pair = jnp.stack([block[:, -1], block[:, 0]])
+        got = lax.ppermute(pair, "gx", ring("gx", 1))
+        xlo, xhi = got[0], got[1]
+    else:
+        xlo = lax.ppermute(block[:, -1], "gx", ring("gx", 1))
+        xhi = lax.ppermute(block[:, 0], "gx", ring("gx", -1))
     ylo = lax.ppermute(block[:, :, -1], "gy", ring("gy", 1))
     yhi = lax.ppermute(block[:, :, 0], "gy", ring("gy", -1))
     return xlo, xhi, ylo, yhi
@@ -112,56 +112,69 @@
     index_x = lax.axis_index("gx")
     index_y = lax.axis_index("gy")
     index_z = lax.axis_index("gz")
-    zglob = index_z * cells_z + jnp.arange(cells_z, dtype=jnp.int32)
-    per_brick = cells_z // BZ
     bottom_brick = index_z == 0
     top_brick = index_z == bricks_z - 1
+    zext = index_z * cells_z + jnp.arange(-1, cells_z + 1, dtype=jnp.int32)
+    zown = zext[1:-1]
 
-    matched = (
-        (front_blocks[:, 0] == index_x)
-        & (front_blocks[:, 1] == index_y)
-        & (front_blocks[:, 2] // per_brick == index_z)
-    )
-    local_block = front_blocks[:, 2] - index_z * per_brick
-    hits = matched[:, None] & (
-        local_block[:, None] == jnp.arange(per_brick, dtype=jnp.int32)[None, :]
-    )
-    block_on = jnp.any(hits, 0)
-    cell_on = jnp.repeat(block_on, BZ)
+    matched = (front_blocks[:, 0] == index_x) & (front_blocks[:, 1] == index_y)
+
+    def active(zpos):
+        block = jnp.floor_divide(zpos, BZ)
+        hits = matched[:, None] & (front_blocks[:, 2][:, None] == block[None, :])
+        return jnp.any(hits, 0)
+
+    on_ext = active(zext)
+    on_own = on_ext[1:-1]
+
+    def step(fields, zlo, zhi, zpos, cell_on, offset):
+        xlo, xhi, ylo, yhi = lateral_halos(fields)
+        side = neighbours(fields, (xlo, xhi, ylo, yhi, zlo, zhi))
+        phi_new = jnp.where(
+            cell_on[None, None, None, :],
+            phase_update(fields, side, zpos, offset, depth),
+            fields[:4],
+        )
+        mu_new = chem_update(fields, side, fields[:4], phi_new)
+        return jnp.concatenate([phi_new, mu_new], 0)
+
+    def close_ext(ext):
+        low = jnp.where(bottom_brick, ext[..., 1:2], ext[..., 0:1])
+        high = jnp.where(top_brick, ext[..., -2:-1], ext[..., -1:])
+        return jnp.concatenate([low, ext[..., 1:-1], high], 3)
+
+    def two_step(ext, offset):
+        mid = close_ext(ext[..., 1:-1])
+        first = step(mid, ext[..., 0], ext[..., -1], zext, on_ext, offset)
+        first = close_ext(first)
+        return step(first[..., 1:-1], first[..., 0], first[..., -1], zown, on_own, offset)
 
     phi_start = jnp.stack([(labels == phase).astype(jnp.float32) for phase in range(4)])
     fields = jnp.concatenate([phi_start, mu_start], 0)
     nf = fields.shape[0]
-    offset = 0
-    for step in range(STEPS):
-        if step == STEPS // 2:
-            offset = lift
-            incoming = lax.ppermute(fields[..., : lift + 1], "gz", line("gz", -1))
-            count = lift + 1
-            ones = jnp.ones((1, cells_x, cells_y, count), jnp.float32)
-            incoming = jnp.where(
-                top_brick,
-                jnp.concatenate([ones, jnp.zeros((nf - 1, cells_x, cells_y, count), jnp.float32)], 0),
-                incoming,
-            )
-            zlo = jnp.where(bottom_brick, fields[..., lift], fields[..., lift - 1])
-            fields = jnp.concatenate([fields[..., lift:], incoming[..., :lift]], 3)
-            zhi = incoming[..., lift]
-            xlo, xhi, ylo, yhi = lateral_halos(fields)
-        else:
-            xlo, xhi, ylo, yhi = lateral_halos(fields)
-            from_below = lax.ppermute(flat_z(fields[..., -1]), "gz", line("gz", 1))
-            from_above = lax.ppermute(flat_z(fields[..., 0]), "gz", line("gz", -1))
-            zlo = jnp.where(bottom_brick, fields[..., 0], from_below.reshape(fields.shape[:3]))
-            zhi = jnp.where(top_brick, fields[..., -1], from_above.reshape(fields.shape[:3]))
-        side = neighbours(fields, (xlo, xhi, ylo, yhi, zlo, zhi))
-        phi_new = jnp.where(
-            cell_on[None, None, None, :],
-            phase_update(fields, side, zglob, offset, depth),
-            fields[:4],
-        )
-        mu_new = chem_update(fields, side, fields[:4], phi_new)
-        fields = jnp.concatenate([phi_new, mu_new], 0)
+    shape_xy = fields.shape[1:3]
+
+    def flat(part):
+        return part.reshape(nf, -1)
+
+    from_above = lax.ppermute(flat(fields[..., :2]), "gz", line("gz", -1))
+    from_below = lax.ppermute(flat(fields[..., -2:]), "gz", line("gz", 1))
+    ext = jnp.concatenate(
+        [from_below.reshape((nf,) + shape_xy + (2,)), fields, from_above.reshape((nf,) + shape_xy + (2,))], 3
+    )
+    fields = two_step(ext, 0)
+
+    count = lift + 2
+    incoming = lax.ppermute(flat(fields[..., :count]), "gz", line("gz", -1))
+    incoming = incoming.reshape((nf,) + shape_xy + (count,))
+    ones = jnp.ones((1,) + shape_xy + (count,), jnp.float32)
+    incoming = jnp.where(
+        top_brick,
+        jnp.concatenate([ones, jnp.zeros((nf - 1,) + shape_xy + (count,), jnp.float32)], 0),
+        incoming,
+    )
+    ext = jnp.concatenate([fields[..., lift - 2 :], incoming], 3)
+    fields = two_step(ext, lift)
     return (fields[:4], fields[4:])
 
 

time: 67.9 us -> 59.1 us (0.87)
  starting transfers between devices: 30 us -> 17.6 us
  local copies, waits for them, and re-layouts: 9.58 us -> 18.6 us
  waiting for transfers between devices: 20.7 us -> 13.4 us
  other arithmetic: 5.43 us -> 7.73 us
    ppermute x15 -> x7, starting transfers between devices: 19 us -> 8.42 us  [the longest x1 5.55 us: shards(): from_below = lax.ppermute(flat(fields[..., -2:]), 'gz', line('gz', 1))]
    ppermute x15 -> x7, waiting for transfers between devices: 13.7 us -> 4.17 us  [the longest x1 4.15 us: shards(): incoming = lax.ppermute(flat(fields[..., :count]), 'gz', line('gz', -1))]
    unnamed x10 -> x26, local copies, waits for them, and re-layouts: 2.87 us -> 8.37 us
    select_n x0 -> x9, local copies, waits for them, and re-layouts: none -> 5.08 us  [the longest x4 2.44 us: close_ext(): low = jnp.where(bottom_brick, ext[..., 1:2], ext[..., 0:1])]
    ppermute x4, starting transfers between devices: 8.2 us -> 5.7 us  [lateral_halos(): yhi = lax.ppermute(block[:, :, 0], 'gy', ring('gy', -1))]
    reshape x12 -> x1, local copies, waits for them, and re-layouts: 2.62 us -> 0.16 us  [flat(): return part.reshape(nf, -1)]
    ppermute x4, waiting for transfers between devices: 1.94 us -> 4.02 us  [lateral_halos(): yhi = lax.ppermute(block[:, :, 0], 'gy', ring('gy', -1))]
    sub x4, other arithmetic: 0.19 us -> 1.08 us  [chem_update(): delta = shape_fn(phi_new) - shape_fn(phi_old)]
  transfers between devices with their start and end apart: 23 -> 15, of which waited for: 10 -> 6; matrix products, arithmetic and copies ran while one was open for 8% -> 18% of each run, Pallas kernels for 0% -> 0%
where the time goes in v2:
time: 59.1 us; the launch traced here: 58.8 us
  local copies, waits for them, and re-layouts  18.6 us (31%)
  starting transfers between devices  17.6 us (30%)
  waiting for transfers between devices  13.4 us (23%)
  other arithmetic  7.73 us (13%)
  between operations  1.38 us (2%)
    unnamed x26, local copies, waits for them, and re-layouts  8.37 us
    ppermute x4, starting transfers between devices, lateral_halos(): yhi = lax.ppermute(block[:, :, 0], 'gy', ring('gy', -1))  5.7 us
    ppermute x1, starting transfers between devices, shards(): from_below = lax.ppermute(flat(fields[..., -2:]), 'gz', line('gz', 1))  5.55 us
    ppermute x4, waiting for transfers between devices, lateral_halos(): ylo = lax.ppermute(block[:, :, -1], 'gy', ring('gy', 1))  5.26 us
    ppermute x1, waiting for transfers between devices, shards(): incoming = lax.ppermute(flat(fields[..., :count]), 'gz', line('gz', -1))  4.15 us
    ppermute x4, waiting for transfers between devices, lateral_halos(): yhi = lax.ppermute(block[:, :, 0], 'gy', ring('gy', -1))  4.02 us
    ppermute x4, starting transfers between devices, lateral_halos(): ylo = lax.ppermute(block[:, :, -1], 'gy', ring('gy', 1))  3.47 us
    select_n x4, local copies, waits for them, and re-layouts, close_ext(): low = jnp.where(bottom_brick, ext[..., 1:2], ext[..., 0:1])  2.44 us
  transfers between devices with their start and end apart: 15, of which 6 were waited for; matrix products, arithmetic and copies ran while one was open for 18% of the time, Pallas kernels for 0%

profile of v2, /device:TPU:0, one launch (start us, length us, event | category | flops | bytes accessed | tf_op | source)
XLA Modules:
  0.0 58.8 jit_solution(1204355785035434012)
XLA Ops:
  0.6 0.8 %bitcast_dynamic-update-slice_fusion.3 = f32[6,8,8,128]{3,2,1,0:T(8,128)S(1)} fusion(s32[8,8,128]{2,1,0:T(8,128)} %param.3), kind=kLoop, calls=%fused_computation.505 | loop fusion | flops 16383 | bytes 65536
  1.5 0.8 %copy-done.2 = f32[2,8,8,128]{3,2,1,0:T(8,128)S(1)} copy-done((f32[2,8,8,128]{3,2,1,0:T(8,128)S(1)}, f32[2,8,8,128]{3,2,1,0:T(8,128)}, u32[]{:S(2)}) %copy-start.2) | copy-done | bytes 65560
  2.4 0.5 copy.117
  2.9 1.3 %collective-permute-start.1 = (f32[6,128]{0,1:T(8,128)S(1)}, f32[6,128]{0,1:T(8,128)S(1)}, u32[]{:S(2)}, u32[]{:S(2)}) collective-permute-start(f32[6,128]{0,1:T(8,128)S(1)} %bitcast.199), channel_id=1, source_target_pairs={{1,0},{2,1},{3,2},{5,4},{6,5},{7,6},{9,8},{10,9},{11,10},{13,12},{... | collective-permute-start | bytes 9224 | tf_op jit(solution)/shard_map/ppermute | solution.py:160
  4.2 0.5 copy.115
  4.8 5.6 %collective-permute-start = (f32[6,128]{0,1:T(8,128)S(1)}, f32[6,128]{0,1:T(8,128)S(1)}, u32[]{:S(2)}, u32[]{:S(2)}) collective-permute-start(f32[6,128]{0,1:T(8,128)S(1)} %bitcast.198), channel_id=1, source_target_pairs={{0,1},{1,2},{2,3},{4,5},{5,6},{6,7},{8,9},{9,10},{10,11},{12,13},{... | collective-permute-start | bytes 9224 | tf_op jit(solution)/shard_map/ppermute | solution.py:161
  10.5 0.7 %copy-done.3 = s32[32,3]{0,1:T(4,128)S(1)} copy-done((s32[32,3]{0,1:T(4,128)S(1)}, s32[32,3]{0,1:T(4,128)}, u32[]{:S(2)}) %copy-start.3) | copy-done | bytes 408
  11.4 0.5 copy.165
  11.9 0.5 copy.164
  12.5 0.6 %copy.119 = f32[6,8,8,1]{3,2,1,0:T(8,128)S(1)} copy(f32[6,8,8,1]{0,3,2,1:T(1,128)S(1)} %get-tuple-element.164) | data formatting | bytes 3072 | tf_op jit(solution)/shard_map/jit(_where)/select_n | solution.py:143
  13.1 0.6 %copy.125 = f32[6,8,8,1]{3,2,1,0:T(8,128)S(1)} copy(f32[6,8,8,1]{0,3,2,1:T(1,128)S(1)} %get-tuple-element.165) | data formatting | bytes 3072 | tf_op jit(solution)/shard_map/slice | solution.py:148
  13.8 0.6 %copy.118 = f32[6,8,8,1]{3,2,1,0:T(8,128)S(1)} copy(f32[6,8,8,1]{0,3,2,1:T(1,128)S(1)} %get-tuple-element.167) | data formatting | bytes 3072 | tf_op jit(solution)/shard_map/jit(_where)/select_n | solution.py:142
  14.4 0.6 %copy.126 = f32[6,8,8,1]{3,2,1,0:T(8,128)S(1)} copy(f32[6,8,8,1]{0,3,2,1:T(1,128)S(1)} %get-tuple-element.166) | data formatting | bytes 3072 | tf_op jit(solution)/shard_map/slice | solution.py:148
  15.0 0.5 pad_maximum_fusion.1
  15.8 2.9 %collective-permute-start.3 = (f32[6,8,130]{2,1,0:T(8,128)S(1)}, f32[6,8,130]{2,1,0:T(8,128)S(1)}, u32[]{:S(2)}, u32[]{:S(2)}) collective-permute-start(f32[6,8,130]{2,1,0:T(8,128)S(1)} %bitcast.200), channel_id=1, source_target_pairs={{0,12},{4,0},{8,4},{12,8},{1,13},{5,1},{9,5},{13,9},{2,14},{6,2},{... | collective-permute-start | bytes 74888 | tf_op jit(solution)/shard_map/ppermute | solution.py:37
  18.8 2.0 %collective-permute-done.3 = f32[6,8,130]{2,1,0:T(8,128)S(1)} collective-permute-done((f32[6,8,130]{2,1,0:T(8,128)S(1)}, f32[6,8,130]{2,1,0:T(8,128)S(1)}, u32[]{:S(2)}, u32[]{:S(2)}) %collective-permute-start.3) | collective-permute-done | bytes 24992 | tf_op jit(solution)/shard_map/ppermute | solution.py:37
  20.9 2.9 %collective-permute-done.4 = f32[6,8,130]{2,1,0:T(8,128)S(1)} collective-permute-done((f32[6,8,130]{2,1,0:T(8,128)S(1)}, f32[6,8,130]{2,1,0:T(8,128)S(1)}, u32[]{:S(2)}, u32[]{:S(2)}) %collective-permute-start.4) | collective-permute-done | bytes 24992 | tf_op jit(solution)/shard_map/ppermute | solution.py:36
  23.8 0.2 slice_multiply_fusion.1
  24.5 0.2 fusion.60
  24.8 0.2 pad_maximum_fusion.40
  25.0 0.2 fusion.324
  25.3 0.2 fusion.322
  25.8 0.6 collective-permute-start.6
  26.3 1.5 %collective-permute-start.7 = (f32[6,8,128]{2,1,0:T(8,128)S(1)}, f32[6,8,128]{2,1,0:T(8,128)S(1)}, u32[]{:S(2)}, u32[]{:S(2)}) collective-permute-start(f32[6,8,128]{2,1,0:T(8,128)S(1)} %bitcast.209), channel_id=1, source_target_pairs={{0,4},{4,8},{8,12},{12,0},{1,5},{5,9},{9,13},{13,1},{2,6},{6,10},{... | collective-permute-start | bytes 73736 | tf_op jit(solution)/shard_map/ppermute | solution.py:36
  27.9 0.5 copy.166
  28.3 0.5 copy.167
  28.8 0.5 copy.168
  29.3 0.5 copy.169
  29.8 0.6 %copy.134 = f32[6,8,8,1]{3,2,1,0:T(8,128)S(1)} copy(f32[6,8,8,1]{0,3,2,1:T(1,128)S(1)} %bitcast.189) | data formatting | bytes 3072 | tf_op jit(solution)/shard_map/jit(_where)/select_n | solution.py:143
  30.4 0.6 %copy.137 = f32[6,8,8,1]{3,2,1,0:T(8,128)S(1)} copy(f32[6,8,8,1]{0,3,2,1:T(1,128)S(1)} %bitcast.191) | data formatting | bytes 3072 | tf_op jit(solution)/shard_map/jit(_where)/select_n | solution.py:142
  31.1 0.2 slice_multiply_fusion.3
  32.1 0.2 fusion.329
  32.3 0.5 copy.170
  32.8 0.5 copy.171
  33.4 1.3 %collective-permute-start.8 = (f32[6,2176]{1,0:T(8,128)S(1)}, f32[6,2176]{1,0:T(8,128)S(1)}, u32[]{:S(2)}, u32[]{:S(2)}) collective-permute-start(f32[6,2176]{1,0:T(8,128)S(1)} %reshape.75), channel_id=1, source_target_pairs={{1,0},{2,1},{3,2},{5,4},{6,5},{7,6},{9,8},{10,9},{11,10},{13,12},{... | collective-permute-start | bytes 156680 | tf_op jit(solution)/shard_map/ppermute | solution.py:168
  34.9 0.6 %copy.142 = f32[6,8,8,1]{3,2,1,0:T(8,128)S(1)} copy(f32[6,8,8,1]{0,3,2,1:T(1,128)S(1)} %bitcast.192) | data formatting | bytes 3072 | tf_op jit(solution)/shard_map/jit(_where)/select_n | solution.py:142
  35.5 4.2 %collective-permute-done.8 = f32[6,2176]{1,0:T(8,128)S(1)} collective-permute-done((f32[6,2176]{1,0:T(8,128)S(1)}, f32[6,2176]{1,0:T(8,128)S(1)}, u32[]{:S(2)}, u32[]{:S(2)}) %collective-permute-start.8) | collective-permute-done | bytes 52256 | tf_op jit(solution)/shard_map/ppermute | solution.py:168
  39.7 0.2 select_n.84
  39.9 0.2 fusion.328
  40.1 0.2 pad_maximum_fusion.8
  40.3 0.5 copy.172
  40.8 0.5 copy.173
  41.3 0.6 %copy.143 = f32[6,8,8,1]{3,2,1,0:T(8,128)S(1)} copy(f32[6,8,8,1]{0,3,2,1:T(1,128)S(1)} %bitcast.195) | data formatting | bytes 3072 | tf_op jit(solution)/shard_map/jit(_where)/select_n | solution.py:143
  41.9 0.5 pad_maximum_fusion.5
  42.6 1.5 %collective-permute-start.10 = (f32[6,8,130]{2,1,0:T(8,128)S(1)}, f32[6,8,130]{2,1,0:T(8,128)S(1)}, u32[]{:S(2)}, u32[]{:S(2)}) collective-permute-start(f32[6,8,130]{2,1,0:T(8,128)S(1)} %bitcast.202), channel_id=1, source_target_pairs={{0,12},{4,0},{8,4},{12,8},{1,13},{5,1},{9,5},{13,9},{2,14},{6,2},{... | collective-permute-start | bytes 74888 | tf_op jit(solution)/shard_map/ppermute | solution.py:37
  44.1 0.6 %collective-permute-start.11 = (f32[6,8,130]{2,1,0:T(8,128)S(1)}, f32[6,8,130]{2,1,0:T(8,128)S(1)}, u32[]{:S(2)}, u32[]{:S(2)}) collective-permute-start(f32[6,8,130]{2,1,0:T(8,128)S(1)} %bitcast.206), channel_id=1, source_target_pairs={{0,4},{4,8},{8,12},{12,0},{1,5},{5,9},{9,13},{13,1},{2,6},{6,10},{... | collective-permute-start | bytes 74888 | tf_op jit(solution)/shard_map/ppermute | solution.py:36
  44.8 2.0 %collective-permute-done.10 = f32[6,8,130]{2,1,0:T(8,128)S(1)} collective-permute-done((f32[6,8,130]{2,1,0:T(8,128)S(1)}, f32[6,8,130]{2,1,0:T(8,128)S(1)}, u32[]{:S(2)}, u32[]{:S(2)}) %collective-permute-start.10) | collective-permute-done | bytes 24992 | tf_op jit(solution)/shard_map/ppermute | solution.py:37
  46.8 2.3 %collective-permute-done.11 = f32[6,8,130]{2,1,0:T(8,128)S(1)} collective-permute-done((f32[6,8,130]{2,1,0:T(8,128)S(1)}, f32[6,8,130]{2,1,0:T(8,128)S(1)}, u32[]{:S(2)}, u32[]{:S(2)}) %collective-permute-start.11) | collective-permute-done | bytes 24992 | tf_op jit(solution)/shard_map/ppermute | solution.py:36
  49.2 0.2 slice_multiply_fusion
  49.8 0.2 fusion.45
  50.1 0.2 pad_maximum_fusion.38
  50.3 0.2 fusion.316
  50.5 0.2 fusion.315
  51.1 0.7 %collective-permute-start.13 = (f32[6,8,128]{2,1,0:T(8,128)S(1)}, f32[6,8,128]{2,1,0:T(8,128)S(1)}, u32[]{:S(2)}, u32[]{:S(2)}) collective-permute-start(f32[6,8,128]{2,1,0:T(8,128)S(1)} %bitcast.210), channel_id=1, source_target_pairs={{0,12},{4,0},{8,4},{12,8},{1,13},{5,1},{9,5},{13,9},{2,14},{6,2},{... | collective-permute-start | bytes 73736 | tf_op jit(solution)/shard_map/ppermute | solution.py:37
  51.8 1.4 %collective-permute-start.14 = (f32[6,8,128]{2,1,0:T(8,128)S(1)}, f32[6,8,128]{2,1,0:T(8,128)S(1)}, u32[]{:S(2)}, u32[]{:S(2)}) collective-permute-start(f32[6,8,128]{2,1,0:T(8,128)S(1)} %bitcast.208), channel_id=1, source_target_pairs={{0,4},{4,8},{8,12},{12,0},{1,5},{5,9},{9,13},{13,1},{2,6},{6,10},{... | collective-permute-start | bytes 73736 | tf_op jit(solution)/shard_map/ppermute | solution.py:36
  53.2 0.5 copy.174
  53.7 0.5 copy.175
  54.2 0.5 copy.176
  54.7 0.5 copy.177
  55.2 0.6 %copy.156 = f32[6,8,8,1]{3,2,1,0:T(8,128)S(1)} copy(f32[6,8,8,1]{0,3,2,1:T(1,128)S(1)} %bitcast.187) | data formatting | bytes 3072 | tf_op jit(solution)/shard_map/jit(_where)/select_n | solution.py:143
  55.8 0.6 %copy.159 = f32[6,8,8,1]{3,2,1,0:T(8,128)S(1)} copy(f32[6,8,8,1]{0,3,2,1:T(1,128)S(1)} %bitcast.190) | data formatting | bytes 3072 | tf_op jit(solution)/shard_map/jit(_where)/select_n | solution.py:142
  56.6 0.2 slice_multiply_fusion.2
  57.1 0.8 %multiply_subtract_fusion.2 = (f32[4,8,8,128]{3,2,1,0:T(8,128)S(1)}, f32[4,8,8,128]{3,2,1,0:T(8,128)}) fusion(f32[4,8,8,130]{3,2,1,0:T(8,128)S(1)} %get-tuple-element.16, f32[1,8,8,128]{3,2,1,0:T(8,128)S(1)} %get-tuple-element.126, f32[1,8,8,128]{3,2,1,0:T(8,128)S(1)} %get-tuple-element.125, f32[1,8,8,128]{3,2,1,0:T(8,128)S(1)} %get-tuple-element.124, ...), kind=kLoop, calls=%fused_computation.184 | loop fusion | flops 425984 | bytes 524416 | tf_op jit(solution)/shard_map/sub | solution.py:94
  58.1 0.6 %pad_maximum_fusion.34 = f32[2,8,8,128]{3,2,1,0:T(8,128)} fusion(f32[1,8,8,128]{3,2,1,0:T(8,128)S(1)} %get-tuple-element.147, f32[1,8,8,128]{3,2,1,0:T(8,128)S(1)} %get-tuple-element.146), kind=kLoop, calls=%fused_computation.346 | loop fusion | flops 16384 | bytes 131072 | tf_op jit(solution)/shard_map/stack | solution.py:104
  (101 shorter events, 5.1 us)
Async XLA Ops:
  0.6 0.8 %copy-start = (s32[8,8,128]{2,1,0:T(8,128)S(1)}, s32[8,8,128]{2,1,0:T(8,128)}, u32[]{:S(2)}) copy-start(s32[8,8,128]{2,1,0:T(8,128)} %param.3) | copy-start | bytes 98308
  1.5 0.8 %copy-start.2 = (f32[2,8,8,128]{3,2,1,0:T(8,128)S(1)}, f32[2,8,8,128]{3,2,1,0:T(8,128)}, u32[]{:S(2)}) copy-start(f32[2,8,8,128]{3,2,1,0:T(8,128)} %param.4) | copy-start | bytes 196612
  2.9 9.5 %collective-permute-start.1 = (f32[6,128]{0,1:T(8,128)S(1)}, f32[6,128]{0,1:T(8,128)S(1)}, u32[]{:S(2)}, u32[]{:S(2)}) collective-permute-start(f32[6,128]{0,1:T(8,128)S(1)} %bitcast.199), channel_id=1, source_target_pairs={{1,0},{2,1},{3,2},{5,4},{6,5},{7,6},{9,8},{10,9},{11,10},{13,12},{... | collective-permute-start | bytes 9224 | tf_op jit(solution)/shard_map/ppermute | solution.py:160
  4.8 9.0 %collective-permute-start = (f32[6,128]{0,1:T(8,128)S(1)}, f32[6,128]{0,1:T(8,128)S(1)}, u32[]{:S(2)}, u32[]{:S(2)}) collective-permute-start(f32[6,128]{0,1:T(8,128)S(1)} %bitcast.198), channel_id=1, source_target_pairs={{0,1},{1,2},{2,3},{4,5},{5,6},{6,7},{8,9},{9,10},{10,11},{12,13},{... | collective-permute-start | bytes 9224 | tf_op jit(solution)/shard_map/ppermute | solution.py:161
  10.5 0.7 %copy-start.3 = (s32[32,3]{0,1:T(4,128)S(1)}, s32[32,3]{0,1:T(4,128)}, u32[]{:S(2)}) copy-start(s32[32,3]{0,1:T(4,128)} %param.5) | copy-start | bytes 1156
  15.7 8.1 %collective-permute-start.2 = (f32[2,6,8,130]{3,2,1,0:T(8,128)S(1)}, f32[2,6,8,130]{3,2,1,0:T(8,128)S(1)}, u32[]{:S(2)}, u32[]{:S(2)}) collective-permute-start(f32[2,6,8,130]{3,2,1,0:T(8,128)S(1)} %pad_maximum_fusion.18), channel_id=1, source_target_pairs={{0,16},{16,0},{1,17},{17,1},{2,18},{18,2},{3,19},{19,3},{4,20},{20... | collective-permute-start | bytes 149768 | tf_op jit(solution)/shard_map/ppermute | solution.py:31
  15.8 5.0 %collective-permute-start.3 = (f32[6,8,130]{2,1,0:T(8,128)S(1)}, f32[6,8,130]{2,1,0:T(8,128)S(1)}, u32[]{:S(2)}, u32[]{:S(2)}) collective-permute-start(f32[6,8,130]{2,1,0:T(8,128)S(1)} %bitcast.200), channel_id=1, source_target_pairs={{0,12},{4,0},{8,4},{12,8},{1,13},{5,1},{9,5},{13,9},{2,14},{6,2},{... | collective-permute-start | bytes 74888 | tf_op jit(solution)/shard_map/ppermute | solution.py:37
  18.7 5.0 %collective-permute-start.4 = (f32[6,8,130]{2,1,0:T(8,128)S(1)}, f32[6,8,130]{2,1,0:T(8,128)S(1)}, u32[]{:S(2)}, u32[]{:S(2)}) collective-permute-start(f32[6,8,130]{2,1,0:T(8,128)S(1)} %bitcast.204), channel_id=1, source_target_pairs={{0,4},{4,8},{8,12},{12,0},{1,5},{5,9},{9,13},{13,1},{2,6},{6,10},{... | collective-permute-start | bytes 74888 | tf_op jit(solution)/shard_map/ppermute | solution.py:36
  25.7 5.4 %collective-permute-start.5 = (f32[2,6,8,128]{3,2,1,0:T(8,128)S(1)}, f32[2,6,8,128]{3,2,1,0:T(8,128)S(1)}, u32[]{:S(2)}, u32[]{:S(2)}) collective-permute-start(f32[2,6,8,128]{3,2,1,0:T(8,128)S(1)} %pad_maximum_fusion.35), channel_id=1, source_target_pairs={{0,16},{16,0},{1,17},{17,1},{2,18},{18,2},{3,19},{19,3},{4,20},{20... | collective-permute-start | bytes 147464 | tf_op jit(solution)/shard_map/ppermute | solution.py:31
  25.8 5.3 %collective-permute-start.6 = (f32[6,8,128]{2,1,0:T(8,128)S(1)}, f32[6,8,128]{2,1,0:T(8,128)S(1)}, u32[]{:S(2)}, u32[]{:S(2)}) collective-permute-start(f32[6,8,128]{2,1,0:T(8,128)S(1)} %bitcast.211), channel_id=1, source_target_pairs={{0,12},{4,0},{8,4},{12,8},{1,13},{5,1},{9,5},{13,9},{2,14},{6,2},{... | collective-permute-start | bytes 73736 | tf_op jit(solution)/shard_map/ppermute | solution.py:37
  26.3 4.8 %collective-permute-start.7 = (f32[6,8,128]{2,1,0:T(8,128)S(1)}, f32[6,8,128]{2,1,0:T(8,128)S(1)}, u32[]{:S(2)}, u32[]{:S(2)}) collective-permute-start(f32[6,8,128]{2,1,0:T(8,128)S(1)} %bitcast.209), channel_id=1, source_target_pairs={{0,4},{4,8},{8,12},{12,0},{1,5},{5,9},{9,13},{13,1},{2,6},{6,10},{... | collective-permute-start | bytes 73736 | tf_op jit(solution)/shard_map/ppermute | solution.py:36
  33.4 6.2 %collective-permute-start.8 = (f32[6,2176]{1,0:T(8,128)S(1)}, f32[6,2176]{1,0:T(8,128)S(1)}, u32[]{:S(2)}, u32[]{:S(2)}) collective-permute-start(f32[6,2176]{1,0:T(8,128)S(1)} %reshape.75), channel_id=1, source_target_pairs={{1,0},{2,1},{3,2},{5,4},{6,5},{7,6},{9,8},{10,9},{11,10},{13,12},{... | collective-permute-start | bytes 156680 | tf_op jit(solution)/shard_map/ppermute | solution.py:168
  34.9 4.8 %copy-start.1 = (f32[6,2176]{1,0:T(8,128)S(1)}, f32[6,2176]{1,0:T(8,128)}, u32[]{:S(2)}) copy-start(f32[6,2176]{1,0:T(8,128)} %constant.27.clone.1) | copy-start | bytes 156676
  42.5 6.6 %collective-permute-start.9 = (f32[2,6,8,130]{3,2,1,0:T(8,128)S(1)}, f32[2,6,8,130]{3,2,1,0:T(8,128)S(1)}, u32[]{:S(2)}, u32[]{:S(2)}) collective-permute-start(f32[2,6,8,130]{3,2,1,0:T(8,128)S(1)} %pad_maximum_fusion.19), channel_id=1, source_target_pairs={{0,16},{16,0},{1,17},{17,1},{2,18},{18,2},{3,19},{19,3},{4,20},{20... | collective-permute-start | bytes 149768 | tf_op jit(solution)/shard_map/ppermute | solution.py:31
  42.6 4.1 %collective-permute-start.10 = (f32[6,8,130]{2,1,0:T(8,128)S(1)}, f32[6,8,130]{2,1,0:T(8,128)S(1)}, u32[]{:S(2)}, u32[]{:S(2)}) collective-permute-start(f32[6,8,130]{2,1,0:T(8,128)S(1)} %bitcast.202), channel_id=1, source_target_pairs={{0,12},{4,0},{8,4},{12,8},{1,13},{5,1},{9,5},{13,9},{2,14},{6,2},{... | collective-permute-start | bytes 74888 | tf_op jit(solution)/shard_map/ppermute | solution.py:37
  44.1 5.0 %collective-permute-start.11 = (f32[6,8,130]{2,1,0:T(8,128)S(1)}, f32[6,8,130]{2,1,0:T(8,128)S(1)}, u32[]{:S(2)}, u32[]{:S(2)}) collective-permute-start(f32[6,8,130]{2,1,0:T(8,128)S(1)} %bitcast.206), channel_id=1, source_target_pairs={{0,4},{4,8},{8,12},{12,0},{1,5},{5,9},{9,13},{13,1},{2,6},{6,10},{... | collective-permute-start | bytes 74888 | tf_op jit(solution)/shard_map/ppermute | solution.py:36
  51.0 5.4 %collective-permute-start.12 = (f32[2,6,8,128]{3,2,1,0:T(8,128)S(1)}, f32[2,6,8,128]{3,2,1,0:T(8,128)S(1)}, u32[]{:S(2)}, u32[]{:S(2)}) collective-permute-start(f32[2,6,8,128]{3,2,1,0:T(8,128)S(1)} %pad_maximum_fusion.36), channel_id=1, source_target_pairs={{0,16},{16,0},{1,17},{17,1},{2,18},{18,2},{3,19},{19,3},{4,20},{20... | collective-permute-start | bytes 147464 | tf_op jit(solution)/shard_map/ppermute | solution.py:31
  51.1 5.3 %collective-permute-start.13 = (f32[6,8,128]{2,1,0:T(8,128)S(1)}, f32[6,8,128]{2,1,0:T(8,128)S(1)}, u32[]{:S(2)}, u32[]{:S(2)}) collective-permute-start(f32[6,8,128]{2,1,0:T(8,128)S(1)} %bitcast.210), channel_id=1, source_target_pairs={{0,12},{4,0},{8,4},{12,8},{1,13},{5,1},{9,5},{13,9},{2,14},{6,2},{... | collective-permute-start | bytes 73736 | tf_op jit(solution)/shard_map/ppermute | solution.py:37
  51.8 4.7 %collective-permute-start.14 = (f32[6,8,128]{2,1,0:T(8,128)S(1)}, f32[6,8,128]{2,1,0:T(8,128)S(1)}, u32[]{:S(2)}, u32[]{:S(2)}) collective-permute-start(f32[6,8,128]{2,1,0:T(8,128)S(1)} %bitcast.208), channel_id=1, source_target_pairs={{0,4},{4,8},{8,12},{12,0},{1,5},{5,9},{9,13},{13,1},{2,6},{6,10},{... | collective-permute-start | bytes 73736 | tf_op jit(solution)/shard_map/ppermute | solution.py:36

commit v3 on v2

--- a/solution.py
+++ b/solution.py
@@ -114,8 +114,7 @@
     index_z = lax.axis_index("gz")
     bottom_brick = index_z == 0
     top_brick = index_z == bricks_z - 1
-    zext = index_z * cells_z + jnp.arange(-1, cells_z + 1, dtype=jnp.int32)
-    zown = zext[1:-1]
+    base_z = index_z * cells_z
 
     matched = (front_blocks[:, 0] == index_x) & (front_blocks[:, 1] == index_y)
 
@@ -124,57 +123,53 @@
         hits = matched[:, None] & (front_blocks[:, 2][:, None] == block[None, :])
         return jnp.any(hits, 0)
 
-    on_ext = active(zext)
-    on_own = on_ext[1:-1]
-
-    def step(fields, zlo, zhi, zpos, cell_on, offset):
+    def step(ext, first, offset):
+        fields = ext[..., 1:-1]
+        zpos = base_z + first + jnp.arange(fields.shape[3], dtype=jnp.int32)
         xlo, xhi, ylo, yhi = lateral_halos(fields)
-        side = neighbours(fields, (xlo, xhi, ylo, yhi, zlo, zhi))
+        side = neighbours(fields, (xlo, xhi, ylo, yhi, ext[..., 0], ext[..., -1]))
         phi_new = jnp.where(
-            cell_on[None, None, None, :],
+            active(zpos)[None, None, None, :],
             phase_update(fields, side, zpos, offset, depth),
             fields[:4],
         )
         mu_new = chem_update(fields, side, fields[:4], phi_new)
         return jnp.concatenate([phi_new, mu_new], 0)
 
-    def close_ext(ext):
-        low = jnp.where(bottom_brick, ext[..., 1:2], ext[..., 0:1])
-        high = jnp.where(top_brick, ext[..., -2:-1], ext[..., -1:])
-        return jnp.concatenate([low, ext[..., 1:-1], high], 3)
+    def layer_index(ext):
+        return lax.broadcasted_iota(jnp.int32, ext.shape, 3)
 
-    def two_step(ext, offset):
-        mid = close_ext(ext[..., 1:-1])
-        first = step(mid, ext[..., 0], ext[..., -1], zext, on_ext, offset)
-        first = close_ext(first)
-        return step(first[..., 1:-1], first[..., 0], first[..., -1], zown, on_own, offset)
+    def edge_at(ext, at, cond):
+        up = jnp.concatenate([ext[..., :1], ext[..., :-1]], 3)
+        return jnp.where(cond & (layer_index(ext) == at), up, ext)
+
+    def edge_below(ext, at, cond):
+        down = jnp.concatenate([ext[..., 1:], ext[..., -1:]], 3)
+        return jnp.where(cond & (layer_index(ext) == at), down, ext)
 
     phi_start = jnp.stack([(labels == phase).astype(jnp.float32) for phase in range(4)])
     fields = jnp.concatenate([phi_start, mu_start], 0)
     nf = fields.shape[0]
     shape_xy = fields.shape[1:3]
 
-    def flat(part):
-        return part.reshape(nf, -1)
-
-    from_above = lax.ppermute(flat(fields[..., :2]), "gz", line("gz", -1))
-    from_below = lax.ppermute(flat(fields[..., -2:]), "gz", line("gz", 1))
-    ext = jnp.concatenate(
-        [from_below.reshape((nf,) + shape_xy + (2,)), fields, from_above.reshape((nf,) + shape_xy + (2,))], 3
+    low = lift - 4
+    count = lift + 4
+    above = lax.ppermute(fields[..., :count].reshape(nf, -1), "gz", line("gz", -1))
+    ext = jnp.concatenate([fields[..., low:], above.reshape((nf,) + shape_xy + (count,))], 3)
+    ext = edge_at(ext, cells_z - low, top_brick)
+    ext = step(ext, low + 1, 0)
+    ext = edge_at(ext, cells_z - low - 1, top_brick)
+    ext = step(ext, low + 2, 0)
+    liquid = jnp.concatenate(
+        [jnp.ones((1,) + ext.shape[1:], jnp.float32), jnp.zeros((nf - 1,) + ext.shape[1:], jnp.float32)], 0
     )
-    fields = two_step(ext, 0)
-
-    count = lift + 2
-    incoming = lax.ppermute(flat(fields[..., :count]), "gz", line("gz", -1))
-    incoming = incoming.reshape((nf,) + shape_xy + (count,))
-    ones = jnp.ones((1,) + shape_xy + (count,), jnp.float32)
-    incoming = jnp.where(
-        top_brick,
-        jnp.concatenate([ones, jnp.zeros((nf - 1,) + shape_xy + (count,), jnp.float32)], 0),
-        incoming,
-    )
-    ext = jnp.concatenate([fields[..., lift - 2 :], incoming], 3)
-    fields = two_step(ext, lift)
+    ext = jnp.where(top_brick & (layer_index(ext) >= cells_z - lift + 2), liquid, ext)
+    ext = edge_below(ext, 1, bottom_brick)
+    ext = edge_at(ext, cells_z + 2, top_brick)
+    ext = step(ext, -1, lift)
+    ext = edge_below(ext, 0, bottom_brick)
+    ext = edge_at(ext, cells_z + 1, top_brick)
+    fields = step(ext, 0, lift)
     return (fields[:4], fields[4:])
 
 

time: 59.1 us -> 44.8 us (0.76)
  local copies, waits for them, and re-layouts: 18.6 us -> 8.42 us
  starting transfers between devices: 17.6 us -> 13.4 us
  waiting for transfers between devices: 13.4 us -> 14.2 us
  other arithmetic: 7.73 us -> 7.06 us
    ppermute x3 -> x1, starting transfers between devices: 8.13 us -> 1.29 us  [shards(): lax.ppermute(fields[..., :count].reshape(nf, -1), 'gz', line('gz', -1))]
    select_n x9 -> x0, local copies, waits for them, and re-layouts: 5.08 us -> none  [the longest x4 2.44 us: close_ext(): low = jnp.where(bottom_brick, ext[..., 1:2], ext[..., 0:1])]
    unnamed x26 -> x10, local copies, waits for them, and re-layouts: 8.37 us -> 3.64 us
    ppermute x4, starting transfers between devices: 3.47 us -> 6.99 us  [lateral_halos(): ylo = lax.ppermute(block[:, :, -1], 'gy', ring('gy', 1))]
    slice x14, local copies, waits for them, and re-layouts: 3.76 us -> 0.84 us  [the longest x4 0.54 us: edge_below(): down = jnp.concatenate([ext[..., 1:], ext[..., -1:]], 3)]
    ppermute x4, waiting for transfers between devices: 5.26 us -> 6.78 us  [lateral_halos(): ylo = lax.ppermute(block[:, :, -1], 'gy', ring('gy', 1))]
    ppermute x4, waiting for transfers between devices: 4.02 us -> 3.01 us  [lateral_halos(): yhi = lax.ppermute(block[:, :, 0], 'gy', ring('gy', -1))]
    select_n x8 -> x7, other arithmetic: 0.12 us -> 1.1 us  [the longest x4 0.79 us: edge_at(): return jnp.where(cond & (layer_index(ext) == at), up, ext)]
  transfers between devices with their start and end apart: 15 -> 13, of which waited for: 6 -> 8; matrix products, arithmetic and copies ran while one was open for 18% -> 5% of each run, Pallas kernels for 0% -> 0%
where the time goes in v3:
time: 44.8 us; the launch traced here: 44.5 us
  waiting for transfers between devices  14.2 us (32%)
  starting transfers between devices  13.4 us (30%)
  local copies, waits for them, and re-layouts  8.42 us (19%)
  other arithmetic  7.06 us (16%)
  between operations  1.34 us (3%)
    ppermute x4, starting transfers between devices, lateral_halos(): ylo = lax.ppermute(block[:, :, -1], 'gy', ring('gy', 1))  6.99 us
    ppermute x4, waiting for transfers between devices, lateral_halos(): ylo = lax.ppermute(block[:, :, -1], 'gy', ring('gy', 1))  6.78 us
    ppermute x4, starting transfers between devices, lateral_halos(): yhi = lax.ppermute(block[:, :, 0], 'gy', ring('gy', -1))  4.95 us
    ppermute x1, waiting for transfers between devices, shards(): lax.ppermute(fields[..., :count].reshape(nf, -1), 'gz', line('gz', -1))  4.39 us
    unnamed x10, local copies, waits for them, and re-layouts  3.64 us
    ppermute x4, waiting for transfers between devices, lateral_halos(): yhi = lax.ppermute(block[:, :, 0], 'gy', ring('gy', -1))  3.01 us
    add x8, other arithmetic, phase_update(): phi[phase] + DT * (rates[phase] - mean_rate)  1.34 us
    ppermute x1, starting transfers between devices, shards(): lax.ppermute(fields[..., :count].reshape(nf, -1), 'gz', line('gz', -1))  1.29 us
  transfers between devices with their start and end apart: 13, of which 8 were waited for; matrix products, arithmetic and copies ran while one was open for 5% of the time, Pallas kernels for 0%

profile of v3, /device:TPU:0, one launch (start us, length us, event | category | flops | bytes accessed | tf_op | source)
XLA Modules:
  0.0 44.5 jit_solution(5411344175420303192)
XLA Ops:
  0.6 0.8 %bitcast_dynamic-update-slice_fusion.3 = f32[6,8,8,128]{3,2,0,1:T(8,128)S(1)} fusion(s32[8,8,128]{2,1,0:T(8,128)} %param.3), kind=kLoop, calls=%fused_computation.486 | loop fusion | flops 16383 | bytes 65536
  1.5 0.8 %copy-done.2 = f32[2,8,8,128]{3,2,1,0:T(8,128)S(1)} copy-done((f32[2,8,8,128]{3,2,1,0:T(8,128)S(1)}, f32[2,8,8,128]{3,2,1,0:T(8,128)}, u32[]{:S(2)}) %copy-start.2) | copy-done | bytes 65560
  2.3 0.2 reshape.136
  2.5 1.3 %collective-permute-start = (f32[6,2304]{1,0:T(8,128)S(1)}, f32[6,2304]{1,0:T(8,128)S(1)}, u32[]{:S(2)}, u32[]{:S(2)}) collective-permute-start(f32[6,2304]{1,0:T(8,128)S(1)} %reshape.136), channel_id=1, source_target_pairs={{1,0},{2,1},{3,2},{5,4},{6,5},{7,6},{9,8},{10,9},{11,10},{13,12},{... | collective-permute-start | bytes 165896 | tf_op jit(solution)/shard_map/ppermute | solution.py:157
  4.1 0.6 %copy-done.3 = s32[32,3]{0,1:T(4,128)S(1)} copy-done((s32[32,3]{0,1:T(4,128)S(1)}, s32[32,3]{0,1:T(4,128)}, u32[]{:S(2)}) %copy-start.3) | copy-done | bytes 408
  5.4 4.4 %collective-permute-done = f32[6,2304]{1,0:T(8,128)S(1)} collective-permute-done((f32[6,2304]{1,0:T(8,128)S(1)}, f32[6,2304]{1,0:T(8,128)S(1)}, u32[]{:S(2)}, u32[]{:S(2)}) %collective-permute-start) | collective-permute-done | bytes 55328 | tf_op jit(solution)/shard_map/ppermute | solution.py:157
  9.8 0.2 reshape.137
  10.0 0.2 fusion
  10.2 0.3 fusion.1
  10.4 0.3 fusion.314
  10.7 0.3 fusion.315
  11.1 2.0 %collective-permute-start.3 = (f32[6,8,134]{2,1,0:T(8,128)S(1)}, f32[6,8,134]{2,1,0:T(8,128)S(1)}, u32[]{:S(2)}, u32[]{:S(2)}) collective-permute-start(f32[6,8,134]{2,1,0:T(8,128)S(1)} %bitcast.134), channel_id=1, source_target_pairs={{0,4},{4,8},{8,12},{12,0},{1,5},{5,9},{9,13},{13,1},{2,6},{6,10},{... | collective-permute-start | bytes 77192 | tf_op jit(solution)/shard_map/ppermute | solution.py:36
  13.1 1.0 %collective-permute-start.2 = (f32[6,8,134]{2,1,0:T(8,128)S(1)}, f32[6,8,134]{2,1,0:T(8,128)S(1)}, u32[]{:S(2)}, u32[]{:S(2)}) collective-permute-start(f32[6,8,134]{2,1,0:T(8,128)S(1)} %bitcast.140), channel_id=1, source_target_pairs={{0,12},{4,0},{8,4},{12,8},{1,13},{5,1},{9,5},{13,9},{2,14},{6,2},{... | collective-permute-start | bytes 77192 | tf_op jit(solution)/shard_map/ppermute | solution.py:37
  14.2 0.2 fusion.313
  14.4 1.7 %collective-permute-done.3 = f32[6,8,134]{2,1,0:T(8,128)S(1)} collective-permute-done((f32[6,8,134]{2,1,0:T(8,128)S(1)}, f32[6,8,134]{2,1,0:T(8,128)S(1)}, u32[]{:S(2)}, u32[]{:S(2)}) %collective-permute-start.3) | collective-permute-done | bytes 25760 | tf_op jit(solution)/shard_map/ppermute | solution.py:36
  16.2 1.0 %collective-permute-done.2 = f32[6,8,134]{2,1,0:T(8,128)S(1)} collective-permute-done((f32[6,8,134]{2,1,0:T(8,128)S(1)}, f32[6,8,134]{2,1,0:T(8,128)S(1)}, u32[]{:S(2)}, u32[]{:S(2)}) %collective-permute-start.2) | collective-permute-done | bytes 25760 | tf_op jit(solution)/shard_map/ppermute | solution.py:37
  17.2 0.2 slice_multiply_fusion.2
  17.5 0.1 fusion.233
  17.6 0.2 multiply_add_fusion.14
  17.8 0.2 multiply_add_fusion.13
  18.0 0.2 multiply_subtract_fusion.2
  18.2 0.2 fusion.73
  18.5 0.2 maximum_select_fusion
  18.7 0.3 fusion.311
  19.0 0.3 fusion.312
  19.3 2.4 %collective-permute-start.6 = (f32[6,8,132]{2,1,0:T(8,128)S(1)}, f32[6,8,132]{2,1,0:T(8,128)S(1)}, u32[]{:S(2)}, u32[]{:S(2)}) collective-permute-start(f32[6,8,132]{2,1,0:T(8,128)S(1)} %bitcast.136), channel_id=1, source_target_pairs={{0,4},{4,8},{8,12},{12,0},{1,5},{5,9},{9,13},{13,1},{2,6},{6,10},{... | collective-permute-start | bytes 76040 | tf_op jit(solution)/shard_map/ppermute | solution.py:36
  21.8 0.5 %collective-permute-start.5 = (f32[6,8,132]{2,1,0:T(8,128)S(1)}, f32[6,8,132]{2,1,0:T(8,128)S(1)}, u32[]{:S(2)}, u32[]{:S(2)}) collective-permute-start(f32[6,8,132]{2,1,0:T(8,128)S(1)} %bitcast.142), channel_id=1, source_target_pairs={{0,12},{4,0},{8,4},{12,8},{1,13},{5,1},{9,5},{13,9},{2,14},{6,2},{... | collective-permute-start | bytes 76040 | tf_op jit(solution)/shard_map/ppermute | solution.py:37
  22.4 0.2 fusion.310
  22.7 1.7 %collective-permute-done.6 = f32[6,8,132]{2,1,0:T(8,128)S(1)} collective-permute-done((f32[6,8,132]{2,1,0:T(8,128)S(1)}, f32[6,8,132]{2,1,0:T(8,128)S(1)}, u32[]{:S(2)}, u32[]{:S(2)}) %collective-permute-start.6) | collective-permute-done | bytes 25376 | tf_op jit(solution)/shard_map/ppermute | solution.py:36
  24.4 1.4 %collective-permute-done.5 = f32[6,8,132]{2,1,0:T(8,128)S(1)} collective-permute-done((f32[6,8,132]{2,1,0:T(8,128)S(1)}, f32[6,8,132]{2,1,0:T(8,128)S(1)}, u32[]{:S(2)}, u32[]{:S(2)}) %collective-permute-start.5) | collective-permute-done | bytes 25376 | tf_op jit(solution)/shard_map/ppermute | solution.py:37
  26.0 0.2 slice_multiply_fusion.1
  26.2 0.1 fusion.213
  26.3 0.2 multiply_add_fusion.9
  26.6 0.2 multiply_add_fusion.8
  26.7 0.2 multiply_subtract_fusion.1
  26.9 0.2 fusion.58
  27.2 0.9 %copy-done.1 = f32[6,8,8,132]{3,2,0,1:T(8,128)S(1)} copy-done((f32[6,8,8,132]{3,2,0,1:T(8,128)S(1)}, f32[6,8,8,132]{3,2,0,1:T(8,128)}, u32[]{:S(2)}) %copy-start.1) | copy-done | bytes 202776
  28.2 0.2 slice.1243
  28.6 0.2 maximum_select_fusion.3
  28.7 0.3 fusion.308
  29.0 0.3 fusion.309
  29.4 1.5 %collective-permute-start.9 = (f32[6,8,130]{2,1,0:T(8,128)S(1)}, f32[6,8,130]{2,1,0:T(8,128)S(1)}, u32[]{:S(2)}, u32[]{:S(2)}) collective-permute-start(f32[6,8,130]{2,1,0:T(8,128)S(1)} %bitcast.138), channel_id=1, source_target_pairs={{0,4},{4,8},{8,12},{12,0},{1,5},{5,9},{9,13},{13,1},{2,6},{6,10},{... | collective-permute-start | bytes 74888 | tf_op jit(solution)/shard_map/ppermute | solution.py:36
  30.9 1.4 %collective-permute-start.8 = (f32[6,8,130]{2,1,0:T(8,128)S(1)}, f32[6,8,130]{2,1,0:T(8,128)S(1)}, u32[]{:S(2)}, u32[]{:S(2)}) collective-permute-start(f32[6,8,130]{2,1,0:T(8,128)S(1)} %bitcast.144), channel_id=1, source_target_pairs={{0,12},{4,0},{8,4},{12,8},{1,13},{5,1},{9,5},{13,9},{2,14},{6,2},{... | collective-permute-start | bytes 74888 | tf_op jit(solution)/shard_map/ppermute | solution.py:37
  32.5 0.2 fusion.307
  32.7 1.7 %collective-permute-done.9 = f32[6,8,130]{2,1,0:T(8,128)S(1)} collective-permute-done((f32[6,8,130]{2,1,0:T(8,128)S(1)}, f32[6,8,130]{2,1,0:T(8,128)S(1)}, u32[]{:S(2)}, u32[]{:S(2)}) %collective-permute-start.9) | collective-permute-done | bytes 24992 | tf_op jit(solution)/shard_map/ppermute | solution.py:36
  34.5 0.5 %collective-permute-done.8 = f32[6,8,130]{2,1,0:T(8,128)S(1)} collective-permute-done((f32[6,8,130]{2,1,0:T(8,128)S(1)}, f32[6,8,130]{2,1,0:T(8,128)S(1)}, u32[]{:S(2)}, u32[]{:S(2)}) %collective-permute-start.8) | collective-permute-done | bytes 24992 | tf_op jit(solution)/shard_map/ppermute | solution.py:37
  35.1 0.2 slice_multiply_fusion
  35.3 0.1 fusion.193
  35.5 0.2 multiply_add_fusion.4
  35.7 0.2 multiply_add_fusion.3
  35.9 0.2 multiply_subtract_fusion
  36.0 0.2 fusion.43
  36.5 0.2 slice.1301
  36.8 0.2 maximum_select_fusion.5
  37.0 0.2 fusion.306
  37.1 0.2 fusion.304
  37.4 1.0 %collective-permute-start.12 = (f32[6,8,128]{2,1,0:T(8,128)S(1)}, f32[6,8,128]{2,1,0:T(8,128)S(1)}, u32[]{:S(2)}, u32[]{:S(2)}) collective-permute-start(f32[6,8,128]{2,1,0:T(8,128)S(1)} %bitcast.146), channel_id=1, source_target_pairs={{0,4},{4,8},{8,12},{12,0},{1,5},{5,9},{9,13},{13,1},{2,6},{6,10},{... | collective-permute-start | bytes 73736 | tf_op jit(solution)/shard_map/ppermute | solution.py:36
  38.4 2.0 %collective-permute-start.11 = (f32[6,8,128]{2,1,0:T(8,128)S(1)}, f32[6,8,128]{2,1,0:T(8,128)S(1)}, u32[]{:S(2)}, u32[]{:S(2)}) collective-permute-start(f32[6,8,128]{2,1,0:T(8,128)S(1)} %bitcast.148), channel_id=1, source_target_pairs={{0,12},{4,0},{8,4},{12,8},{1,13},{5,1},{9,5},{13,9},{2,14},{6,2},{... | collective-permute-start | bytes 73736 | tf_op jit(solution)/shard_map/ppermute | solution.py:37
  40.4 0.1 fusion.305
  40.5 1.6 %collective-permute-done.12 = f32[6,8,128]{2,1,0:T(8,128)S(1)} collective-permute-done((f32[6,8,128]{2,1,0:T(8,128)S(1)}, f32[6,8,128]{2,1,0:T(8,128)S(1)}, u32[]{:S(2)}, u32[]{:S(2)}) %collective-permute-start.12) | collective-permute-done | bytes 24608 | tf_op jit(solution)/shard_map/ppermute | solution.py:36
  42.3 0.2 slice_multiply_fusion.3
  42.6 0.1 multiply_add_fusion.19
  42.9 0.7 %copy.124 = f32[4,8,8,128]{3,2,1,0:T(8,128)} copy(f32[4,8,8,128]{3,2,0,1:T(8,128)S(1)} %get-tuple-element.13) | data formatting | bytes 262144
  43.8 0.6 %copy.125 = f32[2,8,8,128]{3,2,1,0:T(8,128)} copy(f32[2,8,8,128]{3,2,0,1:T(8,128)S(1)} %pad_maximum_fusion.22) | data formatting | bytes 131072
  (92 shorter events, 3.4 us)
Async XLA Ops:
  0.6 0.8 %copy-start = (s32[8,8,128]{2,1,0:T(8,128)S(1)}, s32[8,8,128]{2,1,0:T(8,128)}, u32[]{:S(2)}) copy-start(s32[8,8,128]{2,1,0:T(8,128)} %param.3) | copy-start | bytes 98308
  1.5 0.8 %copy-start.2 = (f32[2,8,8,128]{3,2,1,0:T(8,128)S(1)}, f32[2,8,8,128]{3,2,1,0:T(8,128)}, u32[]{:S(2)}) copy-start(f32[2,8,8,128]{3,2,1,0:T(8,128)} %param.4) | copy-start | bytes 196612
  2.5 7.3 %collective-permute-start = (f32[6,2304]{1,0:T(8,128)S(1)}, f32[6,2304]{1,0:T(8,128)S(1)}, u32[]{:S(2)}, u32[]{:S(2)}) collective-permute-start(f32[6,2304]{1,0:T(8,128)S(1)} %reshape.136), channel_id=1, source_target_pairs={{1,0},{2,1},{3,2},{5,4},{6,5},{7,6},{9,8},{10,9},{11,10},{13,12},{... | collective-permute-start | bytes 165896 | tf_op jit(solution)/shard_map/ppermute | solution.py:157
  4.0 0.7 %copy-start.3 = (s32[32,3]{0,1:T(4,128)S(1)}, s32[32,3]{0,1:T(4,128)}, u32[]{:S(2)}) copy-start(s32[32,3]{0,1:T(4,128)} %param.5) | copy-start | bytes 1156
  11.1 5.0 %collective-permute-start.3 = (f32[6,8,134]{2,1,0:T(8,128)S(1)}, f32[6,8,134]{2,1,0:T(8,128)S(1)}, u32[]{:S(2)}, u32[]{:S(2)}) collective-permute-start(f32[6,8,134]{2,1,0:T(8,128)S(1)} %bitcast.134), channel_id=1, source_target_pairs={{0,4},{4,8},{8,12},{12,0},{1,5},{5,9},{9,13},{13,1},{2,6},{6,10},{... | collective-permute-start | bytes 77192 | tf_op jit(solution)/shard_map/ppermute | solution.py:36
  13.1 4.1 %collective-permute-start.2 = (f32[6,8,134]{2,1,0:T(8,128)S(1)}, f32[6,8,134]{2,1,0:T(8,128)S(1)}, u32[]{:S(2)}, u32[]{:S(2)}) collective-permute-start(f32[6,8,134]{2,1,0:T(8,128)S(1)} %bitcast.140), channel_id=1, source_target_pairs={{0,12},{4,0},{8,4},{12,8},{1,13},{5,1},{9,5},{13,9},{2,14},{6,2},{... | collective-permute-start | bytes 77192 | tf_op jit(solution)/shard_map/ppermute | solution.py:37
  14.1 3.1 %collective-permute-start.1 = (f32[2,6,8,134]{3,2,1,0:T(8,128)S(1)}, f32[2,6,8,134]{3,2,1,0:T(8,128)S(1)}, u32[]{:S(2)}, u32[]{:S(2)}) collective-permute-start(f32[2,6,8,134]{3,2,1,0:T(8,128)S(1)} %pad_maximum_fusion.15), channel_id=1, source_target_pairs={{0,16},{16,0},{1,17},{17,1},{2,18},{18,2},{3,19},{19,3},{4,20},{20... | collective-permute-start | bytes 154376 | tf_op jit(solution)/shard_map/ppermute | solution.py:31
  19.3 5.0 %collective-permute-start.6 = (f32[6,8,132]{2,1,0:T(8,128)S(1)}, f32[6,8,132]{2,1,0:T(8,128)S(1)}, u32[]{:S(2)}, u32[]{:S(2)}) collective-permute-start(f32[6,8,132]{2,1,0:T(8,128)S(1)} %bitcast.136), channel_id=1, source_target_pairs={{0,4},{4,8},{8,12},{12,0},{1,5},{5,9},{9,13},{13,1},{2,6},{6,10},{... | collective-permute-start | bytes 76040 | tf_op jit(solution)/shard_map/ppermute | solution.py:36
  21.8 4.1 %collective-permute-start.5 = (f32[6,8,132]{2,1,0:T(8,128)S(1)}, f32[6,8,132]{2,1,0:T(8,128)S(1)}, u32[]{:S(2)}, u32[]{:S(2)}) collective-permute-start(f32[6,8,132]{2,1,0:T(8,128)S(1)} %bitcast.142), channel_id=1, source_target_pairs={{0,12},{4,0},{8,4},{12,8},{1,13},{5,1},{9,5},{13,9},{2,14},{6,2},{... | collective-permute-start | bytes 76040 | tf_op jit(solution)/shard_map/ppermute | solution.py:37
  22.3 3.6 %collective-permute-start.4 = (f32[2,6,8,132]{3,2,1,0:T(8,128)S(1)}, f32[2,6,8,132]{3,2,1,0:T(8,128)S(1)}, u32[]{:S(2)}, u32[]{:S(2)}) collective-permute-start(f32[2,6,8,132]{3,2,1,0:T(8,128)S(1)} %pad_maximum_fusion.16), channel_id=1, source_target_pairs={{0,16},{16,0},{1,17},{17,1},{2,18},{18,2},{3,19},{19,3},{4,20},{20... | collective-permute-start | bytes 152072 | tf_op jit(solution)/shard_map/ppermute | solution.py:31
  27.1 1.0 %copy-start.1 = (f32[6,8,8,132]{3,2,0,1:T(8,128)S(1)}, f32[6,8,8,132]{3,2,0,1:T(8,128)}, u32[]{:S(2)}) copy-start(f32[6,8,8,132]{3,2,0,1:T(8,128)} %constant.61.clone.1) | copy-start | bytes 608260
  29.4 5.0 %collective-permute-start.9 = (f32[6,8,130]{2,1,0:T(8,128)S(1)}, f32[6,8,130]{2,1,0:T(8,128)S(1)}, u32[]{:S(2)}, u32[]{:S(2)}) collective-permute-start(f32[6,8,130]{2,1,0:T(8,128)S(1)} %bitcast.138), channel_id=1, source_target_pairs={{0,4},{4,8},{8,12},{12,0},{1,5},{5,9},{9,13},{13,1},{2,6},{6,10},{... | collective-permute-start | bytes 74888 | tf_op jit(solution)/shard_map/ppermute | solution.py:36
  30.9 4.1 %collective-permute-start.8 = (f32[6,8,130]{2,1,0:T(8,128)S(1)}, f32[6,8,130]{2,1,0:T(8,128)S(1)}, u32[]{:S(2)}, u32[]{:S(2)}) collective-permute-start(f32[6,8,130]{2,1,0:T(8,128)S(1)} %bitcast.144), channel_id=1, source_target_pairs={{0,12},{4,0},{8,4},{12,8},{1,13},{5,1},{9,5},{13,9},{2,14},{6,2},{... | collective-permute-start | bytes 74888 | tf_op jit(solution)/shard_map/ppermute | solution.py:37
  32.4 2.7 %collective-permute-start.7 = (f32[2,6,8,130]{3,2,1,0:T(8,128)S(1)}, f32[2,6,8,130]{3,2,1,0:T(8,128)S(1)}, u32[]{:S(2)}, u32[]{:S(2)}) collective-permute-start(f32[2,6,8,130]{3,2,1,0:T(8,128)S(1)} %pad_maximum_fusion.17), channel_id=1, source_target_pairs={{0,16},{16,0},{1,17},{17,1},{2,18},{18,2},{3,19},{19,3},{4,20},{20... | collective-permute-start | bytes 149768 | tf_op jit(solution)/shard_map/ppermute | solution.py:31
  37.4 4.8 %collective-permute-start.12 = (f32[6,8,128]{2,1,0:T(8,128)S(1)}, f32[6,8,128]{2,1,0:T(8,128)S(1)}, u32[]{:S(2)}, u32[]{:S(2)}) collective-permute-start(f32[6,8,128]{2,1,0:T(8,128)S(1)} %bitcast.146), channel_id=1, source_target_pairs={{0,4},{4,8},{8,12},{12,0},{1,5},{5,9},{9,13},{13,1},{2,6},{6,10},{... | collective-permute-start | bytes 73736 | tf_op jit(solution)/shard_map/ppermute | solution.py:36
  38.4 3.8 %collective-permute-start.11 = (f32[6,8,128]{2,1,0:T(8,128)S(1)}, f32[6,8,128]{2,1,0:T(8,128)S(1)}, u32[]{:S(2)}, u32[]{:S(2)}) collective-permute-start(f32[6,8,128]{2,1,0:T(8,128)S(1)} %bitcast.148), channel_id=1, source_target_pairs={{0,12},{4,0},{8,4},{12,8},{1,13},{5,1},{9,5},{13,9},{2,14},{6,2},{... | collective-permute-start | bytes 73736 | tf_op jit(solution)/shard_map/ppermute | solution.py:37
  40.4 1.9 %collective-permute-start.10 = (f32[2,6,8,128]{3,2,1,0:T(8,128)S(1)}, f32[2,6,8,128]{3,2,1,0:T(8,128)S(1)}, u32[]{:S(2)}, u32[]{:S(2)}) collective-permute-start(f32[2,6,8,128]{3,2,1,0:T(8,128)S(1)} %pad_maximum_fusion.23), channel_id=1, source_target_pairs={{0,16},{16,0},{1,17},{17,1},{2,18},{18,2},{3,19},{19,3},{4,20},{20... | collective-permute-start | bytes 147464 | tf_op jit(solution)/shard_map/ppermute | solution.py:31

commit v4 on v3

--- a/solution.py
+++ b/solution.py
@@ -25,28 +25,25 @@
     return [(i, i + by) for i in range(count) if 0 <= i + by < count]
 
 
-def lateral_halos(block):
+def x_halos(block):
     if lax.axis_size("gx") == 2:
         pair = jnp.stack([block[:, -1], block[:, 0]])
         got = lax.ppermute(pair, "gx", ring("gx", 1))
-        xlo, xhi = got[0], got[1]
-    else:
-        xlo = lax.ppermute(block[:, -1], "gx", ring("gx", 1))
-        xhi = lax.ppermute(block[:, 0], "gx", ring("gx", -1))
-    ylo = lax.ppermute(block[:, :, -1], "gy", ring("gy", 1))
-    yhi = lax.ppermute(block[:, :, 0], "gy", ring("gy", -1))
-    return xlo, xhi, ylo, yhi
+        return got[0], got[1]
+    xlo = lax.ppermute(block[:, -1], "gx", ring("gx", 1))
+    xhi = lax.ppermute(block[:, 0], "gx", ring("gx", -1))
+    return xlo, xhi
 
 
-def neighbours(fields, halos):
-    xlo, xhi, ylo, yhi, zlo, zhi = halos
+def neighbours(ext, xlo, xhi):
+    fields = ext[:, :, 1:-1, 1:-1]
     return [
         jnp.concatenate([fields[:, 1:], xhi[:, None]], 1),
         jnp.concatenate([xlo[:, None], fields[:, :-1]], 1),
-        jnp.concatenate([fields[:, :, 1:], yhi[:, :, None]], 2),
-        jnp.concatenate([ylo[:, :, None], fields[:, :, :-1]], 2),
-        jnp.concatenate([fields[..., 1:], zhi[..., None]], 3),
-        jnp.concatenate([zlo[..., None], fields[..., :-1]], 3),
+        ext[:, :, 2:, 1:-1],
+        ext[:, :, :-2, 1:-1],
+        ext[:, :, 1:-1, 2:],
+        ext[:, :, 1:-1, :-2],
     ]
 
 
@@ -107,6 +104,7 @@
 def shards(labels, mu_start, front_blocks):
     cells_x, cells_y, cells_z = labels.shape
     lift = cells_z // 4
+    bricks_y = lax.axis_size("gy")
     bricks_z = lax.axis_size("gz")
     depth = cells_z * bricks_z
     index_x = lax.axis_index("gx")
@@ -115,21 +113,28 @@
     bottom_brick = index_z == 0
     top_brick = index_z == bricks_z - 1
     base_z = index_z * cells_z
+    rim_y = 4
 
-    matched = (front_blocks[:, 0] == index_x) & (front_blocks[:, 1] == index_y)
+    in_column = front_blocks[:, 0] == index_x
 
-    def active(zpos):
+    def active(ypos, zpos):
+        brick_y = (index_y + jnp.floor_divide(ypos, cells_y)) % bricks_y
         block = jnp.floor_divide(zpos, BZ)
-        hits = matched[:, None] & (front_blocks[:, 2][:, None] == block[None, :])
+        hits = (
+            in_column[:, None, None]
+            & (front_blocks[:, 1][:, None, None] == brick_y[None, :, None])
+            & (front_blocks[:, 2][:, None, None] == block[None, None, :])
+        )
         return jnp.any(hits, 0)
 
-    def step(ext, first, offset):
-        fields = ext[..., 1:-1]
-        zpos = base_z + first + jnp.arange(fields.shape[3], dtype=jnp.int32)
-        xlo, xhi, ylo, yhi = lateral_halos(fields)
-        side = neighbours(fields, (xlo, xhi, ylo, yhi, ext[..., 0], ext[..., -1]))
+    def step(ext, first_y, first_z, offset):
+        fields = ext[:, :, 1:-1, 1:-1]
+        ypos = first_y + jnp.arange(fields.shape[2], dtype=jnp.int32)
+        zpos = base_z + first_z + jnp.arange(fields.shape[3], dtype=jnp.int32)
+        xlo, xhi = x_halos(fields)
+        side = neighbours(ext, xlo, xhi)
         phi_new = jnp.where(
-            active(zpos)[None, None, None, :],
+            active(ypos, zpos)[None, None],
             phase_update(fields, side, zpos, offset, depth),
             fields[:4],
         )
@@ -156,20 +161,23 @@
     count = lift + 4
     above = lax.ppermute(fields[..., :count].reshape(nf, -1), "gz", line("gz", -1))
     ext = jnp.concatenate([fields[..., low:], above.reshape((nf,) + shape_xy + (count,))], 3)
+    below_y = lax.ppermute(ext[:, :, -rim_y:], "gy", ring("gy", 1))
+    above_y = lax.ppermute(ext[:, :, :rim_y], "gy", ring("gy", -1))
+    ext = jnp.concatenate([below_y, ext, above_y], 2)
     ext = edge_at(ext, cells_z - low, top_brick)
-    ext = step(ext, low + 1, 0)
+    ext = step(ext, 1 - rim_y, low + 1, 0)
     ext = edge_at(ext, cells_z - low - 1, top_brick)
-    ext = step(ext, low + 2, 0)
+    ext = step(ext, 2 - rim_y, low + 2, 0)
     liquid = jnp.concatenate(
         [jnp.ones((1,) + ext.shape[1:], jnp.float32), jnp.zeros((nf - 1,) + ext.shape[1:], jnp.float32)], 0
     )
     ext = jnp.where(top_brick & (layer_index(ext) >= cells_z - lift + 2), liquid, ext)
     ext = edge_below(ext, 1, bottom_brick)
     ext = edge_at(ext, cells_z + 2, top_brick)
-    ext = step(ext, -1, lift)
+    ext = step(ext, 3 - rim_y, -1, lift)
     ext = edge_below(ext, 0, bottom_brick)
     ext = edge_at(ext, cells_z + 1, top_brick)
-    fields = step(ext, 0, lift)
+    fields = step(ext, 4 - rim_y, 0, lift)
     return (fields[:4], fields[4:])
 
 

time: 44.8 us -> 40.5 us (0.904)
  starting transfers between devices: 13.4 us -> 4.93 us
  other arithmetic: 7.06 us -> 10.8 us
  waiting for transfers between devices: 14.2 us -> 15.4 us
  local copies, waits for them, and re-layouts: 8.42 us -> 7.76 us
    ppermute x12 -> x6, starting transfers between devices: 12.2 us -> 3.64 us  [the longest x1 2.93 us: shards(): above_y = lax.ppermute(ext[:, :, :rim_y], 'gy', ring('gy', -1))]
    ppermute x12 -> x6, waiting for transfers between devices: 9.8 us -> 11.8 us  [the longest x1 5.11 us: shards(): above_y = lax.ppermute(ext[:, :, :rim_y], 'gy', ring('gy', -1))]
    slice x16 -> x3, local copies, waits for them, and re-layouts: 1.98 us -> 0.18 us  [the longest x1 0.17 us: x_halos(): pair = jnp.stack([block[:, -1], block[:, 0]])]
    ppermute x1, waiting for transfers between devices: 4.39 us -> 3.58 us  [shards(): lax.ppermute(fields[..., :count].reshape(nf, -1), 'gz', line('gz', -1))]
    mul x4, other arithmetic: 0.85 us -> 1.65 us  [phase_update(): square = phi * phi]
    another operation x4 -> x3, local copies, waits for them, and re-layouts: 0.33 us -> 1.12 us  [x_halos(): pair = jnp.stack([block[:, -1], block[:, 0]])]
    add x8 -> x7, other arithmetic: 1.34 us -> 1.72 us  [phase_update(): phi[phase] + DT * (rates[phase] - mean_rate)]
  transfers between devices with their start and end apart: 13 -> 7, of which waited for: 8 -> 7; matrix products, arithmetic and copies ran while one was open for 5% -> 7% of each run, Pallas kernels for 0% -> 0%
where the time goes in v4:
time: 40.5 us; the launch traced here: 40.2 us
  waiting for transfers between devices  15.4 us (38%)
  other arithmetic  10.8 us (27%)
  local copies, waits for them, and re-layouts  7.76 us (19%)
  starting transfers between devices  4.93 us (12%)
  between operations  1.26 us (3%)
    ppermute x1, waiting for transfers between devices, shards(): above_y = lax.ppermute(ext[:, :, :rim_y], 'gy', ring('gy', -1))  5.11 us
    ppermute x4, waiting for transfers between devices, x_halos(): got = lax.ppermute(pair, 'gx', ring('gx', 1))  3.59 us
    ppermute x1, waiting for transfers between devices, shards(): lax.ppermute(fields[..., :count].reshape(nf, -1), 'gz', line('gz', -1))  3.58 us
    unnamed x10, local copies, waits for them, and re-layouts  3.42 us
    ppermute x1, waiting for transfers between devices, shards(): below_y = lax.ppermute(ext[:, :, -rim_y:], 'gy', ring('gy', 1))  3.1 us
    ppermute x1, starting transfers between devices, shards(): above_y = lax.ppermute(ext[:, :, :rim_y], 'gy', ring('gy', -1))  2.93 us
    add x7, other arithmetic, phase_update(): phi[phase] + DT * (rates[phase] - mean_rate)  1.72 us
    mul x4, other arithmetic, phase_update(): square = phi * phi  1.65 us
  transfers between devices with their start and end apart: 7, of which 7 were waited for; matrix products, arithmetic and copies ran while one was open for 7% of the time, Pallas kernels for 0%

profile of v4, /device:TPU:0, one launch (start us, length us, event | category | flops | bytes accessed | tf_op | source)
XLA Modules:
  0.0 40.2 jit_solution(6597113476018472037)
XLA Ops:
  0.6 0.8 %bitcast_dynamic-update-slice_fusion.3 = f32[6,8,8,128]{3,1,2,0:T(8,128)S(1)} fusion(s32[8,8,128]{2,1,0:T(8,128)} %param.3), kind=kLoop, calls=%fused_computation.429 | loop fusion | flops 16383 | bytes 65536
  1.6 0.8 %copy-done.1 = f32[2,8,8,128]{3,2,1,0:T(8,128)S(1)} copy-done((f32[2,8,8,128]{3,2,1,0:T(8,128)S(1)}, f32[2,8,8,128]{3,2,1,0:T(8,128)}, u32[]{:S(2)}) %copy-start.1) | copy-done | bytes 65560
  2.4 0.2 reshape.578
  2.6 1.3 %collective-permute-start = (f32[6,2304]{1,0:T(8,128)S(1)}, f32[6,2304]{1,0:T(8,128)S(1)}, u32[]{:S(2)}, u32[]{:S(2)}) collective-permute-start(f32[6,2304]{1,0:T(8,128)S(1)} %reshape.578), channel_id=1, source_target_pairs={{1,0},{2,1},{3,2},{5,4},{6,5},{7,6},{9,8},{10,9},{11,10},{13,12},{... | collective-permute-start | bytes 165896 | tf_op jit(solution)/shard_map/ppermute | solution.py:162
  4.2 0.6 %copy-done.3 = s32[32,3]{0,1:T(4,128)S(1)} copy-done((s32[32,3]{0,1:T(4,128)S(1)}, s32[32,3]{0,1:T(4,128)}, u32[]{:S(2)}) %copy-start.3) | copy-done | bytes 408
  5.5 0.2 and_reduce_fusion
  5.7 0.2 and_reduce_fusion.1
  5.9 0.1 and_reduce_fusion.2
  6.2 3.6 %collective-permute-done = f32[6,2304]{1,0:T(8,128)S(1)} collective-permute-done((f32[6,2304]{1,0:T(8,128)S(1)}, f32[6,2304]{1,0:T(8,128)S(1)}, u32[]{:S(2)}, u32[]{:S(2)}) %collective-permute-start) | collective-permute-done | bytes 55328 | tf_op jit(solution)/shard_map/ppermute | solution.py:162
  9.8 0.2 reshape.579
  10.1 0.2 fusion.37
  10.3 2.9 %collective-permute-start.2 = (f32[6,8,4,136]{3,1,2,0:T(8,128)S(1)}, f32[6,8,4,136]{3,1,2,0:T(8,128)S(1)}, u32[]{:S(2)}, u32[]{:S(2)}) collective-permute-start(f32[6,8,4,136]{3,1,2,0:T(8,128)S(1)} %get-tuple-element.114), channel_id=1, source_target_pairs={{0,12},{4,0},{8,4},{12,8},{1,13},{5,1},{9,5},{13,9},{2,14},{6,2},{... | collective-permute-start | bytes 313352 | tf_op jit(solution)/shard_map/ppermute | solution.py:165
  13.2 5.1 %collective-permute-done.2 = f32[6,8,4,136]{3,1,2,0:T(8,128)S(1)} collective-permute-done((f32[6,8,4,136]{3,1,2,0:T(8,128)S(1)}, f32[6,8,4,136]{3,1,2,0:T(8,128)S(1)}, u32[]{:S(2)}, u32[]{:S(2)}) %collective-permute-start.2) | collective-permute-done | bytes 104480 | tf_op jit(solution)/shard_map/ppermute | solution.py:165
  18.3 3.1 %collective-permute-done.1 = f32[6,8,4,136]{3,1,2,0:T(8,128)S(1)} collective-permute-done((f32[6,8,4,136]{3,1,2,0:T(8,128)S(1)}, f32[6,8,4,136]{3,1,2,0:T(8,128)S(1)}, u32[]{:S(2)}, u32[]{:S(2)}) %collective-permute-start.1) | collective-permute-done | bytes 104480 | tf_op jit(solution)/shard_map/ppermute | solution.py:164
  21.4 0.2 pad_maximum_fusion
  21.6 0.4 maximum_select_fusion
  22.0 0.4 %slice_bitcast_fusion.3 = (f32[1,6,14,134]{3,0,2,1:T(1,128)S(1)}, f32[1,6,14,134]{3,0,2,1:T(1,128)S(1)}) fusion(f32[6,8,16,136]{3,1,2,0:T(8,128)S(1)} %maximum_select_fusion), kind=kLoop, calls=%fused_computation.281 | loop fusion | bytes 180096 | tf_op jit(solution)/shard_map/stack;squeeze | solution.py:30
  22.4 0.2 pad_maximum_fusion.8
  22.7 0.4 %fusion.276 = (f32[6,7,14,134]{3,1,2,0:T(8,128)S(1)}, f32[6,7,14,134]{3,1,2,0:T(8,128)S(1)}) fusion(f32[6,8,16,136]{3,1,2,0:T(8,128)S(1)} %maximum_select_fusion), kind=kLoop, calls=%fused_computation.523 | loop fusion | bytes 1260672 | tf_op jit(solution)/shard_map/slice | solution.py:41
  23.1 1.0 %collective-permute-done.3 = f32[2,6,14,134]{3,0,2,1:T(2,128)S(1)} collective-permute-done((f32[2,6,14,134]{3,0,2,1:T(2,128)S(1)}, f32[2,6,14,134]{3,0,2,1:T(2,128)S(1)}, u32[]{:S(2)}, u32[]{:S(2)}) %collective-permute-start.3) | collective-permute-done | bytes 90080 | tf_op jit(solution)/shard_map/ppermute | solution.py:31
  24.1 0.1 slice_bitcast_fusion.1
  24.2 0.5 %slice_multiply_fusion = (f32[4,8,14,134]{3,1,2,0:T(8,128)S(1)}, f32[4,8,14,134]{3,1,2,0:T(8,128)S(1)}) fusion(f32[6,8,16,136]{3,1,2,0:T(8,128)S(1)} %maximum_select_fusion, f32[6,7,14,134]{3,1,2,0:T(8,128)S(1)} %get-tuple-element.63, f32[6,1,14,134]{3,1,2,0:T(1,128)S(1)} %get-tuple-element.116, f32[6,1,14,134]{3,1,2,0:T(1,128)S(1)} %get-tuple-element.115, ...), kind=kLoop, calls=%fused_computation.58 | loop fusion | flops 600320 | bytes 2401280 | tf_op jit(solution)/shard_map/mul | solution.py:63
  24.8 0.2 fusion.111
  25.0 0.3 multiply_add_fusion.4
  25.3 0.3 multiply_add_fusion.3
  25.6 0.2 multiply_subtract_fusion
  25.8 0.3 fusion.25
  26.4 0.2 maximum_select_fusion.1
  26.6 0.4 slice_bitcast_fusion.7
  27.0 0.2 pad_maximum_fusion.11
  27.1 0.2 collective-permute-start.4
  27.4 0.4 fusion.277
  27.7 0.9 %collective-permute-done.4 = f32[2,6,12,132]{3,0,2,1:T(2,128)S(1)} collective-permute-done((f32[2,6,12,132]{3,0,2,1:T(2,128)S(1)}, f32[2,6,12,132]{3,0,2,1:T(2,128)S(1)}, u32[]{:S(2)}, u32[]{:S(2)}) %collective-permute-start.4) | collective-permute-done | bytes 76064 | tf_op jit(solution)/shard_map/ppermute | solution.py:31
  28.7 0.5 %slice_multiply_fusion.1 = (f32[4,8,12,132]{3,1,2,0:T(8,128)S(1)}, f32[4,8,12,132]{3,1,2,0:T(8,128)S(1)}) fusion(f32[6,8,14,134]{3,1,2,0:T(8,128)S(1)} %maximum_select_fusion.1, f32[6,7,12,132]{3,1,2,0:T(8,128)S(1)} %get-tuple-element.77, f32[6,1,12,132]{3,1,2,0:T(1,128)S(1)} %get-tuple-element.118, f32[6,1,12,132]{3,1,2,0:T(1,128)S(1)} %get-tuple-element.117, ...), kind=kLoop, calls=%fused_computation.70 | loop fusion | flops 506880 | bytes 2027520 | tf_op jit(solution)/shard_map/mul | solution.py:63
  29.2 0.2 fusion.153
  29.3 0.3 multiply_add_fusion.9
  29.6 0.3 multiply_add_fusion.8
  29.9 0.2 multiply_subtract_fusion.1
  30.1 0.3 fusion.39
  30.5 0.6 %copy-done.2 = f32[6]{0:T(128)S(1)} copy-done((f32[6]{0:T(128)S(1)}, f32[6]{0:T(128)}, u32[]{:S(2)}) %copy-start.2) | copy-done | bytes 48
  31.4 0.2 slice.1177
  31.7 0.2 maximum_select_fusion.3
  31.9 0.2 maximum_select_fusion.4
  32.1 0.3 slice_bitcast_fusion.11
  32.6 0.2 collective-permute-start.5
  32.8 0.3 fusion.278
  33.1 0.9 %collective-permute-done.5 = f32[2,6,10,130]{3,0,2,1:T(2,128)S(1)} collective-permute-done((f32[2,6,10,130]{3,0,2,1:T(2,128)S(1)}, f32[2,6,10,130]{3,0,2,1:T(2,128)S(1)}, u32[]{:S(2)}, u32[]{:S(2)}) %collective-permute-start.5) | collective-permute-done | bytes 62432 | tf_op jit(solution)/shard_map/ppermute | solution.py:31
  34.1 0.4 %slice_multiply_fusion.2 = (f32[4,8,10,130]{3,1,2,0:T(8,128)S(1)}, f32[4,8,10,130]{3,1,2,0:T(8,128)S(1)}) fusion(f32[6,8,12,132]{3,1,2,0:T(8,128)S(1)} %maximum_select_fusion.4, f32[6,7,10,130]{3,1,2,0:T(8,128)S(1)} %get-tuple-element.92, f32[6,1,10,130]{3,1,2,0:T(1,128)S(1)} %get-tuple-element.120, f32[6,1,10,130]{3,1,2,0:T(1,128)S(1)} %get-tuple-element.119, ...), kind=kLoop, calls=%fused_computation.75 | loop fusion | flops 416000 | bytes 1664000 | tf_op jit(solution)/shard_map/mul | solution.py:63
  34.5 0.1 fusion.195
  34.6 0.2 multiply_add_fusion.14
  34.9 0.2 multiply_add_fusion.13
  35.1 0.2 multiply_subtract_fusion.2
  35.3 0.2 fusion.52
  35.8 0.2 slice.1229
  36.0 0.1 maximum_select_fusion.5
  36.2 0.2 maximum_select_fusion.6
  36.4 0.2 fusion.279
  36.6 0.2 collective-permute-start.6
  36.8 0.2 fusion.280
  37.0 0.9 %collective-permute-done.6 = f32[2,6,8,128]{3,2,1,0:T(8,128)S(1)} collective-permute-done((f32[2,6,8,128]{3,2,1,0:T(8,128)S(1)}, f32[2,6,8,128]{3,2,1,0:T(8,128)S(1)}, u32[]{:S(2)}, u32[]{:S(2)}) %collective-permute-start.6) | collective-permute-done | bytes 49184 | tf_op jit(solution)/shard_map/ppermute | solution.py:31
  37.9 0.2 slice_multiply_fusion.15
  38.6 0.7 %copy.51 = f32[4,8,8,128]{3,2,1,0:T(8,128)} copy(f32[4,8,8,128]{3,1,2,0:T(8,128)S(1)} %get-tuple-element.7) | data formatting | bytes 262144
  39.3 0.1 fusion.199
  39.5 0.6 %copy.52 = f32[2,8,8,128]{3,2,1,0:T(8,128)} copy(f32[2,8,8,128]{3,1,2,0:T(8,128)S(1)} %pad_maximum_fusion.15) | data formatting | bytes 131072
  (70 shorter events, 3.2 us)
Async XLA Ops:
  0.6 0.8 %copy-start = (s32[8,8,128]{2,1,0:T(8,128)S(1)}, s32[8,8,128]{2,1,0:T(8,128)}, u32[]{:S(2)}) copy-start(s32[8,8,128]{2,1,0:T(8,128)} %param.3) | copy-start | bytes 98308
  1.5 0.8 %copy-start.1 = (f32[2,8,8,128]{3,2,1,0:T(8,128)S(1)}, f32[2,8,8,128]{3,2,1,0:T(8,128)}, u32[]{:S(2)}) copy-start(f32[2,8,8,128]{3,2,1,0:T(8,128)} %param.4) | copy-start | bytes 196612
  2.6 7.3 %collective-permute-start = (f32[6,2304]{1,0:T(8,128)S(1)}, f32[6,2304]{1,0:T(8,128)S(1)}, u32[]{:S(2)}, u32[]{:S(2)}) collective-permute-start(f32[6,2304]{1,0:T(8,128)S(1)} %reshape.578), channel_id=1, source_target_pairs={{1,0},{2,1},{3,2},{5,4},{6,5},{7,6},{9,8},{10,9},{11,10},{13,12},{... | collective-permute-start | bytes 165896 | tf_op jit(solution)/shard_map/ppermute | solution.py:162
  4.1 0.7 %copy-start.3 = (s32[32,3]{0,1:T(4,128)S(1)}, s32[32,3]{0,1:T(4,128)}, u32[]{:S(2)}) copy-start(s32[32,3]{0,1:T(4,128)} %param.5) | copy-start | bytes 1156
  10.3 8.1 %collective-permute-start.2 = (f32[6,8,4,136]{3,1,2,0:T(8,128)S(1)}, f32[6,8,4,136]{3,1,2,0:T(8,128)S(1)}, u32[]{:S(2)}, u32[]{:S(2)}) collective-permute-start(f32[6,8,4,136]{3,1,2,0:T(8,128)S(1)} %get-tuple-element.114), channel_id=1, source_target_pairs={{0,12},{4,0},{8,4},{12,8},{1,13},{5,1},{9,5},{13,9},{2,14},{6,2},{... | collective-permute-start | bytes 313352 | tf_op jit(solution)/shard_map/ppermute | solution.py:165
  13.2 8.2 %collective-permute-start.1 = (f32[6,8,4,136]{3,1,2,0:T(8,128)S(1)}, f32[6,8,4,136]{3,1,2,0:T(8,128)S(1)}, u32[]{:S(2)}, u32[]{:S(2)}) collective-permute-start(f32[6,8,4,136]{3,1,2,0:T(8,128)S(1)} %get-tuple-element.113), channel_id=1, source_target_pairs={{0,4},{4,8},{8,12},{12,0},{1,5},{5,9},{9,13},{13,1},{2,6},{6,10},{... | collective-permute-start | bytes 313352 | tf_op jit(solution)/shard_map/ppermute | solution.py:164
  22.6 1.5 %collective-permute-start.3 = (f32[2,6,14,134]{3,0,2,1:T(2,128)S(1)}, f32[2,6,14,134]{3,0,2,1:T(2,128)S(1)}, u32[]{:S(2)}, u32[]{:S(2)}) collective-permute-start(f32[2,6,14,134]{3,0,2,1:T(2,128)S(1)} %pad_maximum_fusion.8), channel_id=1, source_target_pairs={{0,16},{16,0},{1,17},{17,1},{2,18},{18,2},{3,19},{19,3},{4,20},{20... | collective-permute-start | bytes 270152 | tf_op jit(solution)/shard_map/ppermute | solution.py:31
  27.1 1.4 %collective-permute-start.4 = (f32[2,6,12,132]{3,0,2,1:T(2,128)S(1)}, f32[2,6,12,132]{3,0,2,1:T(2,128)S(1)}, u32[]{:S(2)}, u32[]{:S(2)}) collective-permute-start(f32[2,6,12,132]{3,0,2,1:T(2,128)S(1)} %pad_maximum_fusion.11), channel_id=1, source_target_pairs={{0,16},{16,0},{1,17},{17,1},{2,18},{18,2},{3,19},{19,3},{4,20},{20... | collective-permute-start | bytes 228104 | tf_op jit(solution)/shard_map/ppermute | solution.py:31
  30.5 0.7 %copy-start.2 = (f32[6]{0:T(128)S(1)}, f32[6]{0:T(128)}, u32[]{:S(2)}) copy-start(f32[6]{0:T(128)} %constant.132.clone.1) | copy-start | bytes 76
  32.6 1.4 %collective-permute-start.5 = (f32[2,6,10,130]{3,0,2,1:T(2,128)S(1)}, f32[2,6,10,130]{3,0,2,1:T(2,128)S(1)}, u32[]{:S(2)}, u32[]{:S(2)}) collective-permute-start(f32[2,6,10,130]{3,0,2,1:T(2,128)S(1)} %pad_maximum_fusion.12), channel_id=1, source_target_pairs={{0,16},{16,0},{1,17},{17,1},{2,18},{18,2},{3,19},{19,3},{4,20},{20... | collective-permute-start | bytes 187208 | tf_op jit(solution)/shard_map/ppermute | solution.py:31
  36.6 1.3 %collective-permute-start.6 = (f32[2,6,8,128]{3,2,1,0:T(8,128)S(1)}, f32[2,6,8,128]{3,2,1,0:T(8,128)S(1)}, u32[]{:S(2)}, u32[]{:S(2)}) collective-permute-start(f32[2,6,8,128]{3,2,1,0:T(8,128)S(1)} %pad_maximum_fusion.16), channel_id=1, source_target_pairs={{0,16},{16,0},{1,17},{17,1},{2,18},{18,2},{3,19},{19,3},{4,20},{20... | collective-permute-start | bytes 147464 | tf_op jit(solution)/shard_map/ppermute | solution.py:31

commit v5 on v4

--- a/solution.py
+++ b/solution.py
@@ -152,18 +152,19 @@
         down = jnp.concatenate([ext[..., 1:], ext[..., -1:]], 3)
         return jnp.where(cond & (layer_index(ext) == at), down, ext)
 
-    phi_start = jnp.stack([(labels == phase).astype(jnp.float32) for phase in range(4)])
-    fields = jnp.concatenate([phi_start, mu_start], 0)
-    nf = fields.shape[0]
-    shape_xy = fields.shape[1:3]
+    start = jnp.concatenate([labels.astype(jnp.float32)[None], mu_start], 0)
+    nf = 4 + mu_start.shape[0]
+    below_y = lax.ppermute(start[:, :, -rim_y:], "gy", ring("gy", 1))
+    above_y = lax.ppermute(start[:, :, :rim_y], "gy", ring("gy", -1))
+    wide = jnp.concatenate([below_y, start, above_y], 2)
 
     low = lift - 4
     count = lift + 4
-    above = lax.ppermute(fields[..., :count].reshape(nf, -1), "gz", line("gz", -1))
-    ext = jnp.concatenate([fields[..., low:], above.reshape((nf,) + shape_xy + (count,))], 3)
-    below_y = lax.ppermute(ext[:, :, -rim_y:], "gy", ring("gy", 1))
-    above_y = lax.ppermute(ext[:, :, :rim_y], "gy", ring("gy", -1))
-    ext = jnp.concatenate([below_y, ext, above_y], 2)
+    above = lax.ppermute(wide[..., :count].reshape(wide.shape[0], -1), "gz", line("gz", -1))
+    ext = jnp.concatenate([wide[..., low:], above.reshape(wide.shape[:3] + (count,))], 3)
+    ext = jnp.concatenate(
+        [jnp.stack([(ext[0] == phase).astype(jnp.float32) for phase in range(4)]), ext[1:]], 0
+    )
     ext = edge_at(ext, cells_z - low, top_brick)
     ext = step(ext, 1 - rim_y, low + 1, 0)
     ext = edge_at(ext, cells_z - low - 1, top_brick)

time: 40.5 us -> 36.2 us (0.89)
  waiting for transfers between devices: 15.4 us -> 11.1 us
  starting transfers between devices: 4.93 us -> 5.94 us
  local copies, waits for them, and re-layouts: 7.76 us -> 7.06 us
    ppermute x3, waiting for transfers between devices: 11.8 us -> 7.54 us  [the longest x1 4.82 us: shards(): lax.ppermute(wide[..., :count].reshape(wide.shape[0], -1), 'gz', line('gz...]
    ppermute x3, starting transfers between devices: 4.23 us -> 5.24 us  [the longest x1 3.95 us: shards(): above_y = lax.ppermute(start[:, :, :rim_y], 'gy', ring('gy', -1))]
    broadcast_in_dim x0 -> x1, other arithmetic: none -> 0.8 us  [shards(): start = jnp.concatenate([labels.astype(jnp.float32)[None], mu_start], 0)]
    unnamed x10 -> x9, local copies, waits for them, and re-layouts: 3.42 us -> 2.67 us
    unnamed x4, other arithmetic: 0.87 us -> 0.15 us
  transfers between devices with their start and end apart: 7 -> 7, of which waited for: 7 -> 6; matrix products, arithmetic and copies ran while one was open for 7% -> 8% of each run, Pallas kernels for 0% -> 0%
where the time goes in v5:
time: 36.2 us; the launch traced here: 36 us
  waiting for transfers between devices  11.1 us (31%)
  other arithmetic  10.6 us (29%)
  local copies, waits for them, and re-layouts  7.06 us (20%)
  starting transfers between devices  5.94 us (16%)
  between operations  1.26 us (3%)
    ppermute x1, waiting for transfers between devices, shards(): lax.ppermute(wide[..., :count].reshape(wide.shape[0], -1), 'gz', line('gz...  4.82 us
    ppermute x1, starting transfers between devices, shards(): above_y = lax.ppermute(start[:, :, :rim_y], 'gy', ring('gy', -1))  3.95 us
    ppermute x4, waiting for transfers between devices, x_halos(): got = lax.ppermute(pair, 'gx', ring('gx', 1))  3.59 us
    ppermute x1, waiting for transfers between devices, shards(): below_y = lax.ppermute(start[:, :, -rim_y:], 'gy', ring('gy', 1))  2.72 us
    unnamed x9, local copies, waits for them, and re-layouts  2.67 us
    add x7, other arithmetic, phase_update(): phi[phase] + DT * (rates[phase] - mean_rate)  1.72 us
    mul x4, other arithmetic, phase_update(): square = phi * phi  1.65 us
    ppermute x1, starting transfers between devices, shards(): lax.ppermute(wide[..., :count].reshape(wide.shape[0], -1), 'gz', line('gz...  1.29 us
  transfers between devices with their start and end apart: 7, of which 6 were waited for; matrix products, arithmetic and copies ran while one was open for 8% of the time, Pallas kernels for 0%

profile of v5, /device:TPU:0, one launch (start us, length us, event | category | flops | bytes accessed | tf_op | source)
XLA Modules:
  0.0 36.0 jit_solution(3676404065011582366)
XLA Ops:
  0.6 0.8 %fusion.252 = f32[1,8,8,128]{3,1,2,0:T(8,128)S(1)} fusion(s32[8,8,128]{2,1,0:T(8,128)} %param.3), kind=kLoop, calls=%fused_computation.433 | loop fusion | flops 8192 | bytes 65536 | tf_op jit(solution)/shard_map/broadcast_in_dim | solution.py:155
  1.5 3.9 %collective-permute-start.1 = (f32[3,8,4,128]{3,1,2,0:T(8,128)S(1)}, f32[3,8,4,128]{3,1,2,0:T(8,128)S(1)}, u32[]{:S(2)}, u32[]{:S(2)}) collective-permute-start(f32[3,8,4,128]{3,1,2,0:T(8,128)S(1)} %get-tuple-element.122), channel_id=1, source_target_pairs={{0,12},{4,0},{8,4},{12,8},{1,13},{5,1},{9,5},{13,9},{2,14},{6,2},{... | collective-permute-start | bytes 147464 | tf_op jit(solution)/shard_map/ppermute | solution.py:158
  5.8 0.6 %copy-done.2 = s32[32,3]{0,1:T(4,128)S(1)} copy-done((s32[32,3]{0,1:T(4,128)S(1)}, s32[32,3]{0,1:T(4,128)}, u32[]{:S(2)}) %copy-start.2) | copy-done | bytes 408
  7.1 0.2 and_reduce_fusion
  7.3 0.2 and_reduce_fusion.1
  7.4 0.1 and_reduce_fusion.2
  7.7 2.7 %collective-permute-done = f32[3,8,4,128]{3,1,2,0:T(8,128)S(1)} collective-permute-done((f32[3,8,4,128]{3,1,2,0:T(8,128)S(1)}, f32[3,8,4,128]{3,1,2,0:T(8,128)S(1)}, u32[]{:S(2)}, u32[]{:S(2)}) %collective-permute-start) | collective-permute-done | bytes 49184 | tf_op jit(solution)/shard_map/ppermute | solution.py:157
  10.5 0.2 reshape.578
  10.7 1.3 %collective-permute-start.2 = (f32[3,4608]{1,0:T(4,128)S(1)}, f32[3,4608]{1,0:T(4,128)S(1)}, u32[]{:S(2)}, u32[]{:S(2)}) collective-permute-start(f32[3,4608]{1,0:T(4,128)S(1)} %reshape.578), channel_id=1, source_target_pairs={{1,0},{2,1},{3,2},{5,4},{6,5},{7,6},{9,8},{10,9},{11,10},{13,12},{... | collective-permute-start | bytes 165896 | tf_op jit(solution)/shard_map/ppermute | solution.py:163
  12.1 4.8 %collective-permute-done.2 = f32[3,4608]{1,0:T(4,128)S(1)} collective-permute-done((f32[3,4608]{1,0:T(4,128)S(1)}, f32[3,4608]{1,0:T(4,128)S(1)}, u32[]{:S(2)}, u32[]{:S(2)}) %collective-permute-start.2) | collective-permute-done | bytes 55328 | tf_op jit(solution)/shard_map/ppermute | solution.py:163
  16.9 0.2 reshape.579
  17.4 0.1 fusion.24
  17.6 0.3 maximum_select_fusion
  17.9 0.4 %slice_bitcast_fusion.3 = (f32[1,6,14,134]{3,0,2,1:T(1,128)S(1)}, f32[1,6,14,134]{3,0,2,1:T(1,128)S(1)}) fusion(f32[6,8,16,136]{3,1,2,0:T(8,128)S(1)} %maximum_select_fusion), kind=kLoop, calls=%fused_computation.286 | loop fusion | bytes 180096 | tf_op jit(solution)/shard_map/stack;squeeze | solution.py:30
  18.3 0.2 pad_maximum_fusion.8
  18.6 0.4 %fusion.278 = (f32[6,7,14,134]{3,1,2,0:T(8,128)S(1)}, f32[6,7,14,134]{3,1,2,0:T(8,128)S(1)}) fusion(f32[6,8,16,136]{3,1,2,0:T(8,128)S(1)} %maximum_select_fusion), kind=kLoop, calls=%fused_computation.527 | loop fusion | bytes 1260672 | tf_op jit(solution)/shard_map/slice | solution.py:41
  19.0 1.0 %collective-permute-done.3 = f32[2,6,14,134]{3,0,2,1:T(2,128)S(1)} collective-permute-done((f32[2,6,14,134]{3,0,2,1:T(2,128)S(1)}, f32[2,6,14,134]{3,0,2,1:T(2,128)S(1)}, u32[]{:S(2)}, u32[]{:S(2)}) %collective-permute-start.3) | collective-permute-done | bytes 90080 | tf_op jit(solution)/shard_map/ppermute | solution.py:31
  19.9 0.1 slice_bitcast_fusion.1
  20.1 0.5 %slice_multiply_fusion = (f32[4,8,14,134]{3,1,2,0:T(8,128)S(1)}, f32[4,8,14,134]{3,1,2,0:T(8,128)S(1)}) fusion(f32[6,8,16,136]{3,1,2,0:T(8,128)S(1)} %maximum_select_fusion, f32[6,7,14,134]{3,1,2,0:T(8,128)S(1)} %get-tuple-element.65, f32[6,1,14,134]{3,1,2,0:T(1,128)S(1)} %get-tuple-element.116, f32[6,1,14,134]{3,1,2,0:T(1,128)S(1)} %get-tuple-element.115, ...), kind=kLoop, calls=%fused_computation.55 | loop fusion | flops 600320 | bytes 2401280 | tf_op jit(solution)/shard_map/mul | solution.py:63
  20.6 0.2 fusion.111
  20.8 0.3 multiply_add_fusion.4
  21.1 0.3 multiply_add_fusion.3
  21.4 0.2 multiply_subtract_fusion
  21.7 0.3 fusion.26
  22.2 0.2 maximum_select_fusion.1
  22.5 0.4 %slice_bitcast_fusion.7 = (f32[1,6,12,132]{3,0,2,1:T(1,128)S(1)}, f32[1,6,12,132]{3,0,2,1:T(1,128)S(1)}) fusion(f32[6,8,14,134]{3,1,2,0:T(8,128)S(1)} %maximum_select_fusion.1), kind=kLoop, calls=%fused_computation.352 | loop fusion | bytes 152064 | tf_op jit(solution)/shard_map/stack;squeeze | solution.py:30
  22.8 0.2 pad_maximum_fusion.11
  23.0 0.2 collective-permute-start.4
  23.2 0.4 %fusion.279 = (f32[6,7,12,132]{3,1,2,0:T(8,128)S(1)}, f32[6,7,12,132]{3,1,2,0:T(8,128)S(1)}) fusion(f32[6,8,14,134]{3,1,2,0:T(8,128)S(1)} %maximum_select_fusion.1), kind=kLoop, calls=%fused_computation.528 | loop fusion | bytes 1064448 | tf_op jit(solution)/shard_map/slice | solution.py:41
  23.6 0.9 %collective-permute-done.4 = f32[2,6,12,132]{3,0,2,1:T(2,128)S(1)} collective-permute-done((f32[2,6,12,132]{3,0,2,1:T(2,128)S(1)}, f32[2,6,12,132]{3,0,2,1:T(2,128)S(1)}, u32[]{:S(2)}, u32[]{:S(2)}) %collective-permute-start.4) | collective-permute-done | bytes 76064 | tf_op jit(solution)/shard_map/ppermute | solution.py:31
  24.6 0.5 %slice_multiply_fusion.1 = (f32[4,8,12,132]{3,1,2,0:T(8,128)S(1)}, f32[4,8,12,132]{3,1,2,0:T(8,128)S(1)}) fusion(f32[6,8,14,134]{3,1,2,0:T(8,128)S(1)} %maximum_select_fusion.1, f32[6,7,12,132]{3,1,2,0:T(8,128)S(1)} %get-tuple-element.79, f32[6,1,12,132]{3,1,2,0:T(1,128)S(1)} %get-tuple-element.118, f32[6,1,12,132]{3,1,2,0:T(1,128)S(1)} %get-tuple-element.117, ...), kind=kLoop, calls=%fused_computation.67 | loop fusion | flops 506880 | bytes 2027520 | tf_op jit(solution)/shard_map/mul | solution.py:63
  25.0 0.2 fusion.153
  25.2 0.3 multiply_add_fusion.9
  25.5 0.3 multiply_add_fusion.8
  25.7 0.2 multiply_subtract_fusion.1
  25.9 0.3 fusion.39
  26.4 0.6 %copy-done.1 = f32[6]{0:T(128)S(1)} copy-done((f32[6]{0:T(128)S(1)}, f32[6]{0:T(128)}, u32[]{:S(2)}) %copy-start.1) | copy-done | bytes 48
  27.2 0.1 slice.1189
  27.3 0.2 slice.1188
  27.5 0.2 maximum_select_fusion.3
  27.7 0.2 maximum_select_fusion.4
  27.9 0.3 slice_bitcast_fusion.11
  28.4 0.2 collective-permute-start.5
  28.6 0.3 fusion.280
  28.9 0.9 %collective-permute-done.5 = f32[2,6,10,130]{3,0,2,1:T(2,128)S(1)} collective-permute-done((f32[2,6,10,130]{3,0,2,1:T(2,128)S(1)}, f32[2,6,10,130]{3,0,2,1:T(2,128)S(1)}, u32[]{:S(2)}, u32[]{:S(2)}) %collective-permute-start.5) | collective-permute-done | bytes 62432 | tf_op jit(solution)/shard_map/ppermute | solution.py:31
  29.9 0.4 %slice_multiply_fusion.2 = (f32[4,8,10,130]{3,1,2,0:T(8,128)S(1)}, f32[4,8,10,130]{3,1,2,0:T(8,128)S(1)}) fusion(f32[6,8,12,132]{3,1,2,0:T(8,128)S(1)} %maximum_select_fusion.4, f32[6,7,10,130]{3,1,2,0:T(8,128)S(1)} %get-tuple-element.94, f32[6,1,10,130]{3,1,2,0:T(1,128)S(1)} %get-tuple-element.120, f32[6,1,10,130]{3,1,2,0:T(1,128)S(1)} %get-tuple-element.119, ...), kind=kLoop, calls=%fused_computation.72 | loop fusion | flops 416000 | bytes 1664000 | tf_op jit(solution)/shard_map/mul | solution.py:63
  30.3 0.1 fusion.195
  30.5 0.2 multiply_add_fusion.14
  30.7 0.2 multiply_add_fusion.13
  30.9 0.2 multiply_subtract_fusion.2
  31.1 0.2 fusion.52
  31.7 0.2 slice.1240
  31.9 0.1 maximum_select_fusion.5
  32.0 0.2 maximum_select_fusion.6
  32.2 0.2 fusion.281
  32.4 0.2 collective-permute-start.6
  32.6 0.2 fusion.282
  32.8 0.9 %collective-permute-done.6 = f32[2,6,8,128]{3,2,1,0:T(8,128)S(1)} collective-permute-done((f32[2,6,8,128]{3,2,1,0:T(8,128)S(1)}, f32[2,6,8,128]{3,2,1,0:T(8,128)S(1)}, u32[]{:S(2)}, u32[]{:S(2)}) %collective-permute-start.6) | collective-permute-done | bytes 49184 | tf_op jit(solution)/shard_map/ppermute | solution.py:31
  33.7 0.2 slice_multiply_fusion.15
  34.0 0.1 multiply_add_fusion.19
  34.2 0.1 fusion.223
  34.4 0.7 %copy.45 = f32[4,8,8,128]{3,2,1,0:T(8,128)} copy(f32[4,8,8,128]{3,1,2,0:T(8,128)S(1)} %get-tuple-element.7) | data formatting | bytes 262144
  35.1 0.1 fusion.199
  35.4 0.6 %copy.46 = f32[2,8,8,128]{3,2,1,0:T(8,128)} copy(f32[2,8,8,128]{3,1,2,0:T(8,128)S(1)} %pad_maximum_fusion.16) | data formatting | bytes 131072
  (70 shorter events, 3.0 us)
Async XLA Ops:
  0.6 0.8 %copy-start = (f32[2,8,8,128]{3,2,1,0:T(8,128)S(1)}, f32[2,8,8,128]{3,2,1,0:T(8,128)}, u32[]{:S(2)}) copy-start(f32[2,8,8,128]{3,2,1,0:T(8,128)} %param.4) | copy-start | bytes 196612
  1.5 6.2 %collective-permute-start.1 = (f32[3,8,4,128]{3,1,2,0:T(8,128)S(1)}, f32[3,8,4,128]{3,1,2,0:T(8,128)S(1)}, u32[]{:S(2)}, u32[]{:S(2)}) collective-permute-start(f32[3,8,4,128]{3,1,2,0:T(8,128)S(1)} %get-tuple-element.122), channel_id=1, source_target_pairs={{0,12},{4,0},{8,4},{12,8},{1,13},{5,1},{9,5},{13,9},{2,14},{6,2},{... | collective-permute-start | bytes 147464 | tf_op jit(solution)/shard_map/ppermute | solution.py:158
  5.5 5.0 %collective-permute-start = (f32[3,8,4,128]{3,1,2,0:T(8,128)S(1)}, f32[3,8,4,128]{3,1,2,0:T(8,128)S(1)}, u32[]{:S(2)}, u32[]{:S(2)}) collective-permute-start(f32[3,8,4,128]{3,1,2,0:T(8,128)S(1)} %get-tuple-element.121), channel_id=1, source_target_pairs={{0,4},{4,8},{8,12},{12,0},{1,5},{5,9},{9,13},{13,1},{2,6},{6,10},{... | collective-permute-start | bytes 147464 | tf_op jit(solution)/shard_map/ppermute | solution.py:157
  5.7 0.7 %copy-start.2 = (s32[32,3]{0,1:T(4,128)S(1)}, s32[32,3]{0,1:T(4,128)}, u32[]{:S(2)}) copy-start(s32[32,3]{0,1:T(4,128)} %param.5) | copy-start | bytes 1156
  10.7 6.2 %collective-permute-start.2 = (f32[3,4608]{1,0:T(4,128)S(1)}, f32[3,4608]{1,0:T(4,128)S(1)}, u32[]{:S(2)}, u32[]{:S(2)}) collective-permute-start(f32[3,4608]{1,0:T(4,128)S(1)} %reshape.578), channel_id=1, source_target_pairs={{1,0},{2,1},{3,2},{5,4},{6,5},{7,6},{9,8},{10,9},{11,10},{13,12},{... | collective-permute-start | bytes 165896 | tf_op jit(solution)/shard_map/ppermute | solution.py:163
  18.5 1.5 %collective-permute-start.3 = (f32[2,6,14,134]{3,0,2,1:T(2,128)S(1)}, f32[2,6,14,134]{3,0,2,1:T(2,128)S(1)}, u32[]{:S(2)}, u32[]{:S(2)}) collective-permute-start(f32[2,6,14,134]{3,0,2,1:T(2,128)S(1)} %pad_maximum_fusion.8), channel_id=1, source_target_pairs={{0,16},{16,0},{1,17},{17,1},{2,18},{18,2},{3,19},{19,3},{4,20},{20... | collective-permute-start | bytes 270152 | tf_op jit(solution)/shard_map/ppermute | solution.py:31
  23.0 1.4 %collective-permute-start.4 = (f32[2,6,12,132]{3,0,2,1:T(2,128)S(1)}, f32[2,6,12,132]{3,0,2,1:T(2,128)S(1)}, u32[]{:S(2)}, u32[]{:S(2)}) collective-permute-start(f32[2,6,12,132]{3,0,2,1:T(2,128)S(1)} %pad_maximum_fusion.11), channel_id=1, source_target_pairs={{0,16},{16,0},{1,17},{17,1},{2,18},{18,2},{3,19},{19,3},{4,20},{20... | collective-permute-start | bytes 228104 | tf_op jit(solution)/shard_map/ppermute | solution.py:31
  26.4 0.7 %copy-start.1 = (f32[6]{0:T(128)S(1)}, f32[6]{0:T(128)}, u32[]{:S(2)}) copy-start(f32[6]{0:T(128)} %constant.132.clone.1) | copy-start | bytes 76
  28.4 1.4 %collective-permute-start.5 = (f32[2,6,10,130]{3,0,2,1:T(2,128)S(1)}, f32[2,6,10,130]{3,0,2,1:T(2,128)S(1)}, u32[]{:S(2)}, u32[]{:S(2)}) collective-permute-start(f32[2,6,10,130]{3,0,2,1:T(2,128)S(1)} %pad_maximum_fusion.13), channel_id=1, source_target_pairs={{0,16},{16,0},{1,17},{17,1},{2,18},{18,2},{3,19},{19,3},{4,20},{20... | collective-permute-start | bytes 187208 | tf_op jit(solution)/shard_map/ppermute | solution.py:31
  32.4 1.3 %collective-permute-start.6 = (f32[2,6,8,128]{3,2,1,0:T(8,128)S(1)}, f32[2,6,8,128]{3,2,1,0:T(8,128)S(1)}, u32[]{:S(2)}, u32[]{:S(2)}) collective-permute-start(f32[2,6,8,128]{3,2,1,0:T(8,128)S(1)} %pad_maximum_fusion.18), channel_id=1, source_target_pairs={{0,16},{16,0},{1,17},{17,1},{2,18},{18,2},{3,19},{19,3},{4,20},{20... | collective-permute-start | bytes 147464 | tf_op jit(solution)/shard_map/ppermute | solution.py:31

commit v6 on v5

--- a/solution.py
+++ b/solution.py
@@ -2,8 +2,11 @@
 import jax.numpy as jnp
 from jax import lax
 from jax.sharding import PartitionSpec as P
+from jax.experimental import pallas as pl
+from jax.experimental.pallas import tpu as pltpu
 
 BZ = 16
+INTERPRET = False
 
 
 COMP = ((0.0, 0.0), (1.0, -0.5), (-0.5, 1.0), (-0.5, -0.5))
@@ -101,6 +104,107 @@
     return jnp.stack(result)
 
 
+def roll_both(value, axis):
+    size = value.shape[axis]
+    return pltpu.roll(value, 1, axis), pltpu.roll(value, size - 1, axis)
+
+
+def step_kernel(frame_ref, halo_ref, mask_ref, under_ref, fix_ref, out_ref):
+    nx = frame_ref.shape[0]
+    mask = mask_ref[...] > 0.5
+    under = under_ref[...]
+    fix = fix_ref[...]
+    lane = lax.broadcasted_iota(jnp.int32, mask.shape, 1)
+    size = mask.shape[1]
+    rolled = pltpu.roll(lane, 1, 1)
+    forward = rolled == jnp.where(lane == 0, size - 1, lane - 1)
+    take_lower = fix[0:1] > 0.5
+    take_upper = fix[1:2] > 0.5
+    make_liquid = fix[2:3] > 0.5
+
+    def body(x, carry):
+        fields = frame_ref[x]
+        below = frame_ref[jnp.maximum(x - 1, 0)]
+        beyond = frame_ref[jnp.minimum(x + 1, nx - 1)]
+        xm = jnp.where(x == 0, halo_ref[0], below)
+        xp = jnp.where(x == nx - 1, halo_ref[1], beyond)
+        ya, yb = roll_both(fields, 1)
+        za, zb = roll_both(fields, 2)
+        side = [xp, xm, ya, yb, za, zb]
+        phi = fields[:4]
+        chem = fields[4:]
+        beside_all = [s[:4] for s in side]
+        total = (
+            beside_all[0]
+            + beside_all[1]
+            + beside_all[2]
+            + beside_all[3]
+            + beside_all[4]
+            + beside_all[5]
+        )
+        lap = total - 6.0 * phi
+        square = phi * phi
+        summed = square[0] + square[1] + square[2] + square[3]
+        rates = []
+        for phase in range(4):
+            psi = -(COMP[phase][0] * chem[0] + COMP[phase][1] * chem[1]) + LATENT[phase] * under
+            rate = (
+                KAPPA * lap[phase]
+                - WELL * phi[phase] * (summed - square[phase])
+                - 6.0 * phi[phase] * (1.0 - phi[phase]) * psi
+            )
+            rates.append(rate)
+        mean_rate = (rates[0] + rates[1] + rates[2] + rates[3]) * 0.25
+        phi_new = jnp.stack(
+            [jnp.where(mask, phi[phase] + DT * (rates[phase] - mean_rate), phi[phase]) for phase in range(4)]
+        )
+        centre_d = DSOL + (DLIQ - DSOL) * phi[0]
+        side_d = [DSOL + (DLIQ - DSOL) * s[0] for s in side]
+        side_m = [s[4:] for s in side]
+        flux = jnp.zeros_like(chem)
+        for way in range(6):
+            flux = flux + 0.5 * (centre_d + side_d[way]) * (side_m[way] - chem)
+        delta = shape_fn(phi_new) - shape_fn(phi)
+        result = [phi_new[phase] for phase in range(4)]
+        for comp in range(2):
+            change = (
+                COMP[0][comp] * delta[0]
+                + COMP[1][comp] * delta[1]
+                + COMP[2][comp] * delta[2]
+                + COMP[3][comp] * delta[3]
+            )
+            result.append(chem[comp] + DT * flux[comp] - change)
+        new = jnp.stack(result)
+        liquid = jnp.where(lax.broadcasted_iota(jnp.int32, new.shape, 0) == 0, 1.0, 0.0)
+        new = jnp.where(make_liquid, liquid, new)
+        ra, rb = roll_both(new, 2)
+        lower = jnp.where(forward, ra, rb)
+        upper = jnp.where(forward, rb, ra)
+        new = jnp.where(take_upper, upper, new)
+        new = jnp.where(take_lower, lower, new)
+        out_ref[x] = new
+        return carry
+
+    lax.fori_loop(0, nx, body, 0)
+
+
+def run_step(frame, halo, mask, under, fix):
+    return pl.pallas_call(
+        step_kernel,
+        out_shape=jax.ShapeDtypeStruct(frame.shape, frame.dtype),
+        interpret=INTERPRET,
+    )(frame, halo, mask, under, fix)
+
+
+def frame_halos(frame):
+    if lax.axis_size("gx") == 2:
+        pair = jnp.stack([frame[-1], frame[0]])
+        return lax.ppermute(pair, "gx", ring("gx", 1))
+    xlo = lax.ppermute(frame[-1], "gx", ring("gx", 1))
+    xhi = lax.ppermute(frame[0], "gx", ring("gx", -1))
+    return jnp.stack([xlo, xhi])
+
+
 def shards(labels, mu_start, front_blocks):
     cells_x, cells_y, cells_z = labels.shape
     lift = cells_z // 4
@@ -114,72 +218,69 @@
     top_brick = index_z == bricks_z - 1
     base_z = index_z * cells_z
     rim_y = 4
+    rows = 2 * cells_y
+    lanes = 2 * cells_z
+    low = lift - 4
+    count = lift + 4
+
+    row_y = jnp.arange(rows, dtype=jnp.int32)
+    row_y = jnp.where(row_y < cells_y + rim_y, row_y, row_y - rows)
+    lane_z = jnp.arange(lanes, dtype=jnp.int32)
+    lane_z = jnp.where(lane_z < lanes - 4, lane_z, lane_z - lanes)
 
     in_column = front_blocks[:, 0] == index_x
 
-    def active(ypos, zpos):
-        brick_y = (index_y + jnp.floor_divide(ypos, cells_y)) % bricks_y
+    def active(zpos):
+        brick_y = (index_y + jnp.floor_divide(row_y, cells_y)) % bricks_y
         block = jnp.floor_divide(zpos, BZ)
         hits = (
             in_column[:, None, None]
             & (front_blocks[:, 1][:, None, None] == brick_y[None, :, None])
             & (front_blocks[:, 2][:, None, None] == block[None, None, :])
         )
-        return jnp.any(hits, 0)
-
-    def step(ext, first_y, first_z, offset):
-        fields = ext[:, :, 1:-1, 1:-1]
-        ypos = first_y + jnp.arange(fields.shape[2], dtype=jnp.int32)
-        zpos = base_z + first_z + jnp.arange(fields.shape[3], dtype=jnp.int32)
-        xlo, xhi = x_halos(fields)
-        side = neighbours(ext, xlo, xhi)
-        phi_new = jnp.where(
-            active(ypos, zpos)[None, None],
-            phase_update(fields, side, zpos, offset, depth),
-            fields[:4],
-        )
-        mu_new = chem_update(fields, side, fields[:4], phi_new)
-        return jnp.concatenate([phi_new, mu_new], 0)
-
-    def layer_index(ext):
-        return lax.broadcasted_iota(jnp.int32, ext.shape, 3)
-
-    def edge_at(ext, at, cond):
-        up = jnp.concatenate([ext[..., :1], ext[..., :-1]], 3)
-        return jnp.where(cond & (layer_index(ext) == at), up, ext)
-
-    def edge_below(ext, at, cond):
-        down = jnp.concatenate([ext[..., 1:], ext[..., -1:]], 3)
-        return jnp.where(cond & (layer_index(ext) == at), down, ext)
+        return jnp.any(hits, 0).astype(jnp.float32)
+
+    mask_pre = active(base_z + lane_z + lift)
+    mask_post = active(base_z + lane_z)
+    under = 2.0 * ((base_z + lane_z + lift).astype(jnp.float32) / depth - 0.5)
+    under = under[None, :]
+
+    def lane_flag(cond, hit):
+        return jnp.where(cond & hit, 1.0, 0.0).astype(jnp.float32)
+
+    none = jnp.zeros((lanes,), jnp.float32)
+    fixes = [
+        jnp.stack([lane_flag(top_brick, lane_z == cells_z - lift), none, none]),
+        jnp.stack([
+            lane_flag(top_brick, lane_z == cells_z),
+            lane_flag(bottom_brick, lane_z == -1),
+            lane_flag(top_brick, lane_z >= cells_z - lift),
+        ]),
+        jnp.stack([lane_flag(top_brick, lane_z == cells_z), lane_flag(bottom_brick, lane_z == -1), none]),
+        jnp.stack([none, none, none]),
+    ]
+    masks = [mask_pre, mask_pre, mask_post, mask_post]
 
     start = jnp.concatenate([labels.astype(jnp.float32)[None], mu_start], 0)
     nf = 4 + mu_start.shape[0]
-    below_y = lax.ppermute(start[:, :, -rim_y:], "gy", ring("gy", 1))
-    above_y = lax.ppermute(start[:, :, :rim_y], "gy", ring("gy", -1))
-    wide = jnp.concatenate([below_y, start, above_y], 2)
-
-    low = lift - 4
-    count = lift + 4
+    from_up = lax.ppermute(start[:, :, :rim_y], "gy", ring("gy", -1))
+    from_down = lax.ppermute(start[:, :, -rim_y:], "gy", ring("gy", 1))
+    wide = jnp.concatenate([start, from_up, from_down], 2)
     above = lax.ppermute(wide[..., :count].reshape(wide.shape[0], -1), "gz", line("gz", -1))
-    ext = jnp.concatenate([wide[..., low:], above.reshape(wide.shape[:3] + (count,))], 3)
-    ext = jnp.concatenate(
-        [jnp.stack([(ext[0] == phase).astype(jnp.float32) for phase in range(4)]), ext[1:]], 0
+    above = above.reshape(wide.shape[:3] + (count,))
+    gap = jnp.zeros(wide.shape[:3] + (lanes - (cells_z - lift) - count - 4,), jnp.float32)
+    frame = jnp.concatenate([wide[..., lift:], above, gap, wide[..., low:lift]], 3)
+    lower = jnp.concatenate([frame[..., -1:], frame[..., :-1]], 3)
+    at_top = top_brick & (lax.broadcasted_iota(jnp.int32, frame.shape, 3) == cells_z - lift)
+    frame = jnp.where(at_top, lower, frame)
+    frame = jnp.concatenate(
+        [jnp.stack([(frame[0] == phase).astype(jnp.float32) for phase in range(4)]), frame[1:]], 0
     )
-    ext = edge_at(ext, cells_z - low, top_brick)
-    ext = step(ext, 1 - rim_y, low + 1, 0)
-    ext = edge_at(ext, cells_z - low - 1, top_brick)
-    ext = step(ext, 2 - rim_y, low + 2, 0)
-    liquid = jnp.concatenate(
-        [jnp.ones((1,) + ext.shape[1:], jnp.float32), jnp.zeros((nf - 1,) + ext.shape[1:], jnp.float32)], 0
-    )
-    ext = jnp.where(top_brick & (layer_index(ext) >= cells_z - lift + 2), liquid, ext)
-    ext = edge_below(ext, 1, bottom_brick)
-    ext = edge_at(ext, cells_z + 2, top_brick)
-    ext = step(ext, 3 - rim_y, -1, lift)
-    ext = edge_below(ext, 0, bottom_brick)
-    ext = edge_at(ext, cells_z + 1, top_brick)
-    fields = step(ext, 4 - rim_y, 0, lift)
-    return (fields[:4], fields[4:])
+    frame = jnp.transpose(frame, (1, 0, 2, 3))
+    for k in range(4):
+        frame = run_step(frame, frame_halos(frame), masks[k], under, fixes[k][:, None, :][:, 0])
+    out = jnp.transpose(frame[:, :, :cells_y, :cells_z], (1, 0, 2, 3))
+    return out[:4], out[4:]
 
 
 def solution(mesh):

time: 36.2 us -> 50.1 us (1.38)
  Pallas kernels: 0 us -> 17 us
  other arithmetic: 10.6 us -> 4.46 us
  local copies, waits for them, and re-layouts: 7.06 us -> 10.8 us
    pallas_call x0 -> x4, Pallas kernels: none -> 17 us  [run_step(): pl.pallas_call(step_kernel, out_shape=jax.ShapeDtypeStruct(frame.shape, f...]
    add x11 -> x0, other arithmetic: 2.72 us -> none  [the longest x7 1.72 us: phase_update(): phi[phase] + DT * (rates[phase] - mean_rate)]
    unnamed x9 -> x18, local copies, waits for them, and re-layouts: 2.67 us -> 4.7 us
    sub x12 -> x0, other arithmetic: 1.74 us -> none  [the longest x4 0.74 us: chem_update(): delta = shape_fn(phi_new) - shape_fn(phi_old)]
    ppermute x1, waiting for transfers between devices: 4.82 us -> 3.29 us  [shards(): lax.ppermute(wide[..., :count].reshape(wide.shape[0], -1), 'gz', line('gz...]
    convert_element_type x0 -> x2, other arithmetic: none -> 1.22 us  [active(): return jnp.any(hits, 0).astype(jnp.float32)]
    mul x12 -> x1, other arithmetic: 1.84 us -> 0.75 us  [shards(): under = 2.0 * ((base_z + lane_z + lift).astype(jnp.float32) / depth - 0.5)]
    slice x15 -> x10, local copies, waits for them, and re-layouts: 2.32 us -> 3.39 us  [the longest x4 2.87 us: frame_halos(): pair = jnp.stack([frame[-1], frame[0]])]
  transfers between devices with their start and end apart: 7 -> 7, of which waited for: 6 -> 7; matrix products, arithmetic and copies ran while one was open for 8% -> 8% of each run, Pallas kernels for 0% -> 0%
where the time goes in v6:
time: 50.1 us; the launch traced here: 49.6 us
  Pallas kernels  17 us (34%)
  local copies, waits for them, and re-layouts  10.8 us (22%)
  waiting for transfers between devices  10.6 us (21%)
  starting transfers between devices  5.92 us (12%)
  other arithmetic  4.46 us (9%)
  between operations  0.89 us (2%)
    pallas_call x4, Pallas kernels, run_step(): pl.pallas_call(step_kernel, out_shape=jax.ShapeDtypeStruct(frame.shape, f...  17 us
    unnamed x18, local copies, waits for them, and re-layouts  4.7 us
    ppermute x1, starting transfers between devices, shards(): from_up = lax.ppermute(start[:, :, :rim_y], 'gy', ring('gy', -1))  3.95 us
    ppermute x4, waiting for transfers between devices, frame_halos(): return lax.ppermute(pair, 'gx', ring('gx', 1))  3.36 us
    ppermute x1, waiting for transfers between devices, shards(): lax.ppermute(wide[..., :count].reshape(wide.shape[0], -1), 'gz', line('gz...  3.29 us
    ppermute x1, waiting for transfers between devices, shards(): from_down = lax.ppermute(start[:, :, -rim_y:], 'gy', ring('gy', 1))  3.24 us
    slice x4, local copies, waits for them, and re-layouts, frame_halos(): pair = jnp.stack([frame[-1], frame[0]])  2.87 us
    ppermute x1, starting transfers between devices, shards(): lax.ppermute(wide[..., :count].reshape(wide.shape[0], -1), 'gz', line('gz...  1.29 us
  transfers between devices with their start and end apart: 7, of which 7 were waited for; matrix products, arithmetic and copies ran while one was open for 8% of the time, Pallas kernels for 0%

profile of v6, /device:TPU:0, one launch (start us, length us, event | category | flops | bytes accessed | tf_op | source)
XLA Modules:
  0.0 49.6 jit_solution(7175718116119518908)
XLA Ops:
  0.6 0.0 copy-start.2
  0.6 0.8 %convert_bitcast_fusion = f32[1,8,8,128]{3,2,0,1:T(8,128)S(1)} fusion(s32[8,8,128]{2,1,0:T(8,128)} %param.3), kind=kLoop, calls=%fused_computation.19 | loop fusion | flops 8192 | bytes 65536 | tf_op jit(solution)/shard_map/broadcast_in_dim | solution.py:264
  1.4 0.0 copy-done.2
  1.5 3.9 %collective-permute-start = (f32[3,8,4,128]{3,2,0,1:T(4,128)S(1)}, f32[3,8,4,128]{3,2,0,1:T(4,128)S(1)}, u32[]{:S(2)}, u32[]{:S(2)}) collective-permute-start(f32[3,8,4,128]{3,2,0,1:T(4,128)S(1)} %get-tuple-element.18), channel_id=1, source_target_pairs={{0,12},{4,0},{8,4},{12,8},{1,13},{5,1},{9,5},{13,9},{2,14},{6,2},{... | collective-permute-start | bytes 147464 | tf_op jit(solution)/shard_map/ppermute | solution.py:266
  5.4 0.0 collective-permute-start.1
  5.4 0.0 copy-start.7
  5.5 0.7 %copy-done.7 = s32[32,3]{0,1:T(4,128)S(1)} copy-done((s32[32,3]{0,1:T(4,128)S(1)}, s32[32,3]{0,1:T(4,128)}, u32[]{:S(2)}) %copy-start.7) | copy-done | bytes 408
  6.2 0.1 broadcast_compare_fusion.1
  6.2 0.1 compare_and_fusion
  6.3 0.2 and_reduce_fusion
  6.5 0.7 %collective-permute-done = f32[3,8,4,128]{3,2,0,1:T(4,128)S(1)} collective-permute-done((f32[3,8,4,128]{3,2,0,1:T(4,128)S(1)}, f32[3,8,4,128]{3,2,0,1:T(4,128)S(1)}, u32[]{:S(2)}, u32[]{:S(2)}) %collective-permute-start) | collective-permute-done | bytes 49184 | tf_op jit(solution)/shard_map/ppermute | solution.py:266
  7.2 3.2 %collective-permute-done.1 = f32[3,8,4,128]{3,2,0,1:T(4,128)S(1)} collective-permute-done((f32[3,8,4,128]{3,2,0,1:T(4,128)S(1)}, f32[3,8,4,128]{3,2,0,1:T(4,128)S(1)}, u32[]{:S(2)}, u32[]{:S(2)}) %collective-permute-start.1) | collective-permute-done | bytes 49184 | tf_op jit(solution)/shard_map/ppermute | solution.py:267
  10.5 0.2 reshape.283
  10.7 1.3 %collective-permute-start.2 = (f32[3,4608]{1,0:T(4,128)S(1)}, f32[3,4608]{1,0:T(4,128)S(1)}, u32[]{:S(2)}, u32[]{:S(2)}) collective-permute-start(f32[3,4608]{1,0:T(4,128)S(1)} %reshape.283), channel_id=1, source_target_pairs={{1,0},{2,1},{3,2},{5,4},{6,5},{7,6},{9,8},{10,9},{11,10},{13,12},{... | collective-permute-start | bytes 165896 | tf_op jit(solution)/shard_map/ppermute | solution.py:269
  12.0 0.6 %convert_element_type.40.mask_ref = f32[16,256]{1,0:T(8,128)} convert(pred[16,256]{1,0:T(8,128)(4,1)S(1)} %get-tuple-element.9) | non-fusion elementwise | flops 4096 | bytes 20480 | tf_op jit(solution)/shard_map/convert_element_type | solution.py:241
  12.6 0.6 %stack.17.fix_ref = f32[3,256]{1,0:T(4,128)} pad(f32[1,256]{1,0:T(1,128)S(1)} %and_select_fusion.3, f32[]{:T(128)} %constant.88.clone.1), padding=0_2x0_0 | pad | bytes 4100 | tf_op jit(solution)/shard_map/stack | solution.py:253
  13.2 0.1 pad.19.clone
  13.3 0.1 slice.104
  13.4 0.1 slice.106
  13.5 0.1 slice.103
  13.6 3.3 %collective-permute-done.2 = f32[3,4608]{1,0:T(4,128)S(1)} collective-permute-done((f32[3,4608]{1,0:T(4,128)S(1)}, f32[3,4608]{1,0:T(4,128)S(1)}, u32[]{:S(2)}, u32[]{:S(2)}) %collective-permute-start.2) | collective-permute-done | bytes 55328 | tf_op jit(solution)/shard_map/ppermute | solution.py:269
  16.9 0.2 reshape.284
  17.1 0.2 pad_maximum_fusion
  17.4 0.3 maximum_select_fusion
  17.8 0.0 copy-start
  17.9 0.1 collective-permute-start.3
  18.0 0.7 %add_multiply_fusion.under_ref = f32[1,256]{1,0:T(1,128)} fusion(s32[]{:T(128)S(6)} %mul.16), kind=kLoop, calls=%fused_computation.51 | loop fusion | flops 2304 | bytes 1028 | tf_op jit(solution)/shard_map/mul | solution.py:245
  18.7 0.7 %collective-permute-done.3.halo_ref = f32[2,6,16,256]{3,2,1,0:T(8,128)S(1)} collective-permute-done((f32[2,6,16,256]{3,2,1,0:T(8,128)S(1)}, f32[2,6,16,256]{3,2,1,0:T(8,128)S(1)}, u32[]{:S(2)}, u32[]{:S(2)}) %collective-permute-start.3) | collective-permute-done | bytes 196640 | tf_op jit(solution)/shard_map/ppermute | solution.py:202
  19.4 0.0 copy-done
  19.4 0.0 copy-start.4
  19.4 0.7 %copy-done.4 = f32[2,6,16,256]{3,2,1,0:T(8,128)} copy-done((f32[2,6,16,256]{3,2,1,0:T(8,128)}, f32[2,6,16,256]{3,2,1,0:T(8,128)S(1)}, u32[]{:S(2)}) %copy-start.4) | copy-done | bytes 196632
  20.1 4.2 %shard_map.50.frame_ref = f32[8,6,16,256]{3,2,1,0:T(8,128)} custom-call(f32[8,6,16,256]{3,2,1,0:T(8,128)} %bitcast.17, f32[2,6,16,256]{3,2,1,0:T(8,128)} %copy-done.4, f32[16,256]{1,0:T(8,128)} %convert_element_type.40.mask_ref, f32[1,256]{1,0:T(1,128)} %add_multiply_fusion.under_ref, f32[3,256]{1,0:T(4,128)} %stack.17.fix_ref), custom_call_target="tpu_custom_call" | custom-call | tf_op jit(solution)/shard_map/pallas_call | solution.py:192
  24.3 1.0 %fusion.5 = (f32[1,6,16,256]{3,2,1,0:T(8,128)S(1)}, f32[1,6,16,256]{3,2,1,0:T(8,128)S(1)}) fusion(f32[8,6,16,256]{3,2,1,0:T(8,128)} %shard_map.50.frame_ref), kind=kLoop, calls=%fused_computation.57 | loop fusion | bytes 393216 | tf_op jit(solution)/shard_map/slice | solution.py:201
  25.3 0.2 collective-permute-start.4
  25.5 0.6 %pad_maximum_fusion.9 = (f32[3,256]{1,0:T(4,128)}, f32[3,256]{1,0:T(4,128)}) fusion(f32[1,256]{1,0:T(1,128)S(1)} %broadcast_in_dim.34, f32[1,256]{1,0:T(1,128)S(1)} %and_select_fusion.1, f32[1,256]{1,0:T(1,128)S(1)} %get-tuple-element.27, f32[1,256]{1,0:T(1,128)S(1)} %get-tuple-element.26), kind=kLoop, calls=%fused_computation.26 | loop fusion | flops 2304 | bytes 10240 | tf_op jit(solution)/shard_map/stack | solution.py:259
  26.1 0.7 %collective-permute-done.4.halo_ref = f32[2,6,16,256]{3,2,1,0:T(8,128)S(1)} collective-permute-done((f32[2,6,16,256]{3,2,1,0:T(8,128)S(1)}, f32[2,6,16,256]{3,2,1,0:T(8,128)S(1)}, u32[]{:S(2)}, u32[]{:S(2)}) %collective-permute-start.4) | collective-permute-done | bytes 196640 | tf_op jit(solution)/shard_map/ppermute | solution.py:202
  26.8 0.0 copy-start.3
  26.8 0.7 %copy-done.3 = f32[2,6,16,256]{3,2,1,0:T(8,128)} copy-done((f32[2,6,16,256]{3,2,1,0:T(8,128)}, f32[2,6,16,256]{3,2,1,0:T(8,128)S(1)}, u32[]{:S(2)}) %copy-start.3) | copy-done | bytes 196632
  27.5 4.3 %shard_map.51.frame_ref = f32[8,6,16,256]{3,2,1,0:T(8,128)} custom-call(f32[8,6,16,256]{3,2,1,0:T(8,128)} %shard_map.50.frame_ref, f32[2,6,16,256]{3,2,1,0:T(8,128)} %copy-done.3, f32[16,256]{1,0:T(8,128)} %convert_element_type.40.mask_ref, f32[1,256]{1,0:T(1,128)} %add_multiply_fusion.under_ref, f32[3,256]{1,0:T(4,128)} %get-tuple-element.21.fix_ref), custom_call_target="tpu_custom_call" | custom-call | tf_op jit(solution)/shard_map/pallas_call | solution.py:192
  31.7 1.0 %fusion.4 = (f32[1,6,16,256]{3,2,1,0:T(8,128)S(1)}, f32[1,6,16,256]{3,2,1,0:T(8,128)S(1)}) fusion(f32[8,6,16,256]{3,2,1,0:T(8,128)} %shard_map.51.frame_ref), kind=kLoop, calls=%fused_computation.56 | loop fusion | bytes 393216 | tf_op jit(solution)/shard_map/slice | solution.py:201
  32.7 0.2 collective-permute-start.5
  32.9 0.6 %convert_element_type.42.mask_ref = f32[16,256]{1,0:T(8,128)} convert(pred[16,256]{1,0:T(8,128)(4,1)S(1)} %get-tuple-element.8) | non-fusion elementwise | flops 4096 | bytes 20480 | tf_op jit(solution)/shard_map/convert_element_type | solution.py:241
  33.5 0.7 %collective-permute-done.5.halo_ref = f32[2,6,16,256]{3,2,1,0:T(8,128)S(1)} collective-permute-done((f32[2,6,16,256]{3,2,1,0:T(8,128)S(1)}, f32[2,6,16,256]{3,2,1,0:T(8,128)S(1)}, u32[]{:S(2)}, u32[]{:S(2)}) %collective-permute-start.5) | collective-permute-done | bytes 196640 | tf_op jit(solution)/shard_map/ppermute | solution.py:202
  34.2 0.0 copy-start.5
  34.2 0.7 %copy-done.5 = f32[2,6,16,256]{3,2,1,0:T(8,128)} copy-done((f32[2,6,16,256]{3,2,1,0:T(8,128)}, f32[2,6,16,256]{3,2,1,0:T(8,128)S(1)}, u32[]{:S(2)}) %copy-start.5) | copy-done | bytes 196632
  34.9 4.2 %shard_map.52.frame_ref = f32[8,6,16,256]{3,2,1,0:T(8,128)} custom-call(f32[8,6,16,256]{3,2,1,0:T(8,128)} %shard_map.51.frame_ref, f32[2,6,16,256]{3,2,1,0:T(8,128)} %copy-done.5, f32[16,256]{1,0:T(8,128)} %convert_element_type.42.mask_ref, f32[1,256]{1,0:T(1,128)} %add_multiply_fusion.under_ref, f32[3,256]{1,0:T(4,128)} %get-tuple-element.20.fix_ref), custom_call_target="tpu_custom_call" | custom-call | tf_op jit(solution)/shard_map/pallas_call | solution.py:192
  39.1 1.0 %fusion.3 = (f32[1,6,16,256]{3,2,1,0:T(8,128)S(1)}, f32[1,6,16,256]{3,2,1,0:T(8,128)S(1)}) fusion(f32[8,6,16,256]{3,2,1,0:T(8,128)} %shard_map.52.frame_ref), kind=kLoop, calls=%fused_computation.55 | loop fusion | bytes 393216 | tf_op jit(solution)/shard_map/slice | solution.py:201
  40.1 0.2 collective-permute-start.6
  40.3 1.3 %collective-permute-done.6.halo_ref = f32[2,6,16,256]{3,2,1,0:T(8,128)S(1)} collective-permute-done((f32[2,6,16,256]{3,2,1,0:T(8,128)S(1)}, f32[2,6,16,256]{3,2,1,0:T(8,128)S(1)}, u32[]{:S(2)}, u32[]{:S(2)}) %collective-permute-start.6) | collective-permute-done | bytes 196640 | tf_op jit(solution)/shard_map/ppermute | solution.py:202
  41.6 0.0 copy-start.6
  41.6 0.6 %stack.42.fix_ref = f32[3,256]{1,0:T(4,128)} broadcast(f32[]{:T(128)} %constant.88.clone.1), dimensions={} | broadcast | bytes 3076 | tf_op jit(solution)/shard_map/stack | solution.py:260
  42.2 0.0 copy-done.6
  42.3 4.3 %shard_map.53 = f32[8,6,16,256]{3,2,1,0:T(8,128)} custom-call(f32[8,6,16,256]{3,2,1,0:T(8,128)} %shard_map.52.frame_ref, f32[2,6,16,256]{3,2,1,0:T(8,128)} %copy-done.6, f32[16,256]{1,0:T(8,128)} %convert_element_type.42.mask_ref, f32[1,256]{1,0:T(1,128)} %add_multiply_fusion.under_ref, f32[3,256]{1,0:T(4,128)} %stack.42.fix_ref), custom_call_target="tpu_custom_call" | custom-call | tf_op jit(solution)/shard_map/pallas_call | solution.py:192
  46.5 0.9 %slice_bitcast_fusion = f32[6,8,8,128]{3,2,0,1:T(8,128)S(1)} fusion(f32[8,6,16,256]{3,2,1,0:T(8,128)} %shard_map.53), kind=kLoop, calls=%fused_computation.5 | loop fusion | bytes 393216 | tf_op jit(solution)/shard_map/transpose | solution.py:282
  47.5 0.0 copy-start.1
  47.5 0.6 %copy-done.1 = f32[6,8,8,128]{3,2,0,1:T(8,128)} copy-done((f32[6,8,8,128]{3,2,0,1:T(8,128)}, f32[6,8,8,128]{3,2,0,1:T(8,128)S(1)}, u32[]{:S(2)}) %copy-start.1) | copy-done | bytes 196632
  48.2 0.0 slice-start
  48.2 0.7 %copy.16 = f32[4,8,8,128]{3,2,1,0:T(8,128)} copy(f32[4,8,8,128]{3,2,0,1:T(8,128)S(1)} %slice.119) | data formatting | bytes 262144
  48.8 0.2 slice-done
  49.0 0.6 %copy.17 = f32[2,8,8,128]{3,2,1,0:T(8,128)} copy(f32[2,8,8,128]{3,2,0,1:T(8,128)S(1)} %slice-done) | data formatting | bytes 131072
  (24 shorter events, 0.3 us)
Async XLA Ops:
  0.6 0.8 %copy-start.2 = (f32[2,8,8,128]{3,2,1,0:T(8,128)S(1)}, f32[2,8,8,128]{3,2,1,0:T(8,128)}, u32[]{:S(2)}) copy-start(f32[2,8,8,128]{3,2,1,0:T(8,128)} %param.4) | copy-start | bytes 196612
  1.5 5.7 %collective-permute-start = (f32[3,8,4,128]{3,2,0,1:T(4,128)S(1)}, f32[3,8,4,128]{3,2,0,1:T(4,128)S(1)}, u32[]{:S(2)}, u32[]{:S(2)}) collective-permute-start(f32[3,8,4,128]{3,2,0,1:T(4,128)S(1)} %get-tuple-element.18), channel_id=1, source_target_pairs={{0,12},{4,0},{8,4},{12,8},{1,13},{5,1},{9,5},{13,9},{2,14},{6,2},{... | collective-permute-start | bytes 147464 | tf_op jit(solution)/shard_map/ppermute | solution.py:266
  5.4 5.0 %collective-permute-start.1 = (f32[3,8,4,128]{3,2,0,1:T(4,128)S(1)}, f32[3,8,4,128]{3,2,0,1:T(4,128)S(1)}, u32[]{:S(2)}, u32[]{:S(2)}) collective-permute-start(f32[3,8,4,128]{3,2,0,1:T(4,128)S(1)} %get-tuple-element.19), channel_id=1, source_target_pairs={{0,4},{4,8},{8,12},{12,0},{1,5},{5,9},{9,13},{13,1},{2,6},{6,10},{... | collective-permute-start | bytes 147464 | tf_op jit(solution)/shard_map/ppermute | solution.py:267
  5.4 0.7 %copy-start.7 = (s32[32,3]{0,1:T(4,128)S(1)}, s32[32,3]{0,1:T(4,128)}, u32[]{:S(2)}) copy-start(s32[32,3]{0,1:T(4,128)} %param.5) | copy-start | bytes 1156
  10.7 6.2 %collective-permute-start.2 = (f32[3,4608]{1,0:T(4,128)S(1)}, f32[3,4608]{1,0:T(4,128)S(1)}, u32[]{:S(2)}, u32[]{:S(2)}) collective-permute-start(f32[3,4608]{1,0:T(4,128)S(1)} %reshape.283), channel_id=1, source_target_pairs={{1,0},{2,1},{3,2},{5,4},{6,5},{7,6},{9,8},{10,9},{11,10},{13,12},{... | collective-permute-start | bytes 165896 | tf_op jit(solution)/shard_map/ppermute | solution.py:269
  17.8 1.6 %copy-start = (f32[6,8,16,256]{3,2,0,1:T(8,128)}, f32[6,8,16,256]{3,2,0,1:T(8,128)S(1)}, u32[]{:S(2)}) copy-start(f32[6,8,16,256]{3,2,0,1:T(8,128)S(1)} %slice_dynamic-update-slice_fusion) | copy-start | bytes 2359300
  17.9 1.5 %collective-permute-start.3 = (f32[2,6,16,256]{3,2,1,0:T(8,128)S(1)}, f32[2,6,16,256]{3,2,1,0:T(8,128)S(1)}, u32[]{:S(2)}, u32[]{:S(2)}) collective-permute-start(f32[2,6,16,256]{3,2,1,0:T(8,128)S(1)} %pad_maximum_fusion.2), channel_id=1, source_target_pairs={{0,16},{16,0},{1,17},{17,1},{2,18},{18,2},{3,19},{19,3},{4,20},{20... | collective-permute-start | bytes 589832 | tf_op jit(solution)/shard_map/ppermute | solution.py:202
  19.4 0.7 %copy-start.4 = (f32[2,6,16,256]{3,2,1,0:T(8,128)}, f32[2,6,16,256]{3,2,1,0:T(8,128)S(1)}, u32[]{:S(2)}) copy-start(f32[2,6,16,256]{3,2,1,0:T(8,128)S(1)} %collective-permute-done.3.halo_ref) | copy-start | bytes 589828
  25.3 1.5 %collective-permute-start.4 = (f32[2,6,16,256]{3,2,1,0:T(8,128)S(1)}, f32[2,6,16,256]{3,2,1,0:T(8,128)S(1)}, u32[]{:S(2)}, u32[]{:S(2)}) collective-permute-start(f32[2,6,16,256]{3,2,1,0:T(8,128)S(1)} %pad_maximum_fusion.3), channel_id=1, source_target_pairs={{0,16},{16,0},{1,17},{17,1},{2,18},{18,2},{3,19},{19,3},{4,20},{20... | collective-permute-start | bytes 589832 | tf_op jit(solution)/shard_map/ppermute | solution.py:202
  26.8 0.7 %copy-start.3 = (f32[2,6,16,256]{3,2,1,0:T(8,128)}, f32[2,6,16,256]{3,2,1,0:T(8,128)S(1)}, u32[]{:S(2)}) copy-start(f32[2,6,16,256]{3,2,1,0:T(8,128)S(1)} %collective-permute-done.4.halo_ref) | copy-start | bytes 589828
  32.7 1.5 %collective-permute-start.5 = (f32[2,6,16,256]{3,2,1,0:T(8,128)S(1)}, f32[2,6,16,256]{3,2,1,0:T(8,128)S(1)}, u32[]{:S(2)}, u32[]{:S(2)}) collective-permute-start(f32[2,6,16,256]{3,2,1,0:T(8,128)S(1)} %pad_maximum_fusion.4), channel_id=1, source_target_pairs={{0,16},{16,0},{1,17},{17,1},{2,18},{18,2},{3,19},{19,3},{4,20},{20... | collective-permute-start | bytes 589832 | tf_op jit(solution)/shard_map/ppermute | solution.py:202
  34.2 0.7 %copy-start.5 = (f32[2,6,16,256]{3,2,1,0:T(8,128)}, f32[2,6,16,256]{3,2,1,0:T(8,128)S(1)}, u32[]{:S(2)}) copy-start(f32[2,6,16,256]{3,2,1,0:T(8,128)S(1)} %collective-permute-done.5.halo_ref) | copy-start | bytes 589828
  40.1 1.5 %collective-permute-start.6 = (f32[2,6,16,256]{3,2,1,0:T(8,128)S(1)}, f32[2,6,16,256]{3,2,1,0:T(8,128)S(1)}, u32[]{:S(2)}, u32[]{:S(2)}) collective-permute-start(f32[2,6,16,256]{3,2,1,0:T(8,128)S(1)} %pad_maximum_fusion.5), channel_id=1, source_target_pairs={{0,16},{16,0},{1,17},{17,1},{2,18},{18,2},{3,19},{19,3},{4,20},{20... | collective-permute-start | bytes 589832 | tf_op jit(solution)/shard_map/ppermute | solution.py:202
  41.6 0.7 %copy-start.6 = (f32[2,6,16,256]{3,2,1,0:T(8,128)}, f32[2,6,16,256]{3,2,1,0:T(8,128)S(1)}, u32[]{:S(2)}) copy-start(f32[2,6,16,256]{3,2,1,0:T(8,128)S(1)} %collective-permute-done.6.halo_ref) | copy-start | bytes 589828
  47.5 0.7 %copy-start.1 = (f32[6,8,8,128]{3,2,0,1:T(8,128)}, f32[6,8,8,128]{3,2,0,1:T(8,128)S(1)}, u32[]{:S(2)}) copy-start(f32[6,8,8,128]{3,2,0,1:T(8,128)S(1)} %slice_bitcast_fusion) | copy-start | bytes 589828
  48.2 0.8 %slice-start = ((f32[6,8,8,128]{3,2,0,1:T(8,128)}), f32[2,8,8,128]{3,2,0,1:T(8,128)S(1)}, s32[]{:S(2)}) async-start(f32[6,8,8,128]{3,2,0,1:T(8,128)} %copy-done.1), calls=%async_computation | async-start | bytes 131072 | tf_op jit(solution)/shard_map/slice | solution.py:283

commit v7 on v5

--- a/solution.py
+++ b/solution.py
@@ -127,12 +127,9 @@
         )
         return jnp.any(hits, 0)
 
-    def step(ext, first_y, first_z, offset):
-        fields = ext[:, :, 1:-1, 1:-1]
-        ypos = first_y + jnp.arange(fields.shape[2], dtype=jnp.int32)
-        zpos = base_z + first_z + jnp.arange(fields.shape[3], dtype=jnp.int32)
-        xlo, xhi = x_halos(fields)
-        side = neighbours(ext, xlo, xhi)
+    def update(cext, xm, xp, ypos, zpos, offset):
+        fields = cext[:, :, 1:-1, 1:-1]
+        side = [xp, xm, cext[:, :, 2:, 1:-1], cext[:, :, :-2, 1:-1], cext[:, :, 1:-1, 2:], cext[:, :, 1:-1, :-2]]
         phi_new = jnp.where(
             active(ypos, zpos)[None, None],
             phase_update(fields, side, zpos, offset, depth),
@@ -140,6 +137,34 @@
         )
         mu_new = chem_update(fields, side, fields[:4], phi_new)
         return jnp.concatenate([phi_new, mu_new], 0)
+
+    def send_faces(first, last):
+        if lax.axis_size("gx") == 2:
+            got = lax.ppermute(jnp.stack([last, first]), "gx", ring("gx", 1))
+            return got[0], got[1]
+        return (
+            lax.ppermute(last, "gx", ring("gx", 1)),
+            lax.ppermute(first, "gx", ring("gx", -1)),
+        )
+
+    def step(ext, halo, first_y, first_z, offset, fix, last=False):
+        fields = ext[:, :, 1:-1, 1:-1]
+        ypos = first_y + jnp.arange(fields.shape[2], dtype=jnp.int32)
+        zpos = base_z + first_z + jnp.arange(fields.shape[3], dtype=jnp.int32)
+        xlo, xhi = halo
+        faces = update(
+            jnp.stack([ext[:, 0], ext[:, -1]], 1),
+            jnp.stack([xlo, fields[:, -2]], 1),
+            jnp.stack([fields[:, 1], xhi], 1),
+            ypos, zpos, offset,
+        )
+        faces = fix(faces)
+        new_halo = None
+        if not last:
+            inner = faces[:, :, 1:-1, 1:-1]
+            new_halo = send_faces(inner[:, 0], inner[:, 1])
+        middle = fix(update(ext[:, 1:-1], fields[:, :-2], fields[:, 2:], ypos, zpos, offset))
+        return jnp.concatenate([faces[:, :1], middle, faces[:, 1:]], 1), new_halo
 
     def layer_index(ext):
         return lax.broadcasted_iota(jnp.int32, ext.shape, 3)
@@ -166,19 +191,31 @@
         [jnp.stack([(ext[0] == phase).astype(jnp.float32) for phase in range(4)]), ext[1:]], 0
     )
     ext = edge_at(ext, cells_z - low, top_brick)
-    ext = step(ext, 1 - rim_y, low + 1, 0)
-    ext = edge_at(ext, cells_z - low - 1, top_brick)
-    ext = step(ext, 2 - rim_y, low + 2, 0)
-    liquid = jnp.concatenate(
-        [jnp.ones((1,) + ext.shape[1:], jnp.float32), jnp.zeros((nf - 1,) + ext.shape[1:], jnp.float32)], 0
-    )
-    ext = jnp.where(top_brick & (layer_index(ext) >= cells_z - lift + 2), liquid, ext)
-    ext = edge_below(ext, 1, bottom_brick)
-    ext = edge_at(ext, cells_z + 2, top_brick)
-    ext = step(ext, 3 - rim_y, -1, lift)
-    ext = edge_below(ext, 0, bottom_brick)
-    ext = edge_at(ext, cells_z + 1, top_brick)
-    fields = step(ext, 4 - rim_y, 0, lift)
+    inner = ext[:, :, 1:-1, 1:-1]
+    halo = send_faces(inner[:, 0], inner[:, -1])
+
+    def fix0(new):
+        return edge_at(new, cells_z - low - 1, top_brick)
+
+    def fix1(new):
+        liquid = jnp.concatenate(
+            [jnp.ones((1,) + new.shape[1:], jnp.float32), jnp.zeros((nf - 1,) + new.shape[1:], jnp.float32)], 0
+        )
+        new = jnp.where(top_brick & (layer_index(new) >= cells_z - lift + 2), liquid, new)
+        new = edge_below(new, 1, bottom_brick)
+        return edge_at(new, cells_z + 2, top_brick)
+
+    def fix2(new):
+        new = edge_below(new, 0, bottom_brick)
+        return edge_at(new, cells_z + 1, top_brick)
+
+    def fix3(new):
+        return new
+
+    ext, halo = step(ext, halo, 1 - rim_y, low + 1, 0, fix0)
+    ext, halo = step(ext, halo, 2 - rim_y, low + 2, 0, fix1)
+    ext, halo = step(ext, halo, 3 - rim_y, -1, lift, fix2)
+    fields, _ = step(ext, halo, 4 - rim_y, 0, lift, fix3, last=True)
     return (fields[:4], fields[4:])
 
 

time: 36.2 us -> 39 us (1.077)
  other arithmetic: 10.6 us -> 16 us
  waiting for transfers between devices: 11.1 us -> 8.58 us
  local copies, waits for them, and re-layouts: 7.06 us -> 5.84 us
  starting transfers between devices: 5.94 us -> 6.74 us
    ppermute x4, waiting for transfers between devices: 3.59 us -> 1.05 us  [send_faces(): got = lax.ppermute(jnp.stack([last, first]), 'gx', ring('gx', 1))]
    mul x4 -> x8, other arithmetic: 1.65 us -> 2.9 us  [phase_update(): square = phi * phi]
    add x7 -> x16, other arithmetic: 1.72 us -> 2.96 us  [phase_update(): phi[phase] + DT * (rates[phase] - mean_rate)]
    another operation x6 -> x7, local copies, waits for them, and re-layouts: 1.46 us -> 0.36 us  [the longest x3 0.31 us: send_faces(): got = lax.ppermute(jnp.stack([last, first]), 'gx', ring('gx', 1))]
    ppermute x4, starting transfers between devices: 0.7 us -> 1.5 us  [send_faces(): got = lax.ppermute(jnp.stack([last, first]), 'gx', ring('gx', 1))]
    add x4 -> x8, other arithmetic: 1.01 us -> 1.8 us  [chem_update(): flux = flux + 0.5 * (centre_d + side_d[way]) * (side_m[way] - chem)]
    slice x0 -> x1, other arithmetic: none -> 0.64 us  [shards(): return (fields[:4], fields[4:])]
    slice x4 -> x8, local copies, waits for them, and re-layouts: 0.66 us -> 1.1 us  [edge_below(): down = jnp.concatenate([ext[..., 1:], ext[..., -1:]], 3)]
  transfers between devices with their start and end apart: 7 -> 7, of which waited for: 6 -> 4; matrix products, arithmetic and copies ran while one was open for 8% -> 14% of each run, Pallas kernels for 0% -> 0%
where the time goes in v7:
time: 39 us; the launch traced here: 38.7 us
  other arithmetic  16 us (41%)
  waiting for transfers between devices  8.58 us (22%)
  starting transfers between devices  6.74 us (17%)
  local copies, waits for them, and re-layouts  5.84 us (15%)
  between operations  1.58 us (4%)
    ppermute x1, waiting for transfers between devices, shards(): lax.ppermute(wide[..., :count].reshape(wide.shape[0], -1), 'gz', line('gz...  4.82 us
    ppermute x1, starting transfers between devices, shards(): above_y = lax.ppermute(start[:, :, :rim_y], 'gy', ring('gy', -1))  3.95 us
    add x16, other arithmetic, phase_update(): phi[phase] + DT * (rates[phase] - mean_rate)  2.96 us
    mul x8, other arithmetic, phase_update(): square = phi * phi  2.9 us
    ppermute x1, waiting for transfers between devices, shards(): below_y = lax.ppermute(start[:, :, -rim_y:], 'gy', ring('gy', 1))  2.71 us
    unnamed x8, local copies, waits for them, and re-layouts  2.44 us
    add x8, other arithmetic, chem_update(): flux = flux + 0.5 * (centre_d + side_d[way]) * (side_m[way] - chem)  1.8 us
    ppermute x4, starting transfers between devices, send_faces(): got = lax.ppermute(jnp.stack([last, first]), 'gx', ring('gx', 1))  1.5 us
  transfers between devices with their start and end apart: 7, of which 4 were waited for; matrix products, arithmetic and copies ran while one was open for 14% of the time, Pallas kernels for 0%

profile of v7, /device:TPU:0, one launch (start us, length us, event | category | flops | bytes accessed | tf_op | source)
XLA Modules:
  0.0 38.7 jit_solution(7768379548399500691)
XLA Ops:
  0.6 0.8 %convert_bitcast_fusion = f32[1,8,8,128]{3,2,1,0:T(8,128)S(1)} fusion(s32[8,8,128]{2,1,0:T(8,128)} %param.3), kind=kLoop, calls=%fused_computation.741 | loop fusion | flops 8192 | bytes 65536 | tf_op jit(solution)/shard_map/broadcast_in_dim | solution.py:180
  1.5 3.9 %collective-permute-start.1 = (f32[3,8,4,128]{3,2,1,0:T(4,128)S(1)}, f32[3,8,4,128]{3,2,1,0:T(4,128)S(1)}, u32[]{:S(2)}, u32[]{:S(2)}) collective-permute-start(f32[3,8,4,128]{3,2,1,0:T(4,128)S(1)} %get-tuple-element.216), channel_id=1, source_target_pairs={{0,12},{4,0},{8,4},{12,8},{1,13},{5,1},{9,5},{13,9},{2,14},{6,2},{... | collective-permute-start | bytes 147464 | tf_op jit(solution)/shard_map/ppermute | solution.py:183
  5.8 0.6 %copy-done.3 = s32[32,3]{0,1:T(4,128)S(1)} copy-done((s32[32,3]{0,1:T(4,128)S(1)}, s32[32,3]{0,1:T(4,128)}, u32[]{:S(2)}) %copy-start.3) | copy-done | bytes 408
  7.1 0.2 and_reduce_fusion
  7.3 0.2 and_reduce_fusion.1
  7.4 0.1 and_reduce_fusion.2
  7.7 2.7 %collective-permute-done = f32[3,8,4,128]{3,2,1,0:T(4,128)S(1)} collective-permute-done((f32[3,8,4,128]{3,2,1,0:T(4,128)S(1)}, f32[3,8,4,128]{3,2,1,0:T(4,128)S(1)}, u32[]{:S(2)}, u32[]{:S(2)}) %collective-permute-start) | collective-permute-done | bytes 49184 | tf_op jit(solution)/shard_map/ppermute | solution.py:182
  10.5 0.2 reshape.577
  10.6 1.3 %collective-permute-start.2 = (f32[3,4608]{1,0:T(4,128)S(1)}, f32[3,4608]{1,0:T(4,128)S(1)}, u32[]{:S(2)}, u32[]{:S(2)}) collective-permute-start(f32[3,4608]{1,0:T(4,128)S(1)} %reshape.577), channel_id=1, source_target_pairs={{1,0},{2,1},{3,2},{5,4},{6,5},{7,6},{9,8},{10,9},{11,10},{13,12},{... | collective-permute-start | bytes 165896 | tf_op jit(solution)/shard_map/ppermute | solution.py:188
  12.1 4.8 %collective-permute-done.2 = f32[3,4608]{1,0:T(4,128)S(1)} collective-permute-done((f32[3,4608]{1,0:T(4,128)S(1)}, f32[3,4608]{1,0:T(4,128)S(1)}, u32[]{:S(2)}, u32[]{:S(2)}) %collective-permute-start.2) | collective-permute-done | bytes 55328 | tf_op jit(solution)/shard_map/ppermute | solution.py:188
  16.9 0.2 reshape.578
  17.3 0.1 fusion.17
  17.5 0.3 maximum_select_fusion
  17.8 0.2 fusion.550
  18.0 0.7 %slice_multiply_fusion.2 = (f32[4,6,14,134]{3,2,1,0:T(8,128)S(1)}, f32[4,6,14,134]{3,2,1,0:T(8,128)S(1)}) fusion(f32[6,8,16,136]{3,2,1,0:T(8,128)S(1)} %maximum_select_fusion), kind=kLoop, calls=%fused_computation.96 | loop fusion | flops 360192 | bytes 1620864 | tf_op jit(solution)/shard_map/mul | solution.py:63
  18.7 0.2 fusion.200
  18.9 0.3 multiply_add_fusion.14
  19.2 0.3 multiply_add_fusion.13
  19.5 0.2 multiply_subtract_fusion.2
  19.7 0.4 fusion.45
  20.3 0.2 maximum_select_fusion.1
  20.8 0.2 fusion.77
  21.2 0.1 multiply_add_fusion.28
  21.4 0.1 fusion.214
  21.9 0.7 %slice_multiply_fusion.1 = (f32[4,6,12,132]{3,2,1,0:T(8,128)S(1)}, f32[4,6,12,132]{3,2,1,0:T(8,128)S(1)}) fusion(f32[6,6,14,134]{3,2,1,0:T(8,128)S(1)} %maximum_select_fusion.1, f32[6,1,14,134]{3,2,1,0:T(8,128)S(1)} %get-tuple-element.194, f32[6,1,14,134]{3,2,1,0:T(8,128)S(1)} %get-tuple-element.193), kind=kLoop, calls=%fused_computation.95 | loop fusion | flops 380160 | bytes 3056640 | tf_op jit(solution)/shard_map/mul | solution.py:63
  22.6 0.2 fusion.164
  22.8 0.3 multiply_add_fusion.9
  23.1 0.3 multiply_add_fusion.8
  23.4 0.2 multiply_subtract_fusion.1
  23.6 0.4 fusion.32
  24.1 0.9 %copy-done = f32[6,6,12,132]{3,2,1,0:T(8,128)S(1)} copy-done((f32[6,6,12,132]{3,2,1,0:T(8,128)S(1)}, f32[6,6,12,132]{3,2,1,0:T(8,128)}, u32[]{:S(2)}) %copy-start) | copy-done | bytes 228120
  25.2 0.1 slice.2342
  25.3 0.2 slice.2341
  25.5 0.6 %collective-permute-start.4 = (f32[2,6,12,132]{3,2,1,0:T(8,128)S(1)}, f32[2,6,12,132]{3,2,1,0:T(8,128)S(1)}, u32[]{:S(2)}, u32[]{:S(2)}) collective-permute-start(f32[2,6,12,132]{3,2,1,0:T(8,128)S(1)} %pad_maximum_fusion.10), channel_id=1, source_target_pairs={{0,16},{16,0},{1,17},{17,1},{2,18},{18,2},{3,19},{19,3},{4,20},{20... | collective-permute-start | bytes 228104 | tf_op jit(solution)/shard_map/ppermute | solution.py:143
  26.1 0.2 maximum_select_fusion.3
  26.3 0.2 maximum_select_fusion.4
  26.7 0.5 %collective-permute-done.4 = f32[2,6,12,132]{3,2,1,0:T(8,128)S(1)} collective-permute-done((f32[2,6,12,132]{3,2,1,0:T(8,128)S(1)}, f32[2,6,12,132]{3,2,1,0:T(8,128)S(1)}, u32[]{:S(2)}, u32[]{:S(2)}) %collective-permute-start.4) | collective-permute-done | bytes 76064 | tf_op jit(solution)/shard_map/ppermute | solution.py:143
  27.2 0.2 slice_multiply_fusion.4
  27.5 0.1 multiply_add_fusion.24
  27.7 0.1 multiply_add_fusion.23
  27.9 0.1 fusion.235
  28.2 0.8 %copy-done.2 = f32[6,2,12,132]{3,2,1,0:T(8,128)S(1)} copy-done((f32[6,2,12,132]{3,2,1,0:T(8,128)S(1)}, f32[6,2,12,132]{3,2,1,0:T(8,128)}, u32[]{:S(2)}) %copy-start.2) | copy-done | bytes 76056
  29.6 0.7 %slice_multiply_fusion = (f32[4,6,10,130]{3,2,1,0:T(8,128)S(1)}, f32[4,6,10,130]{3,2,1,0:T(8,128)S(1)}) fusion(f32[6,6,12,132]{3,2,1,0:T(8,128)S(1)} %maximum_select_fusion.4, f32[6,1,12,132]{3,2,1,0:T(8,128)S(1)} %get-tuple-element.180, f32[6,1,12,132]{3,2,1,0:T(8,128)S(1)} %get-tuple-element.179), kind=kLoop, calls=%fused_computation.94 | loop fusion | flops 312000 | bytes 3002112 | tf_op jit(solution)/shard_map/mul | solution.py:63
  30.3 0.2 fusion.136
  30.5 0.3 multiply_add_fusion.4
  30.8 0.3 multiply_add_fusion.3
  31.1 0.2 multiply_subtract_fusion
  31.3 0.4 fusion.19
  31.9 0.1 slice.2442
  32.0 0.2 slice.2441
  32.3 0.4 %collective-permute-start.5 = (f32[2,6,10,130]{3,2,1,0:T(8,128)S(1)}, f32[2,6,10,130]{3,2,1,0:T(8,128)S(1)}, u32[]{:S(2)}, u32[]{:S(2)}) collective-permute-start(f32[2,6,10,130]{3,2,1,0:T(8,128)S(1)} %pad_maximum_fusion.11), channel_id=1, source_target_pairs={{0,16},{16,0},{1,17},{17,1},{2,18},{18,2},{3,19},{19,3},{4,20},{20... | collective-permute-start | bytes 187208 | tf_op jit(solution)/shard_map/ppermute | solution.py:143
  32.7 0.2 maximum_select_fusion.5
  32.9 0.2 maximum_select_fusion.6
  33.2 0.5 %collective-permute-done.5 = f32[2,6,10,130]{3,2,1,0:T(8,128)S(1)} collective-permute-done((f32[2,6,10,130]{3,2,1,0:T(8,128)S(1)}, f32[2,6,10,130]{3,2,1,0:T(8,128)S(1)}, u32[]{:S(2)}, u32[]{:S(2)}) %collective-permute-start.5) | collective-permute-done | bytes 62432 | tf_op jit(solution)/shard_map/ppermute | solution.py:143
  33.8 0.2 slice_multiply_fusion.3
  34.1 0.1 multiply_add_fusion.19
  34.2 0.1 multiply_add_fusion.18
  34.5 0.1 fusion.222
  35.3 0.4 %collective-permute-start.6 = (f32[2,6,8,128]{3,2,1,0:T(8,128)S(1)}, f32[2,6,8,128]{3,2,1,0:T(8,128)S(1)}, u32[]{:S(2)}, u32[]{:S(2)}) collective-permute-start(f32[2,6,8,128]{3,2,1,0:T(8,128)S(1)} %pad_maximum_fusion.26), channel_id=1, source_target_pairs={{0,16},{16,0},{1,17},{17,1},{2,18},{18,2},{3,19},{19,3},{4,20},{20... | collective-permute-start | bytes 147464 | tf_op jit(solution)/shard_map/ppermute | solution.py:143
  35.8 0.2 slice_multiply_fusion.43
  36.2 0.1 multiply_add_fusion.33
  36.5 0.1 fusion.256
  37.4 0.6 %pad_maximum_fusion.15 = f32[2,8,8,128]{3,2,1,0:T(8,128)} fusion(f32[6,1,8,128]{3,2,1,0:T(8,128)S(1)} %get-tuple-element.218, f32[6,1,8,128]{3,2,1,0:T(8,128)S(1)} %get-tuple-element.217, f32[1,6,8,128]{3,2,1,0:T(8,128)S(1)} %get-tuple-element.105, f32[1,6,8,128]{3,2,1,0:T(8,128)S(1)} %get-tuple-element.104, f32[4,6,8,128]{3,2,1,0:T(8,128)S(1)} %get-tuple-element.3), kind=kLoop, calls=%fused_computation.455 | loop fusion | flops 65536 | bytes 262144 | tf_op jit(solution)/shard_map/slice | solution.py:219
  38.1 0.7 %slice.2530 = f32[4,8,8,128]{3,2,1,0:T(8,128)} slice(f32[6,8,8,128]{3,2,1,0:T(8,128)S(1)} %pad_maximum_fusion.13), slice={[0:4], [0:8], [0:8], [0:128]} | slice | bytes 262144 | tf_op jit(solution)/shard_map/slice | solution.py:219
  (119 shorter events, 6.0 us)
Async XLA Ops:
  0.6 0.8 %copy-start.1 = (f32[2,8,8,128]{3,2,1,0:T(8,128)S(1)}, f32[2,8,8,128]{3,2,1,0:T(8,128)}, u32[]{:S(2)}) copy-start(f32[2,8,8,128]{3,2,1,0:T(8,128)} %param.4) | copy-start | bytes 196612
  1.5 6.2 %collective-permute-start.1 = (f32[3,8,4,128]{3,2,1,0:T(4,128)S(1)}, f32[3,8,4,128]{3,2,1,0:T(4,128)S(1)}, u32[]{:S(2)}, u32[]{:S(2)}) collective-permute-start(f32[3,8,4,128]{3,2,1,0:T(4,128)S(1)} %get-tuple-element.216), channel_id=1, source_target_pairs={{0,12},{4,0},{8,4},{12,8},{1,13},{5,1},{9,5},{13,9},{2,14},{6,2},{... | collective-permute-start | bytes 147464 | tf_op jit(solution)/shard_map/ppermute | solution.py:183
  5.4 5.0 %collective-permute-start = (f32[3,8,4,128]{3,2,1,0:T(4,128)S(1)}, f32[3,8,4,128]{3,2,1,0:T(4,128)S(1)}, u32[]{:S(2)}, u32[]{:S(2)}) collective-permute-start(f32[3,8,4,128]{3,2,1,0:T(4,128)S(1)} %get-tuple-element.215), channel_id=1, source_target_pairs={{0,4},{4,8},{8,12},{12,0},{1,5},{5,9},{9,13},{13,1},{2,6},{6,10},{... | collective-permute-start | bytes 147464 | tf_op jit(solution)/shard_map/ppermute | solution.py:182
  5.7 0.7 %copy-start.3 = (s32[32,3]{0,1:T(4,128)S(1)}, s32[32,3]{0,1:T(4,128)}, u32[]{:S(2)}) copy-start(s32[32,3]{0,1:T(4,128)} %param.5) | copy-start | bytes 1156
  10.6 6.2 %collective-permute-start.2 = (f32[3,4608]{1,0:T(4,128)S(1)}, f32[3,4608]{1,0:T(4,128)S(1)}, u32[]{:S(2)}, u32[]{:S(2)}) collective-permute-start(f32[3,4608]{1,0:T(4,128)S(1)} %reshape.577), channel_id=1, source_target_pairs={{1,0},{2,1},{3,2},{5,4},{6,5},{7,6},{9,8},{10,9},{11,10},{13,12},{... | collective-permute-start | bytes 165896 | tf_op jit(solution)/shard_map/ppermute | solution.py:188
  18.7 2.1 %collective-permute-start.3 = (f32[2,6,14,134]{3,2,1,0:T(8,128)S(1)}, f32[2,6,14,134]{3,2,1,0:T(8,128)S(1)}, u32[]{:S(2)}, u32[]{:S(2)}) collective-permute-start(f32[2,6,14,134]{3,2,1,0:T(8,128)S(1)} %pad_maximum_fusion.8), channel_id=1, source_target_pairs={{0,16},{16,0},{1,17},{17,1},{2,18},{18,2},{3,19},{19,3},{4,20},{20... | collective-permute-start | bytes 270152 | tf_op jit(solution)/shard_map/ppermute | solution.py:143
  24.0 1.1 %copy-start = (f32[6,6,12,132]{3,2,1,0:T(8,128)S(1)}, f32[6,6,12,132]{3,2,1,0:T(8,128)}, u32[]{:S(2)}) copy-start(f32[6,6,12,132]{3,2,1,0:T(8,128)} %constant.165.clone.1) | copy-start | bytes 684292
  25.5 1.6 %collective-permute-start.4 = (f32[2,6,12,132]{3,2,1,0:T(8,128)S(1)}, f32[2,6,12,132]{3,2,1,0:T(8,128)S(1)}, u32[]{:S(2)}, u32[]{:S(2)}) collective-permute-start(f32[2,6,12,132]{3,2,1,0:T(8,128)S(1)} %pad_maximum_fusion.10), channel_id=1, source_target_pairs={{0,16},{16,0},{1,17},{17,1},{2,18},{18,2},{3,19},{19,3},{4,20},{20... | collective-permute-start | bytes 228104 | tf_op jit(solution)/shard_map/ppermute | solution.py:143
  28.1 0.9 %copy-start.2 = (f32[6,2,12,132]{3,2,1,0:T(8,128)S(1)}, f32[6,2,12,132]{3,2,1,0:T(8,128)}, u32[]{:S(2)}) copy-start(f32[6,2,12,132]{3,2,1,0:T(8,128)} %constant.144.clone.1) | copy-start | bytes 228100
  32.3 1.5 %collective-permute-start.5 = (f32[2,6,10,130]{3,2,1,0:T(8,128)S(1)}, f32[2,6,10,130]{3,2,1,0:T(8,128)S(1)}, u32[]{:S(2)}, u32[]{:S(2)}) collective-permute-start(f32[2,6,10,130]{3,2,1,0:T(8,128)S(1)} %pad_maximum_fusion.11), channel_id=1, source_target_pairs={{0,16},{16,0},{1,17},{17,1},{2,18},{18,2},{3,19},{19,3},{4,20},{20... | collective-permute-start | bytes 187208 | tf_op jit(solution)/shard_map/ppermute | solution.py:143
  35.3 1.4 %collective-permute-start.6 = (f32[2,6,8,128]{3,2,1,0:T(8,128)S(1)}, f32[2,6,8,128]{3,2,1,0:T(8,128)S(1)}, u32[]{:S(2)}, u32[]{:S(2)}) collective-permute-start(f32[2,6,8,128]{3,2,1,0:T(8,128)S(1)} %pad_maximum_fusion.26), channel_id=1, source_target_pairs={{0,16},{16,0},{1,17},{17,1},{2,18},{18,2},{3,19},{19,3},{4,20},{20... | collective-permute-start | bytes 147464 | tf_op jit(solution)/shard_map/ppermute | solution.py:143

commit v8 on v5

--- a/solution.py
+++ b/solution.py
@@ -80,14 +80,13 @@
     return values * values * (3.0 - 2.0 * values)
 
 
-def chem_update(fields, side, phi_old, phi_new):
+def chem_update(fields, side, phi_old, phi_new, centre_d, side_d):
     chem = fields[4:]
-    centre_d = DSOL + (DLIQ - DSOL) * fields[0]
-    side_d = [DSOL + (DLIQ - DSOL) * s[0] for s in side]
     side_m = [s[4:] for s in side]
     flux = jnp.zeros_like(chem)
     for way in range(6):
-        flux = flux + 0.5 * (centre_d + side_d[way]) * (side_m[way] - chem)
+        flux = flux + (centre_d + side_d[way]) * (side_m[way] - chem)
+    flux = 0.5 * flux
     delta = shape_fn(phi_new) - shape_fn(phi_old)
     result = []
     for comp in range(2):
@@ -138,7 +137,12 @@
             phase_update(fields, side, zpos, offset, depth),
             fields[:4],
         )
-        mu_new = chem_update(fields, side, fields[:4], phi_new)
+        diffuse = DSOL + (DLIQ - DSOL) * ext[0:1]
+        dlo = DSOL + (DLIQ - DSOL) * xlo[0:1]
+        dhi = DSOL + (DLIQ - DSOL) * xhi[0:1]
+        side_d = [s[0] for s in neighbours(diffuse, dlo, dhi)]
+        centre_d = diffuse[0, :, 1:-1, 1:-1]
+        mu_new = chem_update(fields, side, fields[:4], phi_new, centre_d, side_d)
         return jnp.concatenate([phi_new, mu_new], 0)
 
     def layer_index(ext):

time: 36.2 us -> 38 us (1.050)
  waiting for transfers between devices: 11.1 us -> 12 us
  local copies, waits for them, and re-layouts: 7.06 us -> 7.48 us
  other arithmetic: 10.6 us -> 11 us
    mul x4 -> x8, other arithmetic: 0.16 us -> 1.64 us  [the longest x4 1.02 us: chem_update(): flux = 0.5 * flux]
    ppermute x4, waiting for transfers between devices: 3.59 us -> 4.44 us  [x_halos(): got = lax.ppermute(pair, 'gx', ring('gx', 1))]
    add x4 -> x8, other arithmetic: 1.01 us -> 0.19 us  [the longest x4 0.12 us: step(): dhi = DSOL + (DLIQ - DSOL) * xhi[0:1]]
    slice x4 -> x8, local copies, waits for them, and re-layouts: 1.28 us -> 1.71 us  [neighbours(): fields[:, 1:]]
    add x7 -> x8, other arithmetic: 1.72 us -> 1.46 us  [phase_update(): phi[phase] + DT * (rates[phase] - mean_rate)]
  transfers between devices with their start and end apart: 7 -> 7, of which waited for: 6 -> 6; matrix products, arithmetic and copies ran while one was open for 8% -> 5% of each run, Pallas kernels for 0% -> 0%
where the time goes in v8:
time: 38 us; the launch traced here: 37.8 us
  waiting for transfers between devices  12 us (32%)
  other arithmetic  11 us (29%)
  local copies, waits for them, and re-layouts  7.48 us (20%)
  starting transfers between devices  5.94 us (16%)
  between operations  1.36 us (4%)
    ppermute x1, waiting for transfers between devices, shards(): lax.ppermute(wide[..., :count].reshape(wide.shape[0], -1), 'gz', line('gz...  4.82 us
    ppermute x4, waiting for transfers between devices, x_halos(): got = lax.ppermute(pair, 'gx', ring('gx', 1))  4.44 us
    ppermute x1, starting transfers between devices, shards(): above_y = lax.ppermute(start[:, :, :rim_y], 'gy', ring('gy', -1))  3.95 us
    ppermute x1, waiting for transfers between devices, shards(): below_y = lax.ppermute(start[:, :, -rim_y:], 'gy', ring('gy', 1))  2.76 us
    unnamed x9, local copies, waits for them, and re-layouts  2.67 us
    slice x8, local copies, waits for them, and re-layouts, neighbours(): fields[:, 1:]  1.71 us
    mul x4, other arithmetic, phase_update(): square = phi * phi  1.65 us
    add x8, other arithmetic, phase_update(): phi[phase] + DT * (rates[phase] - mean_rate)  1.46 us
  transfers between devices with their start and end apart: 7, of which 6 were waited for; matrix products, arithmetic and copies ran while one was open for 5% of the time, Pallas kernels for 0%

profile of v8, /device:TPU:0, one launch (start us, length us, event | category | flops | bytes accessed | tf_op | source)
XLA Modules:
  0.0 37.8 jit_solution(14335167371416728390)
XLA Ops:
  0.6 0.8 %fusion.172 = f32[1,8,8,128]{3,1,2,0:T(8,128)S(1)} fusion(s32[8,8,128]{2,1,0:T(8,128)} %param.3), kind=kLoop, calls=%fused_computation.346 | loop fusion | flops 8192 | bytes 65536 | tf_op jit(solution)/shard_map/broadcast_in_dim | solution.py:159
  1.5 3.9 %collective-permute-start.1 = (f32[3,8,4,128]{3,1,2,0:T(8,128)S(1)}, f32[3,8,4,128]{3,1,2,0:T(8,128)S(1)}, u32[]{:S(2)}, u32[]{:S(2)}) collective-permute-start(f32[3,8,4,128]{3,1,2,0:T(8,128)S(1)} %get-tuple-element.125), channel_id=1, source_target_pairs={{0,12},{4,0},{8,4},{12,8},{1,13},{5,1},{9,5},{13,9},{2,14},{6,2},{... | collective-permute-start | bytes 147464 | tf_op jit(solution)/shard_map/ppermute | solution.py:162
  5.7 0.6 %copy-done.2 = s32[32,3]{0,1:T(4,128)S(1)} copy-done((s32[32,3]{0,1:T(4,128)S(1)}, s32[32,3]{0,1:T(4,128)}, u32[]{:S(2)}) %copy-start.2) | copy-done | bytes 408
  7.1 0.2 and_reduce_fusion
  7.2 0.2 and_reduce_fusion.1
  7.4 0.1 and_reduce_fusion.2
  7.7 2.8 %collective-permute-done = f32[3,8,4,128]{3,1,2,0:T(8,128)S(1)} collective-permute-done((f32[3,8,4,128]{3,1,2,0:T(8,128)S(1)}, f32[3,8,4,128]{3,1,2,0:T(8,128)S(1)}, u32[]{:S(2)}, u32[]{:S(2)}) %collective-permute-start) | collective-permute-done | bytes 49184 | tf_op jit(solution)/shard_map/ppermute | solution.py:161
  10.5 0.2 reshape.618
  10.7 1.3 %collective-permute-start.2 = (f32[3,4608]{1,0:T(4,128)S(1)}, f32[3,4608]{1,0:T(4,128)S(1)}, u32[]{:S(2)}, u32[]{:S(2)}) collective-permute-start(f32[3,4608]{1,0:T(4,128)S(1)} %reshape.618), channel_id=1, source_target_pairs={{1,0},{2,1},{3,2},{5,4},{6,5},{7,6},{9,8},{10,9},{11,10},{13,12},{... | collective-permute-start | bytes 165896 | tf_op jit(solution)/shard_map/ppermute | solution.py:167
  12.1 4.8 %collective-permute-done.2 = f32[3,4608]{1,0:T(4,128)S(1)} collective-permute-done((f32[3,4608]{1,0:T(4,128)S(1)}, f32[3,4608]{1,0:T(4,128)S(1)}, u32[]{:S(2)}, u32[]{:S(2)}) %collective-permute-start.2) | collective-permute-done | bytes 55328 | tf_op jit(solution)/shard_map/ppermute | solution.py:167
  16.9 0.2 reshape.619
  17.4 0.1 fusion.24
  17.6 0.3 maximum_select_fusion
  17.9 0.4 %fusion.212 = (f32[6,7,14,134]{3,1,2,0:T(8,128)S(1)}, f32[6,7,14,134]{3,1,2,0:T(8,128)S(1)}) fusion(f32[6,8,16,136]{3,1,2,0:T(8,128)S(1)} %maximum_select_fusion), kind=kLoop, calls=%fused_computation.461 | loop fusion | bytes 1260672 | tf_op jit(solution)/shard_map/slice | solution.py:41
  18.3 0.4 %slice_bitcast_fusion.3 = (f32[1,6,14,134]{3,0,2,1:T(1,128)S(1)}, f32[1,6,14,134]{3,0,2,1:T(1,128)S(1)}) fusion(f32[6,8,16,136]{3,1,2,0:T(8,128)S(1)} %maximum_select_fusion), kind=kLoop, calls=%fused_computation.237 | loop fusion | bytes 180096 | tf_op jit(solution)/shard_map/stack;squeeze | solution.py:30
  18.7 0.2 pad_maximum_fusion.8
  19.1 1.3 %collective-permute-done.3 = f32[2,6,14,134]{3,0,2,1:T(2,128)S(1)} collective-permute-done((f32[2,6,14,134]{3,0,2,1:T(2,128)S(1)}, f32[2,6,14,134]{3,0,2,1:T(2,128)S(1)}, u32[]{:S(2)}, u32[]{:S(2)}) %collective-permute-start.3) | collective-permute-done | bytes 90080 | tf_op jit(solution)/shard_map/ppermute | solution.py:31
  20.4 0.1 slice_bitcast_fusion.1
  20.5 0.5 %slice_multiply_fusion = (f32[4,8,14,134]{3,1,2,0:T(8,128)S(1)}, f32[4,8,14,134]{3,1,2,0:T(8,128)S(1)}) fusion(f32[6,8,16,136]{3,1,2,0:T(8,128)S(1)} %maximum_select_fusion, f32[6,7,14,134]{3,1,2,0:T(8,128)S(1)} %get-tuple-element.59, f32[6,1,14,134]{3,1,2,0:T(1,128)S(1)} %get-tuple-element.91, f32[6,1,14,134]{3,1,2,0:T(1,128)S(1)} %get-tuple-element.90, ...), kind=kLoop, calls=%fused_computation.43 | loop fusion | flops 600320 | bytes 2401280 | tf_op jit(solution)/shard_map/mul | solution.py:63
  21.1 0.2 fusion.92
  21.3 0.3 multiply_add_fusion.3
  21.6 0.2 fusion.93
  21.8 0.2 multiply_add_fusion.2
  22.0 0.2 multiply_subtract_fusion
  22.2 0.3 fusion.27
  22.8 0.2 maximum_select_fusion.1
  23.0 0.4 fusion.213
  23.4 0.4 slice_bitcast_fusion.7
  23.8 0.2 pad_maximum_fusion.11
  24.0 0.2 collective-permute-start.4
  24.3 1.1 %collective-permute-done.4 = f32[2,6,12,132]{3,0,2,1:T(2,128)S(1)} collective-permute-done((f32[2,6,12,132]{3,0,2,1:T(2,128)S(1)}, f32[2,6,12,132]{3,0,2,1:T(2,128)S(1)}, u32[]{:S(2)}, u32[]{:S(2)}) %collective-permute-start.4) | collective-permute-done | bytes 76064 | tf_op jit(solution)/shard_map/ppermute | solution.py:31
  25.5 0.5 %slice_multiply_fusion.1 = (f32[4,8,12,132]{3,1,2,0:T(8,128)S(1)}, f32[4,8,12,132]{3,1,2,0:T(8,128)S(1)}) fusion(f32[6,8,14,134]{3,1,2,0:T(8,128)S(1)} %maximum_select_fusion.1, f32[6,7,12,132]{3,1,2,0:T(8,128)S(1)} %get-tuple-element.67, f32[6,1,12,132]{3,1,2,0:T(1,128)S(1)} %get-tuple-element.95, f32[6,1,12,132]{3,1,2,0:T(1,128)S(1)} %get-tuple-element.94, ...), kind=kLoop, calls=%fused_computation.55 | loop fusion | flops 506880 | bytes 2027520 | tf_op jit(solution)/shard_map/mul | solution.py:63
  26.0 0.2 fusion.113
  26.2 0.3 multiply_add_fusion.7
  26.5 0.2 fusion.114
  26.7 0.1 multiply_add_fusion.6
  26.8 0.2 multiply_subtract_fusion.1
  27.1 0.3 fusion.41
  27.5 0.6 %copy-done.1 = f32[6]{0:T(128)S(1)} copy-done((f32[6]{0:T(128)S(1)}, f32[6]{0:T(128)}, u32[]{:S(2)}) %copy-start.1) | copy-done | bytes 48
  28.4 0.2 slice.1260
  28.6 0.2 maximum_select_fusion.3
  28.8 0.2 maximum_select_fusion.4
  29.1 0.3 fusion.214
  29.4 0.3 slice_bitcast_fusion.11
  29.9 0.2 collective-permute-start.5
  30.2 1.1 %collective-permute-done.5 = f32[2,6,10,130]{3,0,2,1:T(2,128)S(1)} collective-permute-done((f32[2,6,10,130]{3,0,2,1:T(2,128)S(1)}, f32[2,6,10,130]{3,0,2,1:T(2,128)S(1)}, u32[]{:S(2)}, u32[]{:S(2)}) %collective-permute-start.5) | collective-permute-done | bytes 62432 | tf_op jit(solution)/shard_map/ppermute | solution.py:31
  31.4 0.4 %slice_multiply_fusion.2 = (f32[4,8,10,130]{3,1,2,0:T(8,128)S(1)}, f32[4,8,10,130]{3,1,2,0:T(8,128)S(1)}) fusion(f32[6,8,12,132]{3,1,2,0:T(8,128)S(1)} %maximum_select_fusion.4, f32[6,7,10,130]{3,1,2,0:T(8,128)S(1)} %get-tuple-element.76, f32[6,1,10,130]{3,1,2,0:T(1,128)S(1)} %get-tuple-element.107, f32[6,1,10,130]{3,1,2,0:T(1,128)S(1)} %get-tuple-element.106, ...), kind=kLoop, calls=%fused_computation.56 | loop fusion | flops 416000 | bytes 1664000 | tf_op jit(solution)/shard_map/mul | solution.py:63
  31.8 0.1 fusion.134
  31.9 0.2 multiply_add_fusion.11
  32.2 0.2 fusion.135
  32.5 0.2 multiply_subtract_fusion.2
  32.7 0.2 fusion.55
  33.2 0.2 slice.1314
  33.4 0.1 maximum_select_fusion.5
  33.6 0.2 maximum_select_fusion.6
  33.8 0.2 fusion.215
  34.0 0.2 fusion.216
  34.2 0.2 collective-permute-start.6
  34.5 1.0 %collective-permute-done.6 = f32[2,6,8,128]{3,2,1,0:T(8,128)S(1)} collective-permute-done((f32[2,6,8,128]{3,2,1,0:T(8,128)S(1)}, f32[2,6,8,128]{3,2,1,0:T(8,128)S(1)}, u32[]{:S(2)}, u32[]{:S(2)}) %collective-permute-start.6) | collective-permute-done | bytes 49184 | tf_op jit(solution)/shard_map/ppermute | solution.py:31
  35.5 0.2 slice_multiply_fusion.13
  35.8 0.1 multiply_add_fusion.15
  36.1 0.7 %copy.61 = f32[4,8,8,128]{3,2,1,0:T(8,128)} copy(f32[4,8,8,128]{3,1,2,0:T(8,128)S(1)} %get-tuple-element.7) | data formatting | bytes 262144
  36.9 0.1 fusion.141
  37.2 0.6 %copy.62 = f32[2,8,8,128]{3,2,1,0:T(8,128)} copy(f32[2,8,8,128]{3,1,2,0:T(8,128)S(1)} %pad_maximum_fusion.16) | data formatting | bytes 131072
  (83 shorter events, 4.0 us)
Async XLA Ops:
  0.6 0.8 %copy-start = (f32[2,8,8,128]{3,2,1,0:T(8,128)S(1)}, f32[2,8,8,128]{3,2,1,0:T(8,128)}, u32[]{:S(2)}) copy-start(f32[2,8,8,128]{3,2,1,0:T(8,128)} %param.4) | copy-start | bytes 196612
  1.5 6.2 %collective-permute-start.1 = (f32[3,8,4,128]{3,1,2,0:T(8,128)S(1)}, f32[3,8,4,128]{3,1,2,0:T(8,128)S(1)}, u32[]{:S(2)}, u32[]{:S(2)}) collective-permute-start(f32[3,8,4,128]{3,1,2,0:T(8,128)S(1)} %get-tuple-element.125), channel_id=1, source_target_pairs={{0,12},{4,0},{8,4},{12,8},{1,13},{5,1},{9,5},{13,9},{2,14},{6,2},{... | collective-permute-start | bytes 147464 | tf_op jit(solution)/shard_map/ppermute | solution.py:162
  5.5 5.0 %collective-permute-start = (f32[3,8,4,128]{3,1,2,0:T(8,128)S(1)}, f32[3,8,4,128]{3,1,2,0:T(8,128)S(1)}, u32[]{:S(2)}, u32[]{:S(2)}) collective-permute-start(f32[3,8,4,128]{3,1,2,0:T(8,128)S(1)} %get-tuple-element.124), channel_id=1, source_target_pairs={{0,4},{4,8},{8,12},{12,0},{1,5},{5,9},{9,13},{13,1},{2,6},{6,10},{... | collective-permute-start | bytes 147464 | tf_op jit(solution)/shard_map/ppermute | solution.py:161
  5.7 0.7 %copy-start.2 = (s32[32,3]{0,1:T(4,128)S(1)}, s32[32,3]{0,1:T(4,128)}, u32[]{:S(2)}) copy-start(s32[32,3]{0,1:T(4,128)} %param.5) | copy-start | bytes 1156
  10.7 6.2 %collective-permute-start.2 = (f32[3,4608]{1,0:T(4,128)S(1)}, f32[3,4608]{1,0:T(4,128)S(1)}, u32[]{:S(2)}, u32[]{:S(2)}) collective-permute-start(f32[3,4608]{1,0:T(4,128)S(1)} %reshape.618), channel_id=1, source_target_pairs={{1,0},{2,1},{3,2},{5,4},{6,5},{7,6},{9,8},{10,9},{11,10},{13,12},{... | collective-permute-start | bytes 165896 | tf_op jit(solution)/shard_map/ppermute | solution.py:167
  18.9 1.5 %collective-permute-start.3 = (f32[2,6,14,134]{3,0,2,1:T(2,128)S(1)}, f32[2,6,14,134]{3,0,2,1:T(2,128)S(1)}, u32[]{:S(2)}, u32[]{:S(2)}) collective-permute-start(f32[2,6,14,134]{3,0,2,1:T(2,128)S(1)} %pad_maximum_fusion.8), channel_id=1, source_target_pairs={{0,16},{16,0},{1,17},{17,1},{2,18},{18,2},{3,19},{19,3},{4,20},{20... | collective-permute-start | bytes 270152 | tf_op jit(solution)/shard_map/ppermute | solution.py:31
  24.0 1.4 %collective-permute-start.4 = (f32[2,6,12,132]{3,0,2,1:T(2,128)S(1)}, f32[2,6,12,132]{3,0,2,1:T(2,128)S(1)}, u32[]{:S(2)}, u32[]{:S(2)}) collective-permute-start(f32[2,6,12,132]{3,0,2,1:T(2,128)S(1)} %pad_maximum_fusion.11), channel_id=1, source_target_pairs={{0,16},{16,0},{1,17},{17,1},{2,18},{18,2},{3,19},{19,3},{4,20},{20... | collective-permute-start | bytes 228104 | tf_op jit(solution)/shard_map/ppermute | solution.py:31
  27.5 0.7 %copy-start.1 = (f32[6]{0:T(128)S(1)}, f32[6]{0:T(128)}, u32[]{:S(2)}) copy-start(f32[6]{0:T(128)} %constant.123.clone.1) | copy-start | bytes 76
  29.9 1.4 %collective-permute-start.5 = (f32[2,6,10,130]{3,0,2,1:T(2,128)S(1)}, f32[2,6,10,130]{3,0,2,1:T(2,128)S(1)}, u32[]{:S(2)}, u32[]{:S(2)}) collective-permute-start(f32[2,6,10,130]{3,0,2,1:T(2,128)S(1)} %pad_maximum_fusion.13), channel_id=1, source_target_pairs={{0,16},{16,0},{1,17},{17,1},{2,18},{18,2},{3,19},{19,3},{4,20},{20... | collective-permute-start | bytes 187208 | tf_op jit(solution)/shard_map/ppermute | solution.py:31
  34.2 1.3 %collective-permute-start.6 = (f32[2,6,8,128]{3,2,1,0:T(8,128)S(1)}, f32[2,6,8,128]{3,2,1,0:T(8,128)S(1)}, u32[]{:S(2)}, u32[]{:S(2)}) collective-permute-start(f32[2,6,8,128]{3,2,1,0:T(8,128)S(1)} %pad_maximum_fusion.18), channel_id=1, source_target_pairs={{0,16},{16,0},{1,17},{17,1},{2,18},{18,2},{3,19},{19,3},{4,20},{20... | collective-permute-start | bytes 147464 | tf_op jit(solution)/shard_map/ppermute | solution.py:31

commit v9 on v5

--- a/solution.py
+++ b/solution.py
@@ -145,12 +145,10 @@
         return lax.broadcasted_iota(jnp.int32, ext.shape, 3)
 
     def edge_at(ext, at, cond):
-        up = jnp.concatenate([ext[..., :1], ext[..., :-1]], 3)
-        return jnp.where(cond & (layer_index(ext) == at), up, ext)
+        return ext.at[..., at].set(jnp.where(cond, ext[..., at - 1], ext[..., at]))
 
     def edge_below(ext, at, cond):
-        down = jnp.concatenate([ext[..., 1:], ext[..., -1:]], 3)
-        return jnp.where(cond & (layer_index(ext) == at), down, ext)
+        return ext.at[..., at].set(jnp.where(cond, ext[..., at + 1], ext[..., at]))
 
     start = jnp.concatenate([labels.astype(jnp.float32)[None], mu_start], 0)
     nf = 4 + mu_start.shape[0]
@@ -172,7 +170,8 @@
     liquid = jnp.concatenate(
         [jnp.ones((1,) + ext.shape[1:], jnp.float32), jnp.zeros((nf - 1,) + ext.shape[1:], jnp.float32)], 0
     )
-    ext = jnp.where(top_brick & (layer_index(ext) >= cells_z - lift + 2), liquid, ext)
+    cut = cells_z - lift + 2
+    ext = ext.at[..., cut:].set(jnp.where(top_brick, liquid[..., cut:], ext[..., cut:]))
     ext = edge_below(ext, 1, bottom_brick)
     ext = edge_at(ext, cells_z + 2, top_brick)
     ext = step(ext, 3 - rim_y, -1, lift)

time: 36.2 us -> 80.1 us (2.21)
  local copies, waits for them, and re-layouts: 7.06 us -> 50.8 us
    scatter x0 -> x7, local copies, waits for them, and re-layouts: none -> 44.5 us  [the longest x4 28.2 us: edge_at(): return ext.at[..., at].set(jnp.where(cond, ext[..., at - 1], ext[..., at]))]
  transfers between devices with their start and end apart: 7 -> 7, of which waited for: 6 -> 6; matrix products, arithmetic and copies ran while one was open for 8% -> 4% of each run, Pallas kernels for 0% -> 0%
where the time goes in v9:
time: 80.1 us; the launch traced here: 79.8 us
  local copies, waits for them, and re-layouts  50.8 us (63%)
  waiting for transfers between devices  11.2 us (14%)
  other arithmetic  10.7 us (13%)
  starting transfers between devices  5.94 us (7%)
  between operations  1.25 us (2%)
    scatter x4, local copies, waits for them, and re-layouts, edge_at(): return ext.at[..., at].set(jnp.where(cond, ext[..., at - 1], ext[..., at]))  28.2 us
    scatter x1, local copies, waits for them, and re-layouts, shards(): ext.at[..., cut:]  10.6 us
    scatter x2, local copies, waits for them, and re-layouts, edge_below(): return ext.at[..., at].set(jnp.where(cond, ext[..., at + 1], ext[..., at]))  5.77 us
    ppermute x1, waiting for transfers between devices, shards(): lax.ppermute(wide[..., :count].reshape(wide.shape[0], -1), 'gz', line('gz...  4.81 us
    ppermute x1, starting transfers between devices, shards(): above_y = lax.ppermute(start[:, :, :rim_y], 'gy', ring('gy', -1))  3.95 us
    ppermute x4, waiting for transfers between devices, x_halos(): got = lax.ppermute(pair, 'gx', ring('gx', 1))  3.6 us
    ppermute x1, waiting for transfers between devices, shards(): below_y = lax.ppermute(start[:, :, -rim_y:], 'gy', ring('gy', 1))  2.8 us
    unnamed x9, local copies, waits for them, and re-layouts  2.61 us
  transfers between devices with their start and end apart: 7, of which 6 were waited for; matrix products, arithmetic and copies ran while one was open for 4% of the time, Pallas kernels for 0%

profile of v9, /device:TPU:0, one launch (start us, length us, event | category | flops | bytes accessed | tf_op | source)
XLA Modules:
  0.0 79.8 jit_solution(4303392568187387999)
XLA Ops:
  0.6 0.8 fusion.252
  1.5 3.9 %collective-permute-start.1 = (f32[3,8,4,128]{3,1,2,0:T(8,128)S(1)}, f32[3,8,4,128]{3,1,2,0:T(8,128)S(1)}, u32[]{:S(2)}, u32[]{:S(2)}) collective-permute-start(f32[3,8,4,128]{3,1,2,0:T(8,128)S(1)} %get-tuple-element.206), channel_id=1, source_target_pairs={{0,12},{4,0},{8,4},{12,8},{1,13},{5,1},{9,5},{13,9},{2,14},{6,2},{... | collective-permute-start | bytes 147464 | tf_op jit(solution)/shard_map/ppermute | solution.py:156
  5.7 0.6 copy-done.2
  7.0 0.2 and_reduce_fusion
  7.2 0.2 and_reduce_fusion.1
  7.4 0.1 and_reduce_fusion.2
  7.6 2.8 %collective-permute-done = f32[3,8,4,128]{3,1,2,0:T(8,128)S(1)} collective-permute-done((f32[3,8,4,128]{3,1,2,0:T(8,128)S(1)}, f32[3,8,4,128]{3,1,2,0:T(8,128)S(1)}, u32[]{:S(2)}, u32[]{:S(2)}) %collective-permute-start) | collective-permute-done | bytes 49184 | tf_op jit(solution)/shard_map/ppermute | solution.py:155
  10.5 0.2 reshape.808
  10.7 1.3 %collective-permute-start.2 = (f32[3,4608]{1,0:T(4,128)S(1)}, f32[3,4608]{1,0:T(4,128)S(1)}, u32[]{:S(2)}, u32[]{:S(2)}) collective-permute-start(f32[3,4608]{1,0:T(4,128)S(1)} %reshape.808), channel_id=1, source_target_pairs={{1,0},{2,1},{3,2},{5,4},{6,5},{7,6},{9,8},{10,9},{11,10},{13,12},{... | collective-permute-start | bytes 165896 | tf_op jit(solution)/shard_map/ppermute | solution.py:161
  12.1 4.8 %collective-permute-done.2 = f32[3,4608]{1,0:T(4,128)S(1)} collective-permute-done((f32[3,4608]{1,0:T(4,128)S(1)}, f32[3,4608]{1,0:T(4,128)S(1)}, u32[]{:S(2)}, u32[]{:S(2)}) %collective-permute-start.2) | collective-permute-done | bytes 55328 | tf_op jit(solution)/shard_map/ppermute | solution.py:161
  16.9 0.2 reshape.809
  17.4 0.1 fusion.24
  17.6 0.3 slice_select_fusion
  17.8 9.8 %scatter.24 = f32[6,8,16,136]{3,1,2,0:T(8,128)S(1)} dynamic-update-slice(f32[6,8,16,136]{3,1,2,0:T(8,128)S(1)} %fusion.24, f32[6,8,16,1]{3,1,2,0:T(8,128)S(1)} %slice_select_fusion, s32[]{:T(128)} %constant.421.clone.1, s32[]{:T(128)} %constant.421.clone.1, s32[]{:T(128)} %constant.421.clone.1, s32[]{:T(128)} %constant.436.clone.1) | dynamic-update-slice | bytes 6148 | tf_op jit(solution)/shard_map/scatter | solution.py:148
  27.6 0.4 slice_bitcast_fusion.3
  28.0 0.2 pad_maximum_fusion.9
  28.3 0.4 fusion.278
  28.7 1.0 %collective-permute-done.3 = f32[2,6,14,134]{3,0,2,1:T(2,128)S(1)} collective-permute-done((f32[2,6,14,134]{3,0,2,1:T(2,128)S(1)}, f32[2,6,14,134]{3,0,2,1:T(2,128)S(1)}, u32[]{:S(2)}, u32[]{:S(2)}) %collective-permute-start.3) | collective-permute-done | bytes 90080 | tf_op jit(solution)/shard_map/ppermute | solution.py:31
  29.8 0.6 slice_multiply_fusion
  30.4 0.2 fusion.111
  30.5 0.3 multiply_add_fusion.4
  30.9 0.3 multiply_add_fusion.3
  31.2 0.2 multiply_subtract_fusion
  31.4 0.3 fusion.26
  31.9 0.2 slice_select_fusion.1
  32.2 8.8 %scatter.25 = f32[6,8,14,134]{3,1,2,0:T(8,128)S(1)} dynamic-update-slice(f32[6,8,14,134]{3,1,2,0:T(8,128)S(1)} %pad_maximum_fusion, f32[6,8,14,1]{3,1,2,0:T(8,128)S(1)} %slice_select_fusion.1, s32[]{:T(128)} %constant.421.clone.1, s32[]{:T(128)} %constant.421.clone.1, s32[]{:T(128)} %constant.421.clone.1, s32[]{:T(128)} %constant.447.clone.1) | dynamic-update-slice | bytes 5380 | tf_op jit(solution)/shard_map/scatter | solution.py:148
  41.0 0.4 slice_bitcast_fusion.7
  41.4 0.2 pad_maximum_fusion.12
  41.5 0.2 collective-permute-start.4
  41.7 0.4 fusion.279
  42.1 0.9 %collective-permute-done.4 = f32[2,6,12,132]{3,0,2,1:T(2,128)S(1)} collective-permute-done((f32[2,6,12,132]{3,0,2,1:T(2,128)S(1)}, f32[2,6,12,132]{3,0,2,1:T(2,128)S(1)}, u32[]{:S(2)}, u32[]{:S(2)}) %collective-permute-start.4) | collective-permute-done | bytes 76064 | tf_op jit(solution)/shard_map/ppermute | solution.py:31
  43.1 0.5 slice_multiply_fusion.1
  43.6 0.1 fusion.153
  43.7 0.3 multiply_add_fusion.9
  44.0 0.3 multiply_add_fusion.8
  44.3 0.2 multiply_subtract_fusion.1
  44.5 0.3 fusion.39
  45.0 0.6 copy-done.1
  45.6 0.1 slice_select_fusion.4
  45.7 10.6 %scatter.26 = f32[6,8,12,132]{3,1,2,0:T(8,128)S(1)} dynamic-update-slice(f32[6,8,12,132]{3,1,2,0:T(8,128)S(1)} %pad_maximum_fusion.1, f32[6,8,12,34]{3,1,2,0:T(8,128)S(1)} %slice_select_fusion.4, s32[]{:T(128)} %constant.421.clone.1, s32[]{:T(128)} %constant.421.clone.1, s32[]{:T(128)} %constant.421.clone.1, s32[]{:T(128)} %constant.449.clone.1) | dynamic-update-slice | bytes 156676 | tf_op jit(solution)/shard_map/scatter | solution.py:174
  56.3 0.2 slice_select_fusion.3
  56.5 5.4 %scatter.29 = f32[6,8,12,132]{3,1,2,0:T(8,128)S(1)} dynamic-update-slice(f32[6,8,12,132]{3,1,2,0:T(8,128)S(1)} %scatter.26, f32[6,8,12,1]{3,1,2,0:T(8,128)S(1)} %slice_select_fusion.3, s32[]{:T(128)} %constant.421.clone.1, s32[]{:T(128)} %constant.421.clone.1, s32[]{:T(128)} %constant.421.clone.1, s32[]{:T(128)} %constant.419.clone.1) | dynamic-update-slice | bytes 4612 | tf_op jit(solution)/shard_map/scatter | solution.py:151
  62.0 0.2 slice_select_fusion.2
  62.2 5.2 %scatter.30 = f32[6,8,12,132]{3,1,2,0:T(8,128)S(1)} dynamic-update-slice(f32[6,8,12,132]{3,1,2,0:T(8,128)S(1)} %scatter.29, f32[6,8,12,1]{3,1,2,0:T(8,128)S(1)} %slice_select_fusion.2, s32[]{:T(128)} %constant.421.clone.1, s32[]{:T(128)} %constant.421.clone.1, s32[]{:T(128)} %constant.421.clone.1, s32[]{:T(128)} %constant.450.clone.1) | dynamic-update-slice | bytes 4612 | tf_op jit(solution)/shard_map/scatter | solution.py:148
  67.5 0.3 slice_bitcast_fusion.11
  67.9 0.2 collective-permute-start.5
  68.1 0.3 fusion.280
  68.4 0.9 %collective-permute-done.5 = f32[2,6,10,130]{3,0,2,1:T(2,128)S(1)} collective-permute-done((f32[2,6,10,130]{3,0,2,1:T(2,128)S(1)}, f32[2,6,10,130]{3,0,2,1:T(2,128)S(1)}, u32[]{:S(2)}, u32[]{:S(2)}) %collective-permute-start.5) | collective-permute-done | bytes 62432 | tf_op jit(solution)/shard_map/ppermute | solution.py:31
  69.4 0.4 slice_multiply_fusion.2
  69.8 0.1 fusion.195
  70.0 0.2 multiply_add_fusion.14
  70.2 0.2 multiply_add_fusion.13
  70.4 0.2 multiply_subtract_fusion.2
  70.6 0.2 fusion.52
  71.2 0.3 scatter.31
  71.7 4.4 %scatter.34 = f32[6,8,10,130]{3,1,2,0:T(8,128)S(1)} dynamic-update-slice(f32[6,8,10,130]{3,1,2,0:T(8,128)S(1)} %scatter.31, f32[6,8,10,1]{3,1,2,0:T(8,128)S(1)} %slice_select_fusion.5, s32[]{:T(128)} %constant.421.clone.1, s32[]{:T(128)} %constant.421.clone.1, s32[]{:T(128)} %constant.421.clone.1, s32[]{:T(128)} %constant.452.clone.1) | dynamic-update-slice | bytes 3844 | tf_op jit(solution)/shard_map/scatter | solution.py:148
  76.1 0.2 fusion.281
  76.3 0.2 collective-permute-start.6
  76.5 0.2 fusion.282
  76.6 0.9 %collective-permute-done.6 = f32[2,6,8,128]{3,2,1,0:T(8,128)S(1)} collective-permute-done((f32[2,6,8,128]{3,2,1,0:T(8,128)S(1)}, f32[2,6,8,128]{3,2,1,0:T(8,128)S(1)}, u32[]{:S(2)}, u32[]{:S(2)}) %collective-permute-start.6) | collective-permute-done | bytes 49184 | tf_op jit(solution)/shard_map/ppermute | solution.py:31
  77.6 0.2 slice_multiply_fusion.15
  78.3 0.7 copy.45
  79.0 0.1 fusion.199
  79.2 0.6 copy.46
  (64 shorter events, 3.3 us)
Async XLA Ops:
  0.6 0.8 %copy-start = (f32[2,8,8,128]{3,2,1,0:T(8,128)S(1)}, f32[2,8,8,128]{3,2,1,0:T(8,128)}, u32[]{:S(2)}) copy-start(f32[2,8,8,128]{3,2,1,0:T(8,128)} %param.18) | copy-start | bytes 196612
  1.5 6.1 %collective-permute-start.1 = (f32[3,8,4,128]{3,1,2,0:T(8,128)S(1)}, f32[3,8,4,128]{3,1,2,0:T(8,128)S(1)}, u32[]{:S(2)}, u32[]{:S(2)}) collective-permute-start(f32[3,8,4,128]{3,1,2,0:T(8,128)S(1)} %get-tuple-element.206), channel_id=1, source_target_pairs={{0,12},{4,0},{8,4},{12,8},{1,13},{5,1},{9,5},{13,9},{2,14},{6,2},{... | collective-permute-start | bytes 147464 | tf_op jit(solution)/shard_map/ppermute | solution.py:156
  5.5 5.0 %collective-permute-start = (f32[3,8,4,128]{3,1,2,0:T(8,128)S(1)}, f32[3,8,4,128]{3,1,2,0:T(8,128)S(1)}, u32[]{:S(2)}, u32[]{:S(2)}) collective-permute-start(f32[3,8,4,128]{3,1,2,0:T(8,128)S(1)} %get-tuple-element.205), channel_id=1, source_target_pairs={{0,4},{4,8},{8,12},{12,0},{1,5},{5,9},{9,13},{13,1},{2,6},{6,10},{... | collective-permute-start | bytes 147464 | tf_op jit(solution)/shard_map/ppermute | solution.py:155
  5.6 0.7 copy-start.2
  10.7 6.2 %collective-permute-start.2 = (f32[3,4608]{1,0:T(4,128)S(1)}, f32[3,4608]{1,0:T(4,128)S(1)}, u32[]{:S(2)}, u32[]{:S(2)}) collective-permute-start(f32[3,4608]{1,0:T(4,128)S(1)} %reshape.808), channel_id=1, source_target_pairs={{1,0},{2,1},{3,2},{5,4},{6,5},{7,6},{9,8},{10,9},{11,10},{13,12},{... | collective-permute-start | bytes 165896 | tf_op jit(solution)/shard_map/ppermute | solution.py:161
  28.2 1.5 %collective-permute-start.3 = (f32[2,6,14,134]{3,0,2,1:T(2,128)S(1)}, f32[2,6,14,134]{3,0,2,1:T(2,128)S(1)}, u32[]{:S(2)}, u32[]{:S(2)}) collective-permute-start(f32[2,6,14,134]{3,0,2,1:T(2,128)S(1)} %pad_maximum_fusion.9), channel_id=1, source_target_pairs={{0,16},{16,0},{1,17},{17,1},{2,18},{18,2},{3,19},{19,3},{4,20},{20... | collective-permute-start | bytes 270152 | tf_op jit(solution)/shard_map/ppermute | solution.py:31
  41.5 1.4 %collective-permute-start.4 = (f32[2,6,12,132]{3,0,2,1:T(2,128)S(1)}, f32[2,6,12,132]{3,0,2,1:T(2,128)S(1)}, u32[]{:S(2)}, u32[]{:S(2)}) collective-permute-start(f32[2,6,12,132]{3,0,2,1:T(2,128)S(1)} %pad_maximum_fusion.12), channel_id=1, source_target_pairs={{0,16},{16,0},{1,17},{17,1},{2,18},{18,2},{3,19},{19,3},{4,20},{20... | collective-permute-start | bytes 228104 | tf_op jit(solution)/shard_map/ppermute | solution.py:31
  44.9 0.7 copy-start.1
  67.9 1.4 %collective-permute-start.5 = (f32[2,6,10,130]{3,0,2,1:T(2,128)S(1)}, f32[2,6,10,130]{3,0,2,1:T(2,128)S(1)}, u32[]{:S(2)}, u32[]{:S(2)}) collective-permute-start(f32[2,6,10,130]{3,0,2,1:T(2,128)S(1)} %pad_maximum_fusion.14), channel_id=1, source_target_pairs={{0,16},{16,0},{1,17},{17,1},{2,18},{18,2},{3,19},{19,3},{4,20},{20... | collective-permute-start | bytes 187208 | tf_op jit(solution)/shard_map/ppermute | solution.py:31
  76.3 1.3 %collective-permute-start.6 = (f32[2,6,8,128]{3,2,1,0:T(8,128)S(1)}, f32[2,6,8,128]{3,2,1,0:T(8,128)S(1)}, u32[]{:S(2)}, u32[]{:S(2)}) collective-permute-start(f32[2,6,8,128]{3,2,1,0:T(8,128)S(1)} %pad_maximum_fusion.19), channel_id=1, source_target_pairs={{0,16},{16,0},{1,17},{17,1},{2,18},{18,2},{3,19},{19,3},{4,20},{20... | collective-permute-start | bytes 147464 | tf_op jit(solution)/shard_map/ppermute | solution.py:31

commit v10 on v9

--- a/solution.py
+++ b/solution.py
@@ -35,15 +35,16 @@
     return xlo, xhi
 
 
-def neighbours(ext, xlo, xhi):
-    fields = ext[:, :, 1:-1, 1:-1]
+def neighbours(ext, xlo, xhi, stride):
+    size = ext.shape[2] - 2 * stride
+    fields = ext[..., stride : stride + size]
     return [
         jnp.concatenate([fields[:, 1:], xhi[:, None]], 1),
         jnp.concatenate([xlo[:, None], fields[:, :-1]], 1),
-        ext[:, :, 2:, 1:-1],
-        ext[:, :, :-2, 1:-1],
-        ext[:, :, 1:-1, 2:],
-        ext[:, :, 1:-1, :-2],
+        ext[..., 2 * stride :],
+        ext[..., :size],
+        ext[..., stride + 1 : stride + 1 + size],
+        ext[..., stride - 1 : stride - 1 + size],
     ]
 
 
@@ -127,28 +128,39 @@
         )
         return jnp.any(hits, 0)
 
-    def step(ext, first_y, first_z, offset):
-        fields = ext[:, :, 1:-1, 1:-1]
-        ypos = first_y + jnp.arange(fields.shape[2], dtype=jnp.int32)
-        zpos = base_z + first_z + jnp.arange(fields.shape[3], dtype=jnp.int32)
+    low = lift - 4
+    count = lift + 4
+    stride = cells_z - low + count
+    lane_z = jnp.arange(stride, dtype=jnp.int32)
+    under_z = base_z + low + lane_z
+
+    def step(ext, first_y, zpos, offset):
+        size = ext.shape[2] - 2 * stride
+        fields = ext[..., stride : stride + size]
+        nrows = size // stride
+        ypos = first_y + jnp.arange(nrows, dtype=jnp.int32)
         xlo, xhi = x_halos(fields)
-        side = neighbours(ext, xlo, xhi)
+        side = neighbours(ext, xlo, xhi, stride)
+        on = active(ypos, zpos).reshape(-1)
+        zflat = jnp.tile(under_z, nrows)
         phi_new = jnp.where(
-            active(ypos, zpos)[None, None],
-            phase_update(fields, side, zpos, offset, depth),
+            on[None, None],
+            phase_update(fields, side, zflat, 0, depth),
             fields[:4],
         )
         mu_new = chem_update(fields, side, fields[:4], phi_new)
         return jnp.concatenate([phi_new, mu_new], 0)
 
-    def layer_index(ext):
-        return lax.broadcasted_iota(jnp.int32, ext.shape, 3)
+    def lane_index(ext):
+        return lax.broadcasted_iota(jnp.int32, ext.shape, 2) % stride
 
     def edge_at(ext, at, cond):
-        return ext.at[..., at].set(jnp.where(cond, ext[..., at - 1], ext[..., at]))
+        up = jnp.concatenate([ext[..., :1], ext[..., :-1]], 2)
+        return jnp.where(cond & (lane_index(ext) == at), up, ext)
 
     def edge_below(ext, at, cond):
-        return ext.at[..., at].set(jnp.where(cond, ext[..., at + 1], ext[..., at]))
+        down = jnp.concatenate([ext[..., 1:], ext[..., -1:]], 2)
+        return jnp.where(cond & (lane_index(ext) == at), down, ext)
 
     start = jnp.concatenate([labels.astype(jnp.float32)[None], mu_start], 0)
     nf = 4 + mu_start.shape[0]
@@ -156,28 +168,30 @@
     above_y = lax.ppermute(start[:, :, :rim_y], "gy", ring("gy", -1))
     wide = jnp.concatenate([below_y, start, above_y], 2)
 
-    low = lift - 4
-    count = lift + 4
     above = lax.ppermute(wide[..., :count].reshape(wide.shape[0], -1), "gz", line("gz", -1))
     ext = jnp.concatenate([wide[..., low:], above.reshape(wide.shape[:3] + (count,))], 3)
     ext = jnp.concatenate(
         [jnp.stack([(ext[0] == phase).astype(jnp.float32) for phase in range(4)]), ext[1:]], 0
     )
+    rows = ext.shape[2]
+    ext = ext.reshape(ext.shape[0], ext.shape[1], rows * stride)
+    pre_z = base_z + low + lane_z
+    post_z = pre_z - lift
     ext = edge_at(ext, cells_z - low, top_brick)
-    ext = step(ext, 1 - rim_y, low + 1, 0)
-    ext = edge_at(ext, cells_z - low - 1, top_brick)
-    ext = step(ext, 2 - rim_y, low + 2, 0)
+    ext = step(ext, 1 - rim_y, pre_z, 0)
+    ext = edge_at(ext, cells_z - low, top_brick)
+    ext = step(ext, 2 - rim_y, pre_z, 0)
     liquid = jnp.concatenate(
         [jnp.ones((1,) + ext.shape[1:], jnp.float32), jnp.zeros((nf - 1,) + ext.shape[1:], jnp.float32)], 0
     )
-    cut = cells_z - lift + 2
-    ext = ext.at[..., cut:].set(jnp.where(top_brick, liquid[..., cut:], ext[..., cut:]))
-    ext = edge_below(ext, 1, bottom_brick)
-    ext = edge_at(ext, cells_z + 2, top_brick)
-    ext = step(ext, 3 - rim_y, -1, lift)
-    ext = edge_below(ext, 0, bottom_brick)
-    ext = edge_at(ext, cells_z + 1, top_brick)
-    fields = step(ext, 4 - rim_y, 0, lift)
+    ext = jnp.where(top_brick & (lane_index(ext) >= cells_z - low), liquid, ext)
+    ext = edge_below(ext, lift - low - 1, bottom_brick)
+    ext = edge_at(ext, cells_z + lift - low, top_brick)
+    ext = step(ext, 3 - rim_y, post_z, lift)
+    ext = edge_below(ext, lift - low - 1, bottom_brick)
+    ext = edge_at(ext, cells_z + lift - low, top_brick)
+    fields = step(ext, 4 - rim_y, post_z, lift)
+    fields = fields.reshape(nf, cells_x, cells_y, stride)[..., lift - low : lift - low + cells_z]
     return (fields[:4], fields[4:])
 
 

time: 80.1 us -> 33.9 us (0.42)
  local copies, waits for them, and re-layouts: 50.8 us -> 7.28 us
  other arithmetic: 10.7 us -> 8.81 us
  waiting for transfers between devices: 11.2 us -> 10.3 us
    scatter x7 -> x0, local copies, waits for them, and re-layouts: 44.5 us -> none  [the longest x4 28.2 us: edge_at(): return ext.at[..., at].set(jnp.where(cond, ext[..., at - 1], ext[..., at]))]
    ppermute x1, waiting for transfers between devices: 4.81 us -> 3.55 us  [shards(): lax.ppermute(wide[..., :count].reshape(wide.shape[0], -1), 'gz', line('gz...]
    unnamed x9 -> x10, local copies, waits for them, and re-layouts: 2.61 us -> 1.37 us
    concatenate x0 -> x9, local copies, waits for them, and re-layouts: none -> 1.02 us  [the longest x6 0.66 us: shards(): jnp.concatenate([jnp.stack([(ext[0] == phase).astype(jnp.float32) for pha...]
    slice x3 -> x9, local copies, waits for them, and re-layouts: 0.21 us -> 1.19 us  [the longest x1 0.76 us: shards(): return (fields[:4], fields[4:])]
  transfers between devices with their start and end apart: 7 -> 7, of which waited for: 6 -> 6; matrix products, arithmetic and copies ran while one was open for 4% -> 10% of each run, Pallas kernels for 0% -> 0%
where the time goes in v10:
time: 33.9 us; the launch traced here: 33.7 us
  waiting for transfers between devices  10.3 us (30%)
  other arithmetic  8.81 us (26%)
  local copies, waits for them, and re-layouts  7.28 us (21%)
  starting transfers between devices  5.97 us (18%)
  between operations  1.38 us (4%)
    ppermute x1, starting transfers between devices, shards(): above_y = lax.ppermute(start[:, :, :rim_y], 'gy', ring('gy', -1))  3.95 us
    ppermute x4, waiting for transfers between devices, x_halos(): got = lax.ppermute(pair, 'gx', ring('gx', 1))  3.7 us
    ppermute x1, waiting for transfers between devices, shards(): lax.ppermute(wide[..., :count].reshape(wide.shape[0], -1), 'gz', line('gz...  3.55 us
    ppermute x1, waiting for transfers between devices, shards(): below_y = lax.ppermute(start[:, :, -rim_y:], 'gy', ring('gy', 1))  3.02 us
    unnamed x10, local copies, waits for them, and re-layouts  1.37 us
    ppermute x1, starting transfers between devices, shards(): lax.ppermute(wide[..., :count].reshape(wide.shape[0], -1), 'gz', line('gz...  1.29 us
    add x7, other arithmetic, phase_update(): phi[phase] + DT * (rates[phase] - mean_rate)  1.21 us
    mul x4, other arithmetic, phase_update(): square = phi * phi  1.11 us
  transfers between devices with their start and end apart: 7, of which 6 were waited for; matrix products, arithmetic and copies ran while one was open for 10% of the time, Pallas kernels for 0%

profile of v10, /device:TPU:0, one launch (start us, length us, event | category | flops | bytes accessed | tf_op | source)
XLA Modules:
  0.0 33.7 jit_solution(4667131241459320236)
XLA Ops:
  0.6 0.8 %convert_bitcast_fusion = f32[1,8,8,128]{3,2,1,0:T(8,128)S(1)} fusion(s32[8,8,128]{2,1,0:T(8,128)} %param.3), kind=kLoop, calls=%fused_computation.455 | loop fusion | flops 8192 | bytes 65536 | tf_op jit(solution)/shard_map/broadcast_in_dim | solution.py:165
  1.5 3.9 %collective-permute-start.1 = (f32[3,8,4,128]{3,2,1,0:T(4,128)S(1)}, f32[3,8,4,128]{3,2,1,0:T(4,128)S(1)}, u32[]{:S(2)}, u32[]{:S(2)}) collective-permute-start(f32[3,8,4,128]{3,2,1,0:T(4,128)S(1)} %get-tuple-element.115), channel_id=1, source_target_pairs={{0,12},{4,0},{8,4},{12,8},{1,13},{5,1},{9,5},{13,9},{2,14},{6,2},{... | collective-permute-start | bytes 147464 | tf_op jit(solution)/shard_map/ppermute | solution.py:168
  5.7 0.6 %copy-done.2 = s32[32,3]{0,1:T(4,128)S(1)} copy-done((s32[32,3]{0,1:T(4,128)S(1)}, s32[32,3]{0,1:T(4,128)}, u32[]{:S(2)}) %copy-start.2) | copy-done | bytes 408
  6.6 0.2 and_reduce_fusion
  6.7 0.2 and_reduce_fusion.1
  7.1 0.1 and_reduce_fusion.2
  7.4 3.0 %collective-permute-done = f32[3,8,4,128]{3,2,1,0:T(4,128)S(1)} collective-permute-done((f32[3,8,4,128]{3,2,1,0:T(4,128)S(1)}, f32[3,8,4,128]{3,2,1,0:T(4,128)S(1)}, u32[]{:S(2)}, u32[]{:S(2)}) %collective-permute-start) | collective-permute-done | bytes 49184 | tf_op jit(solution)/shard_map/ppermute | solution.py:167
  10.5 0.2 reshape.928
  10.6 1.3 %collective-permute-start.2 = (f32[3,4608]{1,0:T(4,128)S(1)}, f32[3,4608]{1,0:T(4,128)S(1)}, u32[]{:S(2)}, u32[]{:S(2)}) collective-permute-start(f32[3,4608]{1,0:T(4,128)S(1)} %reshape.928), channel_id=1, source_target_pairs={{1,0},{2,1},{3,2},{5,4},{6,5},{7,6},{9,8},{10,9},{11,10},{13,12},{... | collective-permute-start | bytes 165896 | tf_op jit(solution)/shard_map/ppermute | solution.py:171
  13.3 3.6 %collective-permute-done.2 = f32[3,4608]{1,0:T(4,128)S(1)} collective-permute-done((f32[3,4608]{1,0:T(4,128)S(1)}, f32[3,4608]{1,0:T(4,128)S(1)}, u32[]{:S(2)}, u32[]{:S(2)}) %collective-permute-start.2) | collective-permute-done | bytes 55328 | tf_op jit(solution)/shard_map/ppermute | solution.py:171
  16.9 0.2 reshape.929
  17.2 0.1 pad_maximum_fusion.2
  17.4 0.1 reshape.930
  17.6 0.1 reshape.931
  17.7 0.1 reshape.932
  17.8 0.1 reshape.933
  17.9 0.2 concatenate.108
  18.2 0.2 maximum_select_fusion
  18.4 0.3 slice_bitcast_fusion.3
  18.8 0.3 fusion.295
  19.1 1.0 %collective-permute-done.3 = f32[2,6,1904]{2,0,1:T(2,128)S(1)} collective-permute-done((f32[2,6,1904]{2,0,1:T(2,128)S(1)}, f32[2,6,1904]{2,0,1:T(2,128)S(1)}, u32[]{:S(2)}, u32[]{:S(2)}) %collective-permute-start.3) | collective-permute-done | bytes 91424 | tf_op jit(solution)/shard_map/ppermute | solution.py:31
  20.2 0.3 slice_multiply_fusion
  20.5 0.1 fusion.130
  20.6 0.2 multiply_add_fusion.4
  20.8 0.2 multiply_add_fusion.3
  21.0 0.2 multiply_subtract_fusion
  21.2 0.2 fusion.40
  21.6 0.2 maximum_select_fusion.1
  21.7 0.2 slice_bitcast_fusion.7
  22.1 0.2 collective-permute-start.4
  22.3 0.2 fusion.296
  22.5 0.9 %collective-permute-done.4 = f32[2,6,1632]{2,0,1:T(2,128)S(1)} collective-permute-done((f32[2,6,1632]{2,0,1:T(2,128)S(1)}, f32[2,6,1632]{2,0,1:T(2,128)S(1)}, u32[]{:S(2)}, u32[]{:S(2)}) %collective-permute-start.4) | collective-permute-done | bytes 78368 | tf_op jit(solution)/shard_map/ppermute | solution.py:31
  23.5 0.3 slice_multiply_fusion.1
  23.9 0.2 multiply_add_fusion.9
  24.1 0.2 multiply_add_fusion.8
  24.3 0.1 multiply_subtract_fusion.1
  24.4 0.2 fusion.53
  24.7 0.6 %copy-done.1 = f32[6]{0:T(128)S(1)} copy-done((f32[6]{0:T(128)S(1)}, f32[6]{0:T(128)}, u32[]{:S(2)}) %copy-start.1) | copy-done | bytes 48
  25.5 0.1 slice.1201
  25.7 0.1 maximum_select_fusion.3
  25.8 0.2 maximum_select_fusion.4
  26.0 0.2 slice_bitcast_fusion.11
  26.3 0.2 collective-permute-start.5
  26.5 0.2 fusion.297
  26.7 0.9 %collective-permute-done.5 = f32[2,6,1360]{2,0,1:T(2,128)S(1)} collective-permute-done((f32[2,6,1360]{2,0,1:T(2,128)S(1)}, f32[2,6,1360]{2,0,1:T(2,128)S(1)}, u32[]{:S(2)}, u32[]{:S(2)}) %collective-permute-start.5) | collective-permute-done | bytes 65312 | tf_op jit(solution)/shard_map/ppermute | solution.py:31
  27.7 0.3 slice_multiply_fusion.2
  28.0 0.2 multiply_add_fusion.14
  28.2 0.2 multiply_add_fusion.13
  28.4 0.1 multiply_subtract_fusion.2
  28.5 0.2 fusion.66
  28.9 0.1 slice.1253
  29.1 0.1 maximum_select_fusion.6
  29.2 0.2 slice_bitcast_fusion.15
  29.5 0.2 collective-permute-start.6
  29.7 0.2 fusion.298
  29.9 0.9 %collective-permute-done.6 = f32[2,6,1088]{2,0,1:T(2,128)S(1)} collective-permute-done((f32[2,6,1088]{2,0,1:T(2,128)S(1)}, f32[2,6,1088]{2,0,1:T(2,128)S(1)}, u32[]{:S(2)}, u32[]{:S(2)}) %collective-permute-start.6) | collective-permute-done | bytes 52256 | tf_op jit(solution)/shard_map/ppermute | solution.py:31
  30.8 0.2 slice_multiply_fusion.3
  31.2 0.1 multiply_add_fusion.19
  31.3 0.1 fusion.229
  31.5 0.1 multiply_subtract_fusion.3
  31.6 0.2 concatenate.127
  31.8 0.8 %slice.1286 = f32[4,8,8,128]{3,2,1,0:T(8,128)} slice(f32[4,8,8,136]{3,2,1,0:T(8,128)S(1)} %concatenate.127), slice={[0:4], [0:8], [0:8], [4:132]} | slice | bytes 262144 | tf_op jit(solution)/shard_map/slice | solution.py:195
  32.6 0.1 fusion.79
  33.0 0.7 %pad_maximum_fusion.16 = f32[2,8,8,128]{3,2,1,0:T(8,128)} fusion(f32[1,8,8,136]{3,2,1,0:T(8,128)S(1)} %concatenate.129, f32[1,8,8,136]{3,2,1,0:T(8,128)S(1)} %concatenate.128), kind=kLoop, calls=%fused_computation.191 | loop fusion | flops 16384 | bytes 135168 | tf_op jit(solution)/shard_map/concatenate | solution.py:152
  (87 shorter events, 4.2 us)
Async XLA Ops:
  0.6 0.8 %copy-start = (f32[2,8,8,128]{3,2,1,0:T(8,128)S(1)}, f32[2,8,8,128]{3,2,1,0:T(8,128)}, u32[]{:S(2)}) copy-start(f32[2,8,8,128]{3,2,1,0:T(8,128)} %param.4) | copy-start | bytes 196612
  1.5 5.9 %collective-permute-start.1 = (f32[3,8,4,128]{3,2,1,0:T(4,128)S(1)}, f32[3,8,4,128]{3,2,1,0:T(4,128)S(1)}, u32[]{:S(2)}, u32[]{:S(2)}) collective-permute-start(f32[3,8,4,128]{3,2,1,0:T(4,128)S(1)} %get-tuple-element.115), channel_id=1, source_target_pairs={{0,12},{4,0},{8,4},{12,8},{1,13},{5,1},{9,5},{13,9},{2,14},{6,2},{... | collective-permute-start | bytes 147464 | tf_op jit(solution)/shard_map/ppermute | solution.py:168
  5.4 5.0 %collective-permute-start = (f32[3,8,4,128]{3,2,1,0:T(4,128)S(1)}, f32[3,8,4,128]{3,2,1,0:T(4,128)S(1)}, u32[]{:S(2)}, u32[]{:S(2)}) collective-permute-start(f32[3,8,4,128]{3,2,1,0:T(4,128)S(1)} %get-tuple-element.114), channel_id=1, source_target_pairs={{0,4},{4,8},{8,12},{12,0},{1,5},{5,9},{9,13},{13,1},{2,6},{6,10},{... | collective-permute-start | bytes 147464 | tf_op jit(solution)/shard_map/ppermute | solution.py:167
  5.6 0.7 %copy-start.2 = (s32[32,3]{0,1:T(4,128)S(1)}, s32[32,3]{0,1:T(4,128)}, u32[]{:S(2)}) copy-start(s32[32,3]{0,1:T(4,128)} %param.5) | copy-start | bytes 1156
  10.6 6.2 %collective-permute-start.2 = (f32[3,4608]{1,0:T(4,128)S(1)}, f32[3,4608]{1,0:T(4,128)S(1)}, u32[]{:S(2)}, u32[]{:S(2)}) collective-permute-start(f32[3,4608]{1,0:T(4,128)S(1)} %reshape.928), channel_id=1, source_target_pairs={{1,0},{2,1},{3,2},{5,4},{6,5},{7,6},{9,8},{10,9},{11,10},{13,12},{... | collective-permute-start | bytes 165896 | tf_op jit(solution)/shard_map/ppermute | solution.py:171
  18.7 1.4 %collective-permute-start.3 = (f32[2,6,1904]{2,0,1:T(2,128)S(1)}, f32[2,6,1904]{2,0,1:T(2,128)S(1)}, u32[]{:S(2)}, u32[]{:S(2)}) collective-permute-start(f32[2,6,1904]{2,0,1:T(2,128)S(1)} %pad_maximum_fusion.9), channel_id=1, source_target_pairs={{0,16},{16,0},{1,17},{17,1},{2,18},{18,2},{3,19},{19,3},{4,20},{20... | collective-permute-start | bytes 274184 | tf_op jit(solution)/shard_map/ppermute | solution.py:31
  22.1 1.3 %collective-permute-start.4 = (f32[2,6,1632]{2,0,1:T(2,128)S(1)}, f32[2,6,1632]{2,0,1:T(2,128)S(1)}, u32[]{:S(2)}, u32[]{:S(2)}) collective-permute-start(f32[2,6,1632]{2,0,1:T(2,128)S(1)} %pad_maximum_fusion.12), channel_id=1, source_target_pairs={{0,16},{16,0},{1,17},{17,1},{2,18},{18,2},{3,19},{19,3},{4,20},{20... | collective-permute-start | bytes 235016 | tf_op jit(solution)/shard_map/ppermute | solution.py:31
  24.7 0.7 %copy-start.1 = (f32[6]{0:T(128)S(1)}, f32[6]{0:T(128)}, u32[]{:S(2)}) copy-start(f32[6]{0:T(128)} %constant.166.clone.1) | copy-start | bytes 76
  26.3 1.3 %collective-permute-start.5 = (f32[2,6,1360]{2,0,1:T(2,128)S(1)}, f32[2,6,1360]{2,0,1:T(2,128)S(1)}, u32[]{:S(2)}, u32[]{:S(2)}) collective-permute-start(f32[2,6,1360]{2,0,1:T(2,128)S(1)} %pad_maximum_fusion.15), channel_id=1, source_target_pairs={{0,16},{16,0},{1,17},{17,1},{2,18},{18,2},{3,19},{19,3},{4,20},{20... | collective-permute-start | bytes 195848 | tf_op jit(solution)/shard_map/ppermute | solution.py:31
  29.5 1.3 %collective-permute-start.6 = (f32[2,6,1088]{2,0,1:T(2,128)S(1)}, f32[2,6,1088]{2,0,1:T(2,128)S(1)}, u32[]{:S(2)}, u32[]{:S(2)}) collective-permute-start(f32[2,6,1088]{2,0,1:T(2,128)S(1)} %pad_maximum_fusion.17), channel_id=1, source_target_pairs={{0,16},{16,0},{1,17},{17,1},{2,18},{18,2},{3,19},{19,3},{4,20},{20... | collective-permute-start | bytes 156680 | tf_op jit(solution)/shard_map/ppermute | solution.py:31

commit v11 on v10

--- a/solution.py
+++ b/solution.py
@@ -140,16 +140,54 @@
         nrows = size // stride
         ypos = first_y + jnp.arange(nrows, dtype=jnp.int32)
         xlo, xhi = x_halos(fields)
-        side = neighbours(ext, xlo, xhi, stride)
+        near = [
+            ext[..., 2 * stride :],
+            ext[..., :size],
+            ext[..., stride + 1 : stride + 1 + size],
+            ext[..., stride - 1 : stride - 1 + size],
+        ]
+        phi = fields[:4]
+        chem = fields[4:]
+        centre_d = DSOL + (DLIQ - DSOL) * fields[0]
+        part_lap = near[0][:4] + near[1][:4] + near[2][:4] + near[3][:4]
+        part_flux = jnp.zeros_like(chem)
+        for s in near:
+            part_flux = part_flux + 0.5 * (centre_d + (DSOL + (DLIQ - DSOL) * s[0])) * (s[4:] - chem)
+        part_lap, part_flux = lax.optimization_barrier((part_lap, part_flux))
+        xp = jnp.concatenate([fields[:, 1:], xhi[:, None]], 1)
+        xm = jnp.concatenate([xlo[:, None], fields[:, :-1]], 1)
+        total = part_lap + xp[:4] + xm[:4]
+        lap = total - 6.0 * phi
+        square = phi * phi
+        summed = square[0] + square[1] + square[2] + square[3]
+        under = 2.0 * (jnp.tile(under_z, nrows).astype(jnp.float32) / depth - 0.5)
+        rates = []
+        for phase in range(4):
+            psi = -(COMP[phase][0] * chem[0] + COMP[phase][1] * chem[1]) + LATENT[phase] * under
+            rate = (
+                KAPPA * lap[phase]
+                - WELL * phi[phase] * (summed - square[phase])
+                - 6.0 * phi[phase] * (1.0 - phi[phase]) * psi
+            )
+            rates.append(rate)
+        mean_rate = (rates[0] + rates[1] + rates[2] + rates[3]) * 0.25
+        stepped = jnp.stack([phi[phase] + DT * (rates[phase] - mean_rate) for phase in range(4)])
         on = active(ypos, zpos).reshape(-1)
-        zflat = jnp.tile(under_z, nrows)
-        phi_new = jnp.where(
-            on[None, None],
-            phase_update(fields, side, zflat, 0, depth),
-            fields[:4],
-        )
-        mu_new = chem_update(fields, side, fields[:4], phi_new)
-        return jnp.concatenate([phi_new, mu_new], 0)
+        phi_new = jnp.where(on[None, None], stepped, phi)
+        flux = part_flux
+        for s in (xp, xm):
+            flux = flux + 0.5 * (centre_d + (DSOL + (DLIQ - DSOL) * s[0])) * (s[4:] - chem)
+        delta = shape_fn(phi_new) - shape_fn(phi)
+        result = []
+        for comp in range(2):
+            change = (
+                COMP[0][comp] * delta[0]
+                + COMP[1][comp] * delta[1]
+                + COMP[2][comp] * delta[2]
+                + COMP[3][comp] * delta[3]
+            )
+            result.append(chem[comp] + DT * flux[comp] - change)
+        return jnp.concatenate([phi_new, jnp.stack(result)], 0)
 
     def lane_index(ext):
         return lax.broadcasted_iota(jnp.int32, ext.shape, 2) % stride

time: 33.9 us -> 35.1 us (1.035)
  other arithmetic: 8.81 us -> 9.76 us
    add x11 -> x20, other arithmetic: 1.93 us -> 3.11 us  [the longest x8 1.14 us: step(): phi[phase] + DT * (rates[phase] - mean_rate)]
    mul x6 -> x9, other arithmetic: 1.26 us -> 1.02 us  [the longest x4 0.53 us: step(): square = phi * phi]
  transfers between devices with their start and end apart: 7 -> 7, of which waited for: 6 -> 6; matrix products, arithmetic and copies ran while one was open for 10% -> 9% of each run, Pallas kernels for 0% -> 0%
where the time goes in v11:
time: 35.1 us; the launch traced here: 34.9 us
  waiting for transfers between devices  10.4 us (30%)
  other arithmetic  9.76 us (28%)
  local copies, waits for them, and re-layouts  7.29 us (21%)
  starting transfers between devices  5.97 us (17%)
  between operations  1.43 us (4%)
    ppermute x1, starting transfers between devices, shards(): above_y = lax.ppermute(start[:, :, :rim_y], 'gy', ring('gy', -1))  3.95 us
    ppermute x4, waiting for transfers between devices, x_halos(): got = lax.ppermute(pair, 'gx', ring('gx', 1))  3.84 us
    ppermute x1, waiting for transfers between devices, shards(): lax.ppermute(wide[..., :count].reshape(wide.shape[0], -1), 'gz', line('gz...  3.55 us
    ppermute x1, waiting for transfers between devices, shards(): below_y = lax.ppermute(start[:, :, -rim_y:], 'gy', ring('gy', 1))  3.02 us
    unnamed x10, local copies, waits for them, and re-layouts  1.37 us
    ppermute x1, starting transfers between devices, shards(): lax.ppermute(wide[..., :count].reshape(wide.shape[0], -1), 'gz', line('gz...  1.29 us
    add x8, other arithmetic, step(): phi[phase] + DT * (rates[phase] - mean_rate)  1.14 us
    slice x4, local copies, waits for them, and re-layouts, step(): xp = jnp.concatenate([fields[:, 1:], xhi[:, None]], 1)  0.87 us
  transfers between devices with their start and end apart: 7, of which 6 were waited for; matrix products, arithmetic and copies ran while one was open for 9% of the time, Pallas kernels for 0%

profile of v11, /device:TPU:0, one launch (start us, length us, event | category | flops | bytes accessed | tf_op | source)
XLA Modules:
  0.0 34.9 jit_solution(1212001389723623147)
XLA Ops:
  0.6 0.8 %convert_bitcast_fusion = f32[1,8,8,128]{3,2,1,0:T(8,128)S(1)} fusion(s32[8,8,128]{2,1,0:T(8,128)} %param.3), kind=kLoop, calls=%fused_computation.455 | loop fusion | flops 8192 | bytes 65536 | tf_op jit(solution)/shard_map/broadcast_in_dim | solution.py:203
  1.5 3.9 %collective-permute-start.1 = (f32[3,8,4,128]{3,2,1,0:T(4,128)S(1)}, f32[3,8,4,128]{3,2,1,0:T(4,128)S(1)}, u32[]{:S(2)}, u32[]{:S(2)}) collective-permute-start(f32[3,8,4,128]{3,2,1,0:T(4,128)S(1)} %get-tuple-element.128), channel_id=1, source_target_pairs={{0,12},{4,0},{8,4},{12,8},{1,13},{5,1},{9,5},{13,9},{2,14},{6,2},{... | collective-permute-start | bytes 147464 | tf_op jit(solution)/shard_map/ppermute | solution.py:206
  5.7 0.6 %copy-done.2 = s32[32,3]{0,1:T(4,128)S(1)} copy-done((s32[32,3]{0,1:T(4,128)S(1)}, s32[32,3]{0,1:T(4,128)}, u32[]{:S(2)}) %copy-start.2) | copy-done | bytes 408
  6.6 0.2 and_reduce_fusion
  6.7 0.2 and_reduce_fusion.1
  7.1 0.1 and_reduce_fusion.2
  7.4 3.0 %collective-permute-done = f32[3,8,4,128]{3,2,1,0:T(4,128)S(1)} collective-permute-done((f32[3,8,4,128]{3,2,1,0:T(4,128)S(1)}, f32[3,8,4,128]{3,2,1,0:T(4,128)S(1)}, u32[]{:S(2)}, u32[]{:S(2)}) %collective-permute-start) | collective-permute-done | bytes 49184 | tf_op jit(solution)/shard_map/ppermute | solution.py:205
  10.5 0.2 reshape.928
  10.6 1.3 %collective-permute-start.2 = (f32[3,4608]{1,0:T(4,128)S(1)}, f32[3,4608]{1,0:T(4,128)S(1)}, u32[]{:S(2)}, u32[]{:S(2)}) collective-permute-start(f32[3,4608]{1,0:T(4,128)S(1)} %reshape.928), channel_id=1, source_target_pairs={{1,0},{2,1},{3,2},{5,4},{6,5},{7,6},{9,8},{10,9},{11,10},{13,12},{... | collective-permute-start | bytes 165896 | tf_op jit(solution)/shard_map/ppermute | solution.py:209
  13.3 3.6 %collective-permute-done.2 = f32[3,4608]{1,0:T(4,128)S(1)} collective-permute-done((f32[3,4608]{1,0:T(4,128)S(1)}, f32[3,4608]{1,0:T(4,128)S(1)}, u32[]{:S(2)}, u32[]{:S(2)}) %collective-permute-start.2) | collective-permute-done | bytes 55328 | tf_op jit(solution)/shard_map/ppermute | solution.py:209
  16.9 0.2 reshape.929
  17.2 0.1 pad_maximum_fusion.2
  17.9 0.2 concatenate.108
  18.2 0.2 maximum_select_fusion
  18.4 0.3 fusion.283
  18.6 0.3 slice_bitcast_fusion.3
  18.9 0.3 slice_add_fusion
  19.2 0.1 fusion.118
  19.5 0.2 fusion.34
  19.7 1.1 %collective-permute-done.3 = f32[2,6,1904]{2,0,1:T(2,128)S(1)} collective-permute-done((f32[2,6,1904]{2,0,1:T(2,128)S(1)}, f32[2,6,1904]{2,0,1:T(2,128)S(1)}, u32[]{:S(2)}, u32[]{:S(2)}) %collective-permute-start.3) | collective-permute-done | bytes 91424 | tf_op jit(solution)/shard_map/ppermute | solution.py:31
  20.8 0.1 slice_multiply_fusion
  21.0 0.1 fusion.102
  21.1 0.2 multiply_add_fusion.3
  21.3 0.1 multiply_add_fusion.2
  21.6 0.2 multiply_subtract_fusion
  21.9 0.2 maximum_select_fusion.1
  22.0 0.2 fusion.284
  22.3 0.2 slice_bitcast_fusion.7
  22.5 0.2 slice_add_fusion.3
  22.8 0.1 fusion.160
  23.0 0.2 collective-permute-start.4
  23.2 0.2 fusion.47
  23.4 0.9 %collective-permute-done.4 = f32[2,6,1632]{2,0,1:T(2,128)S(1)} collective-permute-done((f32[2,6,1632]{2,0,1:T(2,128)S(1)}, f32[2,6,1632]{2,0,1:T(2,128)S(1)}, u32[]{:S(2)}, u32[]{:S(2)}) %collective-permute-start.4) | collective-permute-done | bytes 78368 | tf_op jit(solution)/shard_map/ppermute | solution.py:31
  24.4 0.1 slice_multiply_fusion.1
  24.6 0.2 multiply_add_fusion.8
  24.8 0.1 multiply_add_fusion.7
  25.1 0.1 multiply_subtract_fusion.1
  25.3 0.6 %copy-done.1 = f32[6]{0:T(128)S(1)} copy-done((f32[6]{0:T(128)S(1)}, f32[6]{0:T(128)}, u32[]{:S(2)}) %copy-start.1) | copy-done | bytes 48
  26.1 0.1 slice.1185
  26.3 0.1 maximum_select_fusion.3
  26.4 0.2 maximum_select_fusion.4
  26.6 0.2 fusion.285
  26.8 0.2 slice_bitcast_fusion.11
  27.0 0.2 slice_add_fusion.6
  27.4 0.2 collective-permute-start.5
  27.6 0.2 fusion.60
  27.8 0.9 %collective-permute-done.5 = f32[2,6,1360]{2,0,1:T(2,128)S(1)} collective-permute-done((f32[2,6,1360]{2,0,1:T(2,128)S(1)}, f32[2,6,1360]{2,0,1:T(2,128)S(1)}, u32[]{:S(2)}, u32[]{:S(2)}) %collective-permute-start.5) | collective-permute-done | bytes 65312 | tf_op jit(solution)/shard_map/ppermute | solution.py:31
  28.8 0.1 slice_multiply_fusion.2
  29.0 0.2 multiply_add_fusion.13
  29.2 0.1 multiply_add_fusion.12
  29.4 0.1 multiply_subtract_fusion.2
  29.8 0.1 slice.1237
  30.0 0.1 maximum_select_fusion.6
  30.1 0.2 fusion.286
  30.3 0.2 slice_bitcast_fusion.15
  30.6 0.2 collective-permute-start.6
  30.8 0.2 slice_add_fusion.9
  31.0 0.9 %collective-permute-done.6 = f32[2,6,1088]{2,0,1:T(2,128)S(1)} collective-permute-done((f32[2,6,1088]{2,0,1:T(2,128)S(1)}, f32[2,6,1088]{2,0,1:T(2,128)S(1)}, u32[]{:S(2)}, u32[]{:S(2)}) %collective-permute-start.6) | collective-permute-done | bytes 52256 | tf_op jit(solution)/shard_map/ppermute | solution.py:31
  32.0 0.1 fusion.73
  32.2 0.1 slice_multiply_fusion.3
  32.4 0.1 multiply_add_fusion.18
  32.8 0.2 concatenate.127
  33.0 0.8 %slice.1279 = f32[4,8,8,128]{3,2,1,0:T(8,128)} slice(f32[4,8,8,136]{3,2,1,0:T(8,128)S(1)} %concatenate.127), slice={[0:4], [0:8], [0:8], [4:132]} | slice | bytes 262144 | tf_op jit(solution)/shard_map/slice | solution.py:233
  34.1 0.7 %pad_maximum_fusion.16 = f32[2,8,8,128]{3,2,1,0:T(8,128)} fusion(f32[1,8,8,136]{3,2,1,0:T(8,128)S(1)} %concatenate.129, f32[1,8,8,136]{3,2,1,0:T(8,128)S(1)} %concatenate.128), kind=kLoop, calls=%fused_computation.191 | loop fusion | flops 16384 | bytes 135168 | tf_op jit(solution)/shard_map/concatenate | solution.py:190
  (99 shorter events, 5.5 us)
Async XLA Ops:
  0.6 0.8 %copy-start = (f32[2,8,8,128]{3,2,1,0:T(8,128)S(1)}, f32[2,8,8,128]{3,2,1,0:T(8,128)}, u32[]{:S(2)}) copy-start(f32[2,8,8,128]{3,2,1,0:T(8,128)} %param.4) | copy-start | bytes 196612
  1.5 5.9 %collective-permute-start.1 = (f32[3,8,4,128]{3,2,1,0:T(4,128)S(1)}, f32[3,8,4,128]{3,2,1,0:T(4,128)S(1)}, u32[]{:S(2)}, u32[]{:S(2)}) collective-permute-start(f32[3,8,4,128]{3,2,1,0:T(4,128)S(1)} %get-tuple-element.128), channel_id=1, source_target_pairs={{0,12},{4,0},{8,4},{12,8},{1,13},{5,1},{9,5},{13,9},{2,14},{6,2},{... | collective-permute-start | bytes 147464 | tf_op jit(solution)/shard_map/ppermute | solution.py:206
  5.4 5.0 %collective-permute-start = (f32[3,8,4,128]{3,2,1,0:T(4,128)S(1)}, f32[3,8,4,128]{3,2,1,0:T(4,128)S(1)}, u32[]{:S(2)}, u32[]{:S(2)}) collective-permute-start(f32[3,8,4,128]{3,2,1,0:T(4,128)S(1)} %get-tuple-element.127), channel_id=1, source_target_pairs={{0,4},{4,8},{8,12},{12,0},{1,5},{5,9},{9,13},{13,1},{2,6},{6,10},{... | collective-permute-start | bytes 147464 | tf_op jit(solution)/shard_map/ppermute | solution.py:205
  5.6 0.7 %copy-start.2 = (s32[32,3]{0,1:T(4,128)S(1)}, s32[32,3]{0,1:T(4,128)}, u32[]{:S(2)}) copy-start(s32[32,3]{0,1:T(4,128)} %param.5) | copy-start | bytes 1156
  10.6 6.2 %collective-permute-start.2 = (f32[3,4608]{1,0:T(4,128)S(1)}, f32[3,4608]{1,0:T(4,128)S(1)}, u32[]{:S(2)}, u32[]{:S(2)}) collective-permute-start(f32[3,4608]{1,0:T(4,128)S(1)} %reshape.928), channel_id=1, source_target_pairs={{1,0},{2,1},{3,2},{5,4},{6,5},{7,6},{9,8},{10,9},{11,10},{13,12},{... | collective-permute-start | bytes 165896 | tf_op jit(solution)/shard_map/ppermute | solution.py:209
  19.4 1.4 %collective-permute-start.3 = (f32[2,6,1904]{2,0,1:T(2,128)S(1)}, f32[2,6,1904]{2,0,1:T(2,128)S(1)}, u32[]{:S(2)}, u32[]{:S(2)}) collective-permute-start(f32[2,6,1904]{2,0,1:T(2,128)S(1)} %pad_maximum_fusion.9), channel_id=1, source_target_pairs={{0,16},{16,0},{1,17},{17,1},{2,18},{18,2},{3,19},{19,3},{4,20},{20... | collective-permute-start | bytes 274184 | tf_op jit(solution)/shard_map/ppermute | solution.py:31
  23.0 1.3 %collective-permute-start.4 = (f32[2,6,1632]{2,0,1:T(2,128)S(1)}, f32[2,6,1632]{2,0,1:T(2,128)S(1)}, u32[]{:S(2)}, u32[]{:S(2)}) collective-permute-start(f32[2,6,1632]{2,0,1:T(2,128)S(1)} %pad_maximum_fusion.12), channel_id=1, source_target_pairs={{0,16},{16,0},{1,17},{17,1},{2,18},{18,2},{3,19},{19,3},{4,20},{20... | collective-permute-start | bytes 235016 | tf_op jit(solution)/shard_map/ppermute | solution.py:31
  25.3 0.7 %copy-start.1 = (f32[6]{0:T(128)S(1)}, f32[6]{0:T(128)}, u32[]{:S(2)}) copy-start(f32[6]{0:T(128)} %constant.166.clone.1) | copy-start | bytes 76
  27.4 1.3 %collective-permute-start.5 = (f32[2,6,1360]{2,0,1:T(2,128)S(1)}, f32[2,6,1360]{2,0,1:T(2,128)S(1)}, u32[]{:S(2)}, u32[]{:S(2)}) collective-permute-start(f32[2,6,1360]{2,0,1:T(2,128)S(1)} %pad_maximum_fusion.15), channel_id=1, source_target_pairs={{0,16},{16,0},{1,17},{17,1},{2,18},{18,2},{3,19},{19,3},{4,20},{20... | collective-permute-start | bytes 195848 | tf_op jit(solution)/shard_map/ppermute | solution.py:31
  30.6 1.3 %collective-permute-start.6 = (f32[2,6,1088]{2,0,1:T(2,128)S(1)}, f32[2,6,1088]{2,0,1:T(2,128)S(1)}, u32[]{:S(2)}, u32[]{:S(2)}) collective-permute-start(f32[2,6,1088]{2,0,1:T(2,128)S(1)} %pad_maximum_fusion.17), channel_id=1, source_target_pairs={{0,16},{16,0},{1,17},{17,1},{2,18},{18,2},{3,19},{19,3},{4,20},{20... | collective-permute-start | bytes 156680 | tf_op jit(solution)/shard_map/ppermute | solution.py:31

commit v12 on v10

--- a/solution.py
+++ b/solution.py
@@ -181,9 +181,7 @@
     ext = step(ext, 1 - rim_y, pre_z, 0)
     ext = edge_at(ext, cells_z - low, top_brick)
     ext = step(ext, 2 - rim_y, pre_z, 0)
-    liquid = jnp.concatenate(
-        [jnp.ones((1,) + ext.shape[1:], jnp.float32), jnp.zeros((nf - 1,) + ext.shape[1:], jnp.float32)], 0
-    )
+    liquid = jnp.where(lax.broadcasted_iota(jnp.int32, ext.shape, 0) == 0, 1.0, 0.0).astype(jnp.float32)
     ext = jnp.where(top_brick & (lane_index(ext) >= cells_z - low), liquid, ext)
     ext = edge_below(ext, lift - low - 1, bottom_brick)
     ext = edge_at(ext, cells_z + lift - low, top_brick)

time: 33.9 us -> 33.3 us (0.982)
  local copies, waits for them, and re-layouts: 7.28 us -> 6.63 us
    unnamed x10 -> x8, local copies, waits for them, and re-layouts: 1.37 us -> 0.72 us
where the time goes in v12:
time: 33.3 us; the launch traced here: 33.1 us
  waiting for transfers between devices  10.3 us (31%)
  other arithmetic  8.82 us (26%)
  local copies, waits for them, and re-layouts  6.63 us (20%)
  starting transfers between devices  5.97 us (18%)
  between operations  1.38 us (4%)
    ppermute x1, starting transfers between devices, shards(): above_y = lax.ppermute(start[:, :, :rim_y], 'gy', ring('gy', -1))  3.95 us
    ppermute x4, waiting for transfers between devices, x_halos(): got = lax.ppermute(pair, 'gx', ring('gx', 1))  3.7 us
    ppermute x1, waiting for transfers between devices, shards(): lax.ppermute(wide[..., :count].reshape(wide.shape[0], -1), 'gz', line('gz...  3.56 us
    ppermute x1, waiting for transfers between devices, shards(): below_y = lax.ppermute(start[:, :, -rim_y:], 'gy', ring('gy', 1))  3.01 us
    ppermute x1, starting transfers between devices, shards(): lax.ppermute(wide[..., :count].reshape(wide.shape[0], -1), 'gz', line('gz...  1.29 us
    add x7, other arithmetic, phase_update(): phi[phase] + DT * (rates[phase] - mean_rate)  1.21 us
    mul x4, other arithmetic, phase_update(): square = phi * phi  1.11 us
    another operation x4, local copies, waits for them, and re-layouts, x_halos(): pair = jnp.stack([block[:, -1], block[:, 0]])  0.87 us
  transfers between devices with their start and end apart: 7, of which 6 were waited for; matrix products, arithmetic and copies ran while one was open for 10% of the time, Pallas kernels for 0%

profile of v12, /device:TPU:0, one launch (start us, length us, event | category | flops | bytes accessed | tf_op | source)
XLA Modules:
  0.0 33.1 jit_solution(7144004850462752246)
XLA Ops:
  0.6 0.8 %convert_bitcast_fusion = f32[1,8,8,128]{3,2,1,0:T(8,128)S(1)} fusion(s32[8,8,128]{2,1,0:T(8,128)} %param.3), kind=kLoop, calls=%fused_computation.455 | loop fusion | flops 8192 | bytes 65536 | tf_op jit(solution)/shard_map/broadcast_in_dim | solution.py:165
  1.5 3.9 %collective-permute-start.1 = (f32[3,8,4,128]{3,2,1,0:T(4,128)S(1)}, f32[3,8,4,128]{3,2,1,0:T(4,128)S(1)}, u32[]{:S(2)}, u32[]{:S(2)}) collective-permute-start(f32[3,8,4,128]{3,2,1,0:T(4,128)S(1)} %get-tuple-element.115), channel_id=1, source_target_pairs={{0,12},{4,0},{8,4},{12,8},{1,13},{5,1},{9,5},{13,9},{2,14},{6,2},{... | collective-permute-start | bytes 147464 | tf_op jit(solution)/shard_map/ppermute | solution.py:168
  5.7 0.6 %copy-done.1 = s32[32,3]{0,1:T(4,128)S(1)} copy-done((s32[32,3]{0,1:T(4,128)S(1)}, s32[32,3]{0,1:T(4,128)}, u32[]{:S(2)}) %copy-start.1) | copy-done | bytes 408
  6.6 0.2 and_reduce_fusion
  6.7 0.2 and_reduce_fusion.1
  7.1 0.1 and_reduce_fusion.2
  7.4 3.0 %collective-permute-done = f32[3,8,4,128]{3,2,1,0:T(4,128)S(1)} collective-permute-done((f32[3,8,4,128]{3,2,1,0:T(4,128)S(1)}, f32[3,8,4,128]{3,2,1,0:T(4,128)S(1)}, u32[]{:S(2)}, u32[]{:S(2)}) %collective-permute-start) | collective-permute-done | bytes 49184 | tf_op jit(solution)/shard_map/ppermute | solution.py:167
  10.5 0.2 reshape.927
  10.6 1.3 %collective-permute-start.2 = (f32[3,4608]{1,0:T(4,128)S(1)}, f32[3,4608]{1,0:T(4,128)S(1)}, u32[]{:S(2)}, u32[]{:S(2)}) collective-permute-start(f32[3,4608]{1,0:T(4,128)S(1)} %reshape.927), channel_id=1, source_target_pairs={{1,0},{2,1},{3,2},{5,4},{6,5},{7,6},{9,8},{10,9},{11,10},{13,12},{... | collective-permute-start | bytes 165896 | tf_op jit(solution)/shard_map/ppermute | solution.py:171
  13.3 3.6 %collective-permute-done.2 = f32[3,4608]{1,0:T(4,128)S(1)} collective-permute-done((f32[3,4608]{1,0:T(4,128)S(1)}, f32[3,4608]{1,0:T(4,128)S(1)}, u32[]{:S(2)}, u32[]{:S(2)}) %collective-permute-start.2) | collective-permute-done | bytes 55328 | tf_op jit(solution)/shard_map/ppermute | solution.py:171
  16.9 0.2 reshape.928
  17.2 0.1 pad_maximum_fusion.2
  17.4 0.1 reshape.929
  17.6 0.1 reshape.930
  17.7 0.1 reshape.931
  17.8 0.1 reshape.932
  17.9 0.2 concatenate.104
  18.2 0.2 maximum_select_fusion
  18.4 0.3 slice_bitcast_fusion.3
  18.8 0.3 fusion.295
  19.1 1.0 %collective-permute-done.3 = f32[2,6,1904]{2,0,1:T(2,128)S(1)} collective-permute-done((f32[2,6,1904]{2,0,1:T(2,128)S(1)}, f32[2,6,1904]{2,0,1:T(2,128)S(1)}, u32[]{:S(2)}, u32[]{:S(2)}) %collective-permute-start.3) | collective-permute-done | bytes 91424 | tf_op jit(solution)/shard_map/ppermute | solution.py:31
  20.2 0.3 slice_multiply_fusion
  20.5 0.1 fusion.130
  20.6 0.2 multiply_add_fusion.4
  20.8 0.2 multiply_add_fusion.3
  21.0 0.2 multiply_subtract_fusion
  21.2 0.2 fusion.40
  21.6 0.2 maximum_select_fusion.1
  21.7 0.2 slice_bitcast_fusion.7
  22.1 0.2 collective-permute-start.4
  22.3 0.2 fusion.296
  22.5 0.9 %collective-permute-done.4 = f32[2,6,1632]{2,0,1:T(2,128)S(1)} collective-permute-done((f32[2,6,1632]{2,0,1:T(2,128)S(1)}, f32[2,6,1632]{2,0,1:T(2,128)S(1)}, u32[]{:S(2)}, u32[]{:S(2)}) %collective-permute-start.4) | collective-permute-done | bytes 78368 | tf_op jit(solution)/shard_map/ppermute | solution.py:31
  23.5 0.3 slice_multiply_fusion.1
  23.8 0.1 fusion.172
  23.9 0.2 multiply_add_fusion.9
  24.1 0.2 multiply_add_fusion.8
  24.3 0.1 multiply_subtract_fusion.1
  24.4 0.2 fusion.53
  24.9 0.1 slice.1201
  25.0 0.1 maximum_select_fusion.3
  25.2 0.2 maximum_select_fusion.4
  25.3 0.2 slice_bitcast_fusion.11
  25.6 0.2 collective-permute-start.5
  25.8 0.2 fusion.297
  26.0 0.9 %collective-permute-done.5 = f32[2,6,1360]{2,0,1:T(2,128)S(1)} collective-permute-done((f32[2,6,1360]{2,0,1:T(2,128)S(1)}, f32[2,6,1360]{2,0,1:T(2,128)S(1)}, u32[]{:S(2)}, u32[]{:S(2)}) %collective-permute-start.5) | collective-permute-done | bytes 65312 | tf_op jit(solution)/shard_map/ppermute | solution.py:31
  27.0 0.3 slice_multiply_fusion.2
  27.4 0.2 multiply_add_fusion.14
  27.5 0.2 multiply_add_fusion.13
  27.7 0.1 multiply_subtract_fusion.2
  27.8 0.2 fusion.66
  28.2 0.1 slice.1253
  28.4 0.1 maximum_select_fusion.6
  28.6 0.2 slice_bitcast_fusion.15
  28.8 0.2 collective-permute-start.6
  29.1 0.2 fusion.298
  29.2 0.9 %collective-permute-done.6 = f32[2,6,1088]{2,0,1:T(2,128)S(1)} collective-permute-done((f32[2,6,1088]{2,0,1:T(2,128)S(1)}, f32[2,6,1088]{2,0,1:T(2,128)S(1)}, u32[]{:S(2)}, u32[]{:S(2)}) %collective-permute-start.6) | collective-permute-done | bytes 52256 | tf_op jit(solution)/shard_map/ppermute | solution.py:31
  30.2 0.2 slice_multiply_fusion.3
  30.5 0.1 multiply_add_fusion.19
  30.7 0.1 fusion.229
  30.8 0.1 multiply_subtract_fusion.3
  31.0 0.2 concatenate.123
  31.1 0.8 %slice.1286 = f32[4,8,8,128]{3,2,1,0:T(8,128)} slice(f32[4,8,8,136]{3,2,1,0:T(8,128)S(1)} %concatenate.123), slice={[0:4], [0:8], [0:8], [4:132]} | slice | bytes 262144 | tf_op jit(solution)/shard_map/slice | solution.py:193
  31.9 0.1 fusion.79
  32.3 0.7 %pad_maximum_fusion.16 = f32[2,8,8,128]{3,2,1,0:T(8,128)} fusion(f32[1,8,8,136]{3,2,1,0:T(8,128)S(1)} %concatenate.125, f32[1,8,8,136]{3,2,1,0:T(8,128)S(1)} %concatenate.124), kind=kLoop, calls=%fused_computation.191 | loop fusion | flops 16384 | bytes 135168 | tf_op jit(solution)/shard_map/concatenate | solution.py:152
  (86 shorter events, 4.0 us)
Async XLA Ops:
  0.6 0.8 %copy-start = (f32[2,8,8,128]{3,2,1,0:T(8,128)S(1)}, f32[2,8,8,128]{3,2,1,0:T(8,128)}, u32[]{:S(2)}) copy-start(f32[2,8,8,128]{3,2,1,0:T(8,128)} %param.4) | copy-start | bytes 196612
  1.5 5.9 %collective-permute-start.1 = (f32[3,8,4,128]{3,2,1,0:T(4,128)S(1)}, f32[3,8,4,128]{3,2,1,0:T(4,128)S(1)}, u32[]{:S(2)}, u32[]{:S(2)}) collective-permute-start(f32[3,8,4,128]{3,2,1,0:T(4,128)S(1)} %get-tuple-element.115), channel_id=1, source_target_pairs={{0,12},{4,0},{8,4},{12,8},{1,13},{5,1},{9,5},{13,9},{2,14},{6,2},{... | collective-permute-start | bytes 147464 | tf_op jit(solution)/shard_map/ppermute | solution.py:168
  5.4 5.0 %collective-permute-start = (f32[3,8,4,128]{3,2,1,0:T(4,128)S(1)}, f32[3,8,4,128]{3,2,1,0:T(4,128)S(1)}, u32[]{:S(2)}, u32[]{:S(2)}) collective-permute-start(f32[3,8,4,128]{3,2,1,0:T(4,128)S(1)} %get-tuple-element.114), channel_id=1, source_target_pairs={{0,4},{4,8},{8,12},{12,0},{1,5},{5,9},{9,13},{13,1},{2,6},{6,10},{... | collective-permute-start | bytes 147464 | tf_op jit(solution)/shard_map/ppermute | solution.py:167
  5.6 0.7 %copy-start.1 = (s32[32,3]{0,1:T(4,128)S(1)}, s32[32,3]{0,1:T(4,128)}, u32[]{:S(2)}) copy-start(s32[32,3]{0,1:T(4,128)} %param.5) | copy-start | bytes 1156
  10.6 6.2 %collective-permute-start.2 = (f32[3,4608]{1,0:T(4,128)S(1)}, f32[3,4608]{1,0:T(4,128)S(1)}, u32[]{:S(2)}, u32[]{:S(2)}) collective-permute-start(f32[3,4608]{1,0:T(4,128)S(1)} %reshape.927), channel_id=1, source_target_pairs={{1,0},{2,1},{3,2},{5,4},{6,5},{7,6},{9,8},{10,9},{11,10},{13,12},{... | collective-permute-start | bytes 165896 | tf_op jit(solution)/shard_map/ppermute | solution.py:171
  18.7 1.4 %collective-permute-start.3 = (f32[2,6,1904]{2,0,1:T(2,128)S(1)}, f32[2,6,1904]{2,0,1:T(2,128)S(1)}, u32[]{:S(2)}, u32[]{:S(2)}) collective-permute-start(f32[2,6,1904]{2,0,1:T(2,128)S(1)} %pad_maximum_fusion.9), channel_id=1, source_target_pairs={{0,16},{16,0},{1,17},{17,1},{2,18},{18,2},{3,19},{19,3},{4,20},{20... | collective-permute-start | bytes 274184 | tf_op jit(solution)/shard_map/ppermute | solution.py:31
  22.1 1.3 %collective-permute-start.4 = (f32[2,6,1632]{2,0,1:T(2,128)S(1)}, f32[2,6,1632]{2,0,1:T(2,128)S(1)}, u32[]{:S(2)}, u32[]{:S(2)}) collective-permute-start(f32[2,6,1632]{2,0,1:T(2,128)S(1)} %pad_maximum_fusion.12), channel_id=1, source_target_pairs={{0,16},{16,0},{1,17},{17,1},{2,18},{18,2},{3,19},{19,3},{4,20},{20... | collective-permute-start | bytes 235016 | tf_op jit(solution)/shard_map/ppermute | solution.py:31
  25.6 1.3 %collective-permute-start.5 = (f32[2,6,1360]{2,0,1:T(2,128)S(1)}, f32[2,6,1360]{2,0,1:T(2,128)S(1)}, u32[]{:S(2)}, u32[]{:S(2)}) collective-permute-start(f32[2,6,1360]{2,0,1:T(2,128)S(1)} %pad_maximum_fusion.15), channel_id=1, source_target_pairs={{0,16},{16,0},{1,17},{17,1},{2,18},{18,2},{3,19},{19,3},{4,20},{20... | collective-permute-start | bytes 195848 | tf_op jit(solution)/shard_map/ppermute | solution.py:31
  28.8 1.3 %collective-permute-start.6 = (f32[2,6,1088]{2,0,1:T(2,128)S(1)}, f32[2,6,1088]{2,0,1:T(2,128)S(1)}, u32[]{:S(2)}, u32[]{:S(2)}) collective-permute-start(f32[2,6,1088]{2,0,1:T(2,128)S(1)} %pad_maximum_fusion.17), channel_id=1, source_target_pairs={{0,16},{16,0},{1,17},{17,1},{2,18},{18,2},{3,19},{19,3},{4,20},{20... | collective-permute-start | bytes 156680 | tf_op jit(solution)/shard_map/ppermute | solution.py:31

commit v13 on v12

--- a/solution.py
+++ b/solution.py
@@ -188,9 +188,27 @@
     ext = step(ext, 3 - rim_y, post_z, lift)
     ext = edge_below(ext, lift - low - 1, bottom_brick)
     ext = edge_at(ext, cells_z + lift - low, top_brick)
-    fields = step(ext, 4 - rim_y, post_z, lift)
-    fields = fields.reshape(nf, cells_x, cells_y, stride)[..., lift - low : lift - low + cells_z]
-    return (fields[:4], fields[4:])
+    grid = ext.reshape(nf, cells_x, cells_y + 2, stride)
+    first = lift - low
+    fields = grid[:, :, 1:-1, first : first + cells_z]
+    xlo, xhi = x_halos(fields)
+    side = [
+        jnp.concatenate([fields[:, 1:], xhi[:, None]], 1),
+        jnp.concatenate([xlo[:, None], fields[:, :-1]], 1),
+        grid[:, :, 2:, first : first + cells_z],
+        grid[:, :, :-2, first : first + cells_z],
+        grid[:, :, 1:-1, first + 1 : first + 1 + cells_z],
+        grid[:, :, 1:-1, first - 1 : first - 1 + cells_z],
+    ]
+    ypos = jnp.arange(cells_y, dtype=jnp.int32)
+    zlast = post_z[first : first + cells_z]
+    phi_new = jnp.where(
+        active(ypos, zlast)[None, None],
+        phase_update(fields, side, under_z[first : first + cells_z], 0, depth),
+        fields[:4],
+    )
+    mu_new = chem_update(fields, side, fields[:4], phi_new)
+    return (phi_new, mu_new)
 
 
 def solution(mesh):

time: 33.3 us -> 32.9 us (0.988)
  waiting for transfers between devices: 10.3 us -> 8.37 us
  other arithmetic: 8.82 us -> 9.88 us
  local copies, waits for them, and re-layouts: 6.63 us -> 7.09 us
    ppermute x1, waiting for transfers between devices: 3.01 us -> 0.01 us  [shards(): below_y = lax.ppermute(start[:, :, -rim_y:], 'gy', ring('gy', 1))]
    ppermute x1, starting transfers between devices: 0.01 us -> 2.99 us  [shards(): below_y = lax.ppermute(start[:, :, -rim_y:], 'gy', ring('gy', 1))]
    ppermute x1, starting transfers between devices: 3.95 us -> 1.02 us  [shards(): above_y = lax.ppermute(start[:, :, :rim_y], 'gy', ring('gy', -1))]
    concatenate x0 -> x2, local copies, waits for them, and re-layouts: none -> 1.33 us  [the longest x1 0.67 us: edge_at(): up = jnp.concatenate([ext[..., :1], ext[..., :-1]], 2)]
    ppermute x1, waiting for transfers between devices: 0.01 us -> 0.81 us  [shards(): above_y = lax.ppermute(start[:, :, :rim_y], 'gy', ring('gy', -1))]
    concatenate x3 -> x2, other arithmetic: 0.79 us -> 0.06 us  [step(): return jnp.concatenate([phi_new, mu_new], 0)]
    sub x4, other arithmetic: 0.54 us -> 1.19 us  [chem_update(): delta = shape_fn(phi_new) - shape_fn(phi_old)]
    another operation x0 -> x1, other arithmetic: none -> 0.64 us  [chem_update(): return jnp.stack(result)]
where the time goes in v13:
time: 32.9 us; the launch traced here: 32.7 us
  other arithmetic  9.88 us (30%)
  waiting for transfers between devices  8.37 us (25%)
  local copies, waits for them, and re-layouts  7.09 us (22%)
  starting transfers between devices  6.03 us (18%)
  between operations  1.37 us (4%)
    ppermute x1, waiting for transfers between devices, shards(): lax.ppermute(wide[..., :count].reshape(wide.shape[0], -1), 'gz', line('gz...  3.85 us
    ppermute x4, waiting for transfers between devices, x_halos(): got = lax.ppermute(pair, 'gx', ring('gx', 1))  3.71 us
    ppermute x1, starting transfers between devices, shards(): below_y = lax.ppermute(start[:, :, -rim_y:], 'gy', ring('gy', 1))  2.99 us
    ppermute x1, starting transfers between devices, shards(): lax.ppermute(wide[..., :count].reshape(wide.shape[0], -1), 'gz', line('gz...  1.29 us
    add x7, other arithmetic, phase_update(): phi[phase] + DT * (rates[phase] - mean_rate)  1.21 us
    sub x4, other arithmetic, chem_update(): delta = shape_fn(phi_new) - shape_fn(phi_old)  1.19 us
    mul x4, other arithmetic, phase_update(): square = phi * phi  1.13 us
    ppermute x1, starting transfers between devices, shards(): above_y = lax.ppermute(start[:, :, :rim_y], 'gy', ring('gy', -1))  1.02 us
  transfers between devices with their start and end apart: 7, of which 6 were waited for; matrix products, arithmetic and copies ran while one was open for 10% of the time, Pallas kernels for 0%

profile of v13, /device:TPU:0, one launch (start us, length us, event | category | flops | bytes accessed | tf_op | source)
XLA Modules:
  0.0 32.7 jit_solution(14566178308640956497)
XLA Ops:
  0.6 0.8 %convert_bitcast_fusion = f32[1,8,8,128]{3,2,1,0:T(8,128)S(1)} fusion(s32[8,8,128]{2,1,0:T(8,128)} %param.3), kind=kLoop, calls=%fused_computation.460 | loop fusion | flops 8192 | bytes 65536 | tf_op jit(solution)/shard_map/broadcast_in_dim | solution.py:165
  1.5 3.0 %collective-permute-start = (f32[3,8,4,128]{3,2,1,0:T(4,128)S(1)}, f32[3,8,4,128]{3,2,1,0:T(4,128)S(1)}, u32[]{:S(2)}, u32[]{:S(2)}) collective-permute-start(f32[3,8,4,128]{3,2,1,0:T(4,128)S(1)} %get-tuple-element.116), channel_id=1, source_target_pairs={{0,4},{4,8},{8,12},{12,0},{1,5},{5,9},{9,13},{13,1},{2,6},{6,10},{... | collective-permute-start | bytes 147464 | tf_op jit(solution)/shard_map/ppermute | solution.py:167
  4.5 1.0 %collective-permute-start.1 = (f32[3,8,4,128]{3,2,1,0:T(4,128)S(1)}, f32[3,8,4,128]{3,2,1,0:T(4,128)S(1)}, u32[]{:S(2)}, u32[]{:S(2)}) collective-permute-start(f32[3,8,4,128]{3,2,1,0:T(4,128)S(1)} %get-tuple-element.117), channel_id=1, source_target_pairs={{0,12},{4,0},{8,4},{12,8},{1,13},{5,1},{9,5},{13,9},{2,14},{6,2},{... | collective-permute-start | bytes 147464 | tf_op jit(solution)/shard_map/ppermute | solution.py:168
  5.8 0.6 %copy-done.1 = s32[32,3]{0,1:T(4,128)S(1)} copy-done((s32[32,3]{0,1:T(4,128)S(1)}, s32[32,3]{0,1:T(4,128)}, u32[]{:S(2)}) %copy-start.1) | copy-done | bytes 408
  6.7 0.2 and_reduce_fusion
  6.8 0.2 and_reduce_fusion.1
  7.5 0.1 and_reduce_fusion.2
  7.8 0.8 %collective-permute-done.1 = f32[3,8,4,128]{3,2,1,0:T(4,128)S(1)} collective-permute-done((f32[3,8,4,128]{3,2,1,0:T(4,128)S(1)}, f32[3,8,4,128]{3,2,1,0:T(4,128)S(1)}, u32[]{:S(2)}, u32[]{:S(2)}) %collective-permute-start.1) | collective-permute-done | bytes 49184 | tf_op jit(solution)/shard_map/ppermute | solution.py:168
  8.6 0.2 reshape.852
  8.8 1.3 %collective-permute-start.2 = (f32[3,4608]{1,0:T(4,128)S(1)}, f32[3,4608]{1,0:T(4,128)S(1)}, u32[]{:S(2)}, u32[]{:S(2)}) collective-permute-start(f32[3,4608]{1,0:T(4,128)S(1)} %reshape.852), channel_id=1, source_target_pairs={{1,0},{2,1},{3,2},{5,4},{6,5},{7,6},{9,8},{10,9},{11,10},{13,12},{... | collective-permute-start | bytes 165896 | tf_op jit(solution)/shard_map/ppermute | solution.py:171
  11.2 3.9 %collective-permute-done.2 = f32[3,4608]{1,0:T(4,128)S(1)} collective-permute-done((f32[3,4608]{1,0:T(4,128)S(1)}, f32[3,4608]{1,0:T(4,128)S(1)}, u32[]{:S(2)}, u32[]{:S(2)}) %collective-permute-start.2) | collective-permute-done | bytes 55328 | tf_op jit(solution)/shard_map/ppermute | solution.py:171
  15.0 0.2 reshape.853
  15.4 0.1 pad_maximum_fusion.4
  15.6 0.1 reshape.854
  16.1 0.2 concatenate.106
  16.3 0.2 maximum_select_fusion.1
  16.5 0.3 slice_bitcast_fusion.3
  17.0 0.3 fusion.301
  17.2 1.0 %collective-permute-done.3 = f32[2,6,1904]{2,0,1:T(2,128)S(1)} collective-permute-done((f32[2,6,1904]{2,0,1:T(2,128)S(1)}, f32[2,6,1904]{2,0,1:T(2,128)S(1)}, u32[]{:S(2)}, u32[]{:S(2)}) %collective-permute-start.3) | collective-permute-done | bytes 91424 | tf_op jit(solution)/shard_map/ppermute | solution.py:31
  18.3 0.3 %slice_multiply_fusion = (f32[4,8,1904]{2,1,0:T(8,128)S(1)}, f32[4,8,1904]{2,1,0:T(8,128)S(1)}) fusion(f32[6,8,2176]{2,1,0:T(8,128)S(1)} %maximum_select_fusion.1, f32[6,7,1904]{2,1,0:T(8,128)S(1)} %get-tuple-element.83, f32[6,1,1904]{2,1,0:T(1,128)S(1)} %get-tuple-element.119, f32[6,1,1904]{2,1,0:T(1,128)S(1)} %get-tuple-element.118, ...), kind=kLoop, calls=%fused_computation.80 | loop fusion | flops 609280 | bytes 2437120 | tf_op jit(solution)/shard_map/mul | solution.py:64
  18.6 0.1 fusion.133
  18.8 0.2 multiply_add_fusion.4
  19.0 0.2 multiply_add_fusion.3
  19.2 0.2 multiply_subtract_fusion
  19.3 0.2 fusion.43
  19.7 0.2 maximum_select_fusion.2
  19.9 0.2 slice_bitcast_fusion.7
  20.2 0.2 collective-permute-start.4
  20.4 0.2 fusion.302
  20.7 0.9 %collective-permute-done.4 = f32[2,6,1632]{2,0,1:T(2,128)S(1)} collective-permute-done((f32[2,6,1632]{2,0,1:T(2,128)S(1)}, f32[2,6,1632]{2,0,1:T(2,128)S(1)}, u32[]{:S(2)}, u32[]{:S(2)}) %collective-permute-start.4) | collective-permute-done | bytes 78368 | tf_op jit(solution)/shard_map/ppermute | solution.py:31
  21.6 0.3 slice_multiply_fusion.1
  22.0 0.2 multiply_add_fusion.9
  22.2 0.2 multiply_add_fusion.8
  22.4 0.1 multiply_subtract_fusion.1
  22.6 0.2 fusion.56
  23.0 0.1 slice.1195
  23.2 0.1 maximum_select_fusion.4
  23.3 0.2 maximum_select_fusion.5
  23.5 0.2 slice_bitcast_fusion.11
  23.8 0.2 collective-permute-start.5
  24.0 0.2 fusion.303
  24.2 0.9 %collective-permute-done.5 = f32[2,6,1360]{2,0,1:T(2,128)S(1)} collective-permute-done((f32[2,6,1360]{2,0,1:T(2,128)S(1)}, f32[2,6,1360]{2,0,1:T(2,128)S(1)}, u32[]{:S(2)}, u32[]{:S(2)}) %collective-permute-start.5) | collective-permute-done | bytes 65312 | tf_op jit(solution)/shard_map/ppermute | solution.py:31
  25.1 0.3 slice_multiply_fusion.2
  25.5 0.2 multiply_add_fusion.14
  25.7 0.2 multiply_add_fusion.13
  25.9 0.1 multiply_subtract_fusion.2
  26.0 0.2 fusion.69
  26.3 0.1 slice.1247
  26.5 0.4 %concatenate.125 = f32[4,8,10,136]{3,2,1,0:T(8,128)S(1)} reshape(f32[4,8,1360]{2,1,0:T(8,128)S(1)} %get-tuple-element.14) | data formatting | bytes 348160 | tf_op jit(solution)/shard_map/concatenate | solution.py:152
  26.9 0.1 concatenate.126
  27.1 0.1 concatenate.127
  27.3 0.1 pad_maximum_fusion.3
  27.4 0.7 %concatenate.123 = f32[6,8,10,136]{3,2,1,0:T(8,128)S(1)} reshape(f32[6,8,1360]{2,1,0:T(8,128)S(1)} %pad_maximum_fusion.3) | data formatting | bytes 522240 | tf_op jit(solution)/shard_map/concatenate | solution.py:158
  28.1 0.7 %concatenate.124 = f32[6,8,10,136]{3,2,1,0:T(8,128)S(1)} reshape(f32[6,8,1360]{2,1,0:T(8,128)S(1)} %get-tuple-element.12) | data formatting | bytes 522240 | tf_op jit(solution)/shard_map/concatenate | solution.py:162
  28.8 0.3 fusion
  29.1 0.2 collective-permute-start.6
  29.4 0.2 fusion.300
  29.5 0.9 %collective-permute-done.6 = f32[2,6,8,128]{3,2,1,0:T(8,128)S(1)} collective-permute-done((f32[2,6,8,128]{3,2,1,0:T(8,128)S(1)}, f32[2,6,8,128]{3,2,1,0:T(8,128)S(1)}, u32[]{:S(2)}, u32[]{:S(2)}) %collective-permute-start.6) | collective-permute-done | bytes 49184 | tf_op jit(solution)/shard_map/ppermute | solution.py:31
  30.4 0.2 slice_multiply_fusion.3
  30.8 0.1 multiply_add_fusion.19
  30.9 0.1 fusion.232
  31.1 0.8 %multiply_subtract_fusion.3 = (f32[4,8,8,128]{3,2,1,0:T(8,128)S(1)}, f32[4,8,8,128]{3,2,1,0:T(8,128)}) fusion(f32[6,8,10,136]{3,2,1,0:T(8,128)S(1)} %fusion, f32[1,8,8,128]{3,2,1,0:T(8,128)S(1)} %get-tuple-element.51, f32[1,8,8,128]{3,2,1,0:T(8,128)S(1)} %get-tuple-element.52, f32[1,8,8,128]{3,2,1,0:T(8,128)S(1)} %get-tuple-element.53, ...), kind=kLoop, calls=%fused_computation.108 | loop fusion | flops 425984 | bytes 525312 | tf_op jit(solution)/shard_map/sub | solution.py:92
  31.9 0.2 fusion.82
  32.1 0.6 %pad_maximum_fusion.18 = f32[2,8,8,128]{3,2,1,0:T(8,128)} fusion(f32[1,8,8,128]{3,2,1,0:T(8,128)S(1)} %get-tuple-element.43, f32[1,8,8,128]{3,2,1,0:T(8,128)S(1)} %get-tuple-element.42), kind=kLoop, calls=%fused_computation.196 | loop fusion | flops 16384 | bytes 131072 | tf_op jit(solution)/shard_map/stack | solution.py:102
  (89 shorter events, 4.3 us)
Async XLA Ops:
  0.6 0.8 %copy-start = (f32[2,8,8,128]{3,2,1,0:T(8,128)S(1)}, f32[2,8,8,128]{3,2,1,0:T(8,128)}, u32[]{:S(2)}) copy-start(f32[2,8,8,128]{3,2,1,0:T(8,128)} %param.4) | copy-start | bytes 196612
  1.5 6.3 %collective-permute-start = (f32[3,8,4,128]{3,2,1,0:T(4,128)S(1)}, f32[3,8,4,128]{3,2,1,0:T(4,128)S(1)}, u32[]{:S(2)}, u32[]{:S(2)}) collective-permute-start(f32[3,8,4,128]{3,2,1,0:T(4,128)S(1)} %get-tuple-element.116), channel_id=1, source_target_pairs={{0,4},{4,8},{8,12},{12,0},{1,5},{5,9},{9,13},{13,1},{2,6},{6,10},{... | collective-permute-start | bytes 147464 | tf_op jit(solution)/shard_map/ppermute | solution.py:167
  4.5 4.1 %collective-permute-start.1 = (f32[3,8,4,128]{3,2,1,0:T(4,128)S(1)}, f32[3,8,4,128]{3,2,1,0:T(4,128)S(1)}, u32[]{:S(2)}, u32[]{:S(2)}) collective-permute-start(f32[3,8,4,128]{3,2,1,0:T(4,128)S(1)} %get-tuple-element.117), channel_id=1, source_target_pairs={{0,12},{4,0},{8,4},{12,8},{1,13},{5,1},{9,5},{13,9},{2,14},{6,2},{... | collective-permute-start | bytes 147464 | tf_op jit(solution)/shard_map/ppermute | solution.py:168
  5.7 0.7 %copy-start.1 = (s32[32,3]{0,1:T(4,128)S(1)}, s32[32,3]{0,1:T(4,128)}, u32[]{:S(2)}) copy-start(s32[32,3]{0,1:T(4,128)} %param.5) | copy-start | bytes 1156
  8.8 6.2 %collective-permute-start.2 = (f32[3,4608]{1,0:T(4,128)S(1)}, f32[3,4608]{1,0:T(4,128)S(1)}, u32[]{:S(2)}, u32[]{:S(2)}) collective-permute-start(f32[3,4608]{1,0:T(4,128)S(1)} %reshape.852), channel_id=1, source_target_pairs={{1,0},{2,1},{3,2},{5,4},{6,5},{7,6},{9,8},{10,9},{11,10},{13,12},{... | collective-permute-start | bytes 165896 | tf_op jit(solution)/shard_map/ppermute | solution.py:171
  16.9 1.4 %collective-permute-start.3 = (f32[2,6,1904]{2,0,1:T(2,128)S(1)}, f32[2,6,1904]{2,0,1:T(2,128)S(1)}, u32[]{:S(2)}, u32[]{:S(2)}) collective-permute-start(f32[2,6,1904]{2,0,1:T(2,128)S(1)} %pad_maximum_fusion.11), channel_id=1, source_target_pairs={{0,16},{16,0},{1,17},{17,1},{2,18},{18,2},{3,19},{19,3},{4,20},{20... | collective-permute-start | bytes 274184 | tf_op jit(solution)/shard_map/ppermute | solution.py:31
  20.2 1.3 %collective-permute-start.4 = (f32[2,6,1632]{2,0,1:T(2,128)S(1)}, f32[2,6,1632]{2,0,1:T(2,128)S(1)}, u32[]{:S(2)}, u32[]{:S(2)}) collective-permute-start(f32[2,6,1632]{2,0,1:T(2,128)S(1)} %pad_maximum_fusion.14), channel_id=1, source_target_pairs={{0,16},{16,0},{1,17},{17,1},{2,18},{18,2},{3,19},{19,3},{4,20},{20... | collective-permute-start | bytes 235016 | tf_op jit(solution)/shard_map/ppermute | solution.py:31
  23.8 1.3 %collective-permute-start.5 = (f32[2,6,1360]{2,0,1:T(2,128)S(1)}, f32[2,6,1360]{2,0,1:T(2,128)S(1)}, u32[]{:S(2)}, u32[]{:S(2)}) collective-permute-start(f32[2,6,1360]{2,0,1:T(2,128)S(1)} %pad_maximum_fusion.15), channel_id=1, source_target_pairs={{0,16},{16,0},{1,17},{17,1},{2,18},{18,2},{3,19},{19,3},{4,20},{20... | collective-permute-start | bytes 195848 | tf_op jit(solution)/shard_map/ppermute | solution.py:31
  29.1 1.3 %collective-permute-start.6 = (f32[2,6,8,128]{3,2,1,0:T(8,128)S(1)}, f32[2,6,8,128]{3,2,1,0:T(8,128)S(1)}, u32[]{:S(2)}, u32[]{:S(2)}) collective-permute-start(f32[2,6,8,128]{3,2,1,0:T(8,128)S(1)} %pad_maximum_fusion.20), channel_id=1, source_target_pairs={{0,16},{16,0},{1,17},{17,1},{2,18},{18,2},{3,19},{19,3},{4,20},{20... | collective-permute-start | bytes 147464 | tf_op jit(solution)/shard_map/ppermute | solution.py:31

commit v14 on v13

--- a/solution.py
+++ b/solution.py
@@ -134,12 +134,17 @@
     lane_z = jnp.arange(stride, dtype=jnp.int32)
     under_z = base_z + low + lane_z
 
-    def step(ext, first_y, zpos, offset):
+    def step(ext, first_y, zpos, offset, x_rim=False):
         size = ext.shape[2] - 2 * stride
+        if x_rim:
+            rim = ext[..., stride : stride + size]
+            xlo, xhi = rim[:, 0], rim[:, -1]
+            ext = ext[:, 1:-1]
         fields = ext[..., stride : stride + size]
         nrows = size // stride
         ypos = first_y + jnp.arange(nrows, dtype=jnp.int32)
-        xlo, xhi = x_halos(fields)
+        if not x_rim:
+            xlo, xhi = x_halos(fields)
         side = neighbours(ext, xlo, xhi, stride)
         on = active(ypos, zpos).reshape(-1)
         zflat = jnp.tile(under_z, nrows)
@@ -164,6 +169,8 @@
 
     start = jnp.concatenate([labels.astype(jnp.float32)[None], mu_start], 0)
     nf = 4 + mu_start.shape[0]
+    xlo, xhi = x_halos(start)
+    start = jnp.concatenate([xlo[:, None], start, xhi[:, None]], 1)
     below_y = lax.ppermute(start[:, :, -rim_y:], "gy", ring("gy", 1))
     above_y = lax.ppermute(start[:, :, :rim_y], "gy", ring("gy", -1))
     wide = jnp.concatenate([below_y, start, above_y], 2)
@@ -178,7 +185,7 @@
     pre_z = base_z + low + lane_z
     post_z = pre_z - lift
     ext = edge_at(ext, cells_z - low, top_brick)
-    ext = step(ext, 1 - rim_y, pre_z, 0)
+    ext = step(ext, 1 - rim_y, pre_z, 0, x_rim=True)
     ext = edge_at(ext, cells_z - low, top_brick)
     ext = step(ext, 2 - rim_y, pre_z, 0)
     liquid = jnp.where(lax.broadcasted_iota(jnp.int32, ext.shape, 0) == 0, 1.0, 0.0).astype(jnp.float32)

time: 32.9 us -> 36.5 us (1.11)
  waiting for transfers between devices: 8.37 us -> 12 us
    ppermute x1, waiting for transfers between devices: 0.01 us -> 2.57 us  [shards(): below_y = lax.ppermute(start[:, :, -rim_y:], 'gy', ring('gy', 1))]
    ppermute x1, waiting for transfers between devices: 3.85 us -> 5.01 us  [shards(): lax.ppermute(wide[..., :count].reshape(wide.shape[0], -1), 'gz', line('gz...]
    ppermute x4, waiting for transfers between devices: 3.71 us -> 2.84 us  [x_halos(): got = lax.ppermute(pair, 'gx', ring('gx', 1))]
    ppermute x1, waiting for transfers between devices: 0.81 us -> 1.57 us  [shards(): above_y = lax.ppermute(start[:, :, :rim_y], 'gy', ring('gy', -1))]
    ppermute x1, starting transfers between devices: 2.99 us -> 2.57 us  [shards(): below_y = lax.ppermute(start[:, :, -rim_y:], 'gy', ring('gy', 1))]
    another operation x4 -> x3, local copies, waits for them, and re-layouts: 0.78 us -> 0.52 us  [x_halos(): pair = jnp.stack([block[:, -1], block[:, 0]])]
  transfers between devices with their start and end apart: 7 -> 7, of which waited for: 6 -> 6; matrix products, arithmetic and copies ran while one was open for 10% -> 8% of each run, Pallas kernels for 0% -> 0%
where the time goes in v14:
time: 36.5 us; the launch traced here: 36.3 us
  waiting for transfers between devices  12 us (33%)
  other arithmetic  10.1 us (28%)
  local copies, waits for them, and re-layouts  6.91 us (19%)
  starting transfers between devices  5.89 us (16%)
  between operations  1.37 us (4%)
    ppermute x1, waiting for transfers between devices, shards(): lax.ppermute(wide[..., :count].reshape(wide.shape[0], -1), 'gz', line('gz...  5.01 us
    ppermute x4, waiting for transfers between devices, x_halos(): got = lax.ppermute(pair, 'gx', ring('gx', 1))  2.84 us
    ppermute x1, waiting for transfers between devices, shards(): below_y = lax.ppermute(start[:, :, -rim_y:], 'gy', ring('gy', 1))  2.57 us
    ppermute x1, starting transfers between devices, shards(): below_y = lax.ppermute(start[:, :, -rim_y:], 'gy', ring('gy', 1))  2.57 us
    ppermute x1, waiting for transfers between devices, shards(): above_y = lax.ppermute(start[:, :, :rim_y], 'gy', ring('gy', -1))  1.57 us
    ppermute x1, starting transfers between devices, shards(): lax.ppermute(wide[..., :count].reshape(wide.shape[0], -1), 'gz', line('gz...  1.29 us
    mul x4, other arithmetic, phase_update(): square = phi * phi  1.24 us
    add x7, other arithmetic, phase_update(): phi[phase] + DT * (rates[phase] - mean_rate)  1.21 us
  transfers between devices with their start and end apart: 7, of which 6 were waited for; matrix products, arithmetic and copies ran while one was open for 8% of the time, Pallas kernels for 0%

profile of v14, /device:TPU:0, one launch (start us, length us, event | category | flops | bytes accessed | tf_op | source)
XLA Modules:
  0.0 36.3 jit_solution(171769207294338375)
XLA Ops:
  0.6 0.8 %convert_bitcast_fusion = f32[1,8,8,128]{3,2,1,0:T(8,128)S(1)} fusion(s32[8,8,128]{2,1,0:T(8,128)} %param.3), kind=kLoop, calls=%fused_computation.438 | loop fusion | flops 8192 | bytes 65536 | tf_op jit(solution)/shard_map/broadcast_in_dim | solution.py:170
  1.5 0.5 %collective-permute-start = (f32[2,3,8,128]{3,2,1,0:T(8,128)S(1)}, f32[2,3,8,128]{3,2,1,0:T(8,128)S(1)}, u32[]{:S(2)}, u32[]{:S(2)}) collective-permute-start(f32[2,3,8,128]{3,2,1,0:T(8,128)S(1)} %pad_maximum_fusion.18), channel_id=1, source_target_pairs={{0,16},{16,0},{1,17},{17,1},{2,18},{18,2},{3,19},{19,3},{4,20},{20... | collective-permute-start | bytes 73736 | tf_op jit(solution)/shard_map/ppermute | solution.py:31
  2.2 0.6 %copy-done.1 = s32[32,3]{0,1:T(4,128)S(1)} copy-done((s32[32,3]{0,1:T(4,128)S(1)}, s32[32,3]{0,1:T(4,128)}, u32[]{:S(2)}) %copy-start.1) | copy-done | bytes 408
  3.1 0.2 and_reduce_fusion
  3.3 0.2 and_reduce_fusion.1
  3.9 0.1 and_reduce_fusion.2
  5.2 2.6 %collective-permute-start.1 = (f32[3,10,4,128]{3,2,1,0:T(4,128)S(1)}, f32[3,10,4,128]{3,2,1,0:T(4,128)S(1)}, u32[]{:S(2)}, u32[]{:S(2)}) collective-permute-start(f32[3,10,4,128]{3,2,1,0:T(4,128)S(1)} %get-tuple-element.112), channel_id=1, source_target_pairs={{0,4},{4,8},{8,12},{12,0},{1,5},{5,9},{9,13},{13,1},{2,6},{6,10},{... | collective-permute-start | bytes 184328 | tf_op jit(solution)/shard_map/ppermute | solution.py:174
  7.8 1.0 %collective-permute-start.2 = (f32[3,10,4,128]{3,2,1,0:T(4,128)S(1)}, f32[3,10,4,128]{3,2,1,0:T(4,128)S(1)}, u32[]{:S(2)}, u32[]{:S(2)}) collective-permute-start(f32[3,10,4,128]{3,2,1,0:T(4,128)S(1)} %get-tuple-element.113), channel_id=1, source_target_pairs={{0,12},{4,0},{8,4},{12,8},{1,13},{5,1},{9,5},{13,9},{2,14},{6,2},{... | collective-permute-start | bytes 184328 | tf_op jit(solution)/shard_map/ppermute | solution.py:175
  8.8 2.6 %collective-permute-done.1 = f32[3,10,4,128]{3,2,1,0:T(4,128)S(1)} collective-permute-done((f32[3,10,4,128]{3,2,1,0:T(4,128)S(1)}, f32[3,10,4,128]{3,2,1,0:T(4,128)S(1)}, u32[]{:S(2)}, u32[]{:S(2)}) %collective-permute-start.1) | collective-permute-done | bytes 61472 | tf_op jit(solution)/shard_map/ppermute | solution.py:174
  11.4 1.6 %collective-permute-done.2 = f32[3,10,4,128]{3,2,1,0:T(4,128)S(1)} collective-permute-done((f32[3,10,4,128]{3,2,1,0:T(4,128)S(1)}, f32[3,10,4,128]{3,2,1,0:T(4,128)S(1)}, u32[]{:S(2)}, u32[]{:S(2)}) %collective-permute-start.2) | collective-permute-done | bytes 61472 | tf_op jit(solution)/shard_map/ppermute | solution.py:175
  13.0 0.2 reshape.852
  13.2 1.3 %collective-permute-start.3 = (f32[3,5760]{1,0:T(4,128)S(1)}, f32[3,5760]{1,0:T(4,128)S(1)}, u32[]{:S(2)}, u32[]{:S(2)}) collective-permute-start(f32[3,5760]{1,0:T(4,128)S(1)} %reshape.852), channel_id=1, source_target_pairs={{1,0},{2,1},{3,2},{5,4},{6,5},{7,6},{9,8},{10,9},{11,10},{13,12},{... | collective-permute-start | bytes 207368 | tf_op jit(solution)/shard_map/ppermute | solution.py:178
  14.7 5.0 %collective-permute-done.3 = f32[3,5760]{1,0:T(4,128)S(1)} collective-permute-done((f32[3,5760]{1,0:T(4,128)S(1)}, f32[3,5760]{1,0:T(4,128)S(1)}, u32[]{:S(2)}, u32[]{:S(2)}) %collective-permute-start.3) | collective-permute-done | bytes 69152 | tf_op jit(solution)/shard_map/ppermute | solution.py:178
  19.7 0.3 reshape.853
  20.1 0.1 pad_maximum_fusion.1
  20.4 0.2 reshape.858
  20.5 0.2 reshape.859
  20.7 0.2 reshape.860
  20.9 0.2 reshape.861
  21.0 0.2 reshape.862
  21.4 0.3 maximum_select_fusion
  21.7 0.4 %slice_multiply_fusion = (f32[4,8,1904]{2,1,0:T(8,128)S(1)}, f32[4,8,1904]{2,1,0:T(8,128)S(1)}) fusion(f32[6,10,2176]{2,1,0:T(8,128)S(1)} %maximum_select_fusion), kind=kLoop, calls=%fused_computation.71 | loop fusion | flops 487424 | bytes 2193408 | tf_op jit(solution)/shard_map/mul | solution.py:64
  22.2 0.2 multiply_add_fusion.4
  22.4 0.2 multiply_add_fusion.3
  22.7 0.2 multiply_subtract_fusion
  22.8 0.3 fusion.36
  23.2 0.2 maximum_select_fusion.2
  23.4 0.2 slice_bitcast_fusion.3
  23.8 0.2 fusion.288
  24.1 1.0 %collective-permute-done.4 = f32[2,6,1632]{2,0,1:T(2,128)S(1)} collective-permute-done((f32[2,6,1632]{2,0,1:T(2,128)S(1)}, f32[2,6,1632]{2,0,1:T(2,128)S(1)}, u32[]{:S(2)}, u32[]{:S(2)}) %collective-permute-start.4) | collective-permute-done | bytes 78368 | tf_op jit(solution)/shard_map/ppermute | solution.py:31
  25.1 0.3 slice_multiply_fusion.1
  25.6 0.2 multiply_add_fusion.9
  25.8 0.2 multiply_add_fusion.8
  25.9 0.1 multiply_subtract_fusion.1
  26.1 0.2 fusion.47
  26.5 0.1 slice.1200
  26.7 0.1 maximum_select_fusion.4
  26.8 0.2 maximum_select_fusion.5
  27.0 0.2 slice_bitcast_fusion.7
  27.3 0.2 collective-permute-start.5
  27.5 0.2 fusion.289
  27.7 0.9 %collective-permute-done.5 = f32[2,6,1360]{2,0,1:T(2,128)S(1)} collective-permute-done((f32[2,6,1360]{2,0,1:T(2,128)S(1)}, f32[2,6,1360]{2,0,1:T(2,128)S(1)}, u32[]{:S(2)}, u32[]{:S(2)}) %collective-permute-start.5) | collective-permute-done | bytes 65312 | tf_op jit(solution)/shard_map/ppermute | solution.py:31
  28.7 0.3 slice_multiply_fusion.2
  29.1 0.2 multiply_add_fusion.14
  29.2 0.2 multiply_add_fusion.13
  29.4 0.1 multiply_subtract_fusion.2
  29.5 0.2 fusion.60
  29.8 0.1 slice.1252
  30.0 0.4 %concatenate.123 = f32[4,8,10,136]{3,2,1,0:T(8,128)S(1)} reshape(f32[4,8,1360]{2,1,0:T(8,128)S(1)} %get-tuple-element.14) | data formatting | bytes 348160 | tf_op jit(solution)/shard_map/concatenate | solution.py:157
  30.5 0.1 concatenate.124
  30.6 0.1 concatenate.125
  30.8 0.1 pad_maximum_fusion.4
  31.0 0.7 %concatenate.121 = f32[6,8,10,136]{3,2,1,0:T(8,128)S(1)} reshape(f32[6,8,1360]{2,1,0:T(8,128)S(1)} %pad_maximum_fusion.4) | data formatting | bytes 522240 | tf_op jit(solution)/shard_map/concatenate | solution.py:163
  31.6 0.7 %concatenate.122 = f32[6,8,10,136]{3,2,1,0:T(8,128)S(1)} reshape(f32[6,8,1360]{2,1,0:T(8,128)S(1)} %get-tuple-element.12) | data formatting | bytes 522240 | tf_op jit(solution)/shard_map/concatenate | solution.py:167
  32.3 0.3 fusion.1
  32.7 0.2 collective-permute-start.6
  32.9 0.2 fusion.287
  33.1 0.9 %collective-permute-done.6 = f32[2,6,8,128]{3,2,1,0:T(8,128)S(1)} collective-permute-done((f32[2,6,8,128]{3,2,1,0:T(8,128)S(1)}, f32[2,6,8,128]{3,2,1,0:T(8,128)S(1)}, u32[]{:S(2)}, u32[]{:S(2)}) %collective-permute-start.6) | collective-permute-done | bytes 49184 | tf_op jit(solution)/shard_map/ppermute | solution.py:31
  34.0 0.2 slice_multiply_fusion.3
  34.3 0.1 multiply_add_fusion.19
  34.5 0.1 fusion.218
  34.6 0.8 %multiply_subtract_fusion.3 = (f32[4,8,8,128]{3,2,1,0:T(8,128)S(1)}, f32[4,8,8,128]{3,2,1,0:T(8,128)}) fusion(f32[6,8,10,136]{3,2,1,0:T(8,128)S(1)} %fusion.1, f32[1,8,8,128]{3,2,1,0:T(8,128)S(1)} %get-tuple-element.64, f32[1,8,8,128]{3,2,1,0:T(8,128)S(1)} %get-tuple-element.65, f32[1,8,8,128]{3,2,1,0:T(8,128)S(1)} %get-tuple-element.66, ...), kind=kLoop, calls=%fused_computation.102 | loop fusion | flops 425984 | bytes 525312 | tf_op jit(solution)/shard_map/sub | solution.py:92
  35.4 0.2 fusion.73
  35.6 0.6 %pad_maximum_fusion.16 = f32[2,8,8,128]{3,2,1,0:T(8,128)} fusion(f32[1,8,8,128]{3,2,1,0:T(8,128)S(1)} %get-tuple-element.45, f32[1,8,8,128]{3,2,1,0:T(8,128)S(1)} %get-tuple-element.44), kind=kLoop, calls=%fused_computation.182 | loop fusion | flops 16384 | bytes 131072 | tf_op jit(solution)/shard_map/stack | solution.py:102
  (89 shorter events, 4.0 us)
Async XLA Ops:
  0.6 0.8 %copy-start = (f32[2,8,8,128]{3,2,1,0:T(8,128)S(1)}, f32[2,8,8,128]{3,2,1,0:T(8,128)}, u32[]{:S(2)}) copy-start(f32[2,8,8,128]{3,2,1,0:T(8,128)} %param.4) | copy-start | bytes 196612
  1.5 3.7 %collective-permute-start = (f32[2,3,8,128]{3,2,1,0:T(8,128)S(1)}, f32[2,3,8,128]{3,2,1,0:T(8,128)S(1)}, u32[]{:S(2)}, u32[]{:S(2)}) collective-permute-start(f32[2,3,8,128]{3,2,1,0:T(8,128)S(1)} %pad_maximum_fusion.18), channel_id=1, source_target_pairs={{0,16},{16,0},{1,17},{17,1},{2,18},{18,2},{3,19},{19,3},{4,20},{20... | collective-permute-start | bytes 73736 | tf_op jit(solution)/shard_map/ppermute | solution.py:31
  2.2 0.7 %copy-start.1 = (s32[32,3]{0,1:T(4,128)S(1)}, s32[32,3]{0,1:T(4,128)}, u32[]{:S(2)}) copy-start(s32[32,3]{0,1:T(4,128)} %param.5) | copy-start | bytes 1156
  5.2 6.2 %collective-permute-start.1 = (f32[3,10,4,128]{3,2,1,0:T(4,128)S(1)}, f32[3,10,4,128]{3,2,1,0:T(4,128)S(1)}, u32[]{:S(2)}, u32[]{:S(2)}) collective-permute-start(f32[3,10,4,128]{3,2,1,0:T(4,128)S(1)} %get-tuple-element.112), channel_id=1, source_target_pairs={{0,4},{4,8},{8,12},{12,0},{1,5},{5,9},{9,13},{13,1},{2,6},{6,10},{... | collective-permute-start | bytes 184328 | tf_op jit(solution)/shard_map/ppermute | solution.py:174
  7.8 5.2 %collective-permute-start.2 = (f32[3,10,4,128]{3,2,1,0:T(4,128)S(1)}, f32[3,10,4,128]{3,2,1,0:T(4,128)S(1)}, u32[]{:S(2)}, u32[]{:S(2)}) collective-permute-start(f32[3,10,4,128]{3,2,1,0:T(4,128)S(1)} %get-tuple-element.113), channel_id=1, source_target_pairs={{0,12},{4,0},{8,4},{12,8},{1,13},{5,1},{9,5},{13,9},{2,14},{6,2},{... | collective-permute-start | bytes 184328 | tf_op jit(solution)/shard_map/ppermute | solution.py:175
  13.2 6.4 %collective-permute-start.3 = (f32[3,5760]{1,0:T(4,128)S(1)}, f32[3,5760]{1,0:T(4,128)S(1)}, u32[]{:S(2)}, u32[]{:S(2)}) collective-permute-start(f32[3,5760]{1,0:T(4,128)S(1)} %reshape.852), channel_id=1, source_target_pairs={{1,0},{2,1},{3,2},{5,4},{6,5},{7,6},{9,8},{10,9},{11,10},{13,12},{... | collective-permute-start | bytes 207368 | tf_op jit(solution)/shard_map/ppermute | solution.py:178
  23.7 1.3 %collective-permute-start.4 = (f32[2,6,1632]{2,0,1:T(2,128)S(1)}, f32[2,6,1632]{2,0,1:T(2,128)S(1)}, u32[]{:S(2)}, u32[]{:S(2)}) collective-permute-start(f32[2,6,1632]{2,0,1:T(2,128)S(1)} %pad_maximum_fusion.12), channel_id=1, source_target_pairs={{0,16},{16,0},{1,17},{17,1},{2,18},{18,2},{3,19},{19,3},{4,20},{20... | collective-permute-start | bytes 235016 | tf_op jit(solution)/shard_map/ppermute | solution.py:31
  27.3 1.3 %collective-permute-start.5 = (f32[2,6,1360]{2,0,1:T(2,128)S(1)}, f32[2,6,1360]{2,0,1:T(2,128)S(1)}, u32[]{:S(2)}, u32[]{:S(2)}) collective-permute-start(f32[2,6,1360]{2,0,1:T(2,128)S(1)} %pad_maximum_fusion.13), channel_id=1, source_target_pairs={{0,16},{16,0},{1,17},{17,1},{2,18},{18,2},{3,19},{19,3},{4,20},{20... | collective-permute-start | bytes 195848 | tf_op jit(solution)/shard_map/ppermute | solution.py:31
  32.7 1.3 %collective-permute-start.6 = (f32[2,6,8,128]{3,2,1,0:T(8,128)S(1)}, f32[2,6,8,128]{3,2,1,0:T(8,128)S(1)}, u32[]{:S(2)}, u32[]{:S(2)}) collective-permute-start(f32[2,6,8,128]{3,2,1,0:T(8,128)S(1)} %pad_maximum_fusion.17), channel_id=1, source_target_pairs={{0,16},{16,0},{1,17},{17,1},{2,18},{18,2},{3,19},{19,3},{4,20},{20... | collective-permute-start | bytes 147464 | tf_op jit(solution)/shard_map/ppermute | solution.py:31

commit v15 on v13

--- a/solution.py
+++ b/solution.py
@@ -169,10 +169,13 @@
     wide = jnp.concatenate([below_y, start, above_y], 2)
 
     above = lax.ppermute(wide[..., :count].reshape(wide.shape[0], -1), "gz", line("gz", -1))
-    ext = jnp.concatenate([wide[..., low:], above.reshape(wide.shape[:3] + (count,))], 3)
-    ext = jnp.concatenate(
-        [jnp.stack([(ext[0] == phase).astype(jnp.float32) for phase in range(4)]), ext[1:]], 0
-    )
+    def expand(part):
+        return jnp.concatenate(
+            [jnp.stack([(part[0] == phase).astype(jnp.float32) for phase in range(4)]), part[1:]], 0
+        )
+
+    own = lax.optimization_barrier(expand(wide[..., low:]))
+    ext = jnp.concatenate([own, expand(above.reshape(wide.shape[:3] + (count,)))], 3)
     rows = ext.shape[2]
     ext = ext.reshape(ext.shape[0], ext.shape[1], rows * stride)
     pre_z = base_z + low + lane_z

time: 32.9 us -> 33.6 us (1.021)
  other arithmetic: 9.88 us -> 10.4 us
    ppermute x1, waiting for transfers between devices: 0.81 us -> 0.01 us  [shards(): above_y = lax.ppermute(start[:, :, :rim_y], 'gy', ring('gy', -1))]
    ppermute x1, waiting for transfers between devices: 3.85 us -> 4.57 us  [shards(): lax.ppermute(wide[..., :count].reshape(wide.shape[0], -1), 'gz', line('gz...]
    concatenate x6 -> x2, local copies, waits for them, and re-layouts: 0.66 us -> 0.1 us  [expand(): jnp.concatenate([jnp.stack([(part[0] == phase).astype(jnp.float32) for ph...]
    convert_element_type x0 -> x4, local copies, waits for them, and re-layouts: none -> 0.43 us  [expand(): (part[0] == phase).astype(jnp.float32)]
    unnamed x0 -> x4, other arithmetic: none -> 0.34 us
  transfers between devices with their start and end apart: 7 -> 7, of which waited for: 6 -> 5; matrix products, arithmetic and copies ran while one was open for 10% -> 11% of each run, Pallas kernels for 0% -> 0%
where the time goes in v15:
time: 33.6 us; the launch traced here: 33.4 us
  other arithmetic  10.4 us (31%)
  waiting for transfers between devices  8.29 us (25%)
  local copies, waits for them, and re-layouts  7.22 us (21%)
  starting transfers between devices  6.03 us (18%)
  between operations  1.42 us (4%)
    ppermute x1, waiting for transfers between devices, shards(): lax.ppermute(wide[..., :count].reshape(wide.shape[0], -1), 'gz', line('gz...  4.57 us
    ppermute x4, waiting for transfers between devices, x_halos(): got = lax.ppermute(pair, 'gx', ring('gx', 1))  3.71 us
    ppermute x1, starting transfers between devices, shards(): below_y = lax.ppermute(start[:, :, -rim_y:], 'gy', ring('gy', 1))  2.99 us
    ppermute x1, starting transfers between devices, shards(): lax.ppermute(wide[..., :count].reshape(wide.shape[0], -1), 'gz', line('gz...  1.29 us
    add x7, other arithmetic, phase_update(): phi[phase] + DT * (rates[phase] - mean_rate)  1.21 us
    sub x4, other arithmetic, chem_update(): delta = shape_fn(phi_new) - shape_fn(phi_old)  1.19 us
    mul x4, other arithmetic, phase_update(): square = phi * phi  1.13 us
    ppermute x1, starting transfers between devices, shards(): above_y = lax.ppermute(start[:, :, :rim_y], 'gy', ring('gy', -1))  1.02 us
  transfers between devices with their start and end apart: 7, of which 5 were waited for; matrix products, arithmetic and copies ran while one was open for 11% of the time, Pallas kernels for 0%

profile of v15, /device:TPU:0, one launch (start us, length us, event | category | flops | bytes accessed | tf_op | source)
XLA Modules:
  0.0 33.4 jit_solution(18124457044459568030)
XLA Ops:
  0.6 0.8 %convert_bitcast_fusion = f32[1,8,8,128]{3,2,1,0:T(8,128)S(1)} fusion(s32[8,8,128]{2,1,0:T(8,128)} %param.3), kind=kLoop, calls=%fused_computation.464 | loop fusion | flops 8192 | bytes 65536 | tf_op jit(solution)/shard_map/broadcast_in_dim | solution.py:165
  1.5 3.0 %collective-permute-start = (f32[3,8,4,128]{3,2,1,0:T(4,128)S(1)}, f32[3,8,4,128]{3,2,1,0:T(4,128)S(1)}, u32[]{:S(2)}, u32[]{:S(2)}) collective-permute-start(f32[3,8,4,128]{3,2,1,0:T(4,128)S(1)} %get-tuple-element.115), channel_id=1, source_target_pairs={{0,4},{4,8},{8,12},{12,0},{1,5},{5,9},{9,13},{13,1},{2,6},{6,10},{... | collective-permute-start | bytes 147464 | tf_op jit(solution)/shard_map/ppermute | solution.py:167
  4.5 1.0 %collective-permute-start.1 = (f32[3,8,4,128]{3,2,1,0:T(4,128)S(1)}, f32[3,8,4,128]{3,2,1,0:T(4,128)S(1)}, u32[]{:S(2)}, u32[]{:S(2)}) collective-permute-start(f32[3,8,4,128]{3,2,1,0:T(4,128)S(1)} %get-tuple-element.116), channel_id=1, source_target_pairs={{0,12},{4,0},{8,4},{12,8},{1,13},{5,1},{9,5},{13,9},{2,14},{6,2},{... | collective-permute-start | bytes 147464 | tf_op jit(solution)/shard_map/ppermute | solution.py:168
  5.8 0.6 %copy-done.1 = s32[32,3]{0,1:T(4,128)S(1)} copy-done((s32[32,3]{0,1:T(4,128)S(1)}, s32[32,3]{0,1:T(4,128)}, u32[]{:S(2)}) %copy-start.1) | copy-done | bytes 408
  6.7 0.2 and_reduce_fusion
  6.9 0.2 and_reduce_fusion.1
  7.5 0.1 and_reduce_fusion.2
  8.9 0.2 reshape.914
  9.1 1.3 %collective-permute-start.2 = (f32[3,4608]{1,0:T(4,128)S(1)}, f32[3,4608]{1,0:T(4,128)S(1)}, u32[]{:S(2)}, u32[]{:S(2)}) collective-permute-start(f32[3,4608]{1,0:T(4,128)S(1)} %reshape.914), channel_id=1, source_target_pairs={{1,0},{2,1},{3,2},{5,4},{6,5},{7,6},{9,8},{10,9},{11,10},{13,12},{... | collective-permute-start | bytes 165896 | tf_op jit(solution)/shard_map/ppermute | solution.py:171
  10.7 4.6 %collective-permute-done.2 = f32[3,4608]{1,0:T(4,128)S(1)} collective-permute-done((f32[3,4608]{1,0:T(4,128)S(1)}, f32[3,4608]{1,0:T(4,128)S(1)}, u32[]{:S(2)}, u32[]{:S(2)}) %collective-permute-start.2) | collective-permute-done | bytes 55328 | tf_op jit(solution)/shard_map/ppermute | solution.py:171
  15.3 0.2 fusion.266
  16.0 0.2 slice.908
  16.3 0.3 pad_maximum_fusion
  16.5 0.4 %reshape.915 = f32[6,8,2176]{2,1,0:T(8,128)S(1)} reshape(f32[6,8,16,136]{3,2,1,0:T(8,128)S(1)} %pad_maximum_fusion) | data formatting | bytes 835584 | tf_op jit(solution)/shard_map/reshape | solution.py:180
  17.0 0.2 maximum_select_fusion.1
  17.1 0.3 slice_bitcast_fusion.3
  17.6 0.3 fusion.305
  17.8 1.0 %collective-permute-done.3 = f32[2,6,1904]{2,0,1:T(2,128)S(1)} collective-permute-done((f32[2,6,1904]{2,0,1:T(2,128)S(1)}, f32[2,6,1904]{2,0,1:T(2,128)S(1)}, u32[]{:S(2)}, u32[]{:S(2)}) %collective-permute-start.3) | collective-permute-done | bytes 91424 | tf_op jit(solution)/shard_map/ppermute | solution.py:31
  18.9 0.3 slice_multiply_fusion
  19.3 0.1 fusion.133
  19.4 0.2 multiply_add_fusion.4
  19.6 0.2 multiply_add_fusion.3
  19.8 0.2 multiply_subtract_fusion
  20.0 0.2 fusion.43
  20.3 0.2 maximum_select_fusion.2
  20.5 0.2 slice_bitcast_fusion.7
  20.8 0.2 collective-permute-start.4
  21.1 0.2 fusion.306
  21.3 0.9 %collective-permute-done.4 = f32[2,6,1632]{2,0,1:T(2,128)S(1)} collective-permute-done((f32[2,6,1632]{2,0,1:T(2,128)S(1)}, f32[2,6,1632]{2,0,1:T(2,128)S(1)}, u32[]{:S(2)}, u32[]{:S(2)}) %collective-permute-start.4) | collective-permute-done | bytes 78368 | tf_op jit(solution)/shard_map/ppermute | solution.py:31
  22.2 0.3 slice_multiply_fusion.1
  22.5 0.1 fusion.175
  22.7 0.2 multiply_add_fusion.9
  22.9 0.2 multiply_add_fusion.8
  23.0 0.1 multiply_subtract_fusion.1
  23.2 0.2 fusion.56
  23.6 0.1 slice.1213
  23.8 0.1 maximum_select_fusion.4
  23.9 0.2 maximum_select_fusion.5
  24.1 0.2 slice_bitcast_fusion.11
  24.4 0.2 collective-permute-start.5
  24.6 0.2 fusion.307
  24.8 0.9 %collective-permute-done.5 = f32[2,6,1360]{2,0,1:T(2,128)S(1)} collective-permute-done((f32[2,6,1360]{2,0,1:T(2,128)S(1)}, f32[2,6,1360]{2,0,1:T(2,128)S(1)}, u32[]{:S(2)}, u32[]{:S(2)}) %collective-permute-start.5) | collective-permute-done | bytes 65312 | tf_op jit(solution)/shard_map/ppermute | solution.py:31
  25.8 0.3 slice_multiply_fusion.2
  26.2 0.2 multiply_add_fusion.14
  26.3 0.2 multiply_add_fusion.13
  26.5 0.1 multiply_subtract_fusion.2
  26.6 0.2 fusion.69
  26.9 0.1 slice.1265
  27.1 0.4 %concatenate.101 = f32[4,8,10,136]{3,2,1,0:T(8,128)S(1)} reshape(f32[4,8,1360]{2,1,0:T(8,128)S(1)} %get-tuple-element.18) | data formatting | bytes 348160 | tf_op jit(solution)/shard_map/concatenate | solution.py:152
  27.6 0.1 concatenate.102
  27.7 0.1 concatenate.103
  27.9 0.1 pad_maximum_fusion.4
  28.0 0.7 %concatenate.99 = f32[6,8,10,136]{3,2,1,0:T(8,128)S(1)} reshape(f32[6,8,1360]{2,1,0:T(8,128)S(1)} %pad_maximum_fusion.4) | data formatting | bytes 522240 | tf_op jit(solution)/shard_map/concatenate | solution.py:158
  28.7 0.7 %concatenate.100 = f32[6,8,10,136]{3,2,1,0:T(8,128)S(1)} reshape(f32[6,8,1360]{2,1,0:T(8,128)S(1)} %get-tuple-element.16) | data formatting | bytes 522240 | tf_op jit(solution)/shard_map/concatenate | solution.py:162
  29.4 0.3 fusion
  29.8 0.2 collective-permute-start.6
  30.0 0.2 fusion.304
  30.2 0.9 %collective-permute-done.6 = f32[2,6,8,128]{3,2,1,0:T(8,128)S(1)} collective-permute-done((f32[2,6,8,128]{3,2,1,0:T(8,128)S(1)}, f32[2,6,8,128]{3,2,1,0:T(8,128)S(1)}, u32[]{:S(2)}, u32[]{:S(2)}) %collective-permute-start.6) | collective-permute-done | bytes 49184 | tf_op jit(solution)/shard_map/ppermute | solution.py:31
  31.1 0.2 slice_multiply_fusion.3
  31.4 0.1 multiply_add_fusion.19
  31.6 0.1 fusion.232
  31.7 0.8 %multiply_subtract_fusion.3 = (f32[4,8,8,128]{3,2,1,0:T(8,128)S(1)}, f32[4,8,8,128]{3,2,1,0:T(8,128)}) fusion(f32[6,8,10,136]{3,2,1,0:T(8,128)S(1)} %fusion, f32[1,8,8,128]{3,2,1,0:T(8,128)S(1)} %get-tuple-element.53, f32[1,8,8,128]{3,2,1,0:T(8,128)S(1)} %get-tuple-element.54, f32[1,8,8,128]{3,2,1,0:T(8,128)S(1)} %get-tuple-element.55, ...), kind=kLoop, calls=%fused_computation.108 | loop fusion | flops 425984 | bytes 525312 | tf_op jit(solution)/shard_map/sub | solution.py:92
  32.5 0.2 fusion.82
  32.7 0.6 %pad_maximum_fusion.17 = f32[2,8,8,128]{3,2,1,0:T(8,128)} fusion(f32[1,8,8,128]{3,2,1,0:T(8,128)S(1)} %get-tuple-element.45, f32[1,8,8,128]{3,2,1,0:T(8,128)S(1)} %get-tuple-element.44), kind=kLoop, calls=%fused_computation.196 | loop fusion | flops 16384 | bytes 131072 | tf_op jit(solution)/shard_map/stack | solution.py:102
  (93 shorter events, 4.5 us)
Async XLA Ops:
  0.6 0.8 %copy-start = (f32[2,8,8,128]{3,2,1,0:T(8,128)S(1)}, f32[2,8,8,128]{3,2,1,0:T(8,128)}, u32[]{:S(2)}) copy-start(f32[2,8,8,128]{3,2,1,0:T(8,128)} %param.4) | copy-start | bytes 196612
  1.5 7.2 %collective-permute-start = (f32[3,8,4,128]{3,2,1,0:T(4,128)S(1)}, f32[3,8,4,128]{3,2,1,0:T(4,128)S(1)}, u32[]{:S(2)}, u32[]{:S(2)}) collective-permute-start(f32[3,8,4,128]{3,2,1,0:T(4,128)S(1)} %get-tuple-element.115), channel_id=1, source_target_pairs={{0,4},{4,8},{8,12},{12,0},{1,5},{5,9},{9,13},{13,1},{2,6},{6,10},{... | collective-permute-start | bytes 147464 | tf_op jit(solution)/shard_map/ppermute | solution.py:167
  4.5 4.3 %collective-permute-start.1 = (f32[3,8,4,128]{3,2,1,0:T(4,128)S(1)}, f32[3,8,4,128]{3,2,1,0:T(4,128)S(1)}, u32[]{:S(2)}, u32[]{:S(2)}) collective-permute-start(f32[3,8,4,128]{3,2,1,0:T(4,128)S(1)} %get-tuple-element.116), channel_id=1, source_target_pairs={{0,12},{4,0},{8,4},{12,8},{1,13},{5,1},{9,5},{13,9},{2,14},{6,2},{... | collective-permute-start | bytes 147464 | tf_op jit(solution)/shard_map/ppermute | solution.py:168
  5.8 0.7 %copy-start.1 = (s32[32,3]{0,1:T(4,128)S(1)}, s32[32,3]{0,1:T(4,128)}, u32[]{:S(2)}) copy-start(s32[32,3]{0,1:T(4,128)} %param.5) | copy-start | bytes 1156
  9.1 6.2 %collective-permute-start.2 = (f32[3,4608]{1,0:T(4,128)S(1)}, f32[3,4608]{1,0:T(4,128)S(1)}, u32[]{:S(2)}, u32[]{:S(2)}) collective-permute-start(f32[3,4608]{1,0:T(4,128)S(1)} %reshape.914), channel_id=1, source_target_pairs={{1,0},{2,1},{3,2},{5,4},{6,5},{7,6},{9,8},{10,9},{11,10},{13,12},{... | collective-permute-start | bytes 165896 | tf_op jit(solution)/shard_map/ppermute | solution.py:171
  17.5 1.4 %collective-permute-start.3 = (f32[2,6,1904]{2,0,1:T(2,128)S(1)}, f32[2,6,1904]{2,0,1:T(2,128)S(1)}, u32[]{:S(2)}, u32[]{:S(2)}) collective-permute-start(f32[2,6,1904]{2,0,1:T(2,128)S(1)} %pad_maximum_fusion.10), channel_id=1, source_target_pairs={{0,16},{16,0},{1,17},{17,1},{2,18},{18,2},{3,19},{19,3},{4,20},{20... | collective-permute-start | bytes 274184 | tf_op jit(solution)/shard_map/ppermute | solution.py:31
  20.8 1.3 %collective-permute-start.4 = (f32[2,6,1632]{2,0,1:T(2,128)S(1)}, f32[2,6,1632]{2,0,1:T(2,128)S(1)}, u32[]{:S(2)}, u32[]{:S(2)}) collective-permute-start(f32[2,6,1632]{2,0,1:T(2,128)S(1)} %pad_maximum_fusion.13), channel_id=1, source_target_pairs={{0,16},{16,0},{1,17},{17,1},{2,18},{18,2},{3,19},{19,3},{4,20},{20... | collective-permute-start | bytes 235016 | tf_op jit(solution)/shard_map/ppermute | solution.py:31
  24.4 1.3 %collective-permute-start.5 = (f32[2,6,1360]{2,0,1:T(2,128)S(1)}, f32[2,6,1360]{2,0,1:T(2,128)S(1)}, u32[]{:S(2)}, u32[]{:S(2)}) collective-permute-start(f32[2,6,1360]{2,0,1:T(2,128)S(1)} %pad_maximum_fusion.14), channel_id=1, source_target_pairs={{0,16},{16,0},{1,17},{17,1},{2,18},{18,2},{3,19},{19,3},{4,20},{20... | collective-permute-start | bytes 195848 | tf_op jit(solution)/shard_map/ppermute | solution.py:31
  29.8 1.3 %collective-permute-start.6 = (f32[2,6,8,128]{3,2,1,0:T(8,128)S(1)}, f32[2,6,8,128]{3,2,1,0:T(8,128)S(1)}, u32[]{:S(2)}, u32[]{:S(2)}) collective-permute-start(f32[2,6,8,128]{3,2,1,0:T(8,128)S(1)} %pad_maximum_fusion.19), channel_id=1, source_target_pairs={{0,16},{16,0},{1,17},{17,1},{2,18},{18,2},{3,19},{19,3},{4,20},{20... | collective-permute-start | bytes 147464 | tf_op jit(solution)/shard_map/ppermute | solution.py:31

commit v16 on v13

--- a/solution.py
+++ b/solution.py
@@ -164,8 +164,11 @@
 
     start = jnp.concatenate([labels.astype(jnp.float32)[None], mu_start], 0)
     nf = 4 + mu_start.shape[0]
-    below_y = lax.ppermute(start[:, :, -rim_y:], "gy", ring("gy", 1))
-    above_y = lax.ppermute(start[:, :, :rim_y], "gy", ring("gy", -1))
+    def rows_of(lo, hi):
+        return jnp.concatenate([labels[:, lo:hi].astype(jnp.float32)[None], mu_start[:, :, lo:hi]], 0)
+
+    below_y = lax.ppermute(rows_of(cells_y - rim_y, cells_y), "gy", ring("gy", 1))
+    above_y = lax.ppermute(rows_of(0, rim_y), "gy", ring("gy", -1))
     wide = jnp.concatenate([below_y, start, above_y], 2)
 
     above = lax.ppermute(wide[..., :count].reshape(wide.shape[0], -1), "gz", line("gz", -1))

time: 32.9 us -> 33.2 us (level)
  local copies, waits for them, and re-layouts: 7.09 us -> 7.94 us
  other arithmetic: 9.88 us -> 9.11 us
    slice x0 -> x1, local copies, waits for them, and re-layouts: none -> 0.93 us  [rows_of(): mu_start[:, :, lo:hi]]
    broadcast_in_dim x1, other arithmetic: 0.79 us -> 0.01 us  [shards(): start = jnp.concatenate([labels.astype(jnp.float32)[None], mu_start], 0)]
    unnamed x8 -> x10, local copies, waits for them, and re-layouts: 0.72 us -> 0.63 us
where the time goes in v16:
time: 33.2 us; the launch traced here: 32.9 us
  other arithmetic  9.11 us (27%)
  waiting for transfers between devices  8.46 us (25%)
  local copies, waits for them, and re-layouts  7.94 us (24%)
  starting transfers between devices  6.04 us (18%)
  between operations  1.41 us (4%)
    ppermute x1, waiting for transfers between devices, shards(): lax.ppermute(wide[..., :count].reshape(wide.shape[0], -1), 'gz', line('gz...  3.85 us
    ppermute x4, waiting for transfers between devices, x_halos(): got = lax.ppermute(pair, 'gx', ring('gx', 1))  3.71 us
    ppermute x1, starting transfers between devices, shards(): lax.ppermute(rows_of(cells_y - rim_y, cells_y), 'gy', ring('gy', 1))  2.99 us
    ppermute x1, starting transfers between devices, shards(): lax.ppermute(wide[..., :count].reshape(wide.shape[0], -1), 'gz', line('gz...  1.29 us
    add x7, other arithmetic, phase_update(): phi[phase] + DT * (rates[phase] - mean_rate)  1.21 us
    sub x4, other arithmetic, chem_update(): delta = shape_fn(phi_new) - shape_fn(phi_old)  1.19 us
    mul x4, other arithmetic, phase_update(): square = phi * phi  1.13 us
    ppermute x1, starting transfers between devices, shards(): above_y = lax.ppermute(rows_of(0, rim_y), 'gy', ring('gy', -1))  1.03 us
  transfers between devices with their start and end apart: 7, of which 6 were waited for; matrix products, arithmetic and copies ran while one was open for 10% of the time, Pallas kernels for 0%

profile of v16, /device:TPU:0, one launch (start us, length us, event | category | flops | bytes accessed | tf_op | source)
XLA Modules:
  0.0 32.9 jit_solution(10268727806471864427)
XLA Ops:
  0.6 0.9 %fusion.303 = (f32[2,8,4,128]{3,2,1,0:T(4,128)S(1)}, f32[2,8,4,128]{3,2,1,0:T(4,128)S(1)}) fusion(f32[2,8,8,128]{3,2,1,0:T(8,128)} %param.4), kind=kLoop, calls=%fused_computation.561 | loop fusion | bytes 131072 | tf_op jit(solution)/shard_map/slice | solution.py:168
  1.6 3.0 %collective-permute-start = (f32[3,8,4,128]{3,2,1,0:T(4,128)S(1)}, f32[3,8,4,128]{3,2,1,0:T(4,128)S(1)}, u32[]{:S(2)}, u32[]{:S(2)}) collective-permute-start(f32[3,8,4,128]{3,2,1,0:T(4,128)S(1)} %pad_maximum_fusion.19), channel_id=1, source_target_pairs={{0,4},{4,8},{8,12},{12,0},{1,5},{5,9},{9,13},{13,1},{2,6},{6,10},{... | collective-permute-start | bytes 147464 | tf_op jit(solution)/shard_map/ppermute | solution.py:170
  4.6 1.0 %collective-permute-start.1 = (f32[3,8,4,128]{3,2,1,0:T(4,128)S(1)}, f32[3,8,4,128]{3,2,1,0:T(4,128)S(1)}, u32[]{:S(2)}, u32[]{:S(2)}) collective-permute-start(f32[3,8,4,128]{3,2,1,0:T(4,128)S(1)} %pad_maximum_fusion.20), channel_id=1, source_target_pairs={{0,12},{4,0},{8,4},{12,8},{1,13},{5,1},{9,5},{13,9},{2,14},{6,2},{... | collective-permute-start | bytes 147464 | tf_op jit(solution)/shard_map/ppermute | solution.py:171
  6.0 0.6 %copy-done.2 = s32[32,3]{0,1:T(4,128)S(1)} copy-done((s32[32,3]{0,1:T(4,128)S(1)}, s32[32,3]{0,1:T(4,128)}, u32[]{:S(2)}) %copy-start.2) | copy-done | bytes 408
  6.8 0.2 and_reduce_fusion
  7.0 0.2 and_reduce_fusion.1
  7.6 0.1 and_reduce_fusion.2
  7.9 0.9 %collective-permute-done.1 = f32[3,8,4,128]{3,2,1,0:T(4,128)S(1)} collective-permute-done((f32[3,8,4,128]{3,2,1,0:T(4,128)S(1)}, f32[3,8,4,128]{3,2,1,0:T(4,128)S(1)}, u32[]{:S(2)}, u32[]{:S(2)}) %collective-permute-start.1) | collective-permute-done | bytes 49184 | tf_op jit(solution)/shard_map/ppermute | solution.py:171
  8.8 0.2 reshape.852
  9.0 1.3 %collective-permute-start.2 = (f32[3,4608]{1,0:T(4,128)S(1)}, f32[3,4608]{1,0:T(4,128)S(1)}, u32[]{:S(2)}, u32[]{:S(2)}) collective-permute-start(f32[3,4608]{1,0:T(4,128)S(1)} %reshape.852), channel_id=1, source_target_pairs={{1,0},{2,1},{3,2},{5,4},{6,5},{7,6},{9,8},{10,9},{11,10},{13,12},{... | collective-permute-start | bytes 165896 | tf_op jit(solution)/shard_map/ppermute | solution.py:174
  11.4 3.9 %collective-permute-done.2 = f32[3,4608]{1,0:T(4,128)S(1)} collective-permute-done((f32[3,4608]{1,0:T(4,128)S(1)}, f32[3,4608]{1,0:T(4,128)S(1)}, u32[]{:S(2)}, u32[]{:S(2)}) %collective-permute-start.2) | collective-permute-done | bytes 55328 | tf_op jit(solution)/shard_map/ppermute | solution.py:174
  15.2 0.2 reshape.853
  15.6 0.1 pad_maximum_fusion.4
  15.8 0.1 reshape.854
  16.3 0.2 concatenate.114
  16.5 0.2 maximum_select_fusion.1
  16.7 0.3 slice_bitcast_fusion.3
  17.2 0.3 fusion.300
  17.4 1.0 %collective-permute-done.3 = f32[2,6,1904]{2,0,1:T(2,128)S(1)} collective-permute-done((f32[2,6,1904]{2,0,1:T(2,128)S(1)}, f32[2,6,1904]{2,0,1:T(2,128)S(1)}, u32[]{:S(2)}, u32[]{:S(2)}) %collective-permute-start.3) | collective-permute-done | bytes 91424 | tf_op jit(solution)/shard_map/ppermute | solution.py:31
  18.5 0.3 slice_multiply_fusion
  18.8 0.1 fusion.133
  19.0 0.2 multiply_add_fusion.4
  19.2 0.2 multiply_add_fusion.3
  19.4 0.2 multiply_subtract_fusion
  19.5 0.2 fusion.43
  19.9 0.2 maximum_select_fusion.2
  20.1 0.2 slice_bitcast_fusion.7
  20.4 0.2 collective-permute-start.4
  20.6 0.2 fusion.301
  20.9 0.9 %collective-permute-done.4 = f32[2,6,1632]{2,0,1:T(2,128)S(1)} collective-permute-done((f32[2,6,1632]{2,0,1:T(2,128)S(1)}, f32[2,6,1632]{2,0,1:T(2,128)S(1)}, u32[]{:S(2)}, u32[]{:S(2)}) %collective-permute-start.4) | collective-permute-done | bytes 78368 | tf_op jit(solution)/shard_map/ppermute | solution.py:31
  21.8 0.3 slice_multiply_fusion.1
  22.2 0.2 multiply_add_fusion.9
  22.4 0.2 multiply_add_fusion.8
  22.6 0.1 multiply_subtract_fusion.1
  22.8 0.2 fusion.56
  23.2 0.1 slice.1201
  23.4 0.1 maximum_select_fusion.4
  23.5 0.2 maximum_select_fusion.5
  23.7 0.2 slice_bitcast_fusion.11
  24.0 0.2 collective-permute-start.5
  24.2 0.2 fusion.302
  24.4 0.9 %collective-permute-done.5 = f32[2,6,1360]{2,0,1:T(2,128)S(1)} collective-permute-done((f32[2,6,1360]{2,0,1:T(2,128)S(1)}, f32[2,6,1360]{2,0,1:T(2,128)S(1)}, u32[]{:S(2)}, u32[]{:S(2)}) %collective-permute-start.5) | collective-permute-done | bytes 65312 | tf_op jit(solution)/shard_map/ppermute | solution.py:31
  25.3 0.3 slice_multiply_fusion.2
  25.7 0.2 multiply_add_fusion.14
  25.9 0.2 multiply_add_fusion.13
  26.1 0.1 multiply_subtract_fusion.2
  26.2 0.2 fusion.69
  26.5 0.1 slice.1253
  26.7 0.4 %concatenate.133 = f32[4,8,10,136]{3,2,1,0:T(8,128)S(1)} reshape(f32[4,8,1360]{2,1,0:T(8,128)S(1)} %get-tuple-element.14) | data formatting | bytes 348160 | tf_op jit(solution)/shard_map/concatenate | solution.py:152
  27.1 0.1 concatenate.134
  27.3 0.1 concatenate.135
  27.5 0.1 pad_maximum_fusion.3
  27.6 0.7 %concatenate.131 = f32[6,8,10,136]{3,2,1,0:T(8,128)S(1)} reshape(f32[6,8,1360]{2,1,0:T(8,128)S(1)} %pad_maximum_fusion.3) | data formatting | bytes 522240 | tf_op jit(solution)/shard_map/concatenate | solution.py:158
  28.3 0.7 %concatenate.132 = f32[6,8,10,136]{3,2,1,0:T(8,128)S(1)} reshape(f32[6,8,1360]{2,1,0:T(8,128)S(1)} %get-tuple-element.12) | data formatting | bytes 522240 | tf_op jit(solution)/shard_map/concatenate | solution.py:162
  29.0 0.3 fusion
  29.3 0.2 collective-permute-start.6
  29.6 0.2 fusion.299
  29.7 0.9 %collective-permute-done.6 = f32[2,6,8,128]{3,2,1,0:T(8,128)S(1)} collective-permute-done((f32[2,6,8,128]{3,2,1,0:T(8,128)S(1)}, f32[2,6,8,128]{3,2,1,0:T(8,128)S(1)}, u32[]{:S(2)}, u32[]{:S(2)}) %collective-permute-start.6) | collective-permute-done | bytes 49184 | tf_op jit(solution)/shard_map/ppermute | solution.py:31
  30.6 0.2 slice_multiply_fusion.3
  31.0 0.1 multiply_add_fusion.19
  31.1 0.1 fusion.231
  31.3 0.8 %multiply_subtract_fusion.3 = (f32[4,8,8,128]{3,2,1,0:T(8,128)S(1)}, f32[4,8,8,128]{3,2,1,0:T(8,128)}) fusion(f32[6,8,10,136]{3,2,1,0:T(8,128)S(1)} %fusion, f32[1,8,8,128]{3,2,1,0:T(8,128)S(1)} %get-tuple-element.51, f32[1,8,8,128]{3,2,1,0:T(8,128)S(1)} %get-tuple-element.52, f32[1,8,8,128]{3,2,1,0:T(8,128)S(1)} %get-tuple-element.53, ...), kind=kLoop, calls=%fused_computation.108 | loop fusion | flops 425984 | bytes 525312 | tf_op jit(solution)/shard_map/sub | solution.py:92
  32.1 0.2 fusion.82
  32.3 0.6 %pad_maximum_fusion.18 = f32[2,8,8,128]{3,2,1,0:T(8,128)} fusion(f32[1,8,8,128]{3,2,1,0:T(8,128)S(1)} %get-tuple-element.43, f32[1,8,8,128]{3,2,1,0:T(8,128)S(1)} %get-tuple-element.42), kind=kLoop, calls=%fused_computation.194 | loop fusion | flops 16384 | bytes 131072 | tf_op jit(solution)/shard_map/stack | solution.py:102
  (94 shorter events, 4.3 us)
Async XLA Ops:
  0.6 0.9 %copy-start.1 = (s32[8,8,128]{2,1,0:T(8,128)S(1)}, s32[8,8,128]{2,1,0:T(8,128)}, u32[]{:S(2)}) copy-start(s32[8,8,128]{2,1,0:T(8,128)} %param.3) | copy-start | bytes 98308
  1.6 6.3 %collective-permute-start = (f32[3,8,4,128]{3,2,1,0:T(4,128)S(1)}, f32[3,8,4,128]{3,2,1,0:T(4,128)S(1)}, u32[]{:S(2)}, u32[]{:S(2)}) collective-permute-start(f32[3,8,4,128]{3,2,1,0:T(4,128)S(1)} %pad_maximum_fusion.19), channel_id=1, source_target_pairs={{0,4},{4,8},{8,12},{12,0},{1,5},{5,9},{9,13},{13,1},{2,6},{6,10},{... | collective-permute-start | bytes 147464 | tf_op jit(solution)/shard_map/ppermute | solution.py:170
  4.6 4.1 %collective-permute-start.1 = (f32[3,8,4,128]{3,2,1,0:T(4,128)S(1)}, f32[3,8,4,128]{3,2,1,0:T(4,128)S(1)}, u32[]{:S(2)}, u32[]{:S(2)}) collective-permute-start(f32[3,8,4,128]{3,2,1,0:T(4,128)S(1)} %pad_maximum_fusion.20), channel_id=1, source_target_pairs={{0,12},{4,0},{8,4},{12,8},{1,13},{5,1},{9,5},{13,9},{2,14},{6,2},{... | collective-permute-start | bytes 147464 | tf_op jit(solution)/shard_map/ppermute | solution.py:171
  5.9 0.7 %copy-start.2 = (s32[32,3]{0,1:T(4,128)S(1)}, s32[32,3]{0,1:T(4,128)}, u32[]{:S(2)}) copy-start(s32[32,3]{0,1:T(4,128)} %param.5) | copy-start | bytes 1156
  5.9 2.8 %copy-start = (f32[2,8,8,128]{3,2,1,0:T(8,128)S(1)}, f32[2,8,8,128]{3,2,1,0:T(8,128)}, u32[]{:S(2)}) copy-start(f32[2,8,8,128]{3,2,1,0:T(8,128)} %param.4) | copy-start | bytes 196612
  9.0 6.2 %collective-permute-start.2 = (f32[3,4608]{1,0:T(4,128)S(1)}, f32[3,4608]{1,0:T(4,128)S(1)}, u32[]{:S(2)}, u32[]{:S(2)}) collective-permute-start(f32[3,4608]{1,0:T(4,128)S(1)} %reshape.852), channel_id=1, source_target_pairs={{1,0},{2,1},{3,2},{5,4},{6,5},{7,6},{9,8},{10,9},{11,10},{13,12},{... | collective-permute-start | bytes 165896 | tf_op jit(solution)/shard_map/ppermute | solution.py:174
  17.1 1.4 %collective-permute-start.3 = (f32[2,6,1904]{2,0,1:T(2,128)S(1)}, f32[2,6,1904]{2,0,1:T(2,128)S(1)}, u32[]{:S(2)}, u32[]{:S(2)}) collective-permute-start(f32[2,6,1904]{2,0,1:T(2,128)S(1)} %pad_maximum_fusion.11), channel_id=1, source_target_pairs={{0,16},{16,0},{1,17},{17,1},{2,18},{18,2},{3,19},{19,3},{4,20},{20... | collective-permute-start | bytes 274184 | tf_op jit(solution)/shard_map/ppermute | solution.py:31
  20.4 1.3 %collective-permute-start.4 = (f32[2,6,1632]{2,0,1:T(2,128)S(1)}, f32[2,6,1632]{2,0,1:T(2,128)S(1)}, u32[]{:S(2)}, u32[]{:S(2)}) collective-permute-start(f32[2,6,1632]{2,0,1:T(2,128)S(1)} %pad_maximum_fusion.14), channel_id=1, source_target_pairs={{0,16},{16,0},{1,17},{17,1},{2,18},{18,2},{3,19},{19,3},{4,20},{20... | collective-permute-start | bytes 235016 | tf_op jit(solution)/shard_map/ppermute | solution.py:31
  24.0 1.3 %collective-permute-start.5 = (f32[2,6,1360]{2,0,1:T(2,128)S(1)}, f32[2,6,1360]{2,0,1:T(2,128)S(1)}, u32[]{:S(2)}, u32[]{:S(2)}) collective-permute-start(f32[2,6,1360]{2,0,1:T(2,128)S(1)} %pad_maximum_fusion.15), channel_id=1, source_target_pairs={{0,16},{16,0},{1,17},{17,1},{2,18},{18,2},{3,19},{19,3},{4,20},{20... | collective-permute-start | bytes 195848 | tf_op jit(solution)/shard_map/ppermute | solution.py:31
  29.3 1.3 %collective-permute-start.6 = (f32[2,6,8,128]{3,2,1,0:T(8,128)S(1)}, f32[2,6,8,128]{3,2,1,0:T(8,128)S(1)}, u32[]{:S(2)}, u32[]{:S(2)}) collective-permute-start(f32[2,6,8,128]{3,2,1,0:T(8,128)S(1)} %pad_maximum_fusion.21), channel_id=1, source_target_pairs={{0,16},{16,0},{1,17},{17,1},{2,18},{18,2},{3,19},{19,3},{4,20},{20... | collective-permute-start | bytes 147464 | tf_op jit(solution)/shard_map/ppermute | solution.py:31

commit v17 on v13

--- a/solution.py
+++ b/solution.py
@@ -177,17 +177,27 @@
     ext = ext.reshape(ext.shape[0], ext.shape[1], rows * stride)
     pre_z = base_z + low + lane_z
     post_z = pre_z - lift
-    ext = edge_at(ext, cells_z - low, top_brick)
+    def fixes(ext, below_at=None, above_at=None, liquid_from=None):
+        lane = lane_index(ext)
+        if liquid_from is not None:
+            liquid = jnp.where(lax.broadcasted_iota(jnp.int32, ext.shape, 0) == 0, 1.0, 0.0)
+            ext = jnp.where(top_brick & (lane >= liquid_from), liquid.astype(jnp.float32), ext)
+        out = ext
+        if below_at is not None:
+            down = jnp.concatenate([ext[..., 1:], ext[..., -1:]], 2)
+            out = jnp.where(bottom_brick & (lane == below_at), down, out)
+        if above_at is not None:
+            up = jnp.concatenate([ext[..., :1], ext[..., :-1]], 2)
+            out = jnp.where(top_brick & (lane == above_at), up, out)
+        return out
+
+    ext = fixes(ext, above_at=cells_z - low)
     ext = step(ext, 1 - rim_y, pre_z, 0)
-    ext = edge_at(ext, cells_z - low, top_brick)
+    ext = fixes(ext, above_at=cells_z - low)
     ext = step(ext, 2 - rim_y, pre_z, 0)
-    liquid = jnp.where(lax.broadcasted_iota(jnp.int32, ext.shape, 0) == 0, 1.0, 0.0).astype(jnp.float32)
-    ext = jnp.where(top_brick & (lane_index(ext) >= cells_z - low), liquid, ext)
-    ext = edge_below(ext, lift - low - 1, bottom_brick)
-    ext = edge_at(ext, cells_z + lift - low, top_brick)
+    ext = fixes(ext, lift - low - 1, cells_z + lift - low, cells_z - low)
     ext = step(ext, 3 - rim_y, post_z, lift)
-    ext = edge_below(ext, lift - low - 1, bottom_brick)
-    ext = edge_at(ext, cells_z + lift - low, top_brick)
+    ext = fixes(ext, lift - low - 1, cells_z + lift - low)
     grid = ext.reshape(nf, cells_x, cells_y + 2, stride)
     first = lift - low
     fields = grid[:, :, 1:-1, first : first + cells_z]

time: 32.9 us -> 32.7 us (level)
    select_n x8 -> x6, other arithmetic: 1.08 us -> 0.9 us  [the longest x4 0.8 us: fixes(): out = jnp.where(top_brick & (lane == above_at), up, out)]
    add x7 -> x6, other arithmetic: 1.21 us -> 1.04 us  [phase_update(): phi[phase] + DT * (rates[phase] - mean_rate)]
where the time goes in v17:
time: 32.7 us; the launch traced here: 32.5 us
  other arithmetic  9.68 us (30%)
  waiting for transfers between devices  8.4 us (26%)
  local copies, waits for them, and re-layouts  7.02 us (21%)
  starting transfers between devices  6.03 us (18%)
  between operations  1.33 us (4%)
    ppermute x1, waiting for transfers between devices, shards(): lax.ppermute(wide[..., :count].reshape(wide.shape[0], -1), 'gz', line('gz...  3.85 us
    ppermute x4, waiting for transfers between devices, x_halos(): got = lax.ppermute(pair, 'gx', ring('gx', 1))  3.71 us
    ppermute x1, starting transfers between devices, shards(): below_y = lax.ppermute(start[:, :, -rim_y:], 'gy', ring('gy', 1))  2.99 us
    ppermute x1, starting transfers between devices, shards(): lax.ppermute(wide[..., :count].reshape(wide.shape[0], -1), 'gz', line('gz...  1.29 us
    sub x4, other arithmetic, chem_update(): delta = shape_fn(phi_new) - shape_fn(phi_old)  1.19 us
    mul x4, other arithmetic, phase_update(): square = phi * phi  1.13 us
    add x6, other arithmetic, phase_update(): phi[phase] + DT * (rates[phase] - mean_rate)  1.04 us
    ppermute x1, starting transfers between devices, shards(): above_y = lax.ppermute(start[:, :, :rim_y], 'gy', ring('gy', -1))  1.02 us
  transfers between devices with their start and end apart: 7, of which 6 were waited for; matrix products, arithmetic and copies ran while one was open for 10% of the time, Pallas kernels for 0%

profile of v17, /device:TPU:0, one launch (start us, length us, event | category | flops | bytes accessed | tf_op | source)
XLA Modules:
  0.0 32.5 jit_solution(2928303825966432493)
XLA Ops:
  0.6 0.8 %convert_bitcast_fusion = f32[1,8,8,128]{3,2,1,0:T(8,128)S(1)} fusion(s32[8,8,128]{2,1,0:T(8,128)} %param.3), kind=kLoop, calls=%fused_computation.470 | loop fusion | flops 8192 | bytes 65536 | tf_op jit(solution)/shard_map/broadcast_in_dim | solution.py:165
  1.5 3.0 %collective-permute-start = (f32[3,8,4,128]{3,2,1,0:T(4,128)S(1)}, f32[3,8,4,128]{3,2,1,0:T(4,128)S(1)}, u32[]{:S(2)}, u32[]{:S(2)}) collective-permute-start(f32[3,8,4,128]{3,2,1,0:T(4,128)S(1)} %get-tuple-element.125), channel_id=1, source_target_pairs={{0,4},{4,8},{8,12},{12,0},{1,5},{5,9},{9,13},{13,1},{2,6},{6,10},{... | collective-permute-start | bytes 147464 | tf_op jit(solution)/shard_map/ppermute | solution.py:167
  4.5 1.0 %collective-permute-start.1 = (f32[3,8,4,128]{3,2,1,0:T(4,128)S(1)}, f32[3,8,4,128]{3,2,1,0:T(4,128)S(1)}, u32[]{:S(2)}, u32[]{:S(2)}) collective-permute-start(f32[3,8,4,128]{3,2,1,0:T(4,128)S(1)} %get-tuple-element.126), channel_id=1, source_target_pairs={{0,12},{4,0},{8,4},{12,8},{1,13},{5,1},{9,5},{13,9},{2,14},{6,2},{... | collective-permute-start | bytes 147464 | tf_op jit(solution)/shard_map/ppermute | solution.py:168
  5.8 0.6 %copy-done.1 = s32[32,3]{0,1:T(4,128)S(1)} copy-done((s32[32,3]{0,1:T(4,128)S(1)}, s32[32,3]{0,1:T(4,128)}, u32[]{:S(2)}) %copy-start.1) | copy-done | bytes 408
  6.7 0.2 and_reduce_fusion
  6.8 0.2 and_reduce_fusion.1
  7.5 0.1 and_reduce_fusion.2
  7.7 0.8 %collective-permute-done.1 = f32[3,8,4,128]{3,2,1,0:T(4,128)S(1)} collective-permute-done((f32[3,8,4,128]{3,2,1,0:T(4,128)S(1)}, f32[3,8,4,128]{3,2,1,0:T(4,128)S(1)}, u32[]{:S(2)}, u32[]{:S(2)}) %collective-permute-start.1) | collective-permute-done | bytes 49184 | tf_op jit(solution)/shard_map/ppermute | solution.py:168
  8.6 0.2 reshape.852
  8.8 1.3 %collective-permute-start.2 = (f32[3,4608]{1,0:T(4,128)S(1)}, f32[3,4608]{1,0:T(4,128)S(1)}, u32[]{:S(2)}, u32[]{:S(2)}) collective-permute-start(f32[3,4608]{1,0:T(4,128)S(1)} %reshape.852), channel_id=1, source_target_pairs={{1,0},{2,1},{3,2},{5,4},{6,5},{7,6},{9,8},{10,9},{11,10},{13,12},{... | collective-permute-start | bytes 165896 | tf_op jit(solution)/shard_map/ppermute | solution.py:171
  11.2 3.9 %collective-permute-done.2 = f32[3,4608]{1,0:T(4,128)S(1)} collective-permute-done((f32[3,4608]{1,0:T(4,128)S(1)}, f32[3,4608]{1,0:T(4,128)S(1)}, u32[]{:S(2)}, u32[]{:S(2)}) %collective-permute-start.2) | collective-permute-done | bytes 55328 | tf_op jit(solution)/shard_map/ppermute | solution.py:171
  15.0 0.2 reshape.853
  15.4 0.1 pad_maximum_fusion.3
  15.6 0.1 reshape.854
  15.7 0.1 reshape.855
  16.1 0.2 concatenate.106
  16.3 0.2 maximum_select_fusion.1
  16.5 0.3 slice_bitcast_fusion.3
  17.0 0.3 fusion.301
  17.2 1.0 %collective-permute-done.3 = f32[2,6,1904]{2,0,1:T(2,128)S(1)} collective-permute-done((f32[2,6,1904]{2,0,1:T(2,128)S(1)}, f32[2,6,1904]{2,0,1:T(2,128)S(1)}, u32[]{:S(2)}, u32[]{:S(2)}) %collective-permute-start.3) | collective-permute-done | bytes 91424 | tf_op jit(solution)/shard_map/ppermute | solution.py:31
  18.3 0.3 %slice_multiply_fusion = (f32[4,8,1904]{2,1,0:T(8,128)S(1)}, f32[4,8,1904]{2,1,0:T(8,128)S(1)}) fusion(f32[6,8,2176]{2,1,0:T(8,128)S(1)} %maximum_select_fusion.1, f32[6,7,1904]{2,1,0:T(8,128)S(1)} %get-tuple-element.81, f32[6,1,1904]{2,1,0:T(1,128)S(1)} %get-tuple-element.128, f32[6,1,1904]{2,1,0:T(1,128)S(1)} %get-tuple-element.127, ...), kind=kLoop, calls=%fused_computation.90 | loop fusion | flops 609280 | bytes 2437120 | tf_op jit(solution)/shard_map/mul | solution.py:64
  18.6 0.1 fusion.137
  18.8 0.2 multiply_add_fusion.4
  19.0 0.2 multiply_add_fusion.3
  19.2 0.2 multiply_subtract_fusion
  19.3 0.2 fusion.47
  19.7 0.2 maximum_select_fusion.2
  19.9 0.2 slice_bitcast_fusion.7
  20.2 0.2 collective-permute-start.4
  20.4 0.2 fusion.302
  20.7 0.9 %collective-permute-done.4 = f32[2,6,1632]{2,0,1:T(2,128)S(1)} collective-permute-done((f32[2,6,1632]{2,0,1:T(2,128)S(1)}, f32[2,6,1632]{2,0,1:T(2,128)S(1)}, u32[]{:S(2)}, u32[]{:S(2)}) %collective-permute-start.4) | collective-permute-done | bytes 78368 | tf_op jit(solution)/shard_map/ppermute | solution.py:31
  21.6 0.3 slice_multiply_fusion.1
  22.0 0.2 multiply_add_fusion.9
  22.2 0.2 multiply_add_fusion.8
  22.4 0.1 multiply_subtract_fusion.1
  22.6 0.2 fusion.60
  23.0 0.1 fusion.304
  23.2 0.2 maximum_select_fusion.4
  23.4 0.2 slice_bitcast_fusion.11
  23.7 0.2 collective-permute-start.5
  23.9 0.2 fusion.303
  24.1 0.9 %collective-permute-done.5 = f32[2,6,1360]{2,0,1:T(2,128)S(1)} collective-permute-done((f32[2,6,1360]{2,0,1:T(2,128)S(1)}, f32[2,6,1360]{2,0,1:T(2,128)S(1)}, u32[]{:S(2)}, u32[]{:S(2)}) %collective-permute-start.5) | collective-permute-done | bytes 65312 | tf_op jit(solution)/shard_map/ppermute | solution.py:31
  25.0 0.3 slice_multiply_fusion.2
  25.4 0.2 multiply_add_fusion.14
  25.6 0.2 fusion.194
  25.7 0.1 multiply_subtract_fusion.2
  25.9 0.4 %concatenate.125 = f32[4,8,10,136]{3,2,1,0:T(8,128)S(1)} reshape(f32[4,8,1360]{2,1,0:T(8,128)S(1)} %get-tuple-element.12) | data formatting | bytes 348160 | tf_op jit(solution)/shard_map/concatenate | solution.py:152
  26.3 0.2 fusion.73
  26.6 0.1 concatenate.126
  26.7 0.1 concatenate.127
  26.9 0.1 fusion.306
  27.0 0.1 fusion.13
  27.1 0.7 %concatenate.122 = f32[6,8,10,136]{3,2,1,0:T(8,128)S(1)} reshape(f32[6,8,1360]{2,1,0:T(8,128)S(1)} %get-tuple-element.119) | data formatting | bytes 522240 | tf_op jit(solution)/shard_map/concatenate | solution.py:190
  27.8 0.7 %concatenate.124 = f32[6,8,10,136]{3,2,1,0:T(8,128)S(1)} reshape(f32[6,8,1360]{2,1,0:T(8,128)S(1)} %get-tuple-element.118) | data formatting | bytes 522240 | tf_op jit(solution)/shard_map/concatenate | solution.py:187
  28.5 0.3 fusion
  28.9 0.2 collective-permute-start.6
  29.1 0.2 fusion.300
  29.2 0.9 %collective-permute-done.6 = f32[2,6,8,128]{3,2,1,0:T(8,128)S(1)} collective-permute-done((f32[2,6,8,128]{3,2,1,0:T(8,128)S(1)}, f32[2,6,8,128]{3,2,1,0:T(8,128)S(1)}, u32[]{:S(2)}, u32[]{:S(2)}) %collective-permute-start.6) | collective-permute-done | bytes 49184 | tf_op jit(solution)/shard_map/ppermute | solution.py:31
  30.2 0.2 slice_multiply_fusion.3
  30.5 0.1 multiply_add_fusion.19
  30.7 0.1 fusion.236
  30.8 0.8 %multiply_subtract_fusion.3 = (f32[4,8,8,128]{3,2,1,0:T(8,128)S(1)}, f32[4,8,8,128]{3,2,1,0:T(8,128)}) fusion(f32[6,8,10,136]{3,2,1,0:T(8,128)S(1)} %fusion, f32[1,8,8,128]{3,2,1,0:T(8,128)S(1)} %get-tuple-element.49, f32[1,8,8,128]{3,2,1,0:T(8,128)S(1)} %get-tuple-element.50, f32[1,8,8,128]{3,2,1,0:T(8,128)S(1)} %get-tuple-element.51, ...), kind=kLoop, calls=%fused_computation.118 | loop fusion | flops 425984 | bytes 525312 | tf_op jit(solution)/shard_map/sub | solution.py:92
  31.6 0.2 fusion.86
  31.8 0.6 %pad_maximum_fusion.17 = f32[2,8,8,128]{3,2,1,0:T(8,128)} fusion(f32[1,8,8,128]{3,2,1,0:T(8,128)S(1)} %get-tuple-element.41, f32[1,8,8,128]{3,2,1,0:T(8,128)S(1)} %get-tuple-element.40), kind=kLoop, calls=%fused_computation.206 | loop fusion | flops 16384 | bytes 131072 | tf_op jit(solution)/shard_map/stack | solution.py:102
  (82 shorter events, 4.0 us)
Async XLA Ops:
  0.6 0.8 %copy-start = (f32[2,8,8,128]{3,2,1,0:T(8,128)S(1)}, f32[2,8,8,128]{3,2,1,0:T(8,128)}, u32[]{:S(2)}) copy-start(f32[2,8,8,128]{3,2,1,0:T(8,128)} %param.4) | copy-start | bytes 196612
  1.5 6.2 %collective-permute-start = (f32[3,8,4,128]{3,2,1,0:T(4,128)S(1)}, f32[3,8,4,128]{3,2,1,0:T(4,128)S(1)}, u32[]{:S(2)}, u32[]{:S(2)}) collective-permute-start(f32[3,8,4,128]{3,2,1,0:T(4,128)S(1)} %get-tuple-element.125), channel_id=1, source_target_pairs={{0,4},{4,8},{8,12},{12,0},{1,5},{5,9},{9,13},{13,1},{2,6},{6,10},{... | collective-permute-start | bytes 147464 | tf_op jit(solution)/shard_map/ppermute | solution.py:167
  4.5 4.1 %collective-permute-start.1 = (f32[3,8,4,128]{3,2,1,0:T(4,128)S(1)}, f32[3,8,4,128]{3,2,1,0:T(4,128)S(1)}, u32[]{:S(2)}, u32[]{:S(2)}) collective-permute-start(f32[3,8,4,128]{3,2,1,0:T(4,128)S(1)} %get-tuple-element.126), channel_id=1, source_target_pairs={{0,12},{4,0},{8,4},{12,8},{1,13},{5,1},{9,5},{13,9},{2,14},{6,2},{... | collective-permute-start | bytes 147464 | tf_op jit(solution)/shard_map/ppermute | solution.py:168
  5.7 0.7 %copy-start.1 = (s32[32,3]{0,1:T(4,128)S(1)}, s32[32,3]{0,1:T(4,128)}, u32[]{:S(2)}) copy-start(s32[32,3]{0,1:T(4,128)} %param.5) | copy-start | bytes 1156
  8.8 6.2 %collective-permute-start.2 = (f32[3,4608]{1,0:T(4,128)S(1)}, f32[3,4608]{1,0:T(4,128)S(1)}, u32[]{:S(2)}, u32[]{:S(2)}) collective-permute-start(f32[3,4608]{1,0:T(4,128)S(1)} %reshape.852), channel_id=1, source_target_pairs={{1,0},{2,1},{3,2},{5,4},{6,5},{7,6},{9,8},{10,9},{11,10},{13,12},{... | collective-permute-start | bytes 165896 | tf_op jit(solution)/shard_map/ppermute | solution.py:171
  16.9 1.4 %collective-permute-start.3 = (f32[2,6,1904]{2,0,1:T(2,128)S(1)}, f32[2,6,1904]{2,0,1:T(2,128)S(1)}, u32[]{:S(2)}, u32[]{:S(2)}) collective-permute-start(f32[2,6,1904]{2,0,1:T(2,128)S(1)} %pad_maximum_fusion.10), channel_id=1, source_target_pairs={{0,16},{16,0},{1,17},{17,1},{2,18},{18,2},{3,19},{19,3},{4,20},{20... | collective-permute-start | bytes 274184 | tf_op jit(solution)/shard_map/ppermute | solution.py:31
  20.2 1.3 %collective-permute-start.4 = (f32[2,6,1632]{2,0,1:T(2,128)S(1)}, f32[2,6,1632]{2,0,1:T(2,128)S(1)}, u32[]{:S(2)}, u32[]{:S(2)}) collective-permute-start(f32[2,6,1632]{2,0,1:T(2,128)S(1)} %pad_maximum_fusion.13), channel_id=1, source_target_pairs={{0,16},{16,0},{1,17},{17,1},{2,18},{18,2},{3,19},{19,3},{4,20},{20... | collective-permute-start | bytes 235016 | tf_op jit(solution)/shard_map/ppermute | solution.py:31
  23.7 1.3 %collective-permute-start.5 = (f32[2,6,1360]{2,0,1:T(2,128)S(1)}, f32[2,6,1360]{2,0,1:T(2,128)S(1)}, u32[]{:S(2)}, u32[]{:S(2)}) collective-permute-start(f32[2,6,1360]{2,0,1:T(2,128)S(1)} %pad_maximum_fusion.14), channel_id=1, source_target_pairs={{0,16},{16,0},{1,17},{17,1},{2,18},{18,2},{3,19},{19,3},{4,20},{20... | collective-permute-start | bytes 195848 | tf_op jit(solution)/shard_map/ppermute | solution.py:31
  28.9 1.3 %collective-permute-start.6 = (f32[2,6,8,128]{3,2,1,0:T(8,128)S(1)}, f32[2,6,8,128]{3,2,1,0:T(8,128)S(1)}, u32[]{:S(2)}, u32[]{:S(2)}) collective-permute-start(f32[2,6,8,128]{3,2,1,0:T(8,128)S(1)} %pad_maximum_fusion.19), channel_id=1, source_target_pairs={{0,16},{16,0},{1,17},{17,1},{2,18},{18,2},{3,19},{19,3},{4,20},{20... | collective-permute-start | bytes 147464 | tf_op jit(solution)/shard_map/ppermute | solution.py:31

commit v18 on v17

--- a/solution.py
+++ b/solution.py
@@ -168,8 +168,32 @@
     above_y = lax.ppermute(start[:, :, :rim_y], "gy", ring("gy", -1))
     wide = jnp.concatenate([below_y, start, above_y], 2)
 
-    above = lax.ppermute(wide[..., :count].reshape(wide.shape[0], -1), "gz", line("gz", -1))
-    ext = jnp.concatenate([wide[..., low:], above.reshape(wide.shape[:3] + (count,))], 3)
+    bricks_yz = bricks_y * bricks_z
+
+    def diagonal(by):
+        pairs = []
+        for source in range(bricks_yz):
+            sy, sz = source // bricks_z, source % bricks_z
+            if sz >= 1:
+                pairs.append((source, ((sy + by) % bricks_y) * bricks_z + sz - 1))
+        return pairs
+
+    def flat_top(part):
+        return part[..., :count].reshape(part.shape[0], -1)
+
+    top_own = lax.ppermute(flat_top(start), "gz", line("gz", -1))
+    top_low = lax.ppermute(flat_top(start[:, :, -rim_y:]), ("gy", "gz"), diagonal(1))
+    top_high = lax.ppermute(flat_top(start[:, :, :rim_y]), ("gy", "gz"), diagonal(-1))
+    cells_xs = start.shape[:2]
+    above = jnp.concatenate(
+        [
+            top_low.reshape(cells_xs + (rim_y, count)),
+            top_own.reshape(cells_xs + (cells_y, count)),
+            top_high.reshape(cells_xs + (rim_y, count)),
+        ],
+        2,
+    )
+    ext = jnp.concatenate([wide[..., low:], above], 3)
     ext = jnp.concatenate(
         [jnp.stack([(ext[0] == phase).astype(jnp.float32) for phase in range(4)]), ext[1:]], 0
     )

time: 32.7 us -> 35.4 us (1.083)
  starting transfers between devices: 6.03 us -> 8.62 us
  waiting for transfers between devices: 8.4 us -> 7.71 us
    ppermute x1 -> x3, starting transfers between devices: 1.29 us -> 3.88 us  [the longest x1 1.29 us: shards(): lax.ppermute(flat_top(start[:, :, -rim_y:]), ('gy', 'gz'), diagonal(1))]
    ppermute x1, waiting for transfers between devices: 0.84 us -> 0.01 us  [shards(): above_y = lax.ppermute(start[:, :, :rim_y], 'gy', ring('gy', -1))]
    reshape x2 -> x6, local copies, waits for them, and re-layouts: 0.41 us -> 0.75 us  [the longest x3 0.36 us: flat_top(): return part[..., :count].reshape(part.shape[0], -1)]
    ppermute x1 -> x3, waiting for transfers between devices: 3.85 us -> 3.99 us  [the longest x1 3.99 us: shards(): top_own = lax.ppermute(flat_top(start), 'gz', line('gz', -1))]
  transfers between devices with their start and end apart: 7 -> 9, of which waited for: 6 -> 5; matrix products, arithmetic and copies ran while one was open for 10% -> 11% of each run, Pallas kernels for 0% -> 0%
where the time goes in v18:
time: 35.4 us; the launch traced here: 34.8 us
  other arithmetic  9.86 us (28%)
  starting transfers between devices  8.62 us (24%)
  waiting for transfers between devices  7.71 us (22%)
  local copies, waits for them, and re-layouts  7.25 us (20%)
  between operations  1.4 us (4%)
    ppermute x1, waiting for transfers between devices, shards(): top_own = lax.ppermute(flat_top(start), 'gz', line('gz', -1))  3.99 us
    ppermute x4, waiting for transfers between devices, x_halos(): got = lax.ppermute(pair, 'gx', ring('gx', 1))  3.71 us
    ppermute x1, starting transfers between devices, shards(): below_y = lax.ppermute(start[:, :, -rim_y:], 'gy', ring('gy', 1))  2.99 us
    ppermute x1, starting transfers between devices, shards(): lax.ppermute(flat_top(start[:, :, -rim_y:]), ('gy', 'gz'), diagonal(1))  1.29 us
    ppermute x1, starting transfers between devices, shards(): lax.ppermute(flat_top(start[:, :, :rim_y]), ('gy', 'gz'), diagonal(-1))  1.29 us
    ppermute x1, starting transfers between devices, shards(): top_own = lax.ppermute(flat_top(start), 'gz', line('gz', -1))  1.29 us
    sub x4, other arithmetic, chem_update(): delta = shape_fn(phi_new) - shape_fn(phi_old)  1.19 us
    mul x4, other arithmetic, phase_update(): square = phi * phi  1.13 us
  transfers between devices with their start and end apart: 9, of which 5 were waited for; matrix products, arithmetic and copies ran while one was open for 11% of the time, Pallas kernels for 0%

profile of v18, /device:TPU:0, one launch (start us, length us, event | category | flops | bytes accessed | tf_op | source)
XLA Modules:
  0.0 34.8 jit_solution(6161541869647378080)
XLA Ops:
  0.6 0.8 %convert_bitcast_fusion = f32[1,8,8,128]{3,2,1,0:T(8,128)S(1)} fusion(s32[8,8,128]{2,1,0:T(8,128)} %param.3), kind=kLoop, calls=%fused_computation.483 | loop fusion | flops 8192 | bytes 65536 | tf_op jit(solution)/shard_map/broadcast_in_dim | solution.py:165
  1.6 1.3 %collective-permute-start.2 = (f32[3,1152]{1,0:T(4,128)S(1)}, f32[3,1152]{1,0:T(4,128)S(1)}, u32[]{:S(2)}, u32[]{:S(2)}) collective-permute-start(f32[3,1152]{1,0:T(4,128)S(1)} %reshape.864), channel_id=1, source_target_pairs={{1,4},{2,5},{3,6},{5,8},{6,9},{7,10},{9,12},{10,13},{11,14},{13,0}... | collective-permute-start | bytes 41480 | tf_op jit(solution)/shard_map/ppermute | solution.py:185
  3.0 1.3 %collective-permute-start.4 = (f32[3,1152]{1,0:T(4,128)S(1)}, f32[3,1152]{1,0:T(4,128)S(1)}, u32[]{:S(2)}, u32[]{:S(2)}) collective-permute-start(f32[3,1152]{1,0:T(4,128)S(1)} %reshape.868), channel_id=1, source_target_pairs={{1,12},{2,13},{3,14},{5,0},{6,1},{7,2},{9,4},{10,5},{11,6},{13,8},... | collective-permute-start | bytes 41480 | tf_op jit(solution)/shard_map/ppermute | solution.py:186
  4.4 3.0 %collective-permute-start = (f32[3,8,4,128]{3,2,1,0:T(4,128)S(1)}, f32[3,8,4,128]{3,2,1,0:T(4,128)S(1)}, u32[]{:S(2)}, u32[]{:S(2)}) collective-permute-start(f32[3,8,4,128]{3,2,1,0:T(4,128)S(1)} %get-tuple-element.125), channel_id=1, source_target_pairs={{0,4},{4,8},{8,12},{12,0},{1,5},{5,9},{9,13},{13,1},{2,6},{6,10},{... | collective-permute-start | bytes 147464 | tf_op jit(solution)/shard_map/ppermute | solution.py:167
  7.3 1.0 %collective-permute-start.1 = (f32[3,8,4,128]{3,2,1,0:T(4,128)S(1)}, f32[3,8,4,128]{3,2,1,0:T(4,128)S(1)}, u32[]{:S(2)}, u32[]{:S(2)}) collective-permute-start(f32[3,8,4,128]{3,2,1,0:T(4,128)S(1)} %get-tuple-element.126), channel_id=1, source_target_pairs={{0,12},{4,0},{8,4},{12,8},{1,13},{5,1},{9,5},{13,9},{2,14},{6,2},{... | collective-permute-start | bytes 147464 | tf_op jit(solution)/shard_map/ppermute | solution.py:168
  8.4 0.1 reshape.866
  8.5 1.3 %collective-permute-start.3 = (f32[3,2304]{1,0:T(4,128)S(1)}, f32[3,2304]{1,0:T(4,128)S(1)}, u32[]{:S(2)}, u32[]{:S(2)}) collective-permute-start(f32[3,2304]{1,0:T(4,128)S(1)} %reshape.866), channel_id=1, source_target_pairs={{1,0},{2,1},{3,2},{5,4},{6,5},{7,6},{9,8},{10,9},{11,10},{13,12},{... | collective-permute-start | bytes 82952 | tf_op jit(solution)/shard_map/ppermute | solution.py:184
  10.1 0.6 %copy-done.1 = s32[32,3]{0,1:T(4,128)S(1)} copy-done((s32[32,3]{0,1:T(4,128)S(1)}, s32[32,3]{0,1:T(4,128)}, u32[]{:S(2)}) %copy-start.1) | copy-done | bytes 408
  11.0 0.2 and_reduce_fusion
  11.1 0.2 and_reduce_fusion.1
  11.8 0.1 and_reduce_fusion.2
  13.0 0.1 reshape.865
  13.3 4.0 %collective-permute-done.3 = f32[3,2304]{1,0:T(4,128)S(1)} collective-permute-done((f32[3,2304]{1,0:T(4,128)S(1)}, f32[3,2304]{1,0:T(4,128)S(1)}, u32[]{:S(2)}, u32[]{:S(2)}) %collective-permute-start.3) | collective-permute-done | bytes 27680 | tf_op jit(solution)/shard_map/ppermute | solution.py:184
  17.3 0.1 reshape.867
  17.4 0.2 compare_convert_fusion
  18.2 0.3 fusion.14
  18.5 0.2 concatenate.110
  18.7 0.2 maximum_select_fusion.1
  18.9 0.3 slice_bitcast_fusion.3
  19.3 0.3 fusion.305
  19.6 1.0 %collective-permute-done.5 = f32[2,6,1904]{2,0,1:T(2,128)S(1)} collective-permute-done((f32[2,6,1904]{2,0,1:T(2,128)S(1)}, f32[2,6,1904]{2,0,1:T(2,128)S(1)}, u32[]{:S(2)}, u32[]{:S(2)}) %collective-permute-start.5) | collective-permute-done | bytes 91424 | tf_op jit(solution)/shard_map/ppermute | solution.py:31
  20.7 0.3 slice_multiply_fusion
  21.1 0.2 multiply_add_fusion.4
  21.4 0.2 multiply_add_fusion.3
  21.6 0.2 multiply_subtract_fusion
  21.7 0.2 fusion.48
  22.1 0.2 maximum_select_fusion.2
  22.3 0.2 slice_bitcast_fusion.7
  22.6 0.2 collective-permute-start.6
  22.8 0.2 fusion.306
  23.0 0.9 %collective-permute-done.6 = f32[2,6,1632]{2,0,1:T(2,128)S(1)} collective-permute-done((f32[2,6,1632]{2,0,1:T(2,128)S(1)}, f32[2,6,1632]{2,0,1:T(2,128)S(1)}, u32[]{:S(2)}, u32[]{:S(2)}) %collective-permute-start.6) | collective-permute-done | bytes 78368 | tf_op jit(solution)/shard_map/ppermute | solution.py:31
  24.0 0.3 slice_multiply_fusion.1
  24.4 0.2 multiply_add_fusion.9
  24.6 0.2 multiply_add_fusion.8
  24.8 0.1 multiply_subtract_fusion.1
  24.9 0.2 fusion.61
  25.3 0.1 fusion.308
  25.6 0.2 maximum_select_fusion.4
  25.7 0.2 slice_bitcast_fusion.11
  26.0 0.2 collective-permute-start.7
  26.2 0.2 fusion.307
  26.5 0.9 %collective-permute-done.7 = f32[2,6,1360]{2,0,1:T(2,128)S(1)} collective-permute-done((f32[2,6,1360]{2,0,1:T(2,128)S(1)}, f32[2,6,1360]{2,0,1:T(2,128)S(1)}, u32[]{:S(2)}, u32[]{:S(2)}) %collective-permute-start.7) | collective-permute-done | bytes 65312 | tf_op jit(solution)/shard_map/ppermute | solution.py:31
  27.4 0.3 slice_multiply_fusion.2
  27.8 0.2 multiply_add_fusion.14
  28.0 0.2 fusion.198
  28.1 0.1 multiply_subtract_fusion.2
  28.3 0.4 %concatenate.129 = f32[4,8,10,136]{3,2,1,0:T(8,128)S(1)} reshape(f32[4,8,1360]{2,1,0:T(8,128)S(1)} %get-tuple-element.12) | data formatting | bytes 348160 | tf_op jit(solution)/shard_map/concatenate | solution.py:152
  28.7 0.2 fusion.75
  29.0 0.1 concatenate.130
  29.1 0.1 concatenate.131
  29.2 0.1 fusion.310
  29.4 0.1 fusion.13
  29.5 0.7 %concatenate.126 = f32[6,8,10,136]{3,2,1,0:T(8,128)S(1)} reshape(f32[6,8,1360]{2,1,0:T(8,128)S(1)} %get-tuple-element.119) | data formatting | bytes 522240 | tf_op jit(solution)/shard_map/concatenate | solution.py:214
  30.2 0.7 %concatenate.128 = f32[6,8,10,136]{3,2,1,0:T(8,128)S(1)} reshape(f32[6,8,1360]{2,1,0:T(8,128)S(1)} %get-tuple-element.118) | data formatting | bytes 522240 | tf_op jit(solution)/shard_map/concatenate | solution.py:211
  30.9 0.3 fusion
  31.2 0.2 collective-permute-start.8
  31.5 0.2 fusion.304
  31.6 0.9 %collective-permute-done.8 = f32[2,6,8,128]{3,2,1,0:T(8,128)S(1)} collective-permute-done((f32[2,6,8,128]{3,2,1,0:T(8,128)S(1)}, f32[2,6,8,128]{3,2,1,0:T(8,128)S(1)}, u32[]{:S(2)}, u32[]{:S(2)}) %collective-permute-start.8) | collective-permute-done | bytes 49184 | tf_op jit(solution)/shard_map/ppermute | solution.py:31
  32.5 0.2 slice_multiply_fusion.3
  32.9 0.1 multiply_add_fusion.19
  33.0 0.1 fusion.240
  33.2 0.8 %multiply_subtract_fusion.3 = (f32[4,8,8,128]{3,2,1,0:T(8,128)S(1)}, f32[4,8,8,128]{3,2,1,0:T(8,128)}) fusion(f32[6,8,10,136]{3,2,1,0:T(8,128)S(1)} %fusion, f32[1,8,8,128]{3,2,1,0:T(8,128)S(1)} %get-tuple-element.49, f32[1,8,8,128]{3,2,1,0:T(8,128)S(1)} %get-tuple-element.50, f32[1,8,8,128]{3,2,1,0:T(8,128)S(1)} %get-tuple-element.51, ...), kind=kLoop, calls=%fused_computation.126 | loop fusion | flops 425984 | bytes 525312 | tf_op jit(solution)/shard_map/sub | solution.py:92
  33.9 0.2 fusion.88
  34.2 0.6 %pad_maximum_fusion.19 = f32[2,8,8,128]{3,2,1,0:T(8,128)} fusion(f32[1,8,8,128]{3,2,1,0:T(8,128)S(1)} %get-tuple-element.41, f32[1,8,8,128]{3,2,1,0:T(8,128)S(1)} %get-tuple-element.40), kind=kLoop, calls=%fused_computation.217 | loop fusion | flops 16384 | bytes 131072 | tf_op jit(solution)/shard_map/stack | solution.py:102
  (90 shorter events, 4.5 us)
Async XLA Ops:
  0.6 0.8 %copy-start = (f32[2,8,8,128]{3,2,1,0:T(8,128)S(1)}, f32[2,8,8,128]{3,2,1,0:T(8,128)}, u32[]{:S(2)}) copy-start(f32[2,8,8,128]{3,2,1,0:T(8,128)} %param.4) | copy-start | bytes 196612
  1.6 11.4 %collective-permute-start.2 = (f32[3,1152]{1,0:T(4,128)S(1)}, f32[3,1152]{1,0:T(4,128)S(1)}, u32[]{:S(2)}, u32[]{:S(2)}) collective-permute-start(f32[3,1152]{1,0:T(4,128)S(1)} %reshape.864), channel_id=1, source_target_pairs={{1,4},{2,5},{3,6},{5,8},{6,9},{7,10},{9,12},{10,13},{11,14},{13,0}... | collective-permute-start | bytes 41480 | tf_op jit(solution)/shard_map/ppermute | solution.py:185
  3.0 10.1 %collective-permute-start.4 = (f32[3,1152]{1,0:T(4,128)S(1)}, f32[3,1152]{1,0:T(4,128)S(1)}, u32[]{:S(2)}, u32[]{:S(2)}) collective-permute-start(f32[3,1152]{1,0:T(4,128)S(1)} %reshape.868), channel_id=1, source_target_pairs={{1,12},{2,13},{3,14},{5,0},{6,1},{7,2},{9,4},{10,5},{11,6},{13,8},... | collective-permute-start | bytes 41480 | tf_op jit(solution)/shard_map/ppermute | solution.py:186
  4.4 13.1 %collective-permute-start = (f32[3,8,4,128]{3,2,1,0:T(4,128)S(1)}, f32[3,8,4,128]{3,2,1,0:T(4,128)S(1)}, u32[]{:S(2)}, u32[]{:S(2)}) collective-permute-start(f32[3,8,4,128]{3,2,1,0:T(4,128)S(1)} %get-tuple-element.125), channel_id=1, source_target_pairs={{0,4},{4,8},{8,12},{12,0},{1,5},{5,9},{9,13},{13,1},{2,6},{6,10},{... | collective-permute-start | bytes 147464 | tf_op jit(solution)/shard_map/ppermute | solution.py:167
  7.3 10.1 %collective-permute-start.1 = (f32[3,8,4,128]{3,2,1,0:T(4,128)S(1)}, f32[3,8,4,128]{3,2,1,0:T(4,128)S(1)}, u32[]{:S(2)}, u32[]{:S(2)}) collective-permute-start(f32[3,8,4,128]{3,2,1,0:T(4,128)S(1)} %get-tuple-element.126), channel_id=1, source_target_pairs={{0,12},{4,0},{8,4},{12,8},{1,13},{5,1},{9,5},{13,9},{2,14},{6,2},{... | collective-permute-start | bytes 147464 | tf_op jit(solution)/shard_map/ppermute | solution.py:168
  8.5 8.8 %collective-permute-start.3 = (f32[3,2304]{1,0:T(4,128)S(1)}, f32[3,2304]{1,0:T(4,128)S(1)}, u32[]{:S(2)}, u32[]{:S(2)}) collective-permute-start(f32[3,2304]{1,0:T(4,128)S(1)} %reshape.866), channel_id=1, source_target_pairs={{1,0},{2,1},{3,2},{5,4},{6,5},{7,6},{9,8},{10,9},{11,10},{13,12},{... | collective-permute-start | bytes 82952 | tf_op jit(solution)/shard_map/ppermute | solution.py:184
  10.0 0.7 %copy-start.1 = (s32[32,3]{0,1:T(4,128)S(1)}, s32[32,3]{0,1:T(4,128)}, u32[]{:S(2)}) copy-start(s32[32,3]{0,1:T(4,128)} %param.5) | copy-start | bytes 1156
  19.2 1.4 %collective-permute-start.5 = (f32[2,6,1904]{2,0,1:T(2,128)S(1)}, f32[2,6,1904]{2,0,1:T(2,128)S(1)}, u32[]{:S(2)}, u32[]{:S(2)}) collective-permute-start(f32[2,6,1904]{2,0,1:T(2,128)S(1)} %pad_maximum_fusion.12), channel_id=1, source_target_pairs={{0,16},{16,0},{1,17},{17,1},{2,18},{18,2},{3,19},{19,3},{4,20},{20... | collective-permute-start | bytes 274184 | tf_op jit(solution)/shard_map/ppermute | solution.py:31
  22.6 1.3 %collective-permute-start.6 = (f32[2,6,1632]{2,0,1:T(2,128)S(1)}, f32[2,6,1632]{2,0,1:T(2,128)S(1)}, u32[]{:S(2)}, u32[]{:S(2)}) collective-permute-start(f32[2,6,1632]{2,0,1:T(2,128)S(1)} %pad_maximum_fusion.15), channel_id=1, source_target_pairs={{0,16},{16,0},{1,17},{17,1},{2,18},{18,2},{3,19},{19,3},{4,20},{20... | collective-permute-start | bytes 235016 | tf_op jit(solution)/shard_map/ppermute | solution.py:31
  26.0 1.3 %collective-permute-start.7 = (f32[2,6,1360]{2,0,1:T(2,128)S(1)}, f32[2,6,1360]{2,0,1:T(2,128)S(1)}, u32[]{:S(2)}, u32[]{:S(2)}) collective-permute-start(f32[2,6,1360]{2,0,1:T(2,128)S(1)} %pad_maximum_fusion.16), channel_id=1, source_target_pairs={{0,16},{16,0},{1,17},{17,1},{2,18},{18,2},{3,19},{19,3},{4,20},{20... | collective-permute-start | bytes 195848 | tf_op jit(solution)/shard_map/ppermute | solution.py:31
  31.2 1.3 %collective-permute-start.8 = (f32[2,6,8,128]{3,2,1,0:T(8,128)S(1)}, f32[2,6,8,128]{3,2,1,0:T(8,128)S(1)}, u32[]{:S(2)}, u32[]{:S(2)}) collective-permute-start(f32[2,6,8,128]{3,2,1,0:T(8,128)S(1)} %pad_maximum_fusion.21), channel_id=1, source_target_pairs={{0,16},{16,0},{1,17},{17,1},{2,18},{18,2},{3,19},{19,3},{4,20},{20... | collective-permute-start | bytes 147464 | tf_op jit(solution)/shard_map/ppermute | solution.py:31

commit v19 on v17

--- a/solution.py
+++ b/solution.py
@@ -164,8 +164,19 @@
 
     start = jnp.concatenate([labels.astype(jnp.float32)[None], mu_start], 0)
     nf = 4 + mu_start.shape[0]
-    below_y = lax.ppermute(start[:, :, -rim_y:], "gy", ring("gy", 1))
-    above_y = lax.ppermute(start[:, :, :rim_y], "gy", ring("gy", -1))
+    if bricks_y > 2:
+        slot = lax.broadcasted_iota(jnp.int32, (bricks_y,) + start[:, :, :rim_y].shape, 0)
+        send = jnp.where(
+            slot == (index_y + bricks_y - 1) % bricks_y,
+            start[None, :, :, :rim_y],
+            jnp.where(slot == (index_y + 1) % bricks_y, start[None, :, :, -rim_y:], 0.0),
+        )
+        got = lax.all_to_all(send, "gy", 0, 0)
+        below_y = got[(index_y + bricks_y - 1) % bricks_y]
+        above_y = got[(index_y + 1) % bricks_y]
+    else:
+        below_y = lax.ppermute(start[:, :, -rim_y:], "gy", ring("gy", 1))
+        above_y = lax.ppermute(start[:, :, :rim_y], "gy", ring("gy", -1))
     wide = jnp.concatenate([below_y, start, above_y], 2)
 
     above = lax.ppermute(wide[..., :count].reshape(wide.shape[0], -1), "gz", line("gz", -1))

time: 32.7 us -> 36.9 us (1.13)
  waiting for transfers between devices: 8.4 us -> 10.5 us
  starting transfers between devices: 6.03 us -> 7.19 us
  local copies, waits for them, and re-layouts: 7.02 us -> 7.8 us
    all_to_all x0 -> x1, starting transfers between devices: none -> 5.16 us  [shards(): got = lax.all_to_all(send, 'gy', 0, 0)]
    ppermute x2 -> x0, starting transfers between devices: 4.01 us -> none  [the longest x1 2.99 us: shards(): below_y = lax.ppermute(start[:, :, -rim_y:], 'gy', ring('gy', 1))]
    all_to_all x0 -> x1, waiting for transfers between devices: none -> 2.96 us  [shards(): got = lax.all_to_all(send, 'gy', 0, 0)]
    ppermute x2 -> x0, waiting for transfers between devices: 0.84 us -> none  [the longest x1 0.84 us: shards(): above_y = lax.ppermute(start[:, :, :rim_y], 'gy', ring('gy', -1))]
    broadcast_in_dim x1, other arithmetic: 0.79 us -> 0.01 us  [shards(): start = jnp.concatenate([labels.astype(jnp.float32)[None], mu_start], 0)]
    select_n x0 -> x1, other arithmetic: none -> 0.78 us  [shards(): jnp.where(slot == (index_y + bricks_y - 1) % bricks_y, start[None, :, :,...]
    unnamed x8 -> x10, local copies, waits for them, and re-layouts: 0.72 us -> 1.49 us
  transfers between devices with their start and end apart: 7 -> 6, of which waited for: 6 -> 6; matrix products, arithmetic and copies ran while one was open for 10% -> 9% of each run, Pallas kernels for 0% -> 0%
where the time goes in v19:
time: 36.9 us; the launch traced here: 36.6 us
  waiting for transfers between devices  10.5 us (28%)
  other arithmetic  9.68 us (26%)
  local copies, waits for them, and re-layouts  7.8 us (21%)
  starting transfers between devices  7.19 us (19%)
  between operations  1.38 us (4%)
    all_to_all x1, starting transfers between devices, shards(): got = lax.all_to_all(send, 'gy', 0, 0)  5.16 us
    ppermute x1, waiting for transfers between devices, shards(): lax.ppermute(wide[..., :count].reshape(wide.shape[0], -1), 'gz', line('gz...  3.85 us
    ppermute x4, waiting for transfers between devices, x_halos(): got = lax.ppermute(pair, 'gx', ring('gx', 1))  3.71 us
    all_to_all x1, waiting for transfers between devices, shards(): got = lax.all_to_all(send, 'gy', 0, 0)  2.96 us
    unnamed x10, local copies, waits for them, and re-layouts  1.49 us
    ppermute x1, starting transfers between devices, shards(): lax.ppermute(wide[..., :count].reshape(wide.shape[0], -1), 'gz', line('gz...  1.29 us
    sub x4, other arithmetic, chem_update(): delta = shape_fn(phi_new) - shape_fn(phi_old)  1.19 us
    mul x4, other arithmetic, phase_update(): square = phi * phi  1.13 us
  transfers between devices with their start and end apart: 6, of which 6 were waited for; matrix products, arithmetic and copies ran while one was open for 9% of the time, Pallas kernels for 0%

profile of v19, /device:TPU:0, one launch (start us, length us, event | category | flops | bytes accessed | tf_op | source)
XLA Modules:
  0.0 36.6 jit_solution(12889371564427354902)
XLA Ops:
  0.7 0.7 %copy-done.1 = s32[8,8,128]{2,1,0:T(8,128)S(1)} copy-done((s32[8,8,128]{2,1,0:T(8,128)S(1)}, s32[8,8,128]{2,1,0:T(8,128)}, u32[]{:S(2)}) %copy-start.1) | copy-done | bytes 32792
  1.5 0.8 %select_select_fusion = f32[4,3,8,4,128]{4,3,2,1,0:T(4,128)} fusion(f32[3,8,4,128]{3,2,1,0:T(4,128)S(1)} %get-tuple-element.128, f32[3,8,4,128]{3,2,1,0:T(4,128)S(1)} %get-tuple-element.127, pred[4]{0:T(512)(128)(4,1)S(1)} %get-tuple-element.143, pred[4]{0:T(512)(128)(4,1)S(1)} %get-tuple-element.144), kind=kLoop, calls=%fused_computation.96 | loop fusion | flops 98304 | bytes 294920 | tf_op jit(solution)/shard_map/jit(_where)/select_n | solution.py:169
  2.3 5.2 %all-to-all-start = ((f32[4,3,8,4,128]{4,3,2,1,0:T(4,128)}), f32[4,3,8,4,128]{4,3,2,1,0:T(4,128)S(1)}, u32[]{:S(2)}, u32[]{:S(2)}) async-start(f32[4,3,8,4,128]{4,3,2,1,0:T(4,128)} %select_select_fusion), calls=%async_computation | async-start | bytes 393216 | tf_op jit(solution)/shard_map/all_to_all | solution.py:174
  7.7 0.6 %copy-done.2 = s32[32,3]{0,1:T(4,128)S(1)} copy-done((s32[32,3]{0,1:T(4,128)S(1)}, s32[32,3]{0,1:T(4,128)}, u32[]{:S(2)}) %copy-start.2) | copy-done | bytes 408
  9.1 0.2 and_reduce_fusion.1
  9.2 0.1 and_reduce_fusion.2
  9.5 0.2 and_reduce_fusion
  9.7 3.0 %all-to-all-done = f32[4,3,8,4,128]{4,3,2,1,0:T(4,128)S(1)} async-done(((f32[4,3,8,4,128]{4,3,2,1,0:T(4,128)}), f32[4,3,8,4,128]{4,3,2,1,0:T(4,128)S(1)}, u32[]{:S(2)}, u32[]{:S(2)}) %all-to-all-start) | async-done | bytes 196640 | tf_op jit(solution)/shard_map/all_to_all | solution.py:174
  12.7 0.2 reshape.854
  12.9 1.3 %collective-permute-start = (f32[3,4608]{1,0:T(4,128)S(1)}, f32[3,4608]{1,0:T(4,128)S(1)}, u32[]{:S(2)}, u32[]{:S(2)}) collective-permute-start(f32[3,4608]{1,0:T(4,128)S(1)} %reshape.854), channel_id=1, source_target_pairs={{1,0},{2,1},{3,2},{5,4},{6,5},{7,6},{9,8},{10,9},{11,10},{13,12},{... | collective-permute-start | bytes 165896 | tf_op jit(solution)/shard_map/ppermute | solution.py:182
  15.3 3.9 %collective-permute-done = f32[3,4608]{1,0:T(4,128)S(1)} collective-permute-done((f32[3,4608]{1,0:T(4,128)S(1)}, f32[3,4608]{1,0:T(4,128)S(1)}, u32[]{:S(2)}, u32[]{:S(2)}) %collective-permute-start) | collective-permute-done | bytes 55328 | tf_op jit(solution)/shard_map/ppermute | solution.py:182
  19.1 0.2 reshape.855
  19.5 0.1 pad_maximum_fusion.3
  19.7 0.1 reshape.856
  19.8 0.1 reshape.857
  20.2 0.2 concatenate.106
  20.4 0.2 maximum_select_fusion.1
  20.6 0.3 slice_bitcast_fusion.3
  21.1 0.3 fusion.301
  21.3 1.0 %collective-permute-done.1 = f32[2,6,1904]{2,0,1:T(2,128)S(1)} collective-permute-done((f32[2,6,1904]{2,0,1:T(2,128)S(1)}, f32[2,6,1904]{2,0,1:T(2,128)S(1)}, u32[]{:S(2)}, u32[]{:S(2)}) %collective-permute-start.1) | collective-permute-done | bytes 91424 | tf_op jit(solution)/shard_map/ppermute | solution.py:31
  22.4 0.3 slice_multiply_fusion
  22.7 0.1 fusion.137
  22.9 0.2 multiply_add_fusion.4
  23.1 0.2 multiply_add_fusion.3
  23.3 0.2 multiply_subtract_fusion
  23.4 0.2 fusion.47
  23.8 0.2 maximum_select_fusion.2
  24.0 0.2 slice_bitcast_fusion.7
  24.3 0.2 collective-permute-start.2
  24.5 0.2 fusion.302
  24.8 0.9 %collective-permute-done.2 = f32[2,6,1632]{2,0,1:T(2,128)S(1)} collective-permute-done((f32[2,6,1632]{2,0,1:T(2,128)S(1)}, f32[2,6,1632]{2,0,1:T(2,128)S(1)}, u32[]{:S(2)}, u32[]{:S(2)}) %collective-permute-start.2) | collective-permute-done | bytes 78368 | tf_op jit(solution)/shard_map/ppermute | solution.py:31
  25.7 0.3 slice_multiply_fusion.1
  26.1 0.2 multiply_add_fusion.9
  26.3 0.2 multiply_add_fusion.8
  26.5 0.1 multiply_subtract_fusion.1
  26.7 0.2 fusion.60
  27.1 0.1 fusion.304
  27.3 0.2 maximum_select_fusion.4
  27.5 0.2 slice_bitcast_fusion.11
  27.8 0.2 collective-permute-start.3
  28.0 0.2 fusion.303
  28.2 0.9 %collective-permute-done.3 = f32[2,6,1360]{2,0,1:T(2,128)S(1)} collective-permute-done((f32[2,6,1360]{2,0,1:T(2,128)S(1)}, f32[2,6,1360]{2,0,1:T(2,128)S(1)}, u32[]{:S(2)}, u32[]{:S(2)}) %collective-permute-start.3) | collective-permute-done | bytes 65312 | tf_op jit(solution)/shard_map/ppermute | solution.py:31
  29.1 0.3 slice_multiply_fusion.2
  29.5 0.2 multiply_add_fusion.14
  29.7 0.2 fusion.194
  29.8 0.1 multiply_subtract_fusion.2
  30.0 0.4 %concatenate.125 = f32[4,8,10,136]{3,2,1,0:T(8,128)S(1)} reshape(f32[4,8,1360]{2,1,0:T(8,128)S(1)} %get-tuple-element.12) | data formatting | bytes 348160 | tf_op jit(solution)/shard_map/concatenate | solution.py:152
  30.4 0.2 fusion.73
  30.7 0.1 concatenate.126
  30.8 0.1 concatenate.127
  31.0 0.1 fusion.306
  31.1 0.1 fusion.13
  31.2 0.7 %concatenate.122 = f32[6,8,10,136]{3,2,1,0:T(8,128)S(1)} reshape(f32[6,8,1360]{2,1,0:T(8,128)S(1)} %get-tuple-element.119) | data formatting | bytes 522240 | tf_op jit(solution)/shard_map/concatenate | solution.py:201
  31.9 0.7 %concatenate.124 = f32[6,8,10,136]{3,2,1,0:T(8,128)S(1)} reshape(f32[6,8,1360]{2,1,0:T(8,128)S(1)} %get-tuple-element.118) | data formatting | bytes 522240 | tf_op jit(solution)/shard_map/concatenate | solution.py:198
  32.6 0.3 fusion
  33.0 0.2 collective-permute-start.4
  33.2 0.2 fusion.300
  33.3 0.9 %collective-permute-done.4 = f32[2,6,8,128]{3,2,1,0:T(8,128)S(1)} collective-permute-done((f32[2,6,8,128]{3,2,1,0:T(8,128)S(1)}, f32[2,6,8,128]{3,2,1,0:T(8,128)S(1)}, u32[]{:S(2)}, u32[]{:S(2)}) %collective-permute-start.4) | collective-permute-done | bytes 49184 | tf_op jit(solution)/shard_map/ppermute | solution.py:31
  34.3 0.2 slice_multiply_fusion.3
  34.6 0.1 multiply_add_fusion.19
  34.8 0.1 fusion.236
  34.9 0.8 %multiply_subtract_fusion.3 = (f32[4,8,8,128]{3,2,1,0:T(8,128)S(1)}, f32[4,8,8,128]{3,2,1,0:T(8,128)}) fusion(f32[6,8,10,136]{3,2,1,0:T(8,128)S(1)} %fusion, f32[1,8,8,128]{3,2,1,0:T(8,128)S(1)} %get-tuple-element.49, f32[1,8,8,128]{3,2,1,0:T(8,128)S(1)} %get-tuple-element.50, f32[1,8,8,128]{3,2,1,0:T(8,128)S(1)} %get-tuple-element.51, ...), kind=kLoop, calls=%fused_computation.119 | loop fusion | flops 425984 | bytes 525312 | tf_op jit(solution)/shard_map/sub | solution.py:92
  35.7 0.2 fusion.86
  35.9 0.6 %pad_maximum_fusion.17 = f32[2,8,8,128]{3,2,1,0:T(8,128)} fusion(f32[1,8,8,128]{3,2,1,0:T(8,128)S(1)} %get-tuple-element.41, f32[1,8,8,128]{3,2,1,0:T(8,128)S(1)} %get-tuple-element.40), kind=kLoop, calls=%fused_computation.207 | loop fusion | flops 16384 | bytes 131072 | tf_op jit(solution)/shard_map/stack | solution.py:102
  (85 shorter events, 4.1 us)
Async XLA Ops:
  0.6 0.8 %copy-start.1 = (s32[8,8,128]{2,1,0:T(8,128)S(1)}, s32[8,8,128]{2,1,0:T(8,128)}, u32[]{:S(2)}) copy-start(s32[8,8,128]{2,1,0:T(8,128)} %param.3) | copy-start | bytes 98308
  0.6 0.8 %copy-start = (f32[2,8,8,128]{3,2,1,0:T(8,128)S(1)}, f32[2,8,8,128]{3,2,1,0:T(8,128)}, u32[]{:S(2)}) copy-start(f32[2,8,8,128]{3,2,1,0:T(8,128)} %param.4) | copy-start | bytes 196612
  2.3 10.4 %all-to-all-start = ((f32[4,3,8,4,128]{4,3,2,1,0:T(4,128)}), f32[4,3,8,4,128]{4,3,2,1,0:T(4,128)S(1)}, u32[]{:S(2)}, u32[]{:S(2)}) async-start(f32[4,3,8,4,128]{4,3,2,1,0:T(4,128)} %select_select_fusion), calls=%async_computation | async-start | bytes 393216 | tf_op jit(solution)/shard_map/all_to_all | solution.py:174
  7.7 0.7 %copy-start.2 = (s32[32,3]{0,1:T(4,128)S(1)}, s32[32,3]{0,1:T(4,128)}, u32[]{:S(2)}) copy-start(s32[32,3]{0,1:T(4,128)} %param.5) | copy-start | bytes 1156
  12.9 6.2 %collective-permute-start = (f32[3,4608]{1,0:T(4,128)S(1)}, f32[3,4608]{1,0:T(4,128)S(1)}, u32[]{:S(2)}, u32[]{:S(2)}) collective-permute-start(f32[3,4608]{1,0:T(4,128)S(1)} %reshape.854), channel_id=1, source_target_pairs={{1,0},{2,1},{3,2},{5,4},{6,5},{7,6},{9,8},{10,9},{11,10},{13,12},{... | collective-permute-start | bytes 165896 | tf_op jit(solution)/shard_map/ppermute | solution.py:182
  21.0 1.4 %collective-permute-start.1 = (f32[2,6,1904]{2,0,1:T(2,128)S(1)}, f32[2,6,1904]{2,0,1:T(2,128)S(1)}, u32[]{:S(2)}, u32[]{:S(2)}) collective-permute-start(f32[2,6,1904]{2,0,1:T(2,128)S(1)} %pad_maximum_fusion.10), channel_id=1, source_target_pairs={{0,16},{16,0},{1,17},{17,1},{2,18},{18,2},{3,19},{19,3},{4,20},{20... | collective-permute-start | bytes 274184 | tf_op jit(solution)/shard_map/ppermute | solution.py:31
  24.3 1.3 %collective-permute-start.2 = (f32[2,6,1632]{2,0,1:T(2,128)S(1)}, f32[2,6,1632]{2,0,1:T(2,128)S(1)}, u32[]{:S(2)}, u32[]{:S(2)}) collective-permute-start(f32[2,6,1632]{2,0,1:T(2,128)S(1)} %pad_maximum_fusion.13), channel_id=1, source_target_pairs={{0,16},{16,0},{1,17},{17,1},{2,18},{18,2},{3,19},{19,3},{4,20},{20... | collective-permute-start | bytes 235016 | tf_op jit(solution)/shard_map/ppermute | solution.py:31
  27.8 1.3 %collective-permute-start.3 = (f32[2,6,1360]{2,0,1:T(2,128)S(1)}, f32[2,6,1360]{2,0,1:T(2,128)S(1)}, u32[]{:S(2)}, u32[]{:S(2)}) collective-permute-start(f32[2,6,1360]{2,0,1:T(2,128)S(1)} %pad_maximum_fusion.14), channel_id=1, source_target_pairs={{0,16},{16,0},{1,17},{17,1},{2,18},{18,2},{3,19},{19,3},{4,20},{20... | collective-permute-start | bytes 195848 | tf_op jit(solution)/shard_map/ppermute | solution.py:31
  33.0 1.3 %collective-permute-start.4 = (f32[2,6,8,128]{3,2,1,0:T(8,128)S(1)}, f32[2,6,8,128]{3,2,1,0:T(8,128)S(1)}, u32[]{:S(2)}, u32[]{:S(2)}) collective-permute-start(f32[2,6,8,128]{3,2,1,0:T(8,128)S(1)} %pad_maximum_fusion.19), channel_id=1, source_target_pairs={{0,16},{16,0},{1,17},{17,1},{2,18},{18,2},{3,19},{19,3},{4,20},{20... | collective-permute-start | bytes 147464 | tf_op jit(solution)/shard_map/ppermute | solution.py:31

commit v20 on v17

--- a/solution.py
+++ b/solution.py
@@ -26,10 +26,6 @@
 
 
 def x_halos(block):
-    if lax.axis_size("gx") == 2:
-        pair = jnp.stack([block[:, -1], block[:, 0]])
-        got = lax.ppermute(pair, "gx", ring("gx", 1))
-        return got[0], got[1]
     xlo = lax.ppermute(block[:, -1], "gx", ring("gx", 1))
     xhi = lax.ppermute(block[:, 0], "gx", ring("gx", -1))
     return xlo, xhi

time: 32.7 us -> 33.3 us (1.018)
  starting transfers between devices: 6.03 us -> 7.67 us
  waiting for transfers between devices: 8.4 us -> 7.59 us
    ppermute x4 -> x8, starting transfers between devices: 0.73 us -> 2.37 us  [the longest x4 1.25 us: x_halos(): xlo = lax.ppermute(block[:, -1], 'gx', ring('gx', 1))]
    another operation x8 -> x0, local copies, waits for them, and re-layouts: 0.97 us -> none  [the longest x4 0.78 us: x_halos(): pair = jnp.stack([block[:, -1], block[:, 0]])]
    ppermute x4 -> x8, waiting for transfers between devices: 3.71 us -> 2.9 us  [the longest x4 1.89 us: x_halos(): xhi = lax.ppermute(block[:, 0], 'gx', ring('gx', -1))]
    slice x0 -> x3, local copies, waits for them, and re-layouts: none -> 0.69 us  [x_halos(): xhi = lax.ppermute(block[:, 0], 'gx', ring('gx', -1))]
    unnamed x8 -> x14, local copies, waits for them, and re-layouts: 0.72 us -> 0.76 us
  transfers between devices with their start and end apart: 7 -> 11, of which waited for: 6 -> 10; matrix products, arithmetic and copies ran while one was open for 10% -> 10% of each run, Pallas kernels for 0% -> 0%
where the time goes in v20:
time: 33.3 us; the launch traced here: 33.1 us
  other arithmetic  9.44 us (28%)
  starting transfers between devices  7.67 us (23%)
  waiting for transfers between devices  7.59 us (23%)
  local copies, waits for them, and re-layouts  7.04 us (21%)
  between operations  1.34 us (4%)
    ppermute x1, waiting for transfers between devices, shards(): lax.ppermute(wide[..., :count].reshape(wide.shape[0], -1), 'gz', line('gz...  3.85 us
    ppermute x1, starting transfers between devices, shards(): below_y = lax.ppermute(start[:, :, -rim_y:], 'gy', ring('gy', 1))  2.99 us
    ppermute x4, waiting for transfers between devices, x_halos(): xhi = lax.ppermute(block[:, 0], 'gx', ring('gx', -1))  1.89 us
    ppermute x1, starting transfers between devices, shards(): lax.ppermute(wide[..., :count].reshape(wide.shape[0], -1), 'gz', line('gz...  1.29 us
    ppermute x4, starting transfers between devices, x_halos(): xlo = lax.ppermute(block[:, -1], 'gx', ring('gx', 1))  1.25 us
    sub x4, other arithmetic, chem_update(): delta = shape_fn(phi_new) - shape_fn(phi_old)  1.19 us
    mul x4, other arithmetic, phase_update(): square = phi * phi  1.13 us
    ppermute x4, starting transfers between devices, x_halos(): xhi = lax.ppermute(block[:, 0], 'gx', ring('gx', -1))  1.12 us
  transfers between devices with their start and end apart: 11, of which 10 were waited for; matrix products, arithmetic and copies ran while one was open for 10% of the time, Pallas kernels for 0%

profile of v20, /device:TPU:0, one launch (start us, length us, event | category | flops | bytes accessed | tf_op | source)
XLA Modules:
  0.0 33.1 jit_solution(185237314172906941)
XLA Ops:
  0.6 0.8 %convert_bitcast_fusion = f32[1,8,8,128]{3,2,1,0:T(8,128)S(1)} fusion(s32[8,8,128]{2,1,0:T(8,128)} %param.3), kind=kLoop, calls=%fused_computation.460 | loop fusion | flops 8192 | bytes 65536 | tf_op jit(solution)/shard_map/broadcast_in_dim | solution.py:161
  1.5 3.0 %collective-permute-start = (f32[3,8,4,128]{3,2,1,0:T(4,128)S(1)}, f32[3,8,4,128]{3,2,1,0:T(4,128)S(1)}, u32[]{:S(2)}, u32[]{:S(2)}) collective-permute-start(f32[3,8,4,128]{3,2,1,0:T(4,128)S(1)} %get-tuple-element.125), channel_id=1, source_target_pairs={{0,4},{4,8},{8,12},{12,0},{1,5},{5,9},{9,13},{13,1},{2,6},{6,10},{... | collective-permute-start | bytes 147464 | tf_op jit(solution)/shard_map/ppermute | solution.py:163
  4.5 1.0 %collective-permute-start.1 = (f32[3,8,4,128]{3,2,1,0:T(4,128)S(1)}, f32[3,8,4,128]{3,2,1,0:T(4,128)S(1)}, u32[]{:S(2)}, u32[]{:S(2)}) collective-permute-start(f32[3,8,4,128]{3,2,1,0:T(4,128)S(1)} %get-tuple-element.126), channel_id=1, source_target_pairs={{0,12},{4,0},{8,4},{12,8},{1,13},{5,1},{9,5},{13,9},{2,14},{6,2},{... | collective-permute-start | bytes 147464 | tf_op jit(solution)/shard_map/ppermute | solution.py:164
  5.8 0.6 %copy-done.1 = s32[32,3]{0,1:T(4,128)S(1)} copy-done((s32[32,3]{0,1:T(4,128)S(1)}, s32[32,3]{0,1:T(4,128)}, u32[]{:S(2)}) %copy-start.1) | copy-done | bytes 408
  6.7 0.2 and_reduce_fusion
  6.8 0.2 and_reduce_fusion.1
  7.5 0.1 and_reduce_fusion.2
  7.7 0.8 %collective-permute-done.1 = f32[3,8,4,128]{3,2,1,0:T(4,128)S(1)} collective-permute-done((f32[3,8,4,128]{3,2,1,0:T(4,128)S(1)}, f32[3,8,4,128]{3,2,1,0:T(4,128)S(1)}, u32[]{:S(2)}, u32[]{:S(2)}) %collective-permute-start.1) | collective-permute-done | bytes 49184 | tf_op jit(solution)/shard_map/ppermute | solution.py:164
  8.6 0.2 reshape.852
  8.8 1.3 %collective-permute-start.2 = (f32[3,4608]{1,0:T(4,128)S(1)}, f32[3,4608]{1,0:T(4,128)S(1)}, u32[]{:S(2)}, u32[]{:S(2)}) collective-permute-start(f32[3,4608]{1,0:T(4,128)S(1)} %reshape.852), channel_id=1, source_target_pairs={{1,0},{2,1},{3,2},{5,4},{6,5},{7,6},{9,8},{10,9},{11,10},{13,12},{... | collective-permute-start | bytes 165896 | tf_op jit(solution)/shard_map/ppermute | solution.py:167
  11.2 3.9 %collective-permute-done.2 = f32[3,4608]{1,0:T(4,128)S(1)} collective-permute-done((f32[3,4608]{1,0:T(4,128)S(1)}, f32[3,4608]{1,0:T(4,128)S(1)}, u32[]{:S(2)}, u32[]{:S(2)}) %collective-permute-start.2) | collective-permute-done | bytes 55328 | tf_op jit(solution)/shard_map/ppermute | solution.py:167
  15.0 0.2 reshape.853
  16.1 0.2 concatenate.106
  16.3 0.2 maximum_select_fusion.1
  16.5 0.3 fusion.302
  16.9 0.6 %collective-permute-start.4 = (f32[6,1904]{1,0:T(8,128)S(1)}, f32[6,1904]{1,0:T(8,128)S(1)}, u32[]{:S(2)}, u32[]{:S(2)}) collective-permute-start(f32[6,1904]{1,0:T(8,128)S(1)} %bitcast.109), channel_id=1, source_target_pairs={{0,16},{16,0},{1,17},{17,1},{2,18},{18,2},{3,19},{19,3},{4,20},{20... | collective-permute-start | bytes 137096 | tf_op jit(solution)/shard_map/ppermute | solution.py:29
  17.4 0.3 fusion.301
  17.7 0.4 %collective-permute-done.3 = f32[6,1904]{1,0:T(8,128)S(1)} collective-permute-done((f32[6,1904]{1,0:T(8,128)S(1)}, f32[6,1904]{1,0:T(8,128)S(1)}, u32[]{:S(2)}, u32[]{:S(2)}) %collective-permute-start.3) | collective-permute-done | bytes 45728 | tf_op jit(solution)/shard_map/ppermute | solution.py:30
  18.1 0.2 collective-permute-done.4
  18.4 0.3 slice_multiply_fusion
  18.8 0.2 multiply_add_fusion.4
  19.1 0.2 multiply_add_fusion.3
  19.2 0.2 multiply_subtract_fusion
  19.4 0.2 fusion.47
  19.8 0.2 maximum_select_fusion.2
  20.0 0.2 fusion.304
  20.2 0.4 %collective-permute-start.5 = (f32[6,1632]{1,0:T(8,128)S(1)}, f32[6,1632]{1,0:T(8,128)S(1)}, u32[]{:S(2)}, u32[]{:S(2)}) collective-permute-start(f32[6,1632]{1,0:T(8,128)S(1)} %bitcast.110), channel_id=1, source_target_pairs={{0,16},{16,0},{1,17},{17,1},{2,18},{18,2},{3,19},{19,3},{4,20},{20... | collective-permute-start | bytes 117512 | tf_op jit(solution)/shard_map/ppermute | solution.py:30
  20.6 0.2 collective-permute-start.6
  20.8 0.2 fusion.303
  21.0 0.5 %collective-permute-done.5 = f32[6,1632]{1,0:T(8,128)S(1)} collective-permute-done((f32[6,1632]{1,0:T(8,128)S(1)}, f32[6,1632]{1,0:T(8,128)S(1)}, u32[]{:S(2)}, u32[]{:S(2)}) %collective-permute-start.5) | collective-permute-done | bytes 39200 | tf_op jit(solution)/shard_map/ppermute | solution.py:30
  21.5 0.3 collective-permute-done.6
  21.9 0.3 slice_multiply_fusion.1
  22.3 0.2 multiply_add_fusion.9
  22.5 0.2 multiply_add_fusion.8
  22.7 0.1 multiply_subtract_fusion.1
  22.8 0.2 fusion.60
  23.2 0.1 fusion.307
  23.5 0.2 maximum_select_fusion.4
  23.6 0.2 fusion.305
  23.9 0.2 collective-permute-start.7
  24.1 0.3 collective-permute-start.8
  24.4 0.2 fusion.306
  24.7 0.5 %collective-permute-done.7 = f32[6,1360]{1,0:T(8,128)S(1)} collective-permute-done((f32[6,1360]{1,0:T(8,128)S(1)}, f32[6,1360]{1,0:T(8,128)S(1)}, u32[]{:S(2)}, u32[]{:S(2)}) %collective-permute-start.7) | collective-permute-done | bytes 32672 | tf_op jit(solution)/shard_map/ppermute | solution.py:30
  25.2 0.2 collective-permute-done.8
  25.4 0.3 slice_multiply_fusion.2
  25.8 0.2 multiply_add_fusion.14
  25.9 0.2 fusion.194
  26.2 0.4 %concatenate.125 = f32[4,8,10,136]{3,2,1,0:T(8,128)S(1)} reshape(f32[4,8,1360]{2,1,0:T(8,128)S(1)} %get-tuple-element.12) | data formatting | bytes 348160 | tf_op jit(solution)/shard_map/concatenate | solution.py:148
  26.6 0.2 fusion.73
  27.3 0.1 fusion.13
  27.5 0.7 %concatenate.122 = f32[6,8,10,136]{3,2,1,0:T(8,128)S(1)} reshape(f32[6,8,1360]{2,1,0:T(8,128)S(1)} %get-tuple-element.119) | data formatting | bytes 522240 | tf_op jit(solution)/shard_map/concatenate | solution.py:186
  28.2 0.7 %concatenate.124 = f32[6,8,10,136]{3,2,1,0:T(8,128)S(1)} reshape(f32[6,8,1360]{2,1,0:T(8,128)S(1)} %get-tuple-element.118) | data formatting | bytes 522240 | tf_op jit(solution)/shard_map/concatenate | solution.py:183
  28.8 0.3 fusion
  29.2 0.4 %collective-permute-start.9 = (f32[6,8,128]{2,1,0:T(8,128)S(1)}, f32[6,8,128]{2,1,0:T(8,128)S(1)}, u32[]{:S(2)}, u32[]{:S(2)}) collective-permute-start(f32[6,8,128]{2,1,0:T(8,128)S(1)} %get-tuple-element.56), channel_id=1, source_target_pairs={{0,16},{16,0},{1,17},{17,1},{2,18},{18,2},{3,19},{19,3},{4,20},{20... | collective-permute-start | bytes 73736 | tf_op jit(solution)/shard_map/ppermute | solution.py:30
  29.6 0.2 collective-permute-start.10
  29.8 0.2 fusion.300
  29.9 0.5 %collective-permute-done.9 = f32[6,8,128]{2,1,0:T(8,128)S(1)} collective-permute-done((f32[6,8,128]{2,1,0:T(8,128)S(1)}, f32[6,8,128]{2,1,0:T(8,128)S(1)}, u32[]{:S(2)}, u32[]{:S(2)}) %collective-permute-start.9) | collective-permute-done | bytes 24608 | tf_op jit(solution)/shard_map/ppermute | solution.py:30
  30.5 0.3 collective-permute-done.10
  30.8 0.2 slice_multiply_fusion.3
  31.1 0.1 multiply_add_fusion.19
  31.3 0.1 fusion.236
  31.4 0.8 %multiply_subtract_fusion.3 = (f32[4,8,8,128]{3,2,1,0:T(8,128)S(1)}, f32[4,8,8,128]{3,2,1,0:T(8,128)}) fusion(f32[6,8,10,136]{3,2,1,0:T(8,128)S(1)} %fusion, f32[1,8,8,128]{3,2,1,0:T(8,128)S(1)} %get-tuple-element.49, f32[1,8,8,128]{3,2,1,0:T(8,128)S(1)} %get-tuple-element.50, f32[1,8,8,128]{3,2,1,0:T(8,128)S(1)} %get-tuple-element.51, ...), kind=kLoop, calls=%fused_computation.118 | loop fusion | flops 425984 | bytes 525312 | tf_op jit(solution)/shard_map/sub | solution.py:88
  32.2 0.2 fusion.86
  32.4 0.6 %pad_maximum_fusion.14 = f32[2,8,8,128]{3,2,1,0:T(8,128)} fusion(f32[1,8,8,128]{3,2,1,0:T(8,128)S(1)} %get-tuple-element.41, f32[1,8,8,128]{3,2,1,0:T(8,128)S(1)} %get-tuple-element.40), kind=kLoop, calls=%fused_computation.203 | loop fusion | flops 16384 | bytes 131072 | tf_op jit(solution)/shard_map/stack | solution.py:98
  (94 shorter events, 4.8 us)
Async XLA Ops:
  0.6 0.8 %copy-start = (f32[2,8,8,128]{3,2,1,0:T(8,128)S(1)}, f32[2,8,8,128]{3,2,1,0:T(8,128)}, u32[]{:S(2)}) copy-start(f32[2,8,8,128]{3,2,1,0:T(8,128)} %param.4) | copy-start | bytes 196612
  1.5 6.2 %collective-permute-start = (f32[3,8,4,128]{3,2,1,0:T(4,128)S(1)}, f32[3,8,4,128]{3,2,1,0:T(4,128)S(1)}, u32[]{:S(2)}, u32[]{:S(2)}) collective-permute-start(f32[3,8,4,128]{3,2,1,0:T(4,128)S(1)} %get-tuple-element.125), channel_id=1, source_target_pairs={{0,4},{4,8},{8,12},{12,0},{1,5},{5,9},{9,13},{13,1},{2,6},{6,10},{... | collective-permute-start | bytes 147464 | tf_op jit(solution)/shard_map/ppermute | solution.py:163
  4.5 4.1 %collective-permute-start.1 = (f32[3,8,4,128]{3,2,1,0:T(4,128)S(1)}, f32[3,8,4,128]{3,2,1,0:T(4,128)S(1)}, u32[]{:S(2)}, u32[]{:S(2)}) collective-permute-start(f32[3,8,4,128]{3,2,1,0:T(4,128)S(1)} %get-tuple-element.126), channel_id=1, source_target_pairs={{0,12},{4,0},{8,4},{12,8},{1,13},{5,1},{9,5},{13,9},{2,14},{6,2},{... | collective-permute-start | bytes 147464 | tf_op jit(solution)/shard_map/ppermute | solution.py:164
  5.7 0.7 %copy-start.1 = (s32[32,3]{0,1:T(4,128)S(1)}, s32[32,3]{0,1:T(4,128)}, u32[]{:S(2)}) copy-start(s32[32,3]{0,1:T(4,128)} %param.5) | copy-start | bytes 1156
  8.8 6.2 %collective-permute-start.2 = (f32[3,4608]{1,0:T(4,128)S(1)}, f32[3,4608]{1,0:T(4,128)S(1)}, u32[]{:S(2)}, u32[]{:S(2)}) collective-permute-start(f32[3,4608]{1,0:T(4,128)S(1)} %reshape.852), channel_id=1, source_target_pairs={{1,0},{2,1},{3,2},{5,4},{6,5},{7,6},{9,8},{10,9},{11,10},{13,12},{... | collective-permute-start | bytes 165896 | tf_op jit(solution)/shard_map/ppermute | solution.py:167
  16.8 1.3 %collective-permute-start.3 = (f32[6,1904]{1,0:T(8,128)S(1)}, f32[6,1904]{1,0:T(8,128)S(1)}, u32[]{:S(2)}, u32[]{:S(2)}) collective-permute-start(f32[6,1904]{1,0:T(8,128)S(1)} %bitcast.108), channel_id=1, source_target_pairs={{0,16},{16,0},{1,17},{17,1},{2,18},{18,2},{3,19},{19,3},{4,20},{20... | collective-permute-start | bytes 137096 | tf_op jit(solution)/shard_map/ppermute | solution.py:30
  16.9 1.5 %collective-permute-start.4 = (f32[6,1904]{1,0:T(8,128)S(1)}, f32[6,1904]{1,0:T(8,128)S(1)}, u32[]{:S(2)}, u32[]{:S(2)}) collective-permute-start(f32[6,1904]{1,0:T(8,128)S(1)} %bitcast.109), channel_id=1, source_target_pairs={{0,16},{16,0},{1,17},{17,1},{2,18},{18,2},{3,19},{19,3},{4,20},{20... | collective-permute-start | bytes 137096 | tf_op jit(solution)/shard_map/ppermute | solution.py:29
  20.2 1.3 %collective-permute-start.5 = (f32[6,1632]{1,0:T(8,128)S(1)}, f32[6,1632]{1,0:T(8,128)S(1)}, u32[]{:S(2)}, u32[]{:S(2)}) collective-permute-start(f32[6,1632]{1,0:T(8,128)S(1)} %bitcast.110), channel_id=1, source_target_pairs={{0,16},{16,0},{1,17},{17,1},{2,18},{18,2},{3,19},{19,3},{4,20},{20... | collective-permute-start | bytes 117512 | tf_op jit(solution)/shard_map/ppermute | solution.py:30
  20.6 1.2 %collective-permute-start.6 = (f32[6,1632]{1,0:T(8,128)S(1)}, f32[6,1632]{1,0:T(8,128)S(1)}, u32[]{:S(2)}, u32[]{:S(2)}) collective-permute-start(f32[6,1632]{1,0:T(8,128)S(1)} %bitcast.111), channel_id=1, source_target_pairs={{0,16},{16,0},{1,17},{17,1},{2,18},{18,2},{3,19},{19,3},{4,20},{20... | collective-permute-start | bytes 117512 | tf_op jit(solution)/shard_map/ppermute | solution.py:29
  23.9 1.3 %collective-permute-start.7 = (f32[6,1360]{1,0:T(8,128)S(1)}, f32[6,1360]{1,0:T(8,128)S(1)}, u32[]{:S(2)}, u32[]{:S(2)}) collective-permute-start(f32[6,1360]{1,0:T(8,128)S(1)} %bitcast.112), channel_id=1, source_target_pairs={{0,16},{16,0},{1,17},{17,1},{2,18},{18,2},{3,19},{19,3},{4,20},{20... | collective-permute-start | bytes 97928 | tf_op jit(solution)/shard_map/ppermute | solution.py:30
  24.1 1.2 %collective-permute-start.8 = (f32[6,1360]{1,0:T(8,128)S(1)}, f32[6,1360]{1,0:T(8,128)S(1)}, u32[]{:S(2)}, u32[]{:S(2)}) collective-permute-start(f32[6,1360]{1,0:T(8,128)S(1)} %bitcast.113), channel_id=1, source_target_pairs={{0,16},{16,0},{1,17},{17,1},{2,18},{18,2},{3,19},{19,3},{4,20},{20... | collective-permute-start | bytes 97928 | tf_op jit(solution)/shard_map/ppermute | solution.py:29
  29.2 1.3 %collective-permute-start.9 = (f32[6,8,128]{2,1,0:T(8,128)S(1)}, f32[6,8,128]{2,1,0:T(8,128)S(1)}, u32[]{:S(2)}, u32[]{:S(2)}) collective-permute-start(f32[6,8,128]{2,1,0:T(8,128)S(1)} %get-tuple-element.56), channel_id=1, source_target_pairs={{0,16},{16,0},{1,17},{17,1},{2,18},{18,2},{3,19},{19,3},{4,20},{20... | collective-permute-start | bytes 73736 | tf_op jit(solution)/shard_map/ppermute | solution.py:30
  29.6 1.2 %collective-permute-start.10 = (f32[6,8,128]{2,1,0:T(8,128)S(1)}, f32[6,8,128]{2,1,0:T(8,128)S(1)}, u32[]{:S(2)}, u32[]{:S(2)}) collective-permute-start(f32[6,8,128]{2,1,0:T(8,128)S(1)} %get-tuple-element.57), channel_id=1, source_target_pairs={{0,16},{16,0},{1,17},{17,1},{2,18},{18,2},{3,19},{19,3},{4,20},{20... | collective-permute-start | bytes 73736 | tf_op jit(solution)/shard_map/ppermute | solution.py:29
